TPU v7x, 32 devices: a whole 2x2x4 slice. The times are simulated.
32 devices in a mesh: azim: 4 (over y, x), rad: 4 (over z), hgt: 2 (over core).
Axes of the slice: x: 2, y: 2, z: 4, core: 2. Of those that a mesh axis runs over, the one named last changes fastest.
Arguments:
- density: float32 [8, 64, 1024], P('hgt', 'azim', 'rad'), may hold values from 0.2 to 0.8
- labels: int32 [8, 64, 1024], P('hgt', 'azim', 'rad'), may hold values from 0 to 4
- observed: float32 [8, 64, 1024], P('hgt', 'azim', 'rad'), may hold values from 0 to 1
- measured: int32 [8, 64, 1024], P('hgt', 'azim', 'rad'), may hold values 0 or 1
Outputs:
- final_density: float32 [8, 64, 1024], P('hgt', 'azim', 'rad')
- density_gradient: float32 [8, 64, 1024], P('hgt', 'azim', 'rad')
- grain_gradient: float32 [4, 8, 64, 1024], P(None, 'hgt', 'azim', 'rad')
All inputs are finite; a program needn't handle non-finite values. No bound on the sum of `measured` on one device may be relied on, other than what follows from the above.
Results may differ from a plain program's by a relative error of at most 0.0001.
Values sent between devices are 32-bit elements; how exact they have to be, the bound alone decides.
No kernel may reach another device: no remote copies, remote signals or barrier semaphores. Data moves between devices by JAX's collectives and lax.ppermute only.
A program may use at most 64 MiB of HBM per device.

v0:
```python
import jax
import jax.numpy as jnp
from jax import lax
from jax.sharding import PartitionSpec as P

STEPS = 3
GRAINS = 4


bulk_weight = 16.0
grain_weight = 1.0
cahn_step = 0.005
allen_step = 0.05
cahn_gradient = 1.0
allen_gradient = 1.0
full_turn = 6.283185307179586

HALO = 4 * STEPS


def halo_exchange(block, axis, dim, width, cyclic):
    peers, length = (lax.axis_size(axis), block.shape[dim])
    up = [(i, (i + 1) % peers) for i in range(peers) if cyclic or i + 1 < peers]
    down = [(j, i) for i, j in up]
    last = lax.slice_in_dim(block, length - width, length, axis=dim)
    leading = lax.slice_in_dim(block, 0, width, axis=dim)
    before = lax.ppermute(last, axis, up)
    after = lax.ppermute(leading, axis, down)
    return jnp.concatenate([before, block, after], axis=dim)


def gather_axis(block, axis, dim):
    peers = lax.axis_size(axis)
    if peers == 1:
        return block
    own = lax.axis_index(axis)
    parts = [block]
    for shift in range(1, peers):
        parts.append(lax.ppermute(block, axis, [(i, (i + shift) % peers) for i in range(peers)]))
    stacked = jnp.stack(parts)
    order = (own - jnp.arange(peers, dtype=jnp.int32)) % peers
    ordered = jnp.take(stacked, order, axis=0)
    ordered = jnp.moveaxis(ordered, 0, dim)
    shape = list(block.shape)
    shape[dim] = shape[dim] * peers
    return ordered.reshape(shape)


def chip_window(block, width):
    peers, own, rad_peers = (lax.axis_size("hgt"), lax.axis_index("hgt"), lax.axis_size("rad"))
    cols = block.shape[-1]
    part = cols // peers
    piece = jnp.where(own == 0, block[..., :width], block[..., cols - width :])
    pairs = []
    for r in range(rad_peers - 1):
        pairs.append((r * peers + peers - 1, (r + 1) * peers))
        pairs.append(((r + 1) * peers, r * peers + peers - 1))
    received = lax.ppermute(piece, ("rad", "hgt"), pairs)
    padded = jnp.concatenate([received, block, received], axis=-1)
    return lax.dynamic_slice_in_dim(padded, own * part, part + 2 * width, axis=padded.ndim - 1)


def scatter_heights(x, height_rows):
    peers, own = (lax.axis_size("hgt"), lax.axis_index("hgt"))
    parts = []
    for shift in range(peers):
        dest = (own + shift) % peers
        piece = lax.dynamic_slice_in_dim(x, dest * height_rows, height_rows, axis=1)
        if shift:
            piece = lax.ppermute(piece, "hgt", [(i, (i + shift) % peers) for i in range(peers)])
        parts.append(piece)
    stacked = jnp.stack(parts)
    order = (own - jnp.arange(peers, dtype=jnp.int32)) % peers
    ordered = jnp.moveaxis(jnp.take(stacked, order, axis=0), 0, -2)
    shape = ordered.shape
    return ordered.reshape(shape[:-2] + (shape[-2] * shape[-1],))


def crop(x, width, new_width):
    cut = width - new_width
    if cut == 0:
        return x
    return x[..., cut : x.shape[-2] - cut, cut : x.shape[-1] - cut]


def radial_mask(width, geometry):
    rad_start, total_hgt, total_azim, total_rad, cols = geometry
    rad_index = rad_start - width + jnp.arange(cols + 2 * width, dtype=jnp.int32)
    return (rad_index >= 0) & (rad_index < total_rad)


def in_domain(x, width, geometry):
    return jnp.where(radial_mask(width, geometry), x, 0.0)


def laplace(x, width, geometry, transpose):
    rad_start, total_hgt, total_azim, total_rad, cols = geometry
    margin = width - 1
    height_rows = x.shape[-3]
    radius_rows = x.shape[-1] - 2
    rad_index_all = rad_start - margin - 1 + jnp.arange(radius_rows + 2, dtype=jnp.int32)
    radius_all = total_azim / full_turn + rad_index_all.astype(jnp.float32) + 0.5
    rad_index = rad_index_all[1:-1]
    radius = radius_all[1:-1]
    outer_face = (radius + 0.5) * (rad_index < total_rad - 1).astype(jnp.float32)
    inner_face = (radius - 0.5) * (rad_index > 0).astype(jnp.float32)
    hgt_index = jnp.arange(height_rows, dtype=jnp.int32)
    upper_face = (hgt_index < total_hgt - 1).astype(jnp.float32)[:, None, None]
    lower_face = (hgt_index > 0).astype(jnp.float32)[:, None, None]
    leading = x.ndim - 3
    padded = jnp.pad(x, [(0, 0)] * leading + [(1, 1), (0, 0), (0, 0)])
    center = padded[..., 1:-1, 1:-1, 1:-1]
    if transpose:
        scaled = padded[..., 1:-1, 1:-1, :] / radius_all
        radial = outer_face * (scaled[..., 2:] - scaled[..., 1:-1]) - inner_face * (
            scaled[..., 1:-1] - scaled[..., :-2]
        )
    else:
        outward = padded[..., 1:-1, 1:-1, 2:]
        inward = padded[..., 1:-1, 1:-1, :-2]
        radial = (outer_face * (outward - center) - inner_face * (center - inward)) / radius
    arc_length = radius * (full_turn / total_azim)
    azimuthal = (padded[..., 1:-1, 2:, 1:-1] + padded[..., 1:-1, :-2, 1:-1] - 2.0 * center) / (
        arc_length * arc_length
    )
    vertical = upper_face * (padded[..., 2:, 1:-1, 1:-1] - center) + lower_face * (
        padded[..., :-2, 1:-1, 1:-1] - center
    )
    return radial + azimuthal + vertical


def chemical(density, grains):
    square_sum = jnp.sum(grains * grains, axis=0)
    cube_sum = jnp.sum(grains * grains * grains, axis=0)
    bulk_drive = 2.0 * bulk_weight * density * (1.0 - density) * (
        1.0 - 2.0 * density
    ) + grain_weight * (2.0 * density - 6.0 * square_sum + 4.0 * cube_sum)
    grain_drive = (
        12.0
        * grain_weight
        * (grains * (1.0 - density) - grains * grains * (2.0 - density) + grains * square_sum)
    )
    return (bulk_drive, grain_drive)


def shards(density, labels, observed, measured):
    height_rows, azim_rows, radius_rows = density.shape
    total_hgt = height_rows * lax.axis_size("hgt")
    part = radius_rows // lax.axis_size("hgt")
    geometry = (
        lax.axis_index("rad") * radius_rows + lax.axis_index("hgt") * part,
        total_hgt,
        azim_rows * lax.axis_size("azim"),
        radius_rows * lax.axis_size("rad"),
        part,
    )
    target = jnp.where(measured != 0, observed, -1.0)
    packed = jnp.stack([density, labels.astype(jnp.float32), target])
    packed = gather_axis(packed, "hgt", 1)
    packed = chip_window(packed, HALO)
    packed = halo_exchange(packed, "azim", 2, HALO, True)
    density, grain_label, target = packed[0], packed[1], packed[2]

    width = HALO
    grains = (
        grain_label[None] == jnp.arange(GRAINS, dtype=jnp.float32)[:, None, None, None]
    ).astype(jnp.float32)
    density = in_domain(density, width, geometry)
    grains = in_domain(grains, width, geometry)
    d_width, g_width = width, width
    history = []
    for moment in range(STEPS):
        history.append((density, d_width, grains, g_width))
        both = min(d_width, g_width)
        bulk_drive, grain_drive = chemical(crop(density, d_width, both), crop(grains, g_width, both))
        pot_width = min(d_width - 1, both)
        potential = crop(bulk_drive, both, pot_width) - cahn_gradient * crop(
            laplace(density, d_width, geometry, False), d_width - 1, pot_width
        )
        new_d_width = pot_width - 1
        flux_term = laplace(potential, pot_width, geometry, False)
        new_density = crop(density, d_width, new_d_width) + cahn_step * flux_term
        if moment + 1 < STEPS:
            new_g_width = min(g_width - 1, both)
            grain_spread = crop(laplace(grains, g_width, geometry, False), g_width - 1, new_g_width)
            new_grains = crop(grains, g_width, new_g_width) - allen_step * (
                crop(grain_drive, both, new_g_width) - allen_gradient * grain_spread
            )
            grains, g_width = in_domain(new_grains, new_g_width, geometry), new_g_width
        density, d_width = in_domain(new_density, new_d_width, geometry), new_d_width

    target = crop(target, width, d_width)
    costate = in_domain(jnp.where(target >= 0.0, density - target, 0.0), d_width, geometry)
    c_width = d_width
    last_density = crop(density, d_width, 0)
    cograins = jnp.zeros((GRAINS,) + costate.shape, jnp.float32)
    cg_width = c_width
    for moment in range(STEPS - 1, -1, -1):
        fields_density, fd_width, fields_grains, fg_width = history[moment]
        copotential = cahn_step * laplace(costate, c_width, geometry, True)
        nu_width = c_width - 1
        grain_spread = laplace(cograins, cg_width, geometry, True)
        point = min(nu_width, cg_width, fd_width, fg_width)
        unused, pullback = jax.vjp(
            chemical, crop(fields_density, fd_width, point), crop(fields_grains, fg_width, point)
        )
        pull_density, pull_grains = pullback(
            (crop(copotential, nu_width, point), -allen_step * crop(cograins, cg_width, point))
        )
        reaction = laplace(in_domain(copotential, nu_width, geometry), nu_width, geometry, True)
        new_c_width = nu_width - 1
        new_costate = (
            crop(costate, c_width, new_c_width)
            + crop(pull_density, point, new_c_width)
            - cahn_gradient * reaction
        )
        new_cg_width = min(cg_width - 1, point)
        new_cograins = (
            crop(cograins, cg_width, new_cg_width)
            + crop(pull_grains, point, new_cg_width)
            + allen_step * allen_gradient * crop(grain_spread, cg_width - 1, new_cg_width)
        )
        costate, c_width = in_domain(new_costate, new_c_width, geometry), new_c_width
        cograins, cg_width = in_domain(new_cograins, new_cg_width, geometry), new_cg_width

    costate = crop(costate, c_width, 0)
    cograins = crop(cograins, cg_width, 0)
    result = scatter_heights(
        jnp.concatenate([last_density[None], costate[None], cograins], axis=0), height_rows
    )
    return (result[0], result[1], result[2:])


def solution(mesh):
    in_specs = (
        P("hgt", "azim", "rad"),
        P("hgt", "azim", "rad"),
        P("hgt", "azim", "rad"),
        P("hgt", "azim", "rad"),
    )
    out_specs = (P("hgt", "azim", "rad"), P("hgt", "azim", "rad"), P(None, "hgt", "azim", "rad"))
    return jax.shard_map(shards, mesh=mesh, in_specs=in_specs, out_specs=out_specs, check_vma=False)
```

profile of v0, /device:TPU:9, one launch (start us, length us, event | category | flops | bytes accessed | tf_op | source)
XLA Modules:
  0.0 66.5 jit_solution(2579275380759281646)
XLA Ops:
  0.6 0.8 %convert_bitcast_fusion = f32[1,4,16,256]{3,2,1,0:T(8,128)S(1)} fusion(s32[4,16,256]{2,1,0:T(8,128)} %param.5), kind=kLoop, calls=%fused_computation.509 | loop fusion | flops 16384 | bytes 131072 | tf_op jit(solution)/shard_map/stack | solution.py:158
  1.5 0.9 %select_bitcast_fusion.2 = f32[1,4,16,256]{3,2,1,0:T(8,128)S(1)} fusion(f32[4,16,256]{2,1,0:T(8,128)} %param.6, s32[4,16,256]{2,1,0:T(8,128)} %param.7), kind=kLoop, calls=%fused_computation.508 | loop fusion | flops 32768 | bytes 196608 | tf_op jit(solution)/shard_map/stack | solution.py:158
  2.4 0.9 %fusion.301 = (f32[1,3,4,16,256]{4,3,2,1,0:T(8,128)S(1)}, f32[3,4,16,256]{3,2,1,0:T(8,128)S(1)}) fusion(f32[1,4,16,256]{3,2,1,0:T(8,128)S(1)} %select_bitcast_fusion.2, f32[1,4,16,256]{3,2,1,0:T(8,128)S(1)} %convert_bitcast_fusion, f32[1,4,16,256]{3,2,1,0:T(8,128)} %bitcast.41), kind=kLoop, calls=%fused_computation.607 | loop fusion | flops 98304 | bytes 589824 | tf_op jit(solution)/shard_map/stack | solution.py:40
  3.2 0.7 %collective-permute-start = (f32[3,4,16,256]{3,2,1,0:T(8,128)S(1)}, f32[3,4,16,256]{3,2,1,0:T(8,128)S(1)}, u32[]{:S(2)}, u32[]{:S(2)}) collective-permute-start(f32[3,4,16,256]{3,2,1,0:T(8,128)S(1)} %get-tuple-element.98), channel_id=1, source_target_pairs={{0,1},{1,0},{2,3},{3,2},{4,5},{5,4},{6,7},{7,6},{8,9},{9,8},{10,11... | collective-permute-start | bytes 589832 | tf_op jit(solution)/shard_map/ppermute | solution.py:39
  5.2 0.1 divide_add_fusion
  5.5 0.6 gather_fusion
  6.0 0.1 select_bitcast_fusion.1
  6.2 0.1 slice_select_fusion.1
  6.3 3.1 %collective-permute-start.1 = (f32[3,8,16,12]{3,2,1,0:T(8,128)S(1)}, f32[3,8,16,12]{3,2,1,0:T(8,128)S(1)}, u32[]{:S(2)}, u32[]{:S(2)}) collective-permute-start(f32[3,8,16,12]{3,2,1,0:T(8,128)S(1)} %slice_select_fusion.1), channel_id=1, source_target_pairs={{1,2},{2,1},{3,4},{4,3},{5,6},{6,5},{9,10},{10,9},{11,12},{12,11},... | collective-permute-start | bytes 55304 | tf_op jit(solution)/shard_map/ppermute | solution.py:58
  10.0 3.3 %collective-permute-done.1 = f32[3,8,16,12]{3,2,1,0:T(8,128)S(1)} collective-permute-done((f32[3,8,16,12]{3,2,1,0:T(8,128)S(1)}, f32[3,8,16,12]{3,2,1,0:T(8,128)S(1)}, u32[]{:S(2)}, u32[]{:S(2)}) %collective-permute-start.1) | collective-permute-done | bytes 18464 | tf_op jit(solution)/shard_map/ppermute | solution.py:58
  13.3 0.3 fusion.73
  13.7 2.2 %collective-permute-start.3 = (f32[3,8,12,152]{3,2,1,0:T(8,128)S(1)}, f32[3,8,12,152]{3,2,1,0:T(8,128)S(1)}, u32[]{:S(2)}, u32[]{:S(2)}) collective-permute-start(f32[3,8,12,152]{3,2,1,0:T(8,128)S(1)} %get-tuple-element.65), channel_id=1, source_target_pairs={{8,0},{16,8},{24,16},{0,24},{9,1},{17,9},{25,17},{1,25},{10,2},{18... | collective-permute-start | bytes 525320 | tf_op jit(solution)/shard_map/ppermute | solution.py:28
  15.9 0.1 fusion.294
  16.0 8.5 %collective-permute-done.3 = f32[3,8,12,152]{3,2,1,0:T(8,128)S(1)} collective-permute-done((f32[3,8,12,152]{3,2,1,0:T(8,128)S(1)}, f32[3,8,12,152]{3,2,1,0:T(8,128)S(1)}, u32[]{:S(2)}, u32[]{:S(2)}) %collective-permute-start.3) | collective-permute-done | bytes 175136 | tf_op jit(solution)/shard_map/ppermute | solution.py:28
  24.5 9.4 %collective-permute-done.2 = f32[3,8,12,152]{3,2,1,0:T(8,128)S(1)} collective-permute-done((f32[3,8,12,152]{3,2,1,0:T(8,128)S(1)}, f32[3,8,12,152]{3,2,1,0:T(8,128)S(1)}, u32[]{:S(2)}, u32[]{:S(2)}) %collective-permute-start.2) | collective-permute-done | bytes 175136 | tf_op jit(solution)/shard_map/ppermute | solution.py:27
  33.8 0.1 pad_maximum_fusion
  34.0 0.1 subtract_bitcast_fusion.1
  34.1 0.4 multiply_reduce_fusion.2
  34.5 0.2 slice.920
  34.7 0.2 slice.918
  34.8 0.8 %fusion.78 = (f32[8,38,150]{2,1,0:T(8,128)S(1)}, f32[8,38,150]{2,1,0:T(8,128)S(1)}) fusion(f32[8,40,152]{2,1,0:T(8,128)S(1)} %bitcast_select_fusion, f32[8,40,152]{2,1,0:T(8,128)S(1)} %get-tuple-element.16, f32[8]{0:T(128)S(1)} %get-tuple-element.141, f32[8]{0:T(128)S(1)} %get-tuple-element.142, f32[150]{0:T(256)S(1)} %get-tuple-element.137, ...), kind=kLoop, calls=%fused_computation.161 | loop fusion | flops 1276800 | bytes 2991360 | tf_op jit(solution)/shard_map/sub | solution.py:177
  35.6 2.8 %fusion.7 = f32[4,8,38,150]{3,2,1,0:T(8,128)S(1)} fusion(f32[4,8,40,152]{3,2,1,0:T(8,128)S(1)} %get-tuple-element.67, f32[4,8,40,152]{3,2,1,0:T(8,128)S(1)} %get-tuple-element.66, f32[8,38,150]{2,1,0:T(8,128)S(1)} %get-tuple-element.81, f32[8,38,150]{2,1,0:T(8,128)S(1)} %slice.920, f32[8,38,150]{2,1,0:T(8,128)S(1)} %slice.918, f32[8]{0:T(128)S(1)} %get-tuple-element.141, ...), kind=kLoop, calls=%fused_computation.24 | loop fusion | flops 4924800 | bytes 10893312 | tf_op jit(solution)/shard_map/jit(_where)/select_n | solution.py:93
  38.4 0.5 fusion.20
  38.9 0.7 %broadcast_subtract_fusion = (f32[8,36,148]{2,1,0:T(8,128)S(1)}, f32[8,36,148]{2,1,0:T(8,128)S(1)}) fusion(f32[8]{0:T(128)S(1)} %get-tuple-element.141, f32[8,38,150]{2,1,0:T(8,128)S(1)} %get-tuple-element.80, f32[8]{0:T(128)S(1)} %get-tuple-element.142, f32[148]{0:T(256)S(1)} %get-tuple-element.135, f32[148]{0:T(256)S(1)} %get-tuple-element.136, ...), kind=kLoop, calls=%fused_computation.445 | loop fusion | flops 895104 | bytes 2640384 | tf_op jit(solution)/shard_map/sub | solution.py:135
  39.6 2.7 %fusion.17 = f32[4,8,36,148]{3,2,1,0:T(8,128)S(1)} fusion(f32[4,8,38,150]{3,2,1,0:T(8,128)S(1)} %fusion.7, f32[8]{0:T(128)S(1)} %get-tuple-element.141, f32[8]{0:T(128)S(1)} %get-tuple-element.142, f32[148]{0:T(256)S(1)} %get-tuple-element.135, f32[148]{0:T(256)S(1)} %get-tuple-element.136, f32[148]{0:T(256)S(1)} %get-tuple-element.118, ...), kind=kLoop, calls=%fused_computation.34 | loop fusion | flops 4773888 | bytes 9534976 | tf_op jit(solution)/shard_map/jit(_where)/select_n | solution.py:93
  42.3 0.4 multiply_reduce_fusion.1
  42.7 0.4 multiply_reduce_fusion.4
  43.1 0.2 fusion.298
  43.3 0.9 %fusion.94 = f32[8,34,146]{2,1,0:T(8,128)S(1)} fusion(f32[8,36,148]{2,1,0:T(8,128)S(1)} %get-tuple-element.30, f32[8,36,148]{2,1,0:T(8,128)S(1)} %get-tuple-element.14, f32[8,36,148]{2,1,0:T(8,128)S(1)} %get-tuple-element.29, f32[8,36,148]{2,1,0:T(8,128)S(1)} %get-tuple-element.15, f32[8]{0:T(128)S(1)} %get-tuple-element.141, f32[8]{0:T(128)S(1)} %get-tuple-element.142, ...), kind=kLoop, calls=%fused_computation.177 | loop fusion | flops 1072224 | bytes 3113088 | tf_op jit(solution)/shard_map/sub | solution.py:177
  44.2 0.6 fusion.156
  44.7 0.2 fusion.300
  44.9 0.6 fusion.129
  45.6 0.6 select_select_fusion
  46.3 0.6 broadcast_multiply_fusion.3
  46.8 0.1 broadcast_select_fusion
  46.9 0.8 %fusion.45 = f32[4,8,26,138]{3,2,1,0:T(8,128)S(1)} fusion(f32[4,8,36,148]{3,2,1,0:T(8,128)S(1)} %fusion.17, f32[8]{0:T(128)S(1)} %fusion.294, f32[138]{0:T(256)S(1)} %get-tuple-element.26, f32[8,26,138]{2,1,0:T(8,128)S(1)} %get-tuple-element.90, f32[8,26,138]{2,1,0:T(8,128)S(1)} %get-tuple-element.89, f32[8,26,138]{2,1,0:T(8,128)S(1)} %get-tuple-element.83, ...), kind=kLoop, calls=%fused_computation.78 | loop fusion | flops 2066688 | bytes 1493330 | tf_op jit(solution)/shard_map/jit(_where)/select_n | solution.py:93
  47.7 0.5 multiply_reduce_fusion.8
  48.2 1.1 %fusion.307 = (f32[4,8,24,136]{3,2,1,0:T(8,128)S(1)}, f32[4,8,24,136]{3,2,1,0:T(8,128)S(1)}, f32[4,8,24,136]{3,2,1,0:T(8,128)S(1)}, f32[4,8,24,136]{3,2,1,0:T(8,128)S(1)}, f32[4,8,24,136]{3,2,1,0:T(8,128)S(1)}) fusion(f32[4,8,26,138]{3,2,1,0:T(8,128)S(1)} %fusion.45), kind=kLoop, calls=%fused_computation.608 | loop fusion | bytes 5496832 | tf_op jit(solution)/shard_map/slice | solution.py:112
  49.2 0.1 slice_divide_fusion.1
  49.3 0.2 fusion.299
  49.6 0.9 %fusion.219 = f32[8,24,136]{2,1,0:T(8,128)S(1)} fusion(f32[8,26,138]{2,1,0:T(8,128)S(1)} %get-tuple-element.88, f32[8,24,138]{2,1,0:T(8,128)S(1)} %slice_divide_fusion.7, f32[8,26,138]{2,1,0:T(8,128)S(1)} %get-tuple-element.84, f32[8,26,138]{2,1,0:T(8,128)S(1)} %get-tuple-element.87, f32[8,26,138]{2,1,0:T(8,128)S(1)} %get-tuple-element.23, ...), kind=kLoop, calls=%fused_computation.361 | loop fusion | flops 940032 | bytes 3320320 | tf_op jit(solution)/shard_map/jit(_where)/select_n | solution.py:93
  50.5 0.5 fusion.310
  51.0 0.4 broadcast_multiply_fusion.11
  51.5 2.3 %fusion.53 = f32[4,8,22,134]{3,2,1,0:T(8,128)S(1)} fusion(f32[4,8,24,136]{3,2,1,0:T(8,128)S(1)} %get-tuple-element.35, f32[4,8,24,136]{3,2,1,0:T(8,128)S(1)} %get-tuple-element.36, f32[4,8,24,136]{3,2,1,0:T(8,128)S(1)} %get-tuple-element.37, f32[4,8,24,136]{3,2,1,0:T(8,128)S(1)} %get-tuple-element.38, f32[4,8,24,136]{3,2,1,0:T(8,128)S(1)} %get-tuple-element.58, ...), kind=kLoop, calls=%fused_computation.92 | loop fusion | flops 3679104 | bytes 4624270 | tf_op jit(solution)/shard_map/jit(_where)/select_n | solution.py:93
  53.8 0.5 multiply_reduce_fusion.6
  54.3 1.3 %fusion.309 = (f32[4,8,20,132]{3,2,1,0:T(8,128)S(1)}, f32[4,8,20,132]{3,2,1,0:T(8,128)S(1)}, f32[4,8,20,132]{3,2,1,0:T(8,128)S(1)}, f32[4,8,20,132]{3,2,1,0:T(8,128)S(1)}, f32[4,8,20,132]{3,2,1,0:T(8,128)S(1)}) fusion(f32[4,8,22,134]{3,2,1,0:T(8,128)S(1)} %fusion.53), kind=kLoop, calls=%fused_computation.610 | loop fusion | bytes 4835328 | tf_op jit(solution)/shard_map/slice | solution.py:123
  55.6 0.1 slice_divide_fusion
  55.7 0.9 %fusion.205 = f32[8,20,132]{2,1,0:T(8,128)S(1)} fusion(f32[8,22,134]{2,1,0:T(8,128)S(1)} %get-tuple-element.94, f32[8,20,134]{2,1,0:T(8,128)S(1)} %slice_divide_fusion.5, f32[8,22,134]{2,1,0:T(8,128)S(1)} %get-tuple-element.75, f32[8,22,134]{2,1,0:T(8,128)S(1)} %get-tuple-element.78, f32[8,22,134]{2,1,0:T(8,128)S(1)} %get-tuple-element.21, ...), kind=kLoop, calls=%fused_computation.347 | loop fusion | flops 760320 | bytes 3234816 | tf_op jit(solution)/shard_map/jit(_where)/select_n | solution.py:93
  56.7 0.5 fusion.308
  57.2 0.4 broadcast_multiply_fusion.7
  57.7 0.1 slice.1079
  57.8 0.1 slice_bitcast_fusion.3
  57.9 0.6 fusion.56
  58.5 1.1 %fusion.57 = (f32[4,8,18,130]{3,2,1,0:T(8,128)S(1)}, f32[4,8,18,130]{3,2,1,0:T(8,128)S(1)}, f32[4,8,18,130]{3,2,1,0:T(8,128)S(1)}) fusion(f32[4,8,20,132]{3,2,1,0:T(8,128)S(1)} %get-tuple-element.56, f32[4,8,20,132]{3,2,1,0:T(8,128)S(1)} %get-tuple-element.52, f32[4,8,20,132]{3,2,1,0:T(8,128)S(1)} %get-tuple-element.55, ...), kind=kLoop, calls=%fused_computation.99 | loop fusion | flops 374400 | bytes 2396160 | tf_op jit(solution)/shard_map/sub | solution.py:123
  59.7 0.7 %fusion.59 = (f32[4,8,18,130]{3,2,1,0:T(8,128)S(1)}, f32[4,8,18,130]{3,2,1,0:T(8,128)S(1)}) fusion(f32[4,8,20,132]{3,2,1,0:T(8,128)S(1)} %get-tuple-element.46, f32[4,8,20,132]{3,2,1,0:T(8,128)S(1)} %get-tuple-element.48, f32[130]{0:T(256)S(1)} %slice.1071, f32[4,8,20,132]{3,2,1,0:T(8,128)S(1)} %get-tuple-element.47, f32[130]{0:T(256)S(1)} %slice.1072), kind=kLoop, calls=%fused_computation.103 | loop fusion | flops 299520 | bytes 1498640 | tf_op jit(solution)/shard_map/mul | solution.py:115
  60.4 0.4 fusion.274
  60.8 0.8 %fusion.149 = f32[4,8,16,128]{3,2,1,0:T(8,128)S(1)} fusion(f32[4,8,18,130]{3,2,1,0:T(8,128)S(1)} %get-tuple-element.43, f32[4,8,18,130]{3,2,1,0:T(8,128)S(1)} %get-tuple-element.51, f32[4,8,18,130]{3,2,1,0:T(8,128)S(1)} %get-tuple-element.50, f32[4,8,18,130]{3,2,1,0:T(8,128)S(1)} %get-tuple-element.49, f32[4,8,18,130]{3,2,1,0:T(8,128)S(1)} %get-tuple-element.45, ...), kind=kLoop, calls=%fused_computation.253 | loop fusion | flops 983040 | bytes 2687680 | tf_op jit(solution)/shard_map/jit(_where)/select_n | solution.py:93
  61.6 0.9 %collective-permute-start.4 = (f32[6,4,16,128]{3,2,1,0:T(8,128)S(1)}, f32[6,4,16,128]{3,2,1,0:T(8,128)S(1)}, u32[]{:S(2)}, u32[]{:S(2)}) collective-permute-start(f32[6,4,16,128]{3,2,1,0:T(8,128)S(1)} %get-tuple-element.63), channel_id=1, source_target_pairs={{0,1},{1,0},{2,3},{3,2},{4,5},{5,4},{6,7},{7,6},{8,9},{9,8},{10,11... | collective-permute-start | bytes 589832 | tf_op jit(solution)/shard_map/ppermute | solution.py:70
  62.5 1.1 %collective-permute-done.4 = f32[6,4,16,128]{3,2,1,0:T(8,128)S(1)} collective-permute-done((f32[6,4,16,128]{3,2,1,0:T(8,128)S(1)}, f32[6,4,16,128]{3,2,1,0:T(8,128)S(1)}, u32[]{:S(2)}, u32[]{:S(2)}) %collective-permute-start.4) | collective-permute-done | bytes 196640 | tf_op jit(solution)/shard_map/ppermute | solution.py:70
  63.6 0.6 gather_fusion.1
  64.2 0.1 select_bitcast_fusion
  64.3 0.7 %copy_bitcast_fusion = f32[4,4,16,256]{3,2,1,0:T(8,128)} fusion(f32[6,4,16,2,128]{4,2,1,0,3:T(8,128)S(1)} %select_bitcast_fusion), kind=kLoop, calls=%fused_computation.263 | loop fusion | bytes 524288 | tf_op jit(solution)/shard_map/slice | solution.py:231
  65.1 0.7 %squeeze.14 = f32[4,16,256]{2,1,0:T(8,128)} reshape(f32[1,4,16,2,128]{4,3,2,1,0:T(2,128)S(1)} %copy.8) | data formatting | bytes 131072 | tf_op jit(solution)/shard_map/squeeze | solution.py:231
  65.8 0.7 %squeeze.15 = f32[4,16,256]{2,1,0:T(8,128)} reshape(f32[1,4,16,2,128]{4,3,2,1,0:T(2,128)S(1)} %copy.9) | data formatting | bytes 131072 | tf_op jit(solution)/shard_map/squeeze | solution.py:231
  (82 shorter events, 2.3 us)
Async XLA Ops:
  3.2 2.2 %collective-permute-start = (f32[3,4,16,256]{3,2,1,0:T(8,128)S(1)}, f32[3,4,16,256]{3,2,1,0:T(8,128)S(1)}, u32[]{:S(2)}, u32[]{:S(2)}) collective-permute-start(f32[3,4,16,256]{3,2,1,0:T(8,128)S(1)} %get-tuple-element.98), channel_id=1, source_target_pairs={{0,1},{1,0},{2,3},{3,2},{4,5},{5,4},{6,7},{7,6},{8,9},{9,8},{10,11... | collective-permute-start | bytes 589832 | tf_op jit(solution)/shard_map/ppermute | solution.py:39
  6.3 7.0 %collective-permute-start.1 = (f32[3,8,16,12]{3,2,1,0:T(8,128)S(1)}, f32[3,8,16,12]{3,2,1,0:T(8,128)S(1)}, u32[]{:S(2)}, u32[]{:S(2)}) collective-permute-start(f32[3,8,16,12]{3,2,1,0:T(8,128)S(1)} %slice_select_fusion.1), channel_id=1, source_target_pairs={{1,2},{2,1},{3,4},{4,3},{5,6},{6,5},{9,10},{10,9},{11,12},{12,11},... | collective-permute-start | bytes 55304 | tf_op jit(solution)/shard_map/ppermute | solution.py:58
  13.7 10.8 %collective-permute-start.3 = (f32[3,8,12,152]{3,2,1,0:T(8,128)S(1)}, f32[3,8,12,152]{3,2,1,0:T(8,128)S(1)}, u32[]{:S(2)}, u32[]{:S(2)}) collective-permute-start(f32[3,8,12,152]{3,2,1,0:T(8,128)S(1)} %get-tuple-element.65), channel_id=1, source_target_pairs={{8,0},{16,8},{24,16},{0,24},{9,1},{17,9},{25,17},{1,25},{10,2},{18... | collective-permute-start | bytes 525320 | tf_op jit(solution)/shard_map/ppermute | solution.py:28
  15.9 17.9 %collective-permute-start.2 = (f32[3,8,12,152]{3,2,1,0:T(8,128)S(1)}, f32[3,8,12,152]{3,2,1,0:T(8,128)S(1)}, u32[]{:S(2)}, u32[]{:S(2)}) collective-permute-start(f32[3,8,12,152]{3,2,1,0:T(8,128)S(1)} %get-tuple-element.64), channel_id=1, source_target_pairs={{0,8},{8,16},{16,24},{24,0},{1,9},{9,17},{17,25},{25,1},{2,10},{10... | collective-permute-start | bytes 525320 | tf_op jit(solution)/shard_map/ppermute | solution.py:27
  61.6 2.0 %collective-permute-start.4 = (f32[6,4,16,128]{3,2,1,0:T(8,128)S(1)}, f32[6,4,16,128]{3,2,1,0:T(8,128)S(1)}, u32[]{:S(2)}, u32[]{:S(2)}) collective-permute-start(f32[6,4,16,128]{3,2,1,0:T(8,128)S(1)} %get-tuple-element.63), channel_id=1, source_target_pairs={{0,1},{1,0},{2,3},{3,2},{4,5},{5,4},{6,7},{7,6},{8,9},{9,8},{10,11... | collective-permute-start | bytes 589832 | tf_op jit(solution)/shard_map/ppermute | solution.py:70
where the time goes:
time: 66.8 us; the launch traced here: 66.5 us
  other arithmetic  28.2 us (42%)
  waiting for transfers between devices  22.2 us (33%)
  local copies, waits for them, and re-layouts  7.74 us (12%)
  starting transfers between devices  6.97 us (10%)
  between operations  1.42 us (2%)
    select_n x13, other arithmetic, in_domain(): return jnp.where(radial_mask(width, geometry), x, 0.0)  12.6 us
    ppermute x1, waiting for transfers between devices, halo_exchange(): before = lax.ppermute(last, axis, up)  9.38 us
    ppermute x1, waiting for transfers between devices, halo_exchange(): after = lax.ppermute(leading, axis, down)  8.46 us
    ppermute x1, waiting for transfers between devices, chip_window(): received = lax.ppermute(piece, ('rad', 'hgt'), pairs)  3.31 us
    ppermute x1, starting transfers between devices, chip_window(): received = lax.ppermute(piece, ('rad', 'hgt'), pairs)  3.12 us
    sub x3, other arithmetic, shards(): crop(bulk_drive, both, pot_width)  2.28 us
    ppermute x1, starting transfers between devices, halo_exchange(): after = lax.ppermute(leading, axis, down)  2.22 us
    another operation x2, other arithmetic, shards(): packed = jnp.stack([density, labels.astype(jnp.float32), target])  1.73 us
  transfers between devices with their start and end apart: 5, of which 4 were waited for; matrix products, arithmetic and copies ran while one was open for 3% of the time, Pallas kernels for 0%

commit v1 on v0

--- a/solution.py
+++ b/solution.py
@@ -27,6 +27,22 @@
     before = lax.ppermute(last, axis, up)
     after = lax.ppermute(leading, axis, down)
     return jnp.concatenate([before, block, after], axis=dim)
+
+
+def azim_exchange(fields, widths):
+    peers = lax.axis_size("azim")
+    up = [(i, (i + 1) % peers) for i in range(peers)]
+    down = [(j, i) for i, j in up]
+    rows = fields[0].shape[-2]
+    last = jnp.concatenate([f[..., rows - w :, :] for f, w in zip(fields, widths)], axis=-2)
+    leading = jnp.concatenate([f[..., :w, :] for f, w in zip(fields, widths)], axis=-2)
+    before = lax.ppermute(last, "azim", up)
+    after = lax.ppermute(leading, "azim", down)
+    out, at = [], 0
+    for f, w in zip(fields, widths):
+        out.append(jnp.concatenate([before[..., at : at + w, :], f, after[..., at : at + w, :]], axis=-2))
+        at += w
+    return out
 
 
 def gather_axis(block, axis, dim):
@@ -154,20 +170,20 @@
         radius_rows * lax.axis_size("rad"),
         part,
     )
-    target = jnp.where(measured != 0, observed, -1.0)
-    packed = jnp.stack([density, labels.astype(jnp.float32), target])
+    packed = jnp.stack([density, labels.astype(jnp.float32), observed, measured.astype(jnp.float32)])
     packed = gather_axis(packed, "hgt", 1)
     packed = chip_window(packed, HALO)
-    packed = halo_exchange(packed, "azim", 2, HALO, True)
-    density, grain_label, target = packed[0], packed[1], packed[2]
-
-    width = HALO
+    widths = (HALO, HALO - 1, 2 * STEPS, 2 * STEPS)
+    density, grain_label, observed, measured = [
+        f[..., HALO - w : f.shape[-1] - (HALO - w)]
+        for f, w in zip(azim_exchange(list(packed), widths), widths)
+    ]
     grains = (
         grain_label[None] == jnp.arange(GRAINS, dtype=jnp.float32)[:, None, None, None]
     ).astype(jnp.float32)
-    density = in_domain(density, width, geometry)
-    grains = in_domain(grains, width, geometry)
-    d_width, g_width = width, width
+    d_width, g_width = widths[0], widths[1]
+    density = in_domain(density, d_width, geometry)
+    grains = in_domain(grains, g_width, geometry)
     history = []
     for moment in range(STEPS):
         history.append((density, d_width, grains, g_width))
@@ -189,8 +205,9 @@
             grains, g_width = in_domain(new_grains, new_g_width, geometry), new_g_width
         density, d_width = in_domain(new_density, new_d_width, geometry), new_d_width
 
-    target = crop(target, width, d_width)
-    costate = in_domain(jnp.where(target >= 0.0, density - target, 0.0), d_width, geometry)
+    observed = crop(observed, widths[2], d_width)
+    measured = crop(measured, widths[3], d_width)
+    costate = in_domain(measured * (density - observed), d_width, geometry)
     c_width = d_width
     last_density = crop(density, d_width, 0)
     cograins = jnp.zeros((GRAINS,) + costate.shape, jnp.float32)

time: 66.8 us -> 64.8 us (0.970)
  waiting for transfers between devices: 22.2 us -> 19.9 us
    ppermute x2, waiting for transfers between devices: 17.8 us -> 14.8 us  [the longest x1 7.96 us: azim_exchange(): before = lax.ppermute(last, 'azim', up)]
    reduce_sum x2, other arithmetic: 0.84 us -> 3.38 us  [chemical(): cube_sum = jnp.sum(grains * grains * grains, axis=0)]
    select_n x13 -> x12, other arithmetic: 12.6 us -> 10.3 us  [in_domain(): return jnp.where(radial_mask(width, geometry), x, 0.0)]
    another operation x2 -> x1, other arithmetic: 1.73 us -> 0.88 us  [shards(): jnp.stack([density, labels.astype(jnp.float32), observed, measured.astype...]
where the time goes in v1:
time: 64.8 us; the launch traced here: 64.6 us
  other arithmetic  27.9 us (43%)
  waiting for transfers between devices  19.9 us (31%)
  local copies, waits for them, and re-layouts  8.18 us (13%)
  starting transfers between devices  7.15 us (11%)
  between operations  1.53 us (2%)
    select_n x12, other arithmetic, in_domain(): return jnp.where(radial_mask(width, geometry), x, 0.0)  10.3 us
    ppermute x1, waiting for transfers between devices, azim_exchange(): before = lax.ppermute(last, 'azim', up)  7.96 us
    ppermute x1, waiting for transfers between devices, azim_exchange(): after = lax.ppermute(leading, 'azim', down)  6.87 us
    ppermute x1, waiting for transfers between devices, chip_window(): received = lax.ppermute(piece, ('rad', 'hgt'), pairs)  3.96 us
    reduce_sum x2, other arithmetic, chemical(): cube_sum = jnp.sum(grains * grains * grains, axis=0)  3.38 us
    ppermute x1, starting transfers between devices, chip_window(): received = lax.ppermute(piece, ('rad', 'hgt'), pairs)  3.18 us
    ppermute x1, starting transfers between devices, azim_exchange(): after = lax.ppermute(leading, 'azim', down)  2.23 us
    sub x3, other arithmetic, shards(): crop(bulk_drive, both, pot_width)  2.1 us
  transfers between devices with their start and end apart: 5, of which 4 were waited for; matrix products, arithmetic and copies ran while one was open for 3% of the time, Pallas kernels for 0%

profile of v1, /device:TPU:9, one launch (start us, length us, event | category | flops | bytes accessed | tf_op | source)
XLA Modules:
  0.0 64.6 jit_solution(171298239402719609)
XLA Ops:
  0.6 0.9 %convert_bitcast_fusion = (f32[1,4,16,256]{3,2,1,0:T(8,128)S(1)}, f32[1,4,16,256]{3,2,1,0:T(8,128)S(1)}) fusion(s32[4,16,256]{2,1,0:T(8,128)} %param.7, s32[4,16,256]{2,1,0:T(8,128)} %param.5), kind=kLoop, calls=%fused_computation.511 | loop fusion | flops 32768 | bytes 262144 | tf_op jit(solution)/shard_map/stack | solution.py:173
  1.5 0.9 %fusion.300 = (f32[1,4,4,16,256]{4,3,2,1,0:T(8,128)S(1)}, f32[4,4,16,256]{3,2,1,0:T(8,128)S(1)}) fusion(f32[1,4,16,256]{3,2,1,0:T(8,128)S(1)} %get-tuple-element.154, f32[1,4,16,256]{3,2,1,0:T(8,128)} %bitcast.40, f32[1,4,16,256]{3,2,1,0:T(8,128)S(1)} %get-tuple-element.155, f32[1,4,16,256]{3,2,1,0:T(8,128)} %bitcast.41), kind=kLoop, calls=%fused_computation.611 | loop fusion | flops 196608 | bytes 786432 | tf_op jit(solution)/shard_map/stack | solution.py:56
  2.5 0.7 %collective-permute-start = (f32[4,4,16,256]{3,2,1,0:T(8,128)S(1)}, f32[4,4,16,256]{3,2,1,0:T(8,128)S(1)}, u32[]{:S(2)}, u32[]{:S(2)}) collective-permute-start(f32[4,4,16,256]{3,2,1,0:T(8,128)S(1)} %get-tuple-element.99), channel_id=1, source_target_pairs={{0,1},{1,0},{2,3},{3,2},{4,5},{5,4},{6,7},{7,6},{8,9},{9,8},{10,11... | collective-permute-start | bytes 786440 | tf_op jit(solution)/shard_map/ppermute | solution.py:55
  4.5 0.1 divide_add_fusion
  4.7 0.6 gather_fusion
  5.3 0.1 select_bitcast_fusion
  5.4 0.1 slice_select_fusion
  5.6 3.2 %collective-permute-start.1 = (f32[4,8,16,12]{3,2,1,0:T(8,128)S(1)}, f32[4,8,16,12]{3,2,1,0:T(8,128)S(1)}, u32[]{:S(2)}, u32[]{:S(2)}) collective-permute-start(f32[4,8,16,12]{3,2,1,0:T(8,128)S(1)} %slice_select_fusion), channel_id=1, source_target_pairs={{1,2},{2,1},{3,4},{4,3},{5,6},{6,5},{9,10},{10,9},{11,12},{12,11},... | collective-permute-start | bytes 73736 | tf_op jit(solution)/shard_map/ppermute | solution.py:74
  9.3 4.0 %collective-permute-done.1 = f32[4,8,16,12]{3,2,1,0:T(8,128)S(1)} collective-permute-done((f32[4,8,16,12]{3,2,1,0:T(8,128)S(1)}, f32[4,8,16,12]{3,2,1,0:T(8,128)S(1)}, u32[]{:S(2)}, u32[]{:S(2)}) %collective-permute-start.1) | collective-permute-done | bytes 24608 | tf_op jit(solution)/shard_map/ppermute | solution.py:74
  13.3 0.4 fusion.72
  13.9 2.2 %collective-permute-start.3 = (f32[8,35,152]{2,1,0:T(8,128)S(1)}, f32[8,35,152]{2,1,0:T(8,128)S(1)}, u32[]{:S(2)}, u32[]{:S(2)}) collective-permute-start(f32[8,35,152]{2,1,0:T(8,128)S(1)} %pad_maximum_fusion.6), channel_id=1, source_target_pairs={{8,0},{16,8},{24,16},{0,24},{9,1},{17,9},{25,17},{1,25},{10,2},{18... | collective-permute-start | bytes 510728 | tf_op jit(solution)/shard_map/ppermute | solution.py:40
  16.3 0.1 fusion.293
  16.3 6.9 %collective-permute-done.3 = f32[8,35,152]{2,1,0:T(8,128)S(1)} collective-permute-done((f32[8,35,152]{2,1,0:T(8,128)S(1)}, f32[8,35,152]{2,1,0:T(8,128)S(1)}, u32[]{:S(2)}, u32[]{:S(2)}) %collective-permute-start.3) | collective-permute-done | bytes 170272 | tf_op jit(solution)/shard_map/ppermute | solution.py:40
  23.2 8.0 %collective-permute-done.2 = f32[8,35,152]{2,1,0:T(8,128)S(1)} collective-permute-done((f32[8,35,152]{2,1,0:T(8,128)S(1)}, f32[8,35,152]{2,1,0:T(8,128)S(1)}, u32[]{:S(2)}, u32[]{:S(2)}) %collective-permute-start.2) | collective-permute-done | bytes 170272 | tf_op jit(solution)/shard_map/ppermute | solution.py:39
  31.2 0.2 pad_maximum_fusion.3
  31.4 0.4 multiply_reduce_fusion.2
  31.8 0.2 slice.978
  32.1 0.6 fusion.77
  32.7 0.2 slice.977
  32.8 0.2 slice.975
  33.0 0.7 %broadcast_subtract_fusion = (f32[8,36,148]{2,1,0:T(8,128)S(1)}, f32[8,36,148]{2,1,0:T(8,128)S(1)}) fusion(f32[8]{0:T(128)S(1)} %get-tuple-element.158, f32[8,38,150]{2,1,0:T(8,128)S(1)} %get-tuple-element.86, f32[8]{0:T(128)S(1)} %get-tuple-element.159, f32[148]{0:T(256)S(1)} %get-tuple-element.152, f32[148]{0:T(256)S(1)} %get-tuple-element.153, ...), kind=kLoop, calls=%fused_computation.444 | loop fusion | flops 895104 | bytes 2640384 | tf_op jit(solution)/shard_map/sub | solution.py:151
  33.7 3.0 %multiply_reduce_fusion.1 = (f32[8,36,148]{2,1,0:T(8,128)S(1)}, f32[8,36,148]{2,1,0:T(8,128)S(1)}, f32[4,8,36,148]{3,2,1,0:T(8,128)S(1)}) fusion(f32[8]{0:T(128)S(1)} %get-tuple-element.158, f32[4,8,38,150]{3,2,1,0:T(8,128)S(1)} %get-tuple-element.66, f32[8]{0:T(128)S(1)} %get-tuple-element.159, f32[148]{0:T(256)S(1)} %get-tuple-element.152, ...), kind=kLoop, calls=%fused_computation.62 | loop fusion | flops 5200128 | bytes 11186688 | tf_op jit(solution)/shard_map/reduce_sum | solution.py:150
  36.6 0.2 mul.1449
  36.9 0.2 slice.1002
  37.0 0.9 %fusion.93 = (f32[8,34,146]{2,1,0:T(8,128)S(1)}, f32[8,34,146]{2,1,0:T(8,128)S(1)}, f32[8,34,146]{2,1,0:T(8,128)S(1)}) fusion(f32[8,36,148]{2,1,0:T(8,128)S(1)} %get-tuple-element.30, f32[8,36,148]{2,1,0:T(8,128)S(1)} %get-tuple-element.14, f32[8]{0:T(128)S(1)} %get-tuple-element.158, f32[8]{0:T(128)S(1)} %get-tuple-element.159, ...), kind=kLoop, calls=%fused_computation.175 | loop fusion | flops 1072224 | bytes 3430784 | tf_op jit(solution)/shard_map/sub | solution.py:193
  37.9 3.0 %fusion.17 = f32[4,8,34,146]{3,2,1,0:T(8,128)S(1)} fusion(f32[4,8,36,148]{3,2,1,0:T(8,128)S(1)} %get-tuple-element.31, f32[4,8,36,148]{3,2,1,0:T(8,128)S(1)} %mul.1449, f32[8,34,146]{2,1,0:T(8,128)S(1)} %get-tuple-element.80, f32[8,34,146]{2,1,0:T(8,128)S(1)} %slice.1002, f32[8,34,146]{2,1,0:T(8,128)S(1)} %get-tuple-element.81, f32[8]{0:T(128)S(1)} %get-tuple-element.158, ...), kind=kLoop, calls=%fused_computation.31 | loop fusion | flops 4288896 | bytes 10799104 | tf_op jit(solution)/shard_map/jit(_where)/select_n | solution.py:109
  40.9 0.4 multiply_reduce_fusion
  41.3 0.4 multiply_reduce_fusion.4
  41.7 0.2 fusion.297
  41.9 0.5 fusion.152
  42.5 0.2 fusion.299
  42.7 0.6 fusion.125
  43.4 0.8 %fusion.167 = (f32[8,28,140]{2,1,0:T(8,128)S(1)}, f32[8,28,140]{2,1,0:T(8,128)S(1)}) fusion(f32[8,6,152]{2,1,0:T(8,128)S(1)} %get-tuple-element.85, f32[8,16,152]{2,1,0:T(8,128)S(1)} %get-tuple-element.58, f32[8,6,152]{2,1,0:T(8,128)S(1)} %get-tuple-element.83, f32[8,6,152]{2,1,0:T(8,128)S(1)} %get-tuple-element.84, ...), kind=kLoop, calls=%fused_computation.281 | loop fusion | flops 846720 | bytes 2615808 | tf_op jit(solution)/shard_map/jit(_where)/select_n | solution.py:109
  44.2 0.6 broadcast_multiply_fusion.3
  44.8 0.1 broadcast_select_fusion
  44.9 0.8 %fusion.44 = f32[4,8,26,138]{3,2,1,0:T(8,128)S(1)} fusion(f32[4,8,34,146]{3,2,1,0:T(8,128)S(1)} %fusion.17, f32[8]{0:T(128)S(1)} %fusion.293, f32[138]{0:T(256)S(1)} %get-tuple-element.26, f32[8,26,138]{2,1,0:T(8,128)S(1)} %get-tuple-element.97, f32[8,26,138]{2,1,0:T(8,128)S(1)} %get-tuple-element.96, f32[8,26,138]{2,1,0:T(8,128)S(1)} %get-tuple-element.90, ...), kind=kLoop, calls=%fused_computation.76 | loop fusion | flops 2066688 | bytes 1493330 | tf_op jit(solution)/shard_map/jit(_where)/select_n | solution.py:109
  45.6 0.5 multiply_reduce_fusion.8
  46.1 1.1 %fusion.307 = (f32[4,8,24,136]{3,2,1,0:T(8,128)S(1)}, f32[4,8,24,136]{3,2,1,0:T(8,128)S(1)}, f32[4,8,24,136]{3,2,1,0:T(8,128)S(1)}, f32[4,8,24,136]{3,2,1,0:T(8,128)S(1)}, f32[4,8,24,136]{3,2,1,0:T(8,128)S(1)}) fusion(f32[4,8,26,138]{3,2,1,0:T(8,128)S(1)} %fusion.44), kind=kLoop, calls=%fused_computation.612 | loop fusion | bytes 5496832 | tf_op jit(solution)/shard_map/slice | solution.py:128
  47.2 0.1 slice_divide_fusion.1
  47.3 0.2 fusion.298
  47.5 0.9 %fusion.218 = f32[8,24,136]{2,1,0:T(8,128)S(1)} fusion(f32[8,26,138]{2,1,0:T(8,128)S(1)} %get-tuple-element.95, f32[8,24,138]{2,1,0:T(8,128)S(1)} %slice_divide_fusion.7, f32[8,26,138]{2,1,0:T(8,128)S(1)} %get-tuple-element.91, f32[8,26,138]{2,1,0:T(8,128)S(1)} %get-tuple-element.94, f32[8,26,138]{2,1,0:T(8,128)S(1)} %get-tuple-element.23, ...), kind=kLoop, calls=%fused_computation.362 | loop fusion | flops 940032 | bytes 3320320 | tf_op jit(solution)/shard_map/jit(_where)/select_n | solution.py:109
  48.5 0.5 fusion.310
  49.0 0.4 broadcast_multiply_fusion.11
  49.5 2.4 %fusion.52 = f32[4,8,22,134]{3,2,1,0:T(8,128)S(1)} fusion(f32[4,8,24,136]{3,2,1,0:T(8,128)S(1)} %get-tuple-element.36, f32[4,8,24,136]{3,2,1,0:T(8,128)S(1)} %get-tuple-element.37, f32[4,8,24,136]{3,2,1,0:T(8,128)S(1)} %get-tuple-element.38, f32[4,8,24,136]{3,2,1,0:T(8,128)S(1)} %get-tuple-element.39, f32[4,8,24,136]{3,2,1,0:T(8,128)S(1)} %get-tuple-element.55, ...), kind=kLoop, calls=%fused_computation.89 | loop fusion | flops 3679104 | bytes 4624270 | tf_op jit(solution)/shard_map/jit(_where)/select_n | solution.py:109
  51.9 0.5 multiply_reduce_fusion.6
  52.4 1.3 %fusion.309 = (f32[4,8,20,132]{3,2,1,0:T(8,128)S(1)}, f32[4,8,20,132]{3,2,1,0:T(8,128)S(1)}, f32[4,8,20,132]{3,2,1,0:T(8,128)S(1)}, f32[4,8,20,132]{3,2,1,0:T(8,128)S(1)}, f32[4,8,20,132]{3,2,1,0:T(8,128)S(1)}) fusion(f32[4,8,22,134]{3,2,1,0:T(8,128)S(1)} %fusion.52), kind=kLoop, calls=%fused_computation.614 | loop fusion | bytes 4835328 | tf_op jit(solution)/shard_map/slice | solution.py:139
  53.6 0.1 slice_divide_fusion
  53.8 0.9 %fusion.204 = f32[8,20,132]{2,1,0:T(8,128)S(1)} fusion(f32[8,22,134]{2,1,0:T(8,128)S(1)} %get-tuple-element.103, f32[8,20,134]{2,1,0:T(8,128)S(1)} %slice_divide_fusion.5, f32[8,22,134]{2,1,0:T(8,128)S(1)} %get-tuple-element.74, f32[8,22,134]{2,1,0:T(8,128)S(1)} %get-tuple-element.77, f32[8,22,134]{2,1,0:T(8,128)S(1)} %get-tuple-element.21, ...), kind=kLoop, calls=%fused_computation.348 | loop fusion | flops 760320 | bytes 3234816 | tf_op jit(solution)/shard_map/jit(_where)/select_n | solution.py:109
  54.7 0.5 fusion.308
  55.2 0.4 broadcast_multiply_fusion.7
  55.7 0.1 slice.1143
  55.9 0.1 slice_bitcast_fusion.5
  55.9 0.6 fusion.55
  56.5 1.1 %fusion.56 = (f32[4,8,18,130]{3,2,1,0:T(8,128)S(1)}, f32[4,8,18,130]{3,2,1,0:T(8,128)S(1)}, f32[4,8,18,130]{3,2,1,0:T(8,128)S(1)}) fusion(f32[4,8,20,132]{3,2,1,0:T(8,128)S(1)} %get-tuple-element.53, f32[4,8,20,132]{3,2,1,0:T(8,128)S(1)} %get-tuple-element.49, f32[4,8,20,132]{3,2,1,0:T(8,128)S(1)} %get-tuple-element.52, ...), kind=kLoop, calls=%fused_computation.96 | loop fusion | flops 374400 | bytes 2396160 | tf_op jit(solution)/shard_map/sub | solution.py:139
  57.7 0.7 %fusion.58 = (f32[4,8,18,130]{3,2,1,0:T(8,128)S(1)}, f32[4,8,18,130]{3,2,1,0:T(8,128)S(1)}) fusion(f32[4,8,20,132]{3,2,1,0:T(8,128)S(1)} %get-tuple-element.43, f32[4,8,20,132]{3,2,1,0:T(8,128)S(1)} %get-tuple-element.45, f32[130]{0:T(256)S(1)} %slice.1135, f32[4,8,20,132]{3,2,1,0:T(8,128)S(1)} %get-tuple-element.44, f32[130]{0:T(256)S(1)} %slice.1136), kind=kLoop, calls=%fused_computation.100 | loop fusion | flops 299520 | bytes 1498640 | tf_op jit(solution)/shard_map/mul | solution.py:131
  58.4 0.4 fusion.273
  58.8 0.8 %fusion.145 = f32[4,8,16,128]{3,2,1,0:T(8,128)S(1)} fusion(f32[4,8,18,130]{3,2,1,0:T(8,128)S(1)} %get-tuple-element.40, f32[4,8,18,130]{3,2,1,0:T(8,128)S(1)} %get-tuple-element.48, f32[4,8,18,130]{3,2,1,0:T(8,128)S(1)} %get-tuple-element.47, f32[4,8,18,130]{3,2,1,0:T(8,128)S(1)} %get-tuple-element.46, f32[4,8,18,130]{3,2,1,0:T(8,128)S(1)} %get-tuple-element.42, ...), kind=kLoop, calls=%fused_computation.246 | loop fusion | flops 983040 | bytes 2687680 | tf_op jit(solution)/shard_map/jit(_where)/select_n | solution.py:109
  59.7 0.9 %collective-permute-start.4 = (f32[6,4,16,128]{3,2,1,0:T(8,128)S(1)}, f32[6,4,16,128]{3,2,1,0:T(8,128)S(1)}, u32[]{:S(2)}, u32[]{:S(2)}) collective-permute-start(f32[6,4,16,128]{3,2,1,0:T(8,128)S(1)} %get-tuple-element.64), channel_id=1, source_target_pairs={{0,1},{1,0},{2,3},{3,2},{4,5},{5,4},{6,7},{7,6},{8,9},{9,8},{10,11... | collective-permute-start | bytes 589832 | tf_op jit(solution)/shard_map/ppermute | solution.py:86
  60.6 1.1 %collective-permute-done.4 = f32[6,4,16,128]{3,2,1,0:T(8,128)S(1)} collective-permute-done((f32[6,4,16,128]{3,2,1,0:T(8,128)S(1)}, f32[6,4,16,128]{3,2,1,0:T(8,128)S(1)}, u32[]{:S(2)}, u32[]{:S(2)}) %collective-permute-start.4) | collective-permute-done | bytes 196640 | tf_op jit(solution)/shard_map/ppermute | solution.py:86
  61.7 0.6 gather_fusion.1
  62.3 0.1 select_bitcast_fusion.1
  62.4 0.7 %copy_bitcast_fusion = f32[4,4,16,256]{3,2,1,0:T(8,128)} fusion(f32[6,4,16,2,128]{4,2,1,0,3:T(8,128)S(1)} %select_bitcast_fusion.1), kind=kLoop, calls=%fused_computation.256 | loop fusion | bytes 524288 | tf_op jit(solution)/shard_map/slice | solution.py:248
  63.2 0.7 %squeeze.6 = f32[4,16,256]{2,1,0:T(8,128)} reshape(f32[1,4,16,2,128]{4,3,2,1,0:T(2,128)S(1)} %copy.8) | data formatting | bytes 131072 | tf_op jit(solution)/shard_map/squeeze | solution.py:248
  63.9 0.7 %squeeze.7 = f32[4,16,256]{2,1,0:T(8,128)} reshape(f32[1,4,16,2,128]{4,3,2,1,0:T(2,128)S(1)} %copy.9) | data formatting | bytes 131072 | tf_op jit(solution)/shard_map/squeeze | solution.py:248
  (95 shorter events, 2.6 us)
Async XLA Ops:
  2.5 2.2 %collective-permute-start = (f32[4,4,16,256]{3,2,1,0:T(8,128)S(1)}, f32[4,4,16,256]{3,2,1,0:T(8,128)S(1)}, u32[]{:S(2)}, u32[]{:S(2)}) collective-permute-start(f32[4,4,16,256]{3,2,1,0:T(8,128)S(1)} %get-tuple-element.99), channel_id=1, source_target_pairs={{0,1},{1,0},{2,3},{3,2},{4,5},{5,4},{6,7},{7,6},{8,9},{9,8},{10,11... | collective-permute-start | bytes 786440 | tf_op jit(solution)/shard_map/ppermute | solution.py:55
  5.6 7.7 %collective-permute-start.1 = (f32[4,8,16,12]{3,2,1,0:T(8,128)S(1)}, f32[4,8,16,12]{3,2,1,0:T(8,128)S(1)}, u32[]{:S(2)}, u32[]{:S(2)}) collective-permute-start(f32[4,8,16,12]{3,2,1,0:T(8,128)S(1)} %slice_select_fusion), channel_id=1, source_target_pairs={{1,2},{2,1},{3,4},{4,3},{5,6},{6,5},{9,10},{10,9},{11,12},{12,11},... | collective-permute-start | bytes 73736 | tf_op jit(solution)/shard_map/ppermute | solution.py:74
  13.9 9.3 %collective-permute-start.3 = (f32[8,35,152]{2,1,0:T(8,128)S(1)}, f32[8,35,152]{2,1,0:T(8,128)S(1)}, u32[]{:S(2)}, u32[]{:S(2)}) collective-permute-start(f32[8,35,152]{2,1,0:T(8,128)S(1)} %pad_maximum_fusion.6), channel_id=1, source_target_pairs={{8,0},{16,8},{24,16},{0,24},{9,1},{17,9},{25,17},{1,25},{10,2},{18... | collective-permute-start | bytes 510728 | tf_op jit(solution)/shard_map/ppermute | solution.py:40
  16.2 15.0 %collective-permute-start.2 = (f32[8,35,152]{2,1,0:T(8,128)S(1)}, f32[8,35,152]{2,1,0:T(8,128)S(1)}, u32[]{:S(2)}, u32[]{:S(2)}) collective-permute-start(f32[8,35,152]{2,1,0:T(8,128)S(1)} %pad_maximum_fusion.5), channel_id=1, source_target_pairs={{0,8},{8,16},{16,24},{24,0},{1,9},{9,17},{17,25},{25,1},{2,10},{10... | collective-permute-start | bytes 510728 | tf_op jit(solution)/shard_map/ppermute | solution.py:39
  59.7 2.0 %collective-permute-start.4 = (f32[6,4,16,128]{3,2,1,0:T(8,128)S(1)}, f32[6,4,16,128]{3,2,1,0:T(8,128)S(1)}, u32[]{:S(2)}, u32[]{:S(2)}) collective-permute-start(f32[6,4,16,128]{3,2,1,0:T(8,128)S(1)} %get-tuple-element.64), channel_id=1, source_target_pairs={{0,1},{1,0},{2,3},{3,2},{4,5},{5,4},{6,7},{7,6},{8,9},{9,8},{10,11... | collective-permute-start | bytes 589832 | tf_op jit(solution)/shard_map/ppermute | solution.py:86

commit v2 on v1

--- a/solution.py
+++ b/solution.py
@@ -72,6 +72,30 @@
         pairs.append((r * peers + peers - 1, (r + 1) * peers))
         pairs.append(((r + 1) * peers, r * peers + peers - 1))
     received = lax.ppermute(piece, ("rad", "hgt"), pairs)
+    padded = jnp.concatenate([received, block, received], axis=-1)
+    return lax.dynamic_slice_in_dim(padded, own * part, part + 2 * width, axis=padded.ndim - 1)
+
+
+def edge_columns(block, width):
+    own, rad_peers = (lax.axis_index("hgt"), lax.axis_size("rad"))
+    cols = block.shape[-1]
+    first, last = (block[..., :width], block[..., cols - width :])
+    cross, same = ([], [])
+    for r in range(rad_peers - 1):
+        cross += [(2 * r + 1, 2 * r + 2), (2 * r + 2, 2 * r + 1)]
+        same += [(2 * r, 2 * r + 2), (2 * r + 3, 2 * r + 1)]
+    from_cross = lax.ppermute(jnp.where(own == 0, first, last), ("rad", "hgt"), cross)
+    from_same = lax.ppermute(jnp.where(own == 0, last, first), ("rad", "hgt"), same)
+    return jnp.where(
+        own == 0,
+        jnp.concatenate([from_same, from_cross], axis=1),
+        jnp.concatenate([from_cross, from_same], axis=1),
+    )
+
+
+def two_core_window(block, received, width):
+    own = lax.axis_index("hgt")
+    part = block.shape[-1] // 2
     padded = jnp.concatenate([received, block, received], axis=-1)
     return lax.dynamic_slice_in_dim(padded, own * part, part + 2 * width, axis=padded.ndim - 1)
 
@@ -171,8 +195,11 @@
         part,
     )
     packed = jnp.stack([density, labels.astype(jnp.float32), observed, measured.astype(jnp.float32)])
-    packed = gather_axis(packed, "hgt", 1)
-    packed = chip_window(packed, HALO)
+    if lax.axis_size("hgt") == 2:
+        received = edge_columns(packed, HALO)
+        packed = two_core_window(gather_axis(packed, "hgt", 1), received, HALO)
+    else:
+        packed = chip_window(gather_axis(packed, "hgt", 1), HALO)
     widths = (HALO, HALO - 1, 2 * STEPS, 2 * STEPS)
     density, grain_label, observed, measured = [
         f[..., HALO - w : f.shape[-1] - (HALO - w)]

time: 64.8 us -> 65.7 us (1.014); the launches traced: 64.6 us -> 64.4 us
  waiting for transfers between devices: 19.9 us -> 17.2 us
  starting transfers between devices: 7.15 us -> 9.63 us
    ppermute x1 -> x2, waiting for transfers between devices: 3.96 us -> 1.63 us  [the longest x1 1.63 us: edge_columns(): lax.ppermute(jnp.where(own == 0, last, first), ('rad', 'hgt'), same)]
    ppermute x1 -> x2, starting transfers between devices: 3.18 us -> 5.19 us  [the longest x1 3.11 us: edge_columns(): lax.ppermute(jnp.where(own == 0, first, last), ('rad', 'hgt'), cross)]
  transfers between devices with their start and end apart: 5 -> 6, of which waited for: 4 -> 4; matrix products, arithmetic and copies ran while one was open for 3% -> 3% of each run, Pallas kernels for 0% -> 0%
where the time goes in v2:
time: 65.7 us; the launch traced here: 64.4 us
  other arithmetic  27.9 us (42%)
  waiting for transfers between devices  17.2 us (26%)
  starting transfers between devices  9.63 us (15%)
  local copies, waits for them, and re-layouts  8.18 us (12%)
  between operations  1.55 us (2%)
    select_n x12, other arithmetic, in_domain(): return jnp.where(radial_mask(width, geometry), x, 0.0)  10.3 us
    ppermute x1, waiting for transfers between devices, azim_exchange(): before = lax.ppermute(last, 'azim', up)  7.6 us
    ppermute x1, waiting for transfers between devices, azim_exchange(): after = lax.ppermute(leading, 'azim', down)  6.86 us
    reduce_sum x2, other arithmetic, chemical(): cube_sum = jnp.sum(grains * grains * grains, axis=0)  3.38 us
    ppermute x1, starting transfers between devices, edge_columns(): lax.ppermute(jnp.where(own == 0, first, last), ('rad', 'hgt'), cross)  3.11 us
    ppermute x1, starting transfers between devices, azim_exchange(): after = lax.ppermute(leading, 'azim', down)  2.33 us
    sub x3, other arithmetic, shards(): crop(bulk_drive, both, pot_width)  2.1 us
    ppermute x1, starting transfers between devices, edge_columns(): lax.ppermute(jnp.where(own == 0, last, first), ('rad', 'hgt'), same)  2.08 us
  transfers between devices with their start and end apart: 6, of which 4 were waited for; matrix products, arithmetic and copies ran while one was open for 3% of the time, Pallas kernels for 0%

profile of v2, /device:TPU:9, one launch (start us, length us, event | category | flops | bytes accessed | tf_op | source)
XLA Modules:
  0.0 64.4 jit_solution(11405685988867142091)
XLA Ops:
  0.6 0.9 %convert_bitcast_fusion = (f32[1,4,16,256]{3,2,1,0:T(8,128)S(1)}, f32[1,4,16,256]{3,2,1,0:T(8,128)S(1)}) fusion(s32[4,16,256]{2,1,0:T(8,128)} %param.7, s32[4,16,256]{2,1,0:T(8,128)} %param.5), kind=kLoop, calls=%fused_computation.513 | loop fusion | flops 32768 | bytes 262144 | tf_op jit(solution)/shard_map/stack | solution.py:197
  1.5 0.9 %fusion.300 = (f32[1,4,4,16,256]{4,3,2,1,0:T(8,128)S(1)}, f32[4,4,16,256]{3,2,1,0:T(8,128)S(1)}) fusion(f32[1,4,16,256]{3,2,1,0:T(8,128)S(1)} %get-tuple-element.156, f32[1,4,16,256]{3,2,1,0:T(8,128)} %bitcast.39, f32[1,4,16,256]{3,2,1,0:T(8,128)S(1)} %get-tuple-element.157, f32[1,4,16,256]{3,2,1,0:T(8,128)} %bitcast.40), kind=kLoop, calls=%fused_computation.613 | loop fusion | flops 196608 | bytes 786432 | tf_op jit(solution)/shard_map/stack | solution.py:56
  2.5 0.7 %collective-permute-start.2 = (f32[4,4,16,256]{3,2,1,0:T(8,128)S(1)}, f32[4,4,16,256]{3,2,1,0:T(8,128)S(1)}, u32[]{:S(2)}, u32[]{:S(2)}) collective-permute-start(f32[4,4,16,256]{3,2,1,0:T(8,128)S(1)} %get-tuple-element.99), channel_id=1, source_target_pairs={{0,1},{1,0},{2,3},{3,2},{4,5},{5,4},{6,7},{7,6},{8,9},{9,8},{10,11... | collective-permute-start | bytes 786440 | tf_op jit(solution)/shard_map/ppermute | solution.py:55
  3.2 0.1 slice_select_fusion.1
  3.3 3.1 %collective-permute-start.1 = (f32[4,4,16,12]{3,2,1,0:T(8,128)S(1)}, f32[4,4,16,12]{3,2,1,0:T(8,128)S(1)}, u32[]{:S(2)}, u32[]{:S(2)}) collective-permute-start(f32[4,4,16,12]{3,2,1,0:T(8,128)S(1)} %get-tuple-element.101), channel_id=1, source_target_pairs={{1,2},{2,1},{3,4},{4,3},{5,6},{6,5},{9,10},{10,9},{11,12},{12,11},... | collective-permute-start | bytes 36872 | tf_op jit(solution)/shard_map/ppermute | solution.py:87
  6.4 2.1 %collective-permute-start = (f32[4,4,16,12]{3,2,1,0:T(8,128)S(1)}, f32[4,4,16,12]{3,2,1,0:T(8,128)S(1)}, u32[]{:S(2)}, u32[]{:S(2)}) collective-permute-start(f32[4,4,16,12]{3,2,1,0:T(8,128)S(1)} %get-tuple-element.100), channel_id=1, source_target_pairs={{0,2},{3,1},{2,4},{5,3},{4,6},{7,5},{8,10},{11,9},{10,12},{13,11},... | collective-permute-start | bytes 36872 | tf_op jit(solution)/shard_map/ppermute | solution.py:88
  9.9 0.1 divide_add_fusion
  10.5 1.6 %collective-permute-done = f32[4,4,16,12]{3,2,1,0:T(8,128)S(1)} collective-permute-done((f32[4,4,16,12]{3,2,1,0:T(8,128)S(1)}, f32[4,4,16,12]{3,2,1,0:T(8,128)S(1)}, u32[]{:S(2)}, u32[]{:S(2)}) %collective-permute-start) | collective-permute-done | bytes 12320 | tf_op jit(solution)/shard_map/ppermute | solution.py:88
  12.2 0.6 gather_fusion
  12.8 0.1 select_bitcast_fusion
  13.0 0.4 fusion.72
  13.6 2.3 %collective-permute-start.4 = (f32[8,35,152]{2,1,0:T(8,128)S(1)}, f32[8,35,152]{2,1,0:T(8,128)S(1)}, u32[]{:S(2)}, u32[]{:S(2)}) collective-permute-start(f32[8,35,152]{2,1,0:T(8,128)S(1)} %pad_maximum_fusion.6), channel_id=1, source_target_pairs={{8,0},{16,8},{24,16},{0,24},{9,1},{17,9},{25,17},{1,25},{10,2},{18... | collective-permute-start | bytes 510728 | tf_op jit(solution)/shard_map/ppermute | solution.py:40
  16.2 6.9 %collective-permute-done.4 = f32[8,35,152]{2,1,0:T(8,128)S(1)} collective-permute-done((f32[8,35,152]{2,1,0:T(8,128)S(1)}, f32[8,35,152]{2,1,0:T(8,128)S(1)}, u32[]{:S(2)}, u32[]{:S(2)}) %collective-permute-start.4) | collective-permute-done | bytes 170272 | tf_op jit(solution)/shard_map/ppermute | solution.py:40
  23.0 7.6 %collective-permute-done.3 = f32[8,35,152]{2,1,0:T(8,128)S(1)} collective-permute-done((f32[8,35,152]{2,1,0:T(8,128)S(1)}, f32[8,35,152]{2,1,0:T(8,128)S(1)}, u32[]{:S(2)}, u32[]{:S(2)}) %collective-permute-start.3) | collective-permute-done | bytes 170272 | tf_op jit(solution)/shard_map/ppermute | solution.py:39
  30.7 0.2 pad_maximum_fusion.3
  30.8 0.4 multiply_reduce_fusion.2
  31.2 0.2 slice.978
  31.5 0.6 fusion.77
  32.1 0.2 slice.977
  32.3 0.2 slice.975
  32.4 0.7 %broadcast_subtract_fusion = (f32[8,36,148]{2,1,0:T(8,128)S(1)}, f32[8,36,148]{2,1,0:T(8,128)S(1)}) fusion(f32[8]{0:T(128)S(1)} %get-tuple-element.160, f32[8,38,150]{2,1,0:T(8,128)S(1)} %get-tuple-element.86, f32[8]{0:T(128)S(1)} %get-tuple-element.161, f32[148]{0:T(256)S(1)} %get-tuple-element.154, f32[148]{0:T(256)S(1)} %get-tuple-element.155, ...), kind=kLoop, calls=%fused_computation.444 | loop fusion | flops 895104 | bytes 2640384 | tf_op jit(solution)/shard_map/sub | solution.py:175
  33.1 3.0 %multiply_reduce_fusion.1 = (f32[8,36,148]{2,1,0:T(8,128)S(1)}, f32[8,36,148]{2,1,0:T(8,128)S(1)}, f32[4,8,36,148]{3,2,1,0:T(8,128)S(1)}) fusion(f32[8]{0:T(128)S(1)} %get-tuple-element.160, f32[4,8,38,150]{3,2,1,0:T(8,128)S(1)} %get-tuple-element.66, f32[8]{0:T(128)S(1)} %get-tuple-element.161, f32[148]{0:T(256)S(1)} %get-tuple-element.154, ...), kind=kLoop, calls=%fused_computation.62 | loop fusion | flops 5200128 | bytes 11186688 | tf_op jit(solution)/shard_map/reduce_sum | solution.py:174
  36.1 0.2 mul.1449
  36.3 0.2 slice.1002
  36.5 0.9 %fusion.93 = (f32[8,34,146]{2,1,0:T(8,128)S(1)}, f32[8,34,146]{2,1,0:T(8,128)S(1)}, f32[8,34,146]{2,1,0:T(8,128)S(1)}) fusion(f32[8,36,148]{2,1,0:T(8,128)S(1)} %get-tuple-element.30, f32[8,36,148]{2,1,0:T(8,128)S(1)} %get-tuple-element.14, f32[8]{0:T(128)S(1)} %get-tuple-element.160, f32[8]{0:T(128)S(1)} %get-tuple-element.161, ...), kind=kLoop, calls=%fused_computation.175 | loop fusion | flops 1072224 | bytes 3430784 | tf_op jit(solution)/shard_map/sub | solution.py:220
  37.4 3.0 %fusion.17 = f32[4,8,34,146]{3,2,1,0:T(8,128)S(1)} fusion(f32[4,8,36,148]{3,2,1,0:T(8,128)S(1)} %get-tuple-element.31, f32[4,8,36,148]{3,2,1,0:T(8,128)S(1)} %mul.1449, f32[8,34,146]{2,1,0:T(8,128)S(1)} %get-tuple-element.80, f32[8,34,146]{2,1,0:T(8,128)S(1)} %slice.1002, f32[8,34,146]{2,1,0:T(8,128)S(1)} %get-tuple-element.81, f32[8]{0:T(128)S(1)} %get-tuple-element.160, ...), kind=kLoop, calls=%fused_computation.31 | loop fusion | flops 4288896 | bytes 10799104 | tf_op jit(solution)/shard_map/jit(_where)/select_n | solution.py:133
  40.4 0.4 multiply_reduce_fusion
  40.8 0.4 multiply_reduce_fusion.4
  41.2 0.2 fusion.297
  41.3 0.5 fusion.152
  41.9 0.2 fusion.299
  42.1 0.6 fusion.125
  42.8 0.8 %fusion.167 = (f32[8,28,140]{2,1,0:T(8,128)S(1)}, f32[8,28,140]{2,1,0:T(8,128)S(1)}) fusion(f32[8,6,152]{2,1,0:T(8,128)S(1)} %get-tuple-element.85, f32[8,16,152]{2,1,0:T(8,128)S(1)} %get-tuple-element.58, f32[8,6,152]{2,1,0:T(8,128)S(1)} %get-tuple-element.83, f32[8,6,152]{2,1,0:T(8,128)S(1)} %get-tuple-element.84, ...), kind=kLoop, calls=%fused_computation.281 | loop fusion | flops 846720 | bytes 2615808 | tf_op jit(solution)/shard_map/jit(_where)/select_n | solution.py:133
  43.7 0.6 broadcast_multiply_fusion.3
  44.2 0.1 broadcast_select_fusion
  44.3 0.8 %fusion.44 = f32[4,8,26,138]{3,2,1,0:T(8,128)S(1)} fusion(f32[4,8,34,146]{3,2,1,0:T(8,128)S(1)} %fusion.17, f32[8]{0:T(128)S(1)} %fusion.293, f32[138]{0:T(256)S(1)} %get-tuple-element.26, f32[8,26,138]{2,1,0:T(8,128)S(1)} %get-tuple-element.97, f32[8,26,138]{2,1,0:T(8,128)S(1)} %get-tuple-element.96, f32[8,26,138]{2,1,0:T(8,128)S(1)} %get-tuple-element.90, ...), kind=kLoop, calls=%fused_computation.76 | loop fusion | flops 2066688 | bytes 1493330 | tf_op jit(solution)/shard_map/jit(_where)/select_n | solution.py:133
  45.1 0.5 multiply_reduce_fusion.8
  45.6 1.1 %fusion.307 = (f32[4,8,24,136]{3,2,1,0:T(8,128)S(1)}, f32[4,8,24,136]{3,2,1,0:T(8,128)S(1)}, f32[4,8,24,136]{3,2,1,0:T(8,128)S(1)}, f32[4,8,24,136]{3,2,1,0:T(8,128)S(1)}, f32[4,8,24,136]{3,2,1,0:T(8,128)S(1)}) fusion(f32[4,8,26,138]{3,2,1,0:T(8,128)S(1)} %fusion.44), kind=kLoop, calls=%fused_computation.614 | loop fusion | bytes 5496832 | tf_op jit(solution)/shard_map/slice | solution.py:152
  46.6 0.1 slice_divide_fusion.1
  46.7 0.2 fusion.298
  46.9 0.9 %fusion.218 = f32[8,24,136]{2,1,0:T(8,128)S(1)} fusion(f32[8,26,138]{2,1,0:T(8,128)S(1)} %get-tuple-element.95, f32[8,24,138]{2,1,0:T(8,128)S(1)} %slice_divide_fusion.7, f32[8,26,138]{2,1,0:T(8,128)S(1)} %get-tuple-element.91, f32[8,26,138]{2,1,0:T(8,128)S(1)} %get-tuple-element.94, f32[8,26,138]{2,1,0:T(8,128)S(1)} %get-tuple-element.23, ...), kind=kLoop, calls=%fused_computation.362 | loop fusion | flops 940032 | bytes 3320320 | tf_op jit(solution)/shard_map/jit(_where)/select_n | solution.py:133
  47.9 0.5 fusion.310
  48.4 0.4 broadcast_multiply_fusion.11
  49.0 2.4 %fusion.52 = f32[4,8,22,134]{3,2,1,0:T(8,128)S(1)} fusion(f32[4,8,24,136]{3,2,1,0:T(8,128)S(1)} %get-tuple-element.36, f32[4,8,24,136]{3,2,1,0:T(8,128)S(1)} %get-tuple-element.37, f32[4,8,24,136]{3,2,1,0:T(8,128)S(1)} %get-tuple-element.38, f32[4,8,24,136]{3,2,1,0:T(8,128)S(1)} %get-tuple-element.39, f32[4,8,24,136]{3,2,1,0:T(8,128)S(1)} %get-tuple-element.55, ...), kind=kLoop, calls=%fused_computation.89 | loop fusion | flops 3679104 | bytes 4624270 | tf_op jit(solution)/shard_map/jit(_where)/select_n | solution.py:133
  51.3 0.5 multiply_reduce_fusion.6
  51.8 1.3 %fusion.309 = (f32[4,8,20,132]{3,2,1,0:T(8,128)S(1)}, f32[4,8,20,132]{3,2,1,0:T(8,128)S(1)}, f32[4,8,20,132]{3,2,1,0:T(8,128)S(1)}, f32[4,8,20,132]{3,2,1,0:T(8,128)S(1)}, f32[4,8,20,132]{3,2,1,0:T(8,128)S(1)}) fusion(f32[4,8,22,134]{3,2,1,0:T(8,128)S(1)} %fusion.52), kind=kLoop, calls=%fused_computation.616 | loop fusion | bytes 4835328 | tf_op jit(solution)/shard_map/slice | solution.py:163
  53.1 0.1 slice_divide_fusion
  53.2 0.9 %fusion.204 = f32[8,20,132]{2,1,0:T(8,128)S(1)} fusion(f32[8,22,134]{2,1,0:T(8,128)S(1)} %get-tuple-element.105, f32[8,20,134]{2,1,0:T(8,128)S(1)} %slice_divide_fusion.5, f32[8,22,134]{2,1,0:T(8,128)S(1)} %get-tuple-element.74, f32[8,22,134]{2,1,0:T(8,128)S(1)} %get-tuple-element.77, f32[8,22,134]{2,1,0:T(8,128)S(1)} %get-tuple-element.21, ...), kind=kLoop, calls=%fused_computation.348 | loop fusion | flops 760320 | bytes 3234816 | tf_op jit(solution)/shard_map/jit(_where)/select_n | solution.py:133
  54.2 0.5 fusion.308
  54.7 0.4 broadcast_multiply_fusion.7
  55.2 0.1 slice.1143
  55.3 0.1 slice_bitcast_fusion.5
  55.4 0.6 fusion.55
  56.0 1.1 %fusion.56 = (f32[4,8,18,130]{3,2,1,0:T(8,128)S(1)}, f32[4,8,18,130]{3,2,1,0:T(8,128)S(1)}, f32[4,8,18,130]{3,2,1,0:T(8,128)S(1)}) fusion(f32[4,8,20,132]{3,2,1,0:T(8,128)S(1)} %get-tuple-element.53, f32[4,8,20,132]{3,2,1,0:T(8,128)S(1)} %get-tuple-element.49, f32[4,8,20,132]{3,2,1,0:T(8,128)S(1)} %get-tuple-element.52, ...), kind=kLoop, calls=%fused_computation.96 | loop fusion | flops 374400 | bytes 2396160 | tf_op jit(solution)/shard_map/sub | solution.py:163
  57.1 0.7 %fusion.58 = (f32[4,8,18,130]{3,2,1,0:T(8,128)S(1)}, f32[4,8,18,130]{3,2,1,0:T(8,128)S(1)}) fusion(f32[4,8,20,132]{3,2,1,0:T(8,128)S(1)} %get-tuple-element.43, f32[4,8,20,132]{3,2,1,0:T(8,128)S(1)} %get-tuple-element.45, f32[130]{0:T(256)S(1)} %slice.1135, f32[4,8,20,132]{3,2,1,0:T(8,128)S(1)} %get-tuple-element.44, f32[130]{0:T(256)S(1)} %slice.1136), kind=kLoop, calls=%fused_computation.100 | loop fusion | flops 299520 | bytes 1498640 | tf_op jit(solution)/shard_map/mul | solution.py:155
  57.8 0.4 fusion.273
  58.2 0.8 %fusion.145 = f32[4,8,16,128]{3,2,1,0:T(8,128)S(1)} fusion(f32[4,8,18,130]{3,2,1,0:T(8,128)S(1)} %get-tuple-element.40, f32[4,8,18,130]{3,2,1,0:T(8,128)S(1)} %get-tuple-element.48, f32[4,8,18,130]{3,2,1,0:T(8,128)S(1)} %get-tuple-element.47, f32[4,8,18,130]{3,2,1,0:T(8,128)S(1)} %get-tuple-element.46, f32[4,8,18,130]{3,2,1,0:T(8,128)S(1)} %get-tuple-element.42, ...), kind=kLoop, calls=%fused_computation.246 | loop fusion | flops 983040 | bytes 2687680 | tf_op jit(solution)/shard_map/jit(_where)/select_n | solution.py:133
  59.1 1.3 %collective-permute-start.5 = (f32[6,4,16,128]{3,2,1,0:T(8,128)S(1)}, f32[6,4,16,128]{3,2,1,0:T(8,128)S(1)}, u32[]{:S(2)}, u32[]{:S(2)}) collective-permute-start(f32[6,4,16,128]{3,2,1,0:T(8,128)S(1)} %get-tuple-element.64), channel_id=1, source_target_pairs={{0,1},{1,0},{2,3},{3,2},{4,5},{5,4},{6,7},{7,6},{8,9},{9,8},{10,11... | collective-permute-start | bytes 589832 | tf_op jit(solution)/shard_map/ppermute | solution.py:110
  60.4 1.1 %collective-permute-done.5 = f32[6,4,16,128]{3,2,1,0:T(8,128)S(1)} collective-permute-done((f32[6,4,16,128]{3,2,1,0:T(8,128)S(1)}, f32[6,4,16,128]{3,2,1,0:T(8,128)S(1)}, u32[]{:S(2)}, u32[]{:S(2)}) %collective-permute-start.5) | collective-permute-done | bytes 196640 | tf_op jit(solution)/shard_map/ppermute | solution.py:110
  61.5 0.6 gather_fusion.1
  62.1 0.1 select_bitcast_fusion.1
  62.2 0.7 %copy_bitcast_fusion = f32[4,4,16,256]{3,2,1,0:T(8,128)} fusion(f32[6,4,16,2,128]{4,2,1,0,3:T(8,128)S(1)} %select_bitcast_fusion.1), kind=kLoop, calls=%fused_computation.256 | loop fusion | bytes 524288 | tf_op jit(solution)/shard_map/slice | solution.py:275
  63.0 0.7 %squeeze.6 = f32[4,16,256]{2,1,0:T(8,128)} reshape(f32[1,4,16,2,128]{4,3,2,1,0:T(2,128)S(1)} %copy.9) | data formatting | bytes 131072 | tf_op jit(solution)/shard_map/squeeze | solution.py:275
  63.7 0.7 %squeeze.7 = f32[4,16,256]{2,1,0:T(8,128)} reshape(f32[1,4,16,2,128]{4,3,2,1,0:T(2,128)S(1)} %copy.10) | data formatting | bytes 131072 | tf_op jit(solution)/shard_map/squeeze | solution.py:275
  (98 shorter events, 2.7 us)
Async XLA Ops:
  2.5 9.7 %collective-permute-start.2 = (f32[4,4,16,256]{3,2,1,0:T(8,128)S(1)}, f32[4,4,16,256]{3,2,1,0:T(8,128)S(1)}, u32[]{:S(2)}, u32[]{:S(2)}) collective-permute-start(f32[4,4,16,256]{3,2,1,0:T(8,128)S(1)} %get-tuple-element.99), channel_id=1, source_target_pairs={{0,1},{1,0},{2,3},{3,2},{4,5},{5,4},{6,7},{7,6},{8,9},{9,8},{10,11... | collective-permute-start | bytes 786440 | tf_op jit(solution)/shard_map/ppermute | solution.py:55
  3.3 7.2 %collective-permute-start.1 = (f32[4,4,16,12]{3,2,1,0:T(8,128)S(1)}, f32[4,4,16,12]{3,2,1,0:T(8,128)S(1)}, u32[]{:S(2)}, u32[]{:S(2)}) collective-permute-start(f32[4,4,16,12]{3,2,1,0:T(8,128)S(1)} %get-tuple-element.101), channel_id=1, source_target_pairs={{1,2},{2,1},{3,4},{4,3},{5,6},{6,5},{9,10},{10,9},{11,12},{12,11},... | collective-permute-start | bytes 36872 | tf_op jit(solution)/shard_map/ppermute | solution.py:87
  6.4 5.7 %collective-permute-start = (f32[4,4,16,12]{3,2,1,0:T(8,128)S(1)}, f32[4,4,16,12]{3,2,1,0:T(8,128)S(1)}, u32[]{:S(2)}, u32[]{:S(2)}) collective-permute-start(f32[4,4,16,12]{3,2,1,0:T(8,128)S(1)} %get-tuple-element.100), channel_id=1, source_target_pairs={{0,2},{3,1},{2,4},{5,3},{4,6},{7,5},{8,10},{11,9},{10,12},{13,11},... | collective-permute-start | bytes 36872 | tf_op jit(solution)/shard_map/ppermute | solution.py:88
  13.6 9.4 %collective-permute-start.4 = (f32[8,35,152]{2,1,0:T(8,128)S(1)}, f32[8,35,152]{2,1,0:T(8,128)S(1)}, u32[]{:S(2)}, u32[]{:S(2)}) collective-permute-start(f32[8,35,152]{2,1,0:T(8,128)S(1)} %pad_maximum_fusion.6), channel_id=1, source_target_pairs={{8,0},{16,8},{24,16},{0,24},{9,1},{17,9},{25,17},{1,25},{10,2},{18... | collective-permute-start | bytes 510728 | tf_op jit(solution)/shard_map/ppermute | solution.py:40
  16.0 14.6 %collective-permute-start.3 = (f32[8,35,152]{2,1,0:T(8,128)S(1)}, f32[8,35,152]{2,1,0:T(8,128)S(1)}, u32[]{:S(2)}, u32[]{:S(2)}) collective-permute-start(f32[8,35,152]{2,1,0:T(8,128)S(1)} %pad_maximum_fusion.5), channel_id=1, source_target_pairs={{0,8},{8,16},{16,24},{24,0},{1,9},{9,17},{17,25},{25,1},{2,10},{10... | collective-permute-start | bytes 510728 | tf_op jit(solution)/shard_map/ppermute | solution.py:39
  59.1 2.4 %collective-permute-start.5 = (f32[6,4,16,128]{3,2,1,0:T(8,128)S(1)}, f32[6,4,16,128]{3,2,1,0:T(8,128)S(1)}, u32[]{:S(2)}, u32[]{:S(2)}) collective-permute-start(f32[6,4,16,128]{3,2,1,0:T(8,128)S(1)} %get-tuple-element.64), channel_id=1, source_target_pairs={{0,1},{1,0},{2,3},{3,2},{4,5},{5,4},{6,7},{7,6},{8,9},{9,8},{10,11... | collective-permute-start | bytes 589832 | tf_op jit(solution)/shard_map/ppermute | solution.py:110

commit v3 on v2

--- a/solution.py
+++ b/solution.py
@@ -181,6 +181,23 @@
         * (grains * (1.0 - density) - grains * grains * (2.0 - density) + grains * square_sum)
     )
     return (bulk_drive, grain_drive)
+
+
+def chemical_pullback(density, grains, copotential, codrive):
+    square_sum = jnp.sum(grains * grains, axis=0)
+    grain_square = grains * grains
+    drive_slope = 12.0 * grain_weight * (grain_square - grains)
+    bulk_slope = 2.0 * bulk_weight * (1.0 - 6.0 * density + 6.0 * density * density) + 2.0 * grain_weight
+    if codrive is None:
+        return copotential * bulk_slope, copotential * drive_slope
+    pull_density = copotential * bulk_slope + jnp.sum(codrive * drive_slope, axis=0)
+    coupling = jnp.sum(codrive * grains, axis=0)
+    pull_grains = (
+        copotential * drive_slope
+        + 12.0 * grain_weight * codrive * ((1.0 - density) - 2.0 * grains * (2.0 - density) + square_sum)
+        + 24.0 * grain_weight * grains * coupling
+    )
+    return pull_density, pull_grains
 
 
 def shards(density, labels, observed, measured):
@@ -237,20 +254,23 @@
     costate = in_domain(measured * (density - observed), d_width, geometry)
     c_width = d_width
     last_density = crop(density, d_width, 0)
-    cograins = jnp.zeros((GRAINS,) + costate.shape, jnp.float32)
-    cg_width = c_width
+    cograins, cg_width = None, c_width
     for moment in range(STEPS - 1, -1, -1):
         fields_density, fd_width, fields_grains, fg_width = history[moment]
         copotential = cahn_step * laplace(costate, c_width, geometry, True)
         nu_width = c_width - 1
-        grain_spread = laplace(cograins, cg_width, geometry, True)
         point = min(nu_width, cg_width, fd_width, fg_width)
-        unused, pullback = jax.vjp(
-            chemical, crop(fields_density, fd_width, point), crop(fields_grains, fg_width, point)
-        )
-        pull_density, pull_grains = pullback(
-            (crop(copotential, nu_width, point), -allen_step * crop(cograins, cg_width, point))
-        )
+        here_density = crop(fields_density, fd_width, point)
+        here_grains = crop(fields_grains, fg_width, point)
+        here_copotential = crop(copotential, nu_width, point)
+        if cograins is None:
+            pull_density, pull_grains = chemical_pullback(
+                here_density, here_grains, here_copotential, None
+            )
+        else:
+            pull_density, pull_grains = chemical_pullback(
+                here_density, here_grains, here_copotential, -allen_step * crop(cograins, cg_width, point)
+            )
         reaction = laplace(in_domain(copotential, nu_width, geometry), nu_width, geometry, True)
         new_c_width = nu_width - 1
         new_costate = (
@@ -258,12 +278,17 @@
             + crop(pull_density, point, new_c_width)
             - cahn_gradient * reaction
         )
-        new_cg_width = min(cg_width - 1, point)
-        new_cograins = (
-            crop(cograins, cg_width, new_cg_width)
-            + crop(pull_grains, point, new_cg_width)
-            + allen_step * allen_gradient * crop(grain_spread, cg_width - 1, new_cg_width)
-        )
+        if cograins is None:
+            new_cg_width = point
+            new_cograins = pull_grains
+        else:
+            grain_spread = laplace(cograins, cg_width, geometry, True)
+            new_cg_width = min(cg_width - 1, point)
+            new_cograins = (
+                crop(cograins, cg_width, new_cg_width)
+                + crop(pull_grains, point, new_cg_width)
+                + allen_step * allen_gradient * crop(grain_spread, cg_width - 1, new_cg_width)
+            )
         costate, c_width = in_domain(new_costate, new_c_width, geometry), new_c_width
         cograins, cg_width = in_domain(new_cograins, new_cg_width, geometry), new_cg_width
 

time: 65.7 us -> 63.3 us (0.963); the launches traced: 64.4 us -> 63 us
  other arithmetic: 27.9 us -> 26 us
  starting transfers between devices: 9.63 us -> 11.1 us
  waiting for transfers between devices: 17.2 us -> 16.2 us
    ppermute x1, waiting for transfers between devices: 1.63 us -> 0.01 us  [edge_columns(): lax.ppermute(jnp.where(own == 0, last, first), ('rad', 'hgt'), same)]
    ppermute x1, starting transfers between devices: 3.11 us -> 4.68 us  [edge_columns(): lax.ppermute(jnp.where(own == 0, first, last), ('rad', 'hgt'), cross)]
    ppermute x1, starting transfers between devices: 0.06 us -> 1.26 us  [azim_exchange(): before = lax.ppermute(last, 'azim', up)]
    ppermute x1, starting transfers between devices: 2.33 us -> 1.21 us  [azim_exchange(): after = lax.ppermute(leading, 'azim', down)]
    select_n x12, other arithmetic: 10.3 us -> 9.36 us  [in_domain(): return jnp.where(radial_mask(width, geometry), x, 0.0)]
    ppermute x1, waiting for transfers between devices: 0.01 us -> 0.88 us  [edge_columns(): lax.ppermute(jnp.where(own == 0, first, last), ('rad', 'hgt'), cross)]
    reduce_sum x3 -> x2, other arithmetic: 1.38 us -> 1.06 us  [chemical_pullback(): jnp.sum(codrive * drive_slope, axis=0)]
    slice x12 -> x14, local copies, waits for them, and re-layouts: 1.21 us -> 1.42 us  [crop(): return x[..., cut:x.shape[-2] - cut, cut:x.shape[-1] - cut]]
where the time goes in v3:
time: 63.3 us; the launch traced here: 63 us
  other arithmetic  26 us (41%)
  waiting for transfers between devices  16.2 us (26%)
  starting transfers between devices  11.1 us (18%)
  local copies, waits for them, and re-layouts  8.17 us (13%)
  between operations  1.55 us (2%)
    select_n x12, other arithmetic, in_domain(): return jnp.where(radial_mask(width, geometry), x, 0.0)  9.36 us
    ppermute x1, waiting for transfers between devices, azim_exchange(): before = lax.ppermute(last, 'azim', up)  7.23 us
    ppermute x1, waiting for transfers between devices, azim_exchange(): after = lax.ppermute(leading, 'azim', down)  7.06 us
    ppermute x1, starting transfers between devices, edge_columns(): lax.ppermute(jnp.where(own == 0, first, last), ('rad', 'hgt'), cross)  4.68 us
    reduce_sum x2, other arithmetic, chemical(): cube_sum = jnp.sum(grains * grains * grains, axis=0)  3.38 us
    sub x3, other arithmetic, shards(): crop(bulk_drive, both, pot_width)  2.1 us
    ppermute x1, starting transfers between devices, edge_columns(): lax.ppermute(jnp.where(own == 0, last, first), ('rad', 'hgt'), same)  1.92 us
    mul x3, other arithmetic, shards(): copotential = cahn_step * laplace(costate, c_width, geometry, True)  1.64 us
  transfers between devices with their start and end apart: 6, of which 4 were waited for; matrix products, arithmetic and copies ran while one was open for 3% of the time, Pallas kernels for 0%

profile of v3, /device:TPU:9, one launch (start us, length us, event | category | flops | bytes accessed | tf_op | source)
XLA Modules:
  0.0 63.0 jit_solution(17923271426795083158)
XLA Ops:
  0.6 0.9 %convert_bitcast_fusion = (f32[1,4,16,256]{3,2,1,0:T(8,128)S(1)}, f32[1,4,16,256]{3,2,1,0:T(8,128)S(1)}) fusion(s32[4,16,256]{2,1,0:T(8,128)} %param.7, s32[4,16,256]{2,1,0:T(8,128)} %param.5), kind=kLoop, calls=%fused_computation.451 | loop fusion | flops 32768 | bytes 262144 | tf_op jit(solution)/shard_map/stack | solution.py:214
  1.5 0.9 %fusion.267 = (f32[1,4,4,16,256]{4,3,2,1,0:T(8,128)S(1)}, f32[4,4,16,256]{3,2,1,0:T(8,128)S(1)}) fusion(f32[1,4,16,256]{3,2,1,0:T(8,128)S(1)} %get-tuple-element.140, f32[1,4,16,256]{3,2,1,0:T(8,128)} %bitcast.39, f32[1,4,16,256]{3,2,1,0:T(8,128)S(1)} %get-tuple-element.141, f32[1,4,16,256]{3,2,1,0:T(8,128)} %bitcast.40), kind=kLoop, calls=%fused_computation.541 | loop fusion | flops 196608 | bytes 786432 | tf_op jit(solution)/shard_map/stack | solution.py:56
  2.5 0.7 %collective-permute-start.2 = (f32[4,4,16,256]{3,2,1,0:T(8,128)S(1)}, f32[4,4,16,256]{3,2,1,0:T(8,128)S(1)}, u32[]{:S(2)}, u32[]{:S(2)}) collective-permute-start(f32[4,4,16,256]{3,2,1,0:T(8,128)S(1)} %get-tuple-element.83), channel_id=1, source_target_pairs={{0,1},{1,0},{2,3},{3,2},{4,5},{5,4},{6,7},{7,6},{8,9},{9,8},{10,11... | collective-permute-start | bytes 786440 | tf_op jit(solution)/shard_map/ppermute | solution.py:55
  3.2 0.1 slice_select_fusion.1
  3.3 1.9 %collective-permute-start = (f32[4,4,16,12]{3,2,1,0:T(8,128)S(1)}, f32[4,4,16,12]{3,2,1,0:T(8,128)S(1)}, u32[]{:S(2)}, u32[]{:S(2)}) collective-permute-start(f32[4,4,16,12]{3,2,1,0:T(8,128)S(1)} %get-tuple-element.84), channel_id=1, source_target_pairs={{0,2},{3,1},{2,4},{5,3},{4,6},{7,5},{8,10},{11,9},{10,12},{13,11},... | collective-permute-start | bytes 36872 | tf_op jit(solution)/shard_map/ppermute | solution.py:88
  5.2 4.7 %collective-permute-start.1 = (f32[4,4,16,12]{3,2,1,0:T(8,128)S(1)}, f32[4,4,16,12]{3,2,1,0:T(8,128)S(1)}, u32[]{:S(2)}, u32[]{:S(2)}) collective-permute-start(f32[4,4,16,12]{3,2,1,0:T(8,128)S(1)} %get-tuple-element.85), channel_id=1, source_target_pairs={{1,2},{2,1},{3,4},{4,3},{5,6},{6,5},{9,10},{10,9},{11,12},{12,11},... | collective-permute-start | bytes 36872 | tf_op jit(solution)/shard_map/ppermute | solution.py:87
  11.7 0.1 slice.1103
  11.8 0.9 %collective-permute-done.1 = f32[4,4,16,12]{3,2,1,0:T(8,128)S(1)} collective-permute-done((f32[4,4,16,12]{3,2,1,0:T(8,128)S(1)}, f32[4,4,16,12]{3,2,1,0:T(8,128)S(1)}, u32[]{:S(2)}, u32[]{:S(2)}) %collective-permute-start.1) | collective-permute-done | bytes 12320 | tf_op jit(solution)/shard_map/ppermute | solution.py:87
  12.8 0.6 gather_fusion
  13.4 0.1 select_bitcast_fusion
  13.6 0.4 fusion.62
  14.2 1.3 %collective-permute-start.3 = (f32[8,35,152]{2,1,0:T(8,128)S(1)}, f32[8,35,152]{2,1,0:T(8,128)S(1)}, u32[]{:S(2)}, u32[]{:S(2)}) collective-permute-start(f32[8,35,152]{2,1,0:T(8,128)S(1)} %pad_maximum_fusion.5), channel_id=1, source_target_pairs={{0,8},{8,16},{16,24},{24,0},{1,9},{9,17},{17,25},{25,1},{2,10},{10... | collective-permute-start | bytes 510728 | tf_op jit(solution)/shard_map/ppermute | solution.py:39
  15.5 1.2 %collective-permute-start.4 = (f32[8,35,152]{2,1,0:T(8,128)S(1)}, f32[8,35,152]{2,1,0:T(8,128)S(1)}, u32[]{:S(2)}, u32[]{:S(2)}) collective-permute-start(f32[8,35,152]{2,1,0:T(8,128)S(1)} %pad_maximum_fusion.6), channel_id=1, source_target_pairs={{8,0},{16,8},{24,16},{0,24},{9,1},{17,9},{25,17},{1,25},{10,2},{18... | collective-permute-start | bytes 510728 | tf_op jit(solution)/shard_map/ppermute | solution.py:40
  16.8 7.2 %collective-permute-done.3 = f32[8,35,152]{2,1,0:T(8,128)S(1)} collective-permute-done((f32[8,35,152]{2,1,0:T(8,128)S(1)}, f32[8,35,152]{2,1,0:T(8,128)S(1)}, u32[]{:S(2)}, u32[]{:S(2)}) %collective-permute-start.3) | collective-permute-done | bytes 170272 | tf_op jit(solution)/shard_map/ppermute | solution.py:39
  24.0 7.1 %collective-permute-done.4 = f32[8,35,152]{2,1,0:T(8,128)S(1)} collective-permute-done((f32[8,35,152]{2,1,0:T(8,128)S(1)}, f32[8,35,152]{2,1,0:T(8,128)S(1)}, u32[]{:S(2)}, u32[]{:S(2)}) %collective-permute-start.4) | collective-permute-done | bytes 170272 | tf_op jit(solution)/shard_map/ppermute | solution.py:40
  31.1 0.2 pad_maximum_fusion.3
  31.3 0.4 multiply_reduce_fusion.2
  31.7 0.2 slice.942
  32.0 0.6 fusion.67
  32.6 0.7 %broadcast_subtract_fusion = (f32[8,36,148]{2,1,0:T(8,128)S(1)}, f32[8,36,148]{2,1,0:T(8,128)S(1)}) fusion(f32[8]{0:T(128)S(1)} %get-tuple-element.142, f32[8,38,150]{2,1,0:T(8,128)S(1)} %get-tuple-element.77, f32[8]{0:T(128)S(1)} %get-tuple-element.143, f32[148]{0:T(256)S(1)} %get-tuple-element.138, f32[148]{0:T(256)S(1)} %get-tuple-element.139, ...), kind=kLoop, calls=%fused_computation.401 | loop fusion | flops 895104 | bytes 2640384 | tf_op jit(solution)/shard_map/sub | solution.py:175
  33.3 0.1 broadcast_multiply_fusion.9
  33.4 0.2 slice.939
  33.6 0.2 slice.941
  33.7 0.2 slice.966
  33.9 3.0 %multiply_reduce_fusion.1 = (f32[8,36,148]{2,1,0:T(8,128)S(1)}, f32[8,36,148]{2,1,0:T(8,128)S(1)}, f32[4,8,36,148]{3,2,1,0:T(8,128)S(1)}) fusion(f32[8]{0:T(128)S(1)} %get-tuple-element.142, f32[4,8,38,150]{3,2,1,0:T(8,128)S(1)} %get-tuple-element.61, f32[8]{0:T(128)S(1)} %get-tuple-element.143, f32[148]{0:T(256)S(1)} %get-tuple-element.138, ...), kind=kLoop, calls=%fused_computation.59 | loop fusion | flops 5200128 | bytes 11186688 | tf_op jit(solution)/shard_map/reduce_sum | solution.py:174
  36.9 0.2 mul.1278
  37.1 0.9 %fusion.83 = (f32[8,34,146]{2,1,0:T(8,128)S(1)}, f32[8,34,146]{2,1,0:T(8,128)S(1)}, f32[8,34,146]{2,1,0:T(8,128)S(1)}) fusion(f32[8,36,148]{2,1,0:T(8,128)S(1)} %get-tuple-element.24, f32[8,36,148]{2,1,0:T(8,128)S(1)} %get-tuple-element.11, f32[8]{0:T(128)S(1)} %get-tuple-element.142, f32[8]{0:T(128)S(1)} %get-tuple-element.143, ...), kind=kLoop, calls=%fused_computation.156 | loop fusion | flops 1072224 | bytes 3430784 | tf_op jit(solution)/shard_map/sub | solution.py:237
  37.9 3.0 %fusion.17 = f32[4,8,34,146]{3,2,1,0:T(8,128)S(1)} fusion(f32[4,8,36,148]{3,2,1,0:T(8,128)S(1)} %get-tuple-element.25, f32[4,8,36,148]{3,2,1,0:T(8,128)S(1)} %mul.1278, f32[8,34,146]{2,1,0:T(8,128)S(1)} %get-tuple-element.71, f32[8,34,146]{2,1,0:T(8,128)S(1)} %slice.966, f32[8,34,146]{2,1,0:T(8,128)S(1)} %get-tuple-element.72, f32[8]{0:T(128)S(1)} %get-tuple-element.142, ...), kind=kLoop, calls=%fused_computation.28 | loop fusion | flops 4288896 | bytes 10799104 | tf_op jit(solution)/shard_map/jit(_where)/select_n | solution.py:133
  41.0 0.4 multiply_reduce_fusion
  41.4 0.6 fusion.139
  41.9 0.1 slice.999
  42.0 0.6 %fusion.115 = f32[8,30,142]{2,1,0:T(8,128)S(1)} fusion(f32[8,32,144]{2,1,0:T(8,128)S(1)} %fusion.139, f32[8,32,144]{2,1,0:T(8,128)S(1)} %get-tuple-element.10, f32[8,32,144]{2,1,0:T(8,128)S(1)} %get-tuple-element.9, f32[8]{0:T(128)S(1)} %get-tuple-element.142, f32[8]{0:T(128)S(1)} %get-tuple-element.143, f32[142]{0:T(256)S(1)} %get-tuple-element.130, ...), kind=kLoop, calls=%fused_computation.209 | loop fusion | flops 954240 | bytes 2238592 | tf_op jit(solution)/shard_map/sub | solution.py:237
  42.7 0.8 %fusion.158 = (f32[8,28,140]{2,1,0:T(8,128)S(1)}, f32[8,28,140]{2,1,0:T(8,128)S(1)}) fusion(f32[8,6,152]{2,1,0:T(8,128)S(1)} %get-tuple-element.76, f32[8,16,152]{2,1,0:T(8,128)S(1)} %get-tuple-element.53, f32[8,6,152]{2,1,0:T(8,128)S(1)} %get-tuple-element.74, f32[8,6,152]{2,1,0:T(8,128)S(1)} %get-tuple-element.75, ...), kind=kLoop, calls=%fused_computation.267 | loop fusion | flops 846720 | bytes 2615808 | tf_op jit(solution)/shard_map/jit(_where)/select_n | solution.py:133
  43.6 0.5 broadcast_multiply_fusion.2
  44.2 0.4 fusion.42
  44.6 0.5 multiply_reduce_fusion.8
  45.1 1.1 %fusion.274 = (f32[4,8,24,136]{3,2,1,0:T(8,128)S(1)}, f32[4,8,24,136]{3,2,1,0:T(8,128)S(1)}, f32[4,8,24,136]{3,2,1,0:T(8,128)S(1)}, f32[4,8,24,136]{3,2,1,0:T(8,128)S(1)}, f32[4,8,24,136]{3,2,1,0:T(8,128)S(1)}) fusion(f32[4,8,26,138]{3,2,1,0:T(8,128)S(1)} %fusion.42), kind=kLoop, calls=%fused_computation.542 | loop fusion | bytes 5496832 | tf_op jit(solution)/shard_map/slice | solution.py:152
  46.1 0.1 slice_divide_fusion.1
  46.2 0.1 broadcast_multiply_fusion.7
  46.4 0.6 fusion.210
  47.1 0.5 fusion.277
  47.6 0.4 broadcast_multiply_fusion.10
  48.0 2.3 %fusion.53 = f32[4,8,22,134]{3,2,1,0:T(8,128)S(1)} fusion(f32[4,8,24,136]{3,2,1,0:T(8,128)S(1)} %get-tuple-element.30, f32[4,8,24,136]{3,2,1,0:T(8,128)S(1)} %get-tuple-element.31, f32[4,8,24,136]{3,2,1,0:T(8,128)S(1)} %get-tuple-element.32, f32[4,8,24,136]{3,2,1,0:T(8,128)S(1)} %get-tuple-element.33, f32[4,8,24,136]{3,2,1,0:T(8,128)S(1)} %get-tuple-element.50, ...), kind=kLoop, calls=%fused_computation.89 | loop fusion | flops 2924416 | bytes 4624270 | tf_op jit(solution)/shard_map/jit(_where)/select_n | solution.py:133
  50.3 0.5 multiply_reduce_fusion.6
  50.9 0.1 slice_divide_fusion
  51.0 1.0 %fusion.276 = (f32[4,8,20,132]{3,2,1,0:T(8,128)S(1)}, f32[4,8,20,132]{3,2,1,0:T(8,128)S(1)}, f32[4,8,20,132]{3,2,1,0:T(8,128)S(1)}, f32[4,8,20,132]{3,2,1,0:T(8,128)S(1)}, f32[4,8,20,132]{3,2,1,0:T(8,128)S(1)}) fusion(f32[4,8,22,134]{3,2,1,0:T(8,128)S(1)} %fusion.53), kind=kLoop, calls=%fused_computation.544 | loop fusion | bytes 4835328 | tf_op jit(solution)/shard_map/slice | solution.py:163
  52.0 0.7 %fusion.195 = f32[8,20,132]{2,1,0:T(8,128)S(1)} fusion(f32[8,22,134]{2,1,0:T(8,128)S(1)} %get-tuple-element.88, f32[8,20,134]{2,1,0:T(8,128)S(1)} %slice_divide_fusion.5, f32[8,22,134]{2,1,0:T(8,128)S(1)} %get-tuple-element.3, f32[8,22,134]{2,1,0:T(8,128)S(1)} %get-tuple-element.17, f32[8,22,134]{2,1,0:T(8,128)S(1)} %get-tuple-element.69, ...), kind=kLoop, calls=%fused_computation.329 | loop fusion | flops 549120 | bytes 2448384 | tf_op jit(solution)/shard_map/jit(_where)/select_n | solution.py:133
  52.8 0.7 %broadcast_multiply_fusion.8 = (f32[8,18,130]{2,1,0:T(8,128)S(1)}, f32[8,18,130]{2,1,0:T(8,128)S(1)}) fusion(f32[8]{0:T(128)S(1)} %get-tuple-element.142, f32[8,20,132]{2,1,0:T(8,128)S(1)} %fusion.195, f32[8]{0:T(128)S(1)} %get-tuple-element.143, f32[130]{0:T(256)S(1)} %get-tuple-element.123, f32[8,18,132]{2,1,0:T(8,128)S(1)} %slice_divide_fusion.4, ...), kind=kLoop, calls=%fused_computation.420 | loop fusion | flops 318240 | bytes 1530112 | tf_op jit(solution)/shard_map/mul | solution.py:260
  53.5 0.1 slice.1091
  53.6 0.5 fusion.275
  54.1 0.1 slice.1101
  54.2 0.1 slice_bitcast_fusion.5
  54.3 0.3 multiply_subtract_fusion.1
  54.6 0.7 %fusion.47 = (f32[4,8,18,130]{3,2,1,0:T(8,128)S(1)}, f32[4,8,18,130]{3,2,1,0:T(8,128)S(1)}) fusion(f32[4,8,20,132]{3,2,1,0:T(8,128)S(1)} %get-tuple-element.38, f32[4,8,20,132]{3,2,1,0:T(8,128)S(1)} %get-tuple-element.40, f32[130]{0:T(256)S(1)} %slice.1085, f32[4,8,20,132]{3,2,1,0:T(8,128)S(1)} %get-tuple-element.39, f32[130]{0:T(256)S(1)} %slice.1086), kind=kLoop, calls=%fused_computation.81 | loop fusion | flops 299520 | bytes 1498640 | tf_op jit(solution)/shard_map/mul | solution.py:155
  55.3 1.1 %fusion.45 = (f32[4,8,18,130]{3,2,1,0:T(8,128)S(1)}, f32[4,8,18,130]{3,2,1,0:T(8,128)S(1)}, f32[4,8,18,130]{3,2,1,0:T(8,128)S(1)}) fusion(f32[4,8,20,132]{3,2,1,0:T(8,128)S(1)} %get-tuple-element.48, f32[4,8,20,132]{3,2,1,0:T(8,128)S(1)} %get-tuple-element.44, f32[4,8,20,132]{3,2,1,0:T(8,128)S(1)} %get-tuple-element.47, ...), kind=kLoop, calls=%fused_computation.77 | loop fusion | flops 374400 | bytes 2396160 | tf_op jit(solution)/shard_map/sub | solution.py:163
  56.4 0.3 fusion.251
  56.7 0.9 %fusion.143 = f32[4,8,16,128]{3,2,1,0:T(8,128)S(1)} fusion(f32[4,8,18,130]{3,2,1,0:T(8,128)S(1)} %get-tuple-element.35, f32[4,8,18,130]{3,2,1,0:T(8,128)S(1)} %get-tuple-element.28, f32[4,8,18,130]{3,2,1,0:T(8,128)S(1)} %get-tuple-element.43, f32[4,8,18,130]{3,2,1,0:T(8,128)S(1)} %get-tuple-element.42, f32[4,8,18,130]{3,2,1,0:T(8,128)S(1)} %get-tuple-element.41, ...), kind=kLoop, calls=%fused_computation.240 | loop fusion | flops 1048576 | bytes 3015360 | tf_op jit(solution)/shard_map/jit(_where)/select_n | solution.py:133
  57.7 1.3 %collective-permute-start.5 = (f32[6,4,16,128]{3,2,1,0:T(8,128)S(1)}, f32[6,4,16,128]{3,2,1,0:T(8,128)S(1)}, u32[]{:S(2)}, u32[]{:S(2)}) collective-permute-start(f32[6,4,16,128]{3,2,1,0:T(8,128)S(1)} %get-tuple-element.59), channel_id=1, source_target_pairs={{0,1},{1,0},{2,3},{3,2},{4,5},{5,4},{6,7},{7,6},{8,9},{9,8},{10,11... | collective-permute-start | bytes 589832 | tf_op jit(solution)/shard_map/ppermute | solution.py:110
  59.0 1.1 %collective-permute-done.5 = f32[6,4,16,128]{3,2,1,0:T(8,128)S(1)} collective-permute-done((f32[6,4,16,128]{3,2,1,0:T(8,128)S(1)}, f32[6,4,16,128]{3,2,1,0:T(8,128)S(1)}, u32[]{:S(2)}, u32[]{:S(2)}) %collective-permute-start.5) | collective-permute-done | bytes 196640 | tf_op jit(solution)/shard_map/ppermute | solution.py:110
  60.1 0.6 gather_fusion.1
  60.7 0.1 select_bitcast_fusion.1
  60.8 0.7 %copy_bitcast_fusion = f32[4,4,16,256]{3,2,1,0:T(8,128)} fusion(f32[6,4,16,2,128]{4,2,1,0,3:T(8,128)S(1)} %select_bitcast_fusion.1), kind=kLoop, calls=%fused_computation.236 | loop fusion | bytes 524288 | tf_op jit(solution)/shard_map/slice | solution.py:300
  61.6 0.7 %squeeze.6 = f32[4,16,256]{2,1,0:T(8,128)} reshape(f32[1,4,16,2,128]{4,3,2,1,0:T(2,128)S(1)} %copy.9) | data formatting | bytes 131072 | tf_op jit(solution)/shard_map/squeeze | solution.py:300
  62.4 0.7 %squeeze.7 = f32[4,16,256]{2,1,0:T(8,128)} reshape(f32[1,4,16,2,128]{4,3,2,1,0:T(2,128)S(1)} %copy.10) | data formatting | bytes 131072 | tf_op jit(solution)/shard_map/squeeze | solution.py:300
  (95 shorter events, 2.6 us)
Async XLA Ops:
  2.5 10.3 %collective-permute-start.2 = (f32[4,4,16,256]{3,2,1,0:T(8,128)S(1)}, f32[4,4,16,256]{3,2,1,0:T(8,128)S(1)}, u32[]{:S(2)}, u32[]{:S(2)}) collective-permute-start(f32[4,4,16,256]{3,2,1,0:T(8,128)S(1)} %get-tuple-element.83), channel_id=1, source_target_pairs={{0,1},{1,0},{2,3},{3,2},{4,5},{5,4},{6,7},{7,6},{8,9},{9,8},{10,11... | collective-permute-start | bytes 786440 | tf_op jit(solution)/shard_map/ppermute | solution.py:55
  3.3 8.5 %collective-permute-start = (f32[4,4,16,12]{3,2,1,0:T(8,128)S(1)}, f32[4,4,16,12]{3,2,1,0:T(8,128)S(1)}, u32[]{:S(2)}, u32[]{:S(2)}) collective-permute-start(f32[4,4,16,12]{3,2,1,0:T(8,128)S(1)} %get-tuple-element.84), channel_id=1, source_target_pairs={{0,2},{3,1},{2,4},{5,3},{4,6},{7,5},{8,10},{11,9},{10,12},{13,11},... | collective-permute-start | bytes 36872 | tf_op jit(solution)/shard_map/ppermute | solution.py:88
  5.2 7.5 %collective-permute-start.1 = (f32[4,4,16,12]{3,2,1,0:T(8,128)S(1)}, f32[4,4,16,12]{3,2,1,0:T(8,128)S(1)}, u32[]{:S(2)}, u32[]{:S(2)}) collective-permute-start(f32[4,4,16,12]{3,2,1,0:T(8,128)S(1)} %get-tuple-element.85), channel_id=1, source_target_pairs={{1,2},{2,1},{3,4},{4,3},{5,6},{6,5},{9,10},{10,9},{11,12},{12,11},... | collective-permute-start | bytes 36872 | tf_op jit(solution)/shard_map/ppermute | solution.py:87
  14.2 9.8 %collective-permute-start.3 = (f32[8,35,152]{2,1,0:T(8,128)S(1)}, f32[8,35,152]{2,1,0:T(8,128)S(1)}, u32[]{:S(2)}, u32[]{:S(2)}) collective-permute-start(f32[8,35,152]{2,1,0:T(8,128)S(1)} %pad_maximum_fusion.5), channel_id=1, source_target_pairs={{0,8},{8,16},{16,24},{24,0},{1,9},{9,17},{17,25},{25,1},{2,10},{10... | collective-permute-start | bytes 510728 | tf_op jit(solution)/shard_map/ppermute | solution.py:39
  15.5 15.6 %collective-permute-start.4 = (f32[8,35,152]{2,1,0:T(8,128)S(1)}, f32[8,35,152]{2,1,0:T(8,128)S(1)}, u32[]{:S(2)}, u32[]{:S(2)}) collective-permute-start(f32[8,35,152]{2,1,0:T(8,128)S(1)} %pad_maximum_fusion.6), channel_id=1, source_target_pairs={{8,0},{16,8},{24,16},{0,24},{9,1},{17,9},{25,17},{1,25},{10,2},{18... | collective-permute-start | bytes 510728 | tf_op jit(solution)/shard_map/ppermute | solution.py:40
  57.7 2.4 %collective-permute-start.5 = (f32[6,4,16,128]{3,2,1,0:T(8,128)S(1)}, f32[6,4,16,128]{3,2,1,0:T(8,128)S(1)}, u32[]{:S(2)}, u32[]{:S(2)}) collective-permute-start(f32[6,4,16,128]{3,2,1,0:T(8,128)S(1)} %get-tuple-element.59), channel_id=1, source_target_pairs={{0,1},{1,0},{2,3},{3,2},{4,5},{5,4},{6,7},{7,6},{8,9},{9,8},{10,11... | collective-permute-start | bytes 589832 | tf_op jit(solution)/shard_map/ppermute | solution.py:110

commit v4 on v3

--- a/solution.py
+++ b/solution.py
@@ -183,6 +183,19 @@
     return (bulk_drive, grain_drive)
 
 
+def reach():
+    need_lc, need_lg = [0], [0]
+    for moment in range(STEPS):
+        need_lc.append(need_lc[-1] + 2)
+        need_lg.append(max(need_lg[-1] + 1, need_lc[moment]))
+    need_d, need_e = [need_lc[STEPS]], [-1]
+    for moment in range(STEPS - 1, -1, -1):
+        pot_width = need_d[0] + 1
+        need_d.insert(0, max(pot_width + 1, need_e[0], need_lc[moment]))
+        need_e.insert(0, max(pot_width, need_e[0] + 1, need_lc[moment]))
+    return need_d, need_e, need_lc, need_lg
+
+
 def chemical_pullback(density, grains, copotential, codrive):
     square_sum = jnp.sum(grains * grains, axis=0)
     grain_square = grains * grains
@@ -217,7 +230,8 @@
         packed = two_core_window(gather_axis(packed, "hgt", 1), received, HALO)
     else:
         packed = chip_window(gather_axis(packed, "hgt", 1), HALO)
-    widths = (HALO, HALO - 1, 2 * STEPS, 2 * STEPS)
+    need_d, need_e, need_lc, need_lg = reach()
+    widths = (need_d[0], need_e[0], need_lc[STEPS], need_lc[STEPS])
     density, grain_label, observed, measured = [
         f[..., HALO - w : f.shape[-1] - (HALO - w)]
         for f, w in zip(azim_exchange(list(packed), widths), widths)
@@ -225,41 +239,42 @@
     grains = (
         grain_label[None] == jnp.arange(GRAINS, dtype=jnp.float32)[:, None, None, None]
     ).astype(jnp.float32)
-    d_width, g_width = widths[0], widths[1]
-    density = in_domain(density, d_width, geometry)
-    grains = in_domain(grains, g_width, geometry)
+    need_d, need_e, need_lc, need_lg = reach()
+    density = in_domain(density, need_d[0], geometry)
+    grains = in_domain(grains, need_e[0], geometry)
     history = []
     for moment in range(STEPS):
-        history.append((density, d_width, grains, g_width))
-        both = min(d_width, g_width)
-        bulk_drive, grain_drive = chemical(crop(density, d_width, both), crop(grains, g_width, both))
-        pot_width = min(d_width - 1, both)
-        potential = crop(bulk_drive, both, pot_width) - cahn_gradient * crop(
-            laplace(density, d_width, geometry, False), d_width - 1, pot_width
+        d_width, e_width = need_d[moment], need_e[moment]
+        history.append((density, d_width, grains, e_width))
+        pot_width = need_d[moment + 1] + 1
+        next_e = need_e[moment + 1]
+        both = max(pot_width, next_e)
+        bulk_drive, grain_drive = chemical(crop(density, d_width, both), crop(grains, e_width, both))
+        potential = crop(bulk_drive, both, pot_width) - cahn_gradient * laplace(
+            crop(density, d_width, pot_width + 1), pot_width + 1, geometry, False
         )
-        new_d_width = pot_width - 1
         flux_term = laplace(potential, pot_width, geometry, False)
-        new_density = crop(density, d_width, new_d_width) + cahn_step * flux_term
-        if moment + 1 < STEPS:
-            new_g_width = min(g_width - 1, both)
-            grain_spread = crop(laplace(grains, g_width, geometry, False), g_width - 1, new_g_width)
-            new_grains = crop(grains, g_width, new_g_width) - allen_step * (
-                crop(grain_drive, both, new_g_width) - allen_gradient * grain_spread
-            )
-            grains, g_width = in_domain(new_grains, new_g_width, geometry), new_g_width
-        density, d_width = in_domain(new_density, new_d_width, geometry), new_d_width
+        new_density = crop(density, d_width, need_d[moment + 1]) + cahn_step * flux_term
+        if next_e >= 0:
+            grain_spread = laplace(crop(grains, e_width, next_e + 1), next_e + 1, geometry, False)
+            new_grains = crop(grains, e_width, next_e) - allen_step * (
+                crop(grain_drive, both, next_e) - allen_gradient * grain_spread
+            )
+            grains = in_domain(new_grains, next_e, geometry)
+        density = in_domain(new_density, need_d[moment + 1], geometry)
+    d_width = need_d[STEPS]
 
     observed = crop(observed, widths[2], d_width)
     measured = crop(measured, widths[3], d_width)
     costate = in_domain(measured * (density - observed), d_width, geometry)
     c_width = d_width
     last_density = crop(density, d_width, 0)
-    cograins, cg_width = None, c_width
+    cograins, cg_width = None, None
     for moment in range(STEPS - 1, -1, -1):
         fields_density, fd_width, fields_grains, fg_width = history[moment]
-        copotential = cahn_step * laplace(costate, c_width, geometry, True)
-        nu_width = c_width - 1
-        point = min(nu_width, cg_width, fd_width, fg_width)
+        point = need_lc[moment]
+        nu_width = point + 1
+        copotential = cahn_step * laplace(crop(costate, c_width, nu_width + 1), nu_width + 1, geometry, True)
         here_density = crop(fields_density, fd_width, point)
         here_grains = crop(fields_grains, fg_width, point)
         here_copotential = crop(copotential, nu_width, point)
@@ -272,24 +287,20 @@
                 here_density, here_grains, here_copotential, -allen_step * crop(cograins, cg_width, point)
             )
         reaction = laplace(in_domain(copotential, nu_width, geometry), nu_width, geometry, True)
-        new_c_width = nu_width - 1
-        new_costate = (
-            crop(costate, c_width, new_c_width)
-            + crop(pull_density, point, new_c_width)
-            - cahn_gradient * reaction
-        )
+        new_costate = crop(costate, c_width, point) + pull_density - cahn_gradient * reaction
+        new_cg_width = need_lg[moment]
         if cograins is None:
-            new_cg_width = point
-            new_cograins = pull_grains
+            new_cograins = crop(pull_grains, point, new_cg_width)
         else:
-            grain_spread = laplace(cograins, cg_width, geometry, True)
-            new_cg_width = min(cg_width - 1, point)
+            grain_spread = laplace(
+                crop(cograins, cg_width, new_cg_width + 1), new_cg_width + 1, geometry, True
+            )
             new_cograins = (
                 crop(cograins, cg_width, new_cg_width)
                 + crop(pull_grains, point, new_cg_width)
-                + allen_step * allen_gradient * crop(grain_spread, cg_width - 1, new_cg_width)
-            )
-        costate, c_width = in_domain(new_costate, new_c_width, geometry), new_c_width
+                + allen_step * allen_gradient * grain_spread
+            )
+        costate, c_width = in_domain(new_costate, point, geometry), point
         cograins, cg_width = in_domain(new_cograins, new_cg_width, geometry), new_cg_width
 
     costate = crop(costate, c_width, 0)

time: 63.3 us -> 57.6 us (0.910)
  the two profiles are of different devices: /device:TPU:9 before, /device:TPU:0 now
where the time goes in v4:
time: 57.6 us; the launch traced here: 57.4 us
  other arithmetic  21.1 us (37%)
  waiting for transfers between devices  18.3 us (32%)
  starting transfers between devices  10.1 us (18%)
  local copies, waits for them, and re-layouts  6.32 us (11%)
  between operations  1.57 us (3%)
    ppermute x1, waiting for transfers between devices, azim_exchange(): after = lax.ppermute(leading, 'azim', down)  7.9 us
    ppermute x1, waiting for transfers between devices, azim_exchange(): before = lax.ppermute(last, 'azim', up)  7.89 us
    select_n x11, other arithmetic, in_domain(): return jnp.where(radial_mask(width, geometry), x, 0.0)  7.47 us
    ppermute x1, starting transfers between devices, edge_columns(): lax.ppermute(jnp.where(own == 0, last, first), ('rad', 'hgt'), same)  5.76 us
    reduce_sum x2, other arithmetic, chemical(): cube_sum = jnp.sum(grains * grains * grains, axis=0)  3.7 us
    ppermute x1, starting transfers between devices, azim_exchange(): after = lax.ppermute(leading, 'azim', down)  3.03 us
    slice x15, local copies, waits for them, and re-layouts, crop(): return x[..., cut:x.shape[-2] - cut, cut:x.shape[-1] - cut]  2.62 us
    reduce_sum x1, other arithmetic, chemical(): square_sum = jnp.sum(grains * grains, axis=0)  2.29 us
  transfers between devices with their start and end apart: 6, of which 4 were waited for; matrix products, arithmetic and copies ran while one was open for 2% of the time, Pallas kernels for 0%

profile of v4, /device:TPU:0, one launch (start us, length us, event | category | flops | bytes accessed | tf_op | source)
XLA Modules:
  0.0 57.4 jit_solution(5093753199857143452)
XLA Ops:
  0.6 0.9 %convert_bitcast_fusion = (f32[1,4,16,256]{3,2,1,0:T(8,128)S(1)}, f32[1,4,16,256]{3,2,1,0:T(8,128)S(1)}) fusion(s32[4,16,256]{2,1,0:T(8,128)} %param.7, s32[4,16,256]{2,1,0:T(8,128)} %param.5), kind=kLoop, calls=%fused_computation.436 | loop fusion | flops 32768 | bytes 262144 | tf_op jit(solution)/shard_map/stack | solution.py:227
  1.5 0.9 %fusion.278 = (f32[1,4,4,16,256]{4,3,2,1,0:T(8,128)S(1)}, f32[4,4,16,256]{3,2,1,0:T(8,128)S(1)}) fusion(f32[1,4,16,256]{3,2,1,0:T(8,128)S(1)} %get-tuple-element.114, f32[1,4,16,256]{3,2,1,0:T(8,128)} %bitcast.39, f32[1,4,16,256]{3,2,1,0:T(8,128)S(1)} %get-tuple-element.115, f32[1,4,16,256]{3,2,1,0:T(8,128)} %bitcast.40), kind=kLoop, calls=%fused_computation.530 | loop fusion | flops 196608 | bytes 786432 | tf_op jit(solution)/shard_map/stack | solution.py:56
  2.5 0.5 collective-permute-start.2
  3.0 0.1 slice_select_fusion.1
  3.1 0.7 %collective-permute-start.1 = (f32[4,4,16,12]{3,2,1,0:T(8,128)S(1)}, f32[4,4,16,12]{3,2,1,0:T(8,128)S(1)}, u32[]{:S(2)}, u32[]{:S(2)}) collective-permute-start(f32[4,4,16,12]{3,2,1,0:T(8,128)S(1)} %get-tuple-element.63), channel_id=1, source_target_pairs={{1,2},{2,1},{3,4},{4,3},{5,6},{6,5},{9,10},{10,9},{11,12},{12,11},... | collective-permute-start | bytes 36872 | tf_op jit(solution)/shard_map/ppermute | solution.py:87
  3.8 5.8 %collective-permute-start = (f32[4,4,16,12]{3,2,1,0:T(8,128)S(1)}, f32[4,4,16,12]{3,2,1,0:T(8,128)S(1)}, u32[]{:S(2)}, u32[]{:S(2)}) collective-permute-start(f32[4,4,16,12]{3,2,1,0:T(8,128)S(1)} %get-tuple-element.62), channel_id=1, source_target_pairs={{0,2},{3,1},{2,4},{5,3},{4,6},{7,5},{8,10},{11,9},{10,12},{13,11},... | collective-permute-start | bytes 36872 | tf_op jit(solution)/shard_map/ppermute | solution.py:88
  10.1 0.1 compare_select_fusion.24
  10.1 0.1 compare_select_fusion.28
  10.2 0.1 compare_select_fusion.29
  10.9 1.1 %collective-permute-done = f32[4,4,16,12]{3,2,1,0:T(8,128)S(1)} collective-permute-done((f32[4,4,16,12]{3,2,1,0:T(8,128)S(1)}, f32[4,4,16,12]{3,2,1,0:T(8,128)S(1)}, u32[]{:S(2)}, u32[]{:S(2)}) %collective-permute-start) | collective-permute-done | bytes 12320 | tf_op jit(solution)/shard_map/ppermute | solution.py:88
  12.1 0.6 %gather_fusion = f32[2,4,4,16,256]{4,3,2,1,0:T(8,128)S(1)} fusion(f32[2,4,4,16,256]{4,3,2,1,0:T(8,128)S(1)} %pad_maximum_fusion, s32[1024]{0:T(1024)S(1)} %pad_clamp_fusion), kind=kCustom, calls=%fused_computation | custom fusion | bytes 1048584 | tf_op jit(solution)/shard_map/jit(_take)/gather | solution.py:58
  12.7 0.1 select_bitcast_fusion
  12.9 0.4 fusion.64
  13.5 3.0 %collective-permute-start.4 = (f32[8,35,152]{2,1,0:T(8,128)S(1)}, f32[8,35,152]{2,1,0:T(8,128)S(1)}, u32[]{:S(2)}, u32[]{:S(2)}) collective-permute-start(f32[8,35,152]{2,1,0:T(8,128)S(1)} %pad_maximum_fusion.6), channel_id=1, source_target_pairs={{8,0},{16,8},{24,16},{0,24},{9,1},{17,9},{25,17},{1,25},{10,2},{18... | collective-permute-start | bytes 510728 | tf_op jit(solution)/shard_map/ppermute | solution.py:40
  16.7 0.1 compare_select_fusion.7
  16.7 7.9 %collective-permute-done.4 = f32[8,35,152]{2,1,0:T(8,128)S(1)} collective-permute-done((f32[8,35,152]{2,1,0:T(8,128)S(1)}, f32[8,35,152]{2,1,0:T(8,128)S(1)}, u32[]{:S(2)}, u32[]{:S(2)}) %collective-permute-start.4) | collective-permute-done | bytes 170272 | tf_op jit(solution)/shard_map/ppermute | solution.py:40
  24.6 7.9 %collective-permute-done.3 = f32[8,35,152]{2,1,0:T(8,128)S(1)} collective-permute-done((f32[8,35,152]{2,1,0:T(8,128)S(1)}, f32[8,35,152]{2,1,0:T(8,128)S(1)}, u32[]{:S(2)}, u32[]{:S(2)}) %collective-permute-start.3) | collective-permute-done | bytes 170272 | tf_op jit(solution)/shard_map/ppermute | solution.py:39
  32.6 0.2 pad_maximum_fusion.3
  32.7 0.4 multiply_reduce_fusion.2
  33.1 0.4 slice.945
  33.6 0.2 slice.940
  33.8 0.6 %fusion.69 = (f32[8,38,150]{2,1,0:T(8,128)S(1)}, f32[8,38,150]{2,1,0:T(8,128)S(1)}, f32[8,38,150]{2,1,0:T(8,128)S(1)}) fusion(f32[8,40,152]{2,1,0:T(8,128)S(1)} %maximum_select_fusion, f32[8,38,150]{2,1,0:T(8,128)S(1)} %get-tuple-element.13, f32[8,38,150]{2,1,0:T(8,128)S(1)} %get-tuple-element.14, f32[8]{0:T(128)S(1)} %get-tuple-element.116, ...), kind=kLoop, calls=%fused_computation.131 | loop fusion | flops 1322400 | bytes 3173760 | tf_op jit(solution)/shard_map/sub | solution.py:253
  34.4 0.2 slice.939
  34.6 0.2 slice.937
  34.8 3.3 %multiply_reduce_fusion.1 = (f32[8,34,146]{2,1,0:T(8,128)S(1)}, f32[8,34,146]{2,1,0:T(8,128)S(1)}, f32[4,8,34,146]{3,2,1,0:T(8,128)S(1)}) fusion(f32[8]{0:T(128)S(1)} %get-tuple-element.116, f32[4,8,36,148]{3,2,1,0:T(8,128)S(1)} %slice.945, f32[8]{0:T(128)S(1)} %get-tuple-element.117, f32[146]{0:T(256)S(1)} %get-tuple-element.112, ...), kind=kLoop, calls=%fused_computation.32 | loop fusion | flops 4844864 | bytes 5926514 | tf_op jit(solution)/shard_map/reduce_sum | solution.py:174
  38.1 0.4 slice.967
  38.4 0.2 mul.1276
  38.6 0.1 slice.962
  38.8 0.7 %fusion.78 = f32[8,36,148]{2,1,0:T(8,128)S(1)} fusion(f32[8,38,150]{2,1,0:T(8,128)S(1)} %get-tuple-element.51, f32[8,40,152]{2,1,0:T(8,128)S(1)} %maximum_select_fusion, f32[8]{0:T(128)S(1)} %get-tuple-element.116, f32[8]{0:T(128)S(1)} %get-tuple-element.117, f32[148]{0:T(256)S(1)} %get-tuple-element.108, f32[148]{0:T(256)S(1)} %get-tuple-element.109, ...), kind=kLoop, calls=%fused_computation.140 | loop fusion | flops 852480 | bytes 2469888 | tf_op jit(solution)/shard_map/jit(_where)/select_n | solution.py:133
  39.4 0.6 %slice_subtract_fusion.13 = (f32[8,34,146]{2,1,0:T(8,128)S(1)}, f32[8,34,146]{2,1,0:T(8,128)S(1)}, f32[8,34,146]{2,1,0:T(8,128)S(1)}) fusion(f32[8,36,148]{2,1,0:T(8,128)S(1)} %fusion.78, f32[8]{0:T(128)S(1)} %get-tuple-element.116, f32[8]{0:T(128)S(1)} %get-tuple-element.117, f32[146]{0:T(256)S(1)} %get-tuple-element.112, f32[146]{0:T(256)S(1)} %get-tuple-element.113, ...), kind=kLoop, calls=%fused_computation.190 | loop fusion | flops 1151648 | bytes 3103104 | tf_op jit(solution)/shard_map/sub | solution.py:175
  40.0 0.1 slice.961
  40.2 0.1 slice.959
  40.3 0.6 fusion.140
  40.9 2.3 %multiply_reduce_fusion = (f32[8,30,142]{2,1,0:T(8,128)S(1)}, f32[8,30,142]{2,1,0:T(8,128)S(1)}, f32[4,8,30,142]{3,2,1,0:T(8,128)S(1)}) fusion(f32[8]{0:T(128)S(1)} %get-tuple-element.116, f32[4,8,32,144]{3,2,1,0:T(8,128)S(1)} %slice.967, f32[8]{0:T(128)S(1)} %get-tuple-element.117, f32[142]{0:T(256)S(1)} %get-tuple-element.104, ...), kind=kLoop, calls=%fused_computation.5 | loop fusion | flops 4157760 | bytes 5090862 | tf_op jit(solution)/shard_map/reduce_sum | solution.py:173
  43.2 0.5 fusion.115
  43.7 0.8 %fusion.166 = (f32[8,28,140]{2,1,0:T(8,128)S(1)}, f32[8,28,140]{2,1,0:T(8,128)S(1)}) fusion(f32[8,6,152]{2,1,0:T(8,128)S(1)} %get-tuple-element.57, f32[8,16,152]{2,1,0:T(8,128)S(1)} %get-tuple-element.33, f32[8,6,152]{2,1,0:T(8,128)S(1)} %get-tuple-element.55, f32[8,6,152]{2,1,0:T(8,128)S(1)} %get-tuple-element.56, ...), kind=kLoop, calls=%fused_computation.262 | loop fusion | flops 846720 | bytes 2615808 | tf_op jit(solution)/shard_map/jit(_where)/select_n | solution.py:133
  44.5 0.6 broadcast_select_fusion
  45.1 0.6 %fusion.217 = (f32[8,24,136]{2,1,0:T(8,128)S(1)}, f32[8,24,136]{2,1,0:T(8,128)S(1)}) fusion(f32[8,26,138]{2,1,0:T(8,128)S(1)} %get-tuple-element.19, f32[8,24,138]{2,1,0:T(8,128)S(1)} %slice_divide_fusion.6, f32[8,32,144]{2,1,0:T(8,128)S(1)} %fusion.140, f32[8,28,140]{2,1,0:T(8,128)S(1)} %get-tuple-element.22, f32[8,26,138]{2,1,0:T(8,128)S(1)} %get-tuple-element.20, ...), kind=kLoop, calls=%fused_computation.339 | loop fusion | flops 705024 | bytes 2245120 | tf_op jit(solution)/shard_map/jit(_where)/select_n | solution.py:133
  45.7 0.1 slice.1011
  45.9 0.3 slice.1009
  46.2 0.6 %fusion.286 = (f32[4,8,20,132]{3,2,1,0:T(8,128)S(1)}, f32[4,8,20,132]{3,2,1,0:T(8,128)S(1)}, f32[8,20,132]{2,1,0:T(8,128)S(1)}, f32[8,20,132]{2,1,0:T(8,128)S(1)...) fusion(f32[4,8,34,146]{3,2,1,0:T(8,128)S(1)} %get-tuple-element.25, f32[8,20,132]{2,1,0:T(8,128)S(1)} %slice.1011, ...), kind=kLoop, calls=%fused_computation.531 | loop fusion | flops 1034880 | bytes 2027652 | tf_op jit(solution)/shard_map/slice | solution.py:123
  46.8 0.1 slice_divide_fusion
  46.9 0.1 slice.1038
  47.1 0.4 broadcast_select_fusion.2
  47.5 0.1 slice_multiply_fusion.4
  47.6 0.1 slice.1037
  47.8 0.1 slice.1035
  47.9 0.6 %fusion.201 = (f32[8,20,132]{2,1,0:T(8,128)S(1)}, f32[8,20,132]{2,1,0:T(8,128)S(1)}, f32[8,20,132]{2,1,0:T(8,128)S(1)}) fusion(f32[8,22,134]{2,1,0:T(8,128)S(1)} %get-tuple-element.17, f32[8,20,132]{2,1,0:T(8,128)S(1)} %get-tuple-element.30, f32[8,20,134]{2,1,0:T(8,128)S(1)} %slice_divide_fusion.4, f32[8,24,136]{2,1,0:T(8,128)S(1)} %get-tuple-element.58, ...), kind=kLoop, calls=%fused_computation.323 | loop fusion | flops 633600 | bytes 2420736 | tf_op jit(solution)/shard_map/jit(_where)/select_n | solution.py:133
  48.5 0.1 slice.1033
  48.6 0.1 slice.1032
  48.8 2.1 %fusion.49 = f32[4,8,18,130]{3,2,1,0:T(8,128)S(1)} fusion(f32[4,8,20,132]{3,2,1,0:T(8,128)S(1)} %get-tuple-element.31, f32[4,8,18,132]{3,2,1,0:T(8,128)S(1)} %slice_divide_fusion, f32[4,8,20,132]{3,2,1,0:T(8,128)S(1)} %get-tuple-element.27, f32[4,8,20,132]{3,2,1,0:T(8,128)S(1)} %get-tuple-element.26, f32[8,18,130]{2,1,0:T(8,128)S(1)} %slice.1038, ...), kind=kLoop, calls=%fused_computation.76 | loop fusion | flops 2171520 | bytes 8365056 | tf_op jit(solution)/shard_map/jit(_where)/select_n | solution.py:133
  50.9 0.1 slice_divide_fusion.1
  51.0 0.2 multiply_reduce_fusion.9
  51.3 0.4 broadcast_select_fusion.1
  51.8 0.1 slice_multiply_fusion.6
  51.9 0.1 slice_bitcast_fusion.5
  51.9 0.3 fusion.262
  52.2 0.7 %fusion.149 = f32[4,8,16,128]{3,2,1,0:T(8,128)S(1)} fusion(f32[4,8,18,130]{3,2,1,0:T(8,128)S(1)} %fusion.49, f32[4,8,16,130]{3,2,1,0:T(8,128)S(1)} %slice_divide_fusion.1, f32[4,8,38,150]{3,2,1,0:T(8,128)S(1)} %get-tuple-element.41, f32[8]{0:T(128)S(1)} %get-tuple-element.116, f32[8]{0:T(128)S(1)} %get-tuple-element.117, f32[128]{0:T(128)S(1)} %get-tuple-element.97, ...), kind=kLoop, calls=%fused_computation.235 | loop fusion | flops 2031616 | bytes 3214336 | tf_op jit(solution)/shard_map/jit(_where)/select_n | solution.py:133
  53.0 1.4 %collective-permute-done.5 = f32[6,4,16,128]{3,2,1,0:T(8,128)S(1)} collective-permute-done((f32[6,4,16,128]{3,2,1,0:T(8,128)S(1)}, f32[6,4,16,128]{3,2,1,0:T(8,128)S(1)}, u32[]{:S(2)}, u32[]{:S(2)}) %collective-permute-start.5) | collective-permute-done | bytes 196640 | tf_op jit(solution)/shard_map/ppermute | solution.py:110
  54.5 0.6 %gather_fusion.1 = f32[2,6,4,16,128]{4,3,2,1,0:T(8,128)S(1)} fusion(f32[2,6,4,16,128]{4,3,2,1,0:T(8,128)S(1)} %pad_maximum_fusion.2, s32[1024]{0:T(1024)S(1)} %pad_clamp_fusion), kind=kCustom, calls=%fused_computation.1 | custom fusion | bytes 786440 | tf_op jit(solution)/shard_map/jit(_take)/gather | solution.py:114
  55.1 0.1 select_bitcast_fusion.1
  55.2 0.7 %copy_bitcast_fusion = f32[4,4,16,256]{3,2,1,0:T(8,128)} fusion(f32[6,4,16,2,128]{4,2,1,0,3:T(8,128)S(1)} %select_bitcast_fusion.1), kind=kLoop, calls=%fused_computation.238 | loop fusion | bytes 524288 | tf_op jit(solution)/shard_map/slice | solution.py:311
  56.0 0.7 %squeeze.6 = f32[4,16,256]{2,1,0:T(8,128)} reshape(f32[1,4,16,2,128]{4,3,2,1,0:T(2,128)S(1)} %copy.9) | data formatting | bytes 131072 | tf_op jit(solution)/shard_map/squeeze | solution.py:311
  56.7 0.7 %squeeze.7 = f32[4,16,256]{2,1,0:T(8,128)} reshape(f32[1,4,16,2,128]{4,3,2,1,0:T(2,128)S(1)} %copy.10) | data formatting | bytes 131072 | tf_op jit(solution)/shard_map/squeeze | solution.py:311
  (84 shorter events, 1.8 us)
Async XLA Ops:
  2.5 9.6 %collective-permute-start.2 = (f32[4,4,16,256]{3,2,1,0:T(8,128)S(1)}, f32[4,4,16,256]{3,2,1,0:T(8,128)S(1)}, u32[]{:S(2)}, u32[]{:S(2)}) collective-permute-start(f32[4,4,16,256]{3,2,1,0:T(8,128)S(1)} %get-tuple-element.61), channel_id=1, source_target_pairs={{0,1},{1,0},{2,3},{3,2},{4,5},{5,4},{6,7},{7,6},{8,9},{9,8},{10,11... | collective-permute-start | bytes 786440 | tf_op jit(solution)/shard_map/ppermute | solution.py:55
  3.1 7.9 %collective-permute-start.1 = (f32[4,4,16,12]{3,2,1,0:T(8,128)S(1)}, f32[4,4,16,12]{3,2,1,0:T(8,128)S(1)}, u32[]{:S(2)}, u32[]{:S(2)}) collective-permute-start(f32[4,4,16,12]{3,2,1,0:T(8,128)S(1)} %get-tuple-element.63), channel_id=1, source_target_pairs={{1,2},{2,1},{3,4},{4,3},{5,6},{6,5},{9,10},{10,9},{11,12},{12,11},... | collective-permute-start | bytes 36872 | tf_op jit(solution)/shard_map/ppermute | solution.py:87
  3.8 8.3 %collective-permute-start = (f32[4,4,16,12]{3,2,1,0:T(8,128)S(1)}, f32[4,4,16,12]{3,2,1,0:T(8,128)S(1)}, u32[]{:S(2)}, u32[]{:S(2)}) collective-permute-start(f32[4,4,16,12]{3,2,1,0:T(8,128)S(1)} %get-tuple-element.62), channel_id=1, source_target_pairs={{0,2},{3,1},{2,4},{5,3},{4,6},{7,5},{8,10},{11,9},{10,12},{13,11},... | collective-permute-start | bytes 36872 | tf_op jit(solution)/shard_map/ppermute | solution.py:88
  13.5 11.1 %collective-permute-start.4 = (f32[8,35,152]{2,1,0:T(8,128)S(1)}, f32[8,35,152]{2,1,0:T(8,128)S(1)}, u32[]{:S(2)}, u32[]{:S(2)}) collective-permute-start(f32[8,35,152]{2,1,0:T(8,128)S(1)} %pad_maximum_fusion.6), channel_id=1, source_target_pairs={{8,0},{16,8},{24,16},{0,24},{9,1},{17,9},{25,17},{1,25},{10,2},{18... | collective-permute-start | bytes 510728 | tf_op jit(solution)/shard_map/ppermute | solution.py:40
  16.6 15.9 %collective-permute-start.3 = (f32[8,35,152]{2,1,0:T(8,128)S(1)}, f32[8,35,152]{2,1,0:T(8,128)S(1)}, u32[]{:S(2)}, u32[]{:S(2)}) collective-permute-start(f32[8,35,152]{2,1,0:T(8,128)S(1)} %pad_maximum_fusion.5), channel_id=1, source_target_pairs={{0,8},{8,16},{16,24},{24,0},{1,9},{9,17},{17,25},{25,1},{2,10},{10... | collective-permute-start | bytes 510728 | tf_op jit(solution)/shard_map/ppermute | solution.py:39
  53.0 1.5 %collective-permute-start.5 = (f32[6,4,16,128]{3,2,1,0:T(8,128)S(1)}, f32[6,4,16,128]{3,2,1,0:T(8,128)S(1)}, u32[]{:S(2)}, u32[]{:S(2)}) collective-permute-start(f32[6,4,16,128]{3,2,1,0:T(8,128)S(1)} %get-tuple-element.39), channel_id=1, source_target_pairs={{0,1},{1,0},{2,3},{3,2},{4,5},{5,4},{6,7},{7,6},{8,9},{9,8},{10,11... | collective-permute-start | bytes 589832 | tf_op jit(solution)/shard_map/ppermute | solution.py:110

commit v5 on v4

--- a/solution.py
+++ b/solution.py
@@ -232,9 +232,13 @@
         packed = chip_window(gather_axis(packed, "hgt", 1), HALO)
     need_d, need_e, need_lc, need_lg = reach()
     widths = (need_d[0], need_e[0], need_lc[STEPS], need_lc[STEPS])
-    density, grain_label, observed, measured = [
-        f[..., HALO - w : f.shape[-1] - (HALO - w)]
-        for f, w in zip(azim_exchange(list(packed), widths), widths)
+    trim = lambda f, w: f[..., HALO - w : f.shape[-1] - (HALO - w)]
+    density, grain_label = [
+        trim(f, w) for f, w in zip(azim_exchange([packed[0], packed[1]], widths[:2]), widths[:2])
+    ]
+    misfit_terms, density = lax.optimization_barrier((packed[2:], density))
+    observed, measured = [
+        trim(f, w) for f, w in zip(azim_exchange([misfit_terms[0], misfit_terms[1]], widths[2:]), widths[2:])
     ]
     grains = (
         grain_label[None] == jnp.arange(GRAINS, dtype=jnp.float32)[:, None, None, None]

time: 57.6 us -> 55.2 us (0.958)
  the two profiles are of different devices: /device:TPU:0 before, /device:TPU:9 now
where the time goes in v5:
time: 55.2 us; the launch traced here: 54.9 us
  other arithmetic  20.7 us (38%)
  starting transfers between devices  14.5 us (26%)
  waiting for transfers between devices  11.7 us (21%)
  local copies, waits for them, and re-layouts  6.39 us (12%)
  between operations  1.61 us (3%)
    select_n x11, other arithmetic, in_domain(): return jnp.where(radial_mask(width, geometry), x, 0.0)  7.23 us
    ppermute x2, waiting for transfers between devices, azim_exchange(): after = lax.ppermute(leading, 'azim', down)  4.77 us
    ppermute x1, starting transfers between devices, edge_columns(): lax.ppermute(jnp.where(own == 0, first, last), ('rad', 'hgt'), cross)  4.68 us
    ppermute x2, waiting for transfers between devices, azim_exchange(): before = lax.ppermute(last, 'azim', up)  4.52 us
    reduce_sum x2, other arithmetic, chemical(): cube_sum = jnp.sum(grains * grains * grains, axis=0)  3.52 us
    slice x15, local copies, waits for them, and re-layouts, crop(): return x[..., cut:x.shape[-2] - cut, cut:x.shape[-1] - cut]  2.62 us
    ppermute x2, starting transfers between devices, azim_exchange(): after = lax.ppermute(leading, 'azim', down)  2.59 us
    ppermute x2, starting transfers between devices, azim_exchange(): before = lax.ppermute(last, 'azim', up)  2.53 us
  transfers between devices with their start and end apart: 8, of which 5 were waited for; matrix products, arithmetic and copies ran while one was open for 9% of the time, Pallas kernels for 0%

profile of v5, /device:TPU:9, one launch (start us, length us, event | category | flops | bytes accessed | tf_op | source)
XLA Modules:
  0.0 54.9 jit_solution(5080730656125790267)
XLA Ops:
  0.6 0.9 %convert_bitcast_fusion = (f32[1,4,16,256]{3,2,1,0:T(8,128)S(1)}, f32[1,4,16,256]{3,2,1,0:T(8,128)S(1)}) fusion(s32[4,16,256]{2,1,0:T(8,128)} %param.7, s32[4,16,256]{2,1,0:T(8,128)} %param.5), kind=kLoop, calls=%fused_computation.439 | loop fusion | flops 32768 | bytes 262144 | tf_op jit(solution)/shard_map/stack | solution.py:227
  1.5 0.9 %fusion.278 = (f32[1,4,4,16,256]{4,3,2,1,0:T(8,128)S(1)}, f32[4,4,16,256]{3,2,1,0:T(8,128)S(1)}) fusion(f32[1,4,16,256]{3,2,1,0:T(8,128)S(1)} %get-tuple-element.118, f32[1,4,16,256]{3,2,1,0:T(8,128)} %bitcast.39, f32[1,4,16,256]{3,2,1,0:T(8,128)S(1)} %get-tuple-element.119, f32[1,4,16,256]{3,2,1,0:T(8,128)} %bitcast.40), kind=kLoop, calls=%fused_computation.533 | loop fusion | flops 196608 | bytes 786432 | tf_op jit(solution)/shard_map/stack | solution.py:56
  2.5 0.7 %collective-permute-start.2 = (f32[4,4,16,256]{3,2,1,0:T(8,128)S(1)}, f32[4,4,16,256]{3,2,1,0:T(8,128)S(1)}, u32[]{:S(2)}, u32[]{:S(2)}) collective-permute-start(f32[4,4,16,256]{3,2,1,0:T(8,128)S(1)} %get-tuple-element.61), channel_id=1, source_target_pairs={{0,1},{1,0},{2,3},{3,2},{4,5},{5,4},{6,7},{7,6},{8,9},{9,8},{10,11... | collective-permute-start | bytes 786440 | tf_op jit(solution)/shard_map/ppermute | solution.py:55
  3.2 0.1 slice_select_fusion.1
  3.3 1.9 %collective-permute-start = (f32[4,4,16,12]{3,2,1,0:T(8,128)S(1)}, f32[4,4,16,12]{3,2,1,0:T(8,128)S(1)}, u32[]{:S(2)}, u32[]{:S(2)}) collective-permute-start(f32[4,4,16,12]{3,2,1,0:T(8,128)S(1)} %get-tuple-element.62), channel_id=1, source_target_pairs={{0,2},{3,1},{2,4},{5,3},{4,6},{7,5},{8,10},{11,9},{10,12},{13,11},... | collective-permute-start | bytes 36872 | tf_op jit(solution)/shard_map/ppermute | solution.py:88
  5.2 4.7 %collective-permute-start.1 = (f32[4,4,16,12]{3,2,1,0:T(8,128)S(1)}, f32[4,4,16,12]{3,2,1,0:T(8,128)S(1)}, u32[]{:S(2)}, u32[]{:S(2)}) collective-permute-start(f32[4,4,16,12]{3,2,1,0:T(8,128)S(1)} %get-tuple-element.63), channel_id=1, source_target_pairs={{1,2},{2,1},{3,4},{4,3},{5,6},{6,5},{9,10},{10,9},{11,12},{12,11},... | collective-permute-start | bytes 36872 | tf_op jit(solution)/shard_map/ppermute | solution.py:87
  11.4 1.3 %collective-permute-done.1 = f32[4,4,16,12]{3,2,1,0:T(8,128)S(1)} collective-permute-done((f32[4,4,16,12]{3,2,1,0:T(8,128)S(1)}, f32[4,4,16,12]{3,2,1,0:T(8,128)S(1)}, u32[]{:S(2)}, u32[]{:S(2)}) %collective-permute-start.1) | collective-permute-done | bytes 12320 | tf_op jit(solution)/shard_map/ppermute | solution.py:87
  12.8 0.6 %gather_fusion = f32[2,4,4,16,256]{4,3,2,1,0:T(8,128)S(1)} fusion(f32[2,4,4,16,256]{4,3,2,1,0:T(8,128)S(1)} %pad_maximum_fusion, s32[1024]{0:T(1024)S(1)} %pad_clamp_fusion), kind=kCustom, calls=%fused_computation | custom fusion | bytes 1048584 | tf_op jit(solution)/shard_map/jit(_take)/gather | solution.py:58
  13.4 0.1 select_bitcast_fusion
  13.6 0.4 fusion.64
  14.1 1.3 %collective-permute-start.3 = (f32[8,23,152]{2,1,0:T(8,128)S(1)}, f32[8,23,152]{2,1,0:T(8,128)S(1)}, u32[]{:S(2)}, u32[]{:S(2)}) collective-permute-start(f32[8,23,152]{2,1,0:T(8,128)S(1)} %pad_maximum_fusion.11), channel_id=1, source_target_pairs={{0,8},{8,16},{16,24},{24,0},{1,9},{9,17},{17,25},{25,1},{2,10},{10... | collective-permute-start | bytes 335624 | tf_op jit(solution)/shard_map/ppermute | solution.py:39
  15.4 1.2 %collective-permute-start.4 = (f32[8,23,152]{2,1,0:T(8,128)S(1)}, f32[8,23,152]{2,1,0:T(8,128)S(1)}, u32[]{:S(2)}, u32[]{:S(2)}) collective-permute-start(f32[8,23,152]{2,1,0:T(8,128)S(1)} %pad_maximum_fusion.12), channel_id=1, source_target_pairs={{8,0},{16,8},{24,16},{0,24},{9,1},{17,9},{25,17},{1,25},{10,2},{18... | collective-permute-start | bytes 335624 | tf_op jit(solution)/shard_map/ppermute | solution.py:40
  16.6 4.5 %collective-permute-done.3 = f32[8,23,152]{2,1,0:T(8,128)S(1)} collective-permute-done((f32[8,23,152]{2,1,0:T(8,128)S(1)}, f32[8,23,152]{2,1,0:T(8,128)S(1)}, u32[]{:S(2)}, u32[]{:S(2)}) %collective-permute-start.3) | collective-permute-done | bytes 111904 | tf_op jit(solution)/shard_map/ppermute | solution.py:39
  21.1 4.3 %collective-permute-done.4 = f32[8,23,152]{2,1,0:T(8,128)S(1)} collective-permute-done((f32[8,23,152]{2,1,0:T(8,128)S(1)}, f32[8,23,152]{2,1,0:T(8,128)S(1)}, u32[]{:S(2)}, u32[]{:S(2)}) %collective-permute-start.4) | collective-permute-done | bytes 111904 | tf_op jit(solution)/shard_map/ppermute | solution.py:40
  25.5 0.2 pad_maximum_fusion.3
  25.7 0.4 multiply_reduce_fusion.2
  26.1 0.2 slice.959
  26.3 0.6 %fusion.69 = (f32[8,38,150]{2,1,0:T(8,128)S(1)}, f32[8,38,150]{2,1,0:T(8,128)S(1)}, f32[8,38,150]{2,1,0:T(8,128)S(1)}) fusion(f32[8,40,152]{2,1,0:T(8,128)S(1)} %broadcast_select_fusion, f32[8,38,150]{2,1,0:T(8,128)S(1)} %get-tuple-element.17, f32[8,38,150]{2,1,0:T(8,128)S(1)} %get-tuple-element.18, f32[8]{0:T(128)S(1)} %get-tuple-element.120, ...), kind=kLoop, calls=%fused_computation.131 | loop fusion | flops 1322400 | bytes 3173760 | tf_op jit(solution)/shard_map/sub | solution.py:257
  26.9 0.2 slice.956
  27.0 0.2 slice.958
  27.2 0.4 slice.964
  27.6 3.1 %multiply_reduce_fusion.1 = (f32[8,34,146]{2,1,0:T(8,128)S(1)}, f32[8,34,146]{2,1,0:T(8,128)S(1)}, f32[4,8,34,146]{3,2,1,0:T(8,128)S(1)}) fusion(f32[8]{0:T(128)S(1)} %get-tuple-element.120, f32[4,8,36,148]{3,2,1,0:T(8,128)S(1)} %slice.964, f32[8]{0:T(128)S(1)} %get-tuple-element.121, f32[146]{0:T(256)S(1)} %get-tuple-element.116, ...), kind=kLoop, calls=%fused_computation.32 | loop fusion | flops 4844864 | bytes 5926514 | tf_op jit(solution)/shard_map/reduce_sum | solution.py:174
  30.8 0.2 mul.1276
  31.0 0.4 slice.986
  31.3 0.1 slice.981
  31.5 0.7 %fusion.78 = f32[8,36,148]{2,1,0:T(8,128)S(1)} fusion(f32[8,38,150]{2,1,0:T(8,128)S(1)} %get-tuple-element.53, f32[8,40,152]{2,1,0:T(8,128)S(1)} %broadcast_select_fusion, f32[8]{0:T(128)S(1)} %get-tuple-element.120, f32[8]{0:T(128)S(1)} %get-tuple-element.121, f32[148]{0:T(256)S(1)} %get-tuple-element.112, f32[148]{0:T(256)S(1)} %get-tuple-element.113, ...), kind=kLoop, calls=%fused_computation.140 | loop fusion | flops 852480 | bytes 2469888 | tf_op jit(solution)/shard_map/jit(_where)/select_n | solution.py:133
  32.2 0.6 %slice_subtract_fusion.13 = (f32[8,34,146]{2,1,0:T(8,128)S(1)}, f32[8,34,146]{2,1,0:T(8,128)S(1)}, f32[8,34,146]{2,1,0:T(8,128)S(1)}) fusion(f32[8,36,148]{2,1,0:T(8,128)S(1)} %fusion.78, f32[8]{0:T(128)S(1)} %get-tuple-element.120, f32[8]{0:T(128)S(1)} %get-tuple-element.121, f32[146]{0:T(256)S(1)} %get-tuple-element.116, f32[146]{0:T(256)S(1)} %get-tuple-element.117, ...), kind=kLoop, calls=%fused_computation.188 | loop fusion | flops 1151648 | bytes 3103104 | tf_op jit(solution)/shard_map/sub | solution.py:175
  32.8 0.1 slice.978
  32.9 0.1 slice.980
  33.2 1.3 %collective-permute-start.5 = (f32[8,12,152]{2,1,0:T(8,128)S(1)}, f32[8,12,152]{2,1,0:T(8,128)S(1)}, u32[]{:S(2)}, u32[]{:S(2)}) collective-permute-start(f32[8,12,152]{2,1,0:T(8,128)S(1)} %pad_maximum_fusion.13), channel_id=1, source_target_pairs={{0,8},{8,16},{16,24},{24,0},{1,9},{9,17},{17,25},{25,1},{2,10},{10... | collective-permute-start | bytes 175112 | tf_op jit(solution)/shard_map/ppermute | solution.py:39
  34.5 1.4 %collective-permute-start.6 = (f32[8,12,152]{2,1,0:T(8,128)S(1)}, f32[8,12,152]{2,1,0:T(8,128)S(1)}, u32[]{:S(2)}, u32[]{:S(2)}) collective-permute-start(f32[8,12,152]{2,1,0:T(8,128)S(1)} %pad_maximum_fusion.14), channel_id=1, source_target_pairs={{8,0},{16,8},{24,16},{0,24},{9,1},{17,9},{25,17},{1,25},{10,2},{18... | collective-permute-start | bytes 175112 | tf_op jit(solution)/shard_map/ppermute | solution.py:40
  35.9 0.6 %fusion.140 = f32[8,32,144]{2,1,0:T(8,128)S(1)} fusion(f32[8,34,146]{2,1,0:T(8,128)S(1)} %get-tuple-element.52, f32[8,36,148]{2,1,0:T(8,128)S(1)} %fusion.78, f32[8]{0:T(128)S(1)} %get-tuple-element.120, f32[8]{0:T(128)S(1)} %get-tuple-element.121, f32[144]{0:T(256)S(1)} %get-tuple-element.110, f32[144]{0:T(256)S(1)} %get-tuple-element.111, ...), kind=kLoop, calls=%fused_computation.224 | loop fusion | flops 737280 | bytes 2053632 | tf_op jit(solution)/shard_map/jit(_where)/select_n | solution.py:133
  36.4 2.3 %multiply_reduce_fusion = (f32[8,30,142]{2,1,0:T(8,128)S(1)}, f32[8,30,142]{2,1,0:T(8,128)S(1)}, f32[4,8,30,142]{3,2,1,0:T(8,128)S(1)}) fusion(f32[8]{0:T(128)S(1)} %get-tuple-element.120, f32[4,8,32,144]{3,2,1,0:T(8,128)S(1)} %slice.986, f32[8]{0:T(128)S(1)} %get-tuple-element.121, f32[142]{0:T(256)S(1)} %get-tuple-element.108, ...), kind=kLoop, calls=%fused_computation.5 | loop fusion | flops 4157760 | bytes 5090862 | tf_op jit(solution)/shard_map/reduce_sum | solution.py:173
  38.7 0.5 fusion.115
  39.2 0.3 slice.1032
  39.5 0.5 collective-permute-done.6
  40.1 0.8 %fusion.166 = (f32[8,28,140]{2,1,0:T(8,128)S(1)}, f32[8,28,140]{2,1,0:T(8,128)S(1)}) fusion(f32[8,6,152]{2,1,0:T(8,128)S(1)} %get-tuple-element.67, f32[8,16,152]{2,1,0:T(8,128)S(1)} %get-tuple-element.58, f32[8,6,152]{2,1,0:T(8,128)S(1)} %get-tuple-element.65, f32[8,6,152]{2,1,0:T(8,128)S(1)} %get-tuple-element.66, ...), kind=kLoop, calls=%fused_computation.260 | loop fusion | flops 846720 | bytes 2615808 | tf_op jit(solution)/shard_map/jit(_where)/select_n | solution.py:133
  40.9 0.6 %broadcast_select_fusion.1 = (f32[8,26,138]{2,1,0:T(8,128)S(1)}, f32[8,26,138]{2,1,0:T(8,128)S(1)}) fusion(pred[138]{0:T(512)(128)(4,1)S(1)} %compare_and_fusion.2, f32[8]{0:T(128)S(1)} %get-tuple-element.120, f32[8,28,140]{2,1,0:T(8,128)S(1)} %get-tuple-element.26, f32[8]{0:T(128)S(1)} %get-tuple-element.121, f32[138]{0:T(256)S(1)} %get-tuple-element.105, ...), kind=kLoop, calls=%fused_computation.403 | loop fusion | flops 516672 | bytes 2069248 | tf_op jit(solution)/shard_map/jit(_where)/select_n | solution.py:133
  41.5 0.6 %fusion.217 = (f32[8,24,136]{2,1,0:T(8,128)S(1)}, f32[8,24,136]{2,1,0:T(8,128)S(1)}) fusion(f32[8,26,138]{2,1,0:T(8,128)S(1)} %get-tuple-element.23, f32[8,24,138]{2,1,0:T(8,128)S(1)} %slice_divide_fusion.6, f32[8,32,144]{2,1,0:T(8,128)S(1)} %fusion.140, f32[8,28,140]{2,1,0:T(8,128)S(1)} %get-tuple-element.26, f32[8,26,138]{2,1,0:T(8,128)S(1)} %get-tuple-element.24, ...), kind=kLoop, calls=%fused_computation.337 | loop fusion | flops 705024 | bytes 2245120 | tf_op jit(solution)/shard_map/jit(_where)/select_n | solution.py:133
  42.2 0.4 broadcast_select_fusion.3
  42.6 0.1 slice.1034
  42.8 0.1 slice_multiply_fusion.4
  42.9 0.6 %fusion.286 = (f32[4,8,20,132]{3,2,1,0:T(8,128)S(1)}, f32[4,8,20,132]{3,2,1,0:T(8,128)S(1)}, f32[8,20,132]{2,1,0:T(8,128)S(1)}, f32[8,20,132]{2,1,0:T(8,128)S(1)...) fusion(f32[4,8,34,146]{3,2,1,0:T(8,128)S(1)} %get-tuple-element.29, f32[8,20,132]{2,1,0:T(8,128)S(1)} %slice.1034, ...), kind=kLoop, calls=%fused_computation.534 | loop fusion | flops 1034880 | bytes 2027652 | tf_op jit(solution)/shard_map/slice | solution.py:123
  43.5 0.6 %fusion.201 = (f32[8,20,132]{2,1,0:T(8,128)S(1)}, f32[8,20,132]{2,1,0:T(8,128)S(1)}, f32[8,20,132]{2,1,0:T(8,128)S(1)}) fusion(f32[8,22,134]{2,1,0:T(8,128)S(1)} %get-tuple-element.21, f32[8,20,132]{2,1,0:T(8,128)S(1)} %get-tuple-element.34, f32[8,20,134]{2,1,0:T(8,128)S(1)} %slice_divide_fusion.4, f32[8,24,136]{2,1,0:T(8,128)S(1)} %get-tuple-element.56, ...), kind=kLoop, calls=%fused_computation.321 | loop fusion | flops 633600 | bytes 2420736 | tf_op jit(solution)/shard_map/jit(_where)/select_n | solution.py:133
  44.1 0.1 slice.1055
  44.2 0.1 slice.1056
  44.4 0.1 slice.1060
  44.5 0.1 slice_divide_fusion
  44.6 0.1 slice.1061
  44.7 0.1 slice.1058
  44.9 1.9 %fusion.49 = f32[4,8,18,130]{3,2,1,0:T(8,128)S(1)} fusion(f32[4,8,20,132]{3,2,1,0:T(8,128)S(1)} %get-tuple-element.35, f32[4,8,18,132]{3,2,1,0:T(8,128)S(1)} %slice_divide_fusion, f32[4,8,20,132]{3,2,1,0:T(8,128)S(1)} %get-tuple-element.31, f32[4,8,20,132]{3,2,1,0:T(8,128)S(1)} %get-tuple-element.30, f32[8,18,130]{2,1,0:T(8,128)S(1)} %slice.1061, ...), kind=kLoop, calls=%fused_computation.76 | loop fusion | flops 2171520 | bytes 8365056 | tf_op jit(solution)/shard_map/jit(_where)/select_n | solution.py:133
  46.8 0.2 multiply_reduce_fusion.9
  47.1 0.4 broadcast_select_fusion.2
  47.6 0.1 slice_multiply_fusion.6
  47.7 0.1 slice_bitcast_fusion.5
  47.8 0.3 fusion.262
  48.1 0.7 %fusion.149 = f32[4,8,16,128]{3,2,1,0:T(8,128)S(1)} fusion(f32[4,8,18,130]{3,2,1,0:T(8,128)S(1)} %fusion.49, f32[4,8,16,130]{3,2,1,0:T(8,128)S(1)} %slice_divide_fusion.1, f32[4,8,38,150]{3,2,1,0:T(8,128)S(1)} %get-tuple-element.43, f32[8]{0:T(128)S(1)} %get-tuple-element.120, f32[8]{0:T(128)S(1)} %get-tuple-element.121, f32[128]{0:T(128)S(1)} %get-tuple-element.101, ...), kind=kLoop, calls=%fused_computation.233 | loop fusion | flops 2031616 | bytes 3214336 | tf_op jit(solution)/shard_map/jit(_where)/select_n | solution.py:133
  48.8 2.0 %collective-permute-start.7 = (f32[6,4,16,128]{3,2,1,0:T(8,128)S(1)}, f32[6,4,16,128]{3,2,1,0:T(8,128)S(1)}, u32[]{:S(2)}, u32[]{:S(2)}) collective-permute-start(f32[6,4,16,128]{3,2,1,0:T(8,128)S(1)} %get-tuple-element.41), channel_id=1, source_target_pairs={{0,1},{1,0},{2,3},{3,2},{4,5},{5,4},{6,7},{7,6},{8,9},{9,8},{10,11... | collective-permute-start | bytes 589832 | tf_op jit(solution)/shard_map/ppermute | solution.py:110
  50.9 1.1 %collective-permute-done.7 = f32[6,4,16,128]{3,2,1,0:T(8,128)S(1)} collective-permute-done((f32[6,4,16,128]{3,2,1,0:T(8,128)S(1)}, f32[6,4,16,128]{3,2,1,0:T(8,128)S(1)}, u32[]{:S(2)}, u32[]{:S(2)}) %collective-permute-start.7) | collective-permute-done | bytes 196640 | tf_op jit(solution)/shard_map/ppermute | solution.py:110
  52.0 0.6 %gather_fusion.1 = f32[2,6,4,16,128]{4,3,2,1,0:T(8,128)S(1)} fusion(f32[2,6,4,16,128]{4,3,2,1,0:T(8,128)S(1)} %pad_maximum_fusion.2, s32[1024]{0:T(1024)S(1)} %pad_clamp_fusion), kind=kCustom, calls=%fused_computation.1 | custom fusion | bytes 786440 | tf_op jit(solution)/shard_map/jit(_take)/gather | solution.py:114
  52.5 0.1 select_bitcast_fusion.1
  52.7 0.7 %copy_bitcast_fusion = f32[4,4,16,256]{3,2,1,0:T(8,128)} fusion(f32[6,4,16,2,128]{4,2,1,0,3:T(8,128)S(1)} %select_bitcast_fusion.1), kind=kLoop, calls=%fused_computation.236 | loop fusion | bytes 524288 | tf_op jit(solution)/shard_map/slice | solution.py:315
  53.5 0.7 %squeeze.22 = f32[4,16,256]{2,1,0:T(8,128)} reshape(f32[1,4,16,2,128]{4,3,2,1,0:T(2,128)S(1)} %copy.9) | data formatting | bytes 131072 | tf_op jit(solution)/shard_map/squeeze | solution.py:315
  54.2 0.7 %squeeze.23 = f32[4,16,256]{2,1,0:T(8,128)} reshape(f32[1,4,16,2,128]{4,3,2,1,0:T(2,128)S(1)} %copy.10) | data formatting | bytes 131072 | tf_op jit(solution)/shard_map/squeeze | solution.py:315
  (96 shorter events, 2.1 us)
Async XLA Ops:
  2.5 10.3 %collective-permute-start.2 = (f32[4,4,16,256]{3,2,1,0:T(8,128)S(1)}, f32[4,4,16,256]{3,2,1,0:T(8,128)S(1)}, u32[]{:S(2)}, u32[]{:S(2)}) collective-permute-start(f32[4,4,16,256]{3,2,1,0:T(8,128)S(1)} %get-tuple-element.61), channel_id=1, source_target_pairs={{0,1},{1,0},{2,3},{3,2},{4,5},{5,4},{6,7},{7,6},{8,9},{9,8},{10,11... | collective-permute-start | bytes 786440 | tf_op jit(solution)/shard_map/ppermute | solution.py:55
  3.3 8.1 %collective-permute-start = (f32[4,4,16,12]{3,2,1,0:T(8,128)S(1)}, f32[4,4,16,12]{3,2,1,0:T(8,128)S(1)}, u32[]{:S(2)}, u32[]{:S(2)}) collective-permute-start(f32[4,4,16,12]{3,2,1,0:T(8,128)S(1)} %get-tuple-element.62), channel_id=1, source_target_pairs={{0,2},{3,1},{2,4},{5,3},{4,6},{7,5},{8,10},{11,9},{10,12},{13,11},... | collective-permute-start | bytes 36872 | tf_op jit(solution)/shard_map/ppermute | solution.py:88
  5.2 7.5 %collective-permute-start.1 = (f32[4,4,16,12]{3,2,1,0:T(8,128)S(1)}, f32[4,4,16,12]{3,2,1,0:T(8,128)S(1)}, u32[]{:S(2)}, u32[]{:S(2)}) collective-permute-start(f32[4,4,16,12]{3,2,1,0:T(8,128)S(1)} %get-tuple-element.63), channel_id=1, source_target_pairs={{1,2},{2,1},{3,4},{4,3},{5,6},{6,5},{9,10},{10,9},{11,12},{12,11},... | collective-permute-start | bytes 36872 | tf_op jit(solution)/shard_map/ppermute | solution.py:87
  14.0 2.6 %copy-start = (f32[4,8,16,152]{3,2,1,0:T(8,128)}, f32[4,8,16,152]{3,2,1,0:T(8,128)S(1)}, u32[]{:S(2)}) copy-start(f32[4,8,16,152]{3,2,1,0:T(8,128)S(1)} %fusion.64) | copy-start | bytes 933892
  14.1 7.0 %collective-permute-start.3 = (f32[8,23,152]{2,1,0:T(8,128)S(1)}, f32[8,23,152]{2,1,0:T(8,128)S(1)}, u32[]{:S(2)}, u32[]{:S(2)}) collective-permute-start(f32[8,23,152]{2,1,0:T(8,128)S(1)} %pad_maximum_fusion.11), channel_id=1, source_target_pairs={{0,8},{8,16},{16,24},{24,0},{1,9},{9,17},{17,25},{25,1},{2,10},{10... | collective-permute-start | bytes 335624 | tf_op jit(solution)/shard_map/ppermute | solution.py:39
  15.4 10.0 %collective-permute-start.4 = (f32[8,23,152]{2,1,0:T(8,128)S(1)}, f32[8,23,152]{2,1,0:T(8,128)S(1)}, u32[]{:S(2)}, u32[]{:S(2)}) collective-permute-start(f32[8,23,152]{2,1,0:T(8,128)S(1)} %pad_maximum_fusion.12), channel_id=1, source_target_pairs={{8,0},{16,8},{24,16},{0,24},{9,1},{17,9},{25,17},{1,25},{10,2},{18... | collective-permute-start | bytes 335624 | tf_op jit(solution)/shard_map/ppermute | solution.py:40
  32.2 1.0 %slice-start = ((f32[4,8,16,152]{3,2,1,0:T(8,128)}), f32[2,8,16,152]{3,2,1,0:T(8,128)S(1)}, s32[]{:S(2)}) async-start(f32[4,8,16,152]{3,2,1,0:T(8,128)} %copy-done), calls=%async_computation | async-start | bytes 524288 | tf_op jit(solution)/shard_map/slice | solution.py:239
  33.2 6.3 %collective-permute-start.5 = (f32[8,12,152]{2,1,0:T(8,128)S(1)}, f32[8,12,152]{2,1,0:T(8,128)S(1)}, u32[]{:S(2)}, u32[]{:S(2)}) collective-permute-start(f32[8,12,152]{2,1,0:T(8,128)S(1)} %pad_maximum_fusion.13), channel_id=1, source_target_pairs={{0,8},{8,16},{16,24},{24,0},{1,9},{9,17},{17,25},{25,1},{2,10},{10... | collective-permute-start | bytes 175112 | tf_op jit(solution)/shard_map/ppermute | solution.py:39
  34.5 5.6 %collective-permute-start.6 = (f32[8,12,152]{2,1,0:T(8,128)S(1)}, f32[8,12,152]{2,1,0:T(8,128)S(1)}, u32[]{:S(2)}, u32[]{:S(2)}) collective-permute-start(f32[8,12,152]{2,1,0:T(8,128)S(1)} %pad_maximum_fusion.14), channel_id=1, source_target_pairs={{8,0},{16,8},{24,16},{0,24},{9,1},{17,9},{25,17},{1,25},{10,2},{18... | collective-permute-start | bytes 175112 | tf_op jit(solution)/shard_map/ppermute | solution.py:40
  48.8 3.1 %collective-permute-start.7 = (f32[6,4,16,128]{3,2,1,0:T(8,128)S(1)}, f32[6,4,16,128]{3,2,1,0:T(8,128)S(1)}, u32[]{:S(2)}, u32[]{:S(2)}) collective-permute-start(f32[6,4,16,128]{3,2,1,0:T(8,128)S(1)} %get-tuple-element.41), channel_id=1, source_target_pairs={{0,1},{1,0},{2,3},{3,2},{4,5},{5,4},{6,7},{7,6},{8,9},{9,8},{10,11... | collective-permute-start | bytes 589832 | tf_op jit(solution)/shard_map/ppermute | solution.py:110

commit v6 on v5

--- a/solution.py
+++ b/solution.py
@@ -144,29 +144,24 @@
     radius = radius_all[1:-1]
     outer_face = (radius + 0.5) * (rad_index < total_rad - 1).astype(jnp.float32)
     inner_face = (radius - 0.5) * (rad_index > 0).astype(jnp.float32)
+    if transpose:
+        outward_weight = outer_face / radius_all[2:]
+        inward_weight = inner_face / radius_all[:-2]
+    else:
+        outward_weight = outer_face / radius
+        inward_weight = inner_face / radius
+    arc_length = radius * (full_turn / total_azim)
+    arc_weight = 1.0 / (arc_length * arc_length)
     hgt_index = jnp.arange(height_rows, dtype=jnp.int32)
-    upper_face = (hgt_index < total_hgt - 1).astype(jnp.float32)[:, None, None]
-    lower_face = (hgt_index > 0).astype(jnp.float32)[:, None, None]
+    faces = (hgt_index < total_hgt - 1).astype(jnp.float32) + (hgt_index > 0).astype(jnp.float32)
+    center_weight = (outer_face + inner_face) / radius + 2.0 * arc_weight + faces[:, None, None]
     leading = x.ndim - 3
     padded = jnp.pad(x, [(0, 0)] * leading + [(1, 1), (0, 0), (0, 0)])
     center = padded[..., 1:-1, 1:-1, 1:-1]
-    if transpose:
-        scaled = padded[..., 1:-1, 1:-1, :] / radius_all
-        radial = outer_face * (scaled[..., 2:] - scaled[..., 1:-1]) - inner_face * (
-            scaled[..., 1:-1] - scaled[..., :-2]
-        )
-    else:
-        outward = padded[..., 1:-1, 1:-1, 2:]
-        inward = padded[..., 1:-1, 1:-1, :-2]
-        radial = (outer_face * (outward - center) - inner_face * (center - inward)) / radius
-    arc_length = radius * (full_turn / total_azim)
-    azimuthal = (padded[..., 1:-1, 2:, 1:-1] + padded[..., 1:-1, :-2, 1:-1] - 2.0 * center) / (
-        arc_length * arc_length
-    )
-    vertical = upper_face * (padded[..., 2:, 1:-1, 1:-1] - center) + lower_face * (
-        padded[..., :-2, 1:-1, 1:-1] - center
-    )
-    return radial + azimuthal + vertical
+    radial = outward_weight * padded[..., 1:-1, 1:-1, 2:] + inward_weight * padded[..., 1:-1, 1:-1, :-2]
+    azimuthal = arc_weight * (padded[..., 1:-1, 2:, 1:-1] + padded[..., 1:-1, :-2, 1:-1])
+    vertical = padded[..., 2:, 1:-1, 1:-1] + padded[..., :-2, 1:-1, 1:-1]
+    return radial + azimuthal + vertical - center_weight * center
 
 
 def chemical(density, grains):

time: 55.2 us -> 53.3 us (0.966)
  waiting for transfers between devices: 11.7 us -> 10.8 us
  other arithmetic: 20.7 us -> 19.9 us
    mul x14 -> x0, other arithmetic: 1.08 us -> none  [the longest x12 0.88 us: laplace(): (radius + 0.5) * (rad_index < total_rad - 1).astype(jnp.float32)]
    ppermute x1, waiting for transfers between devices: 1.3 us -> 0.33 us  [edge_columns(): lax.ppermute(jnp.where(own == 0, first, last), ('rad', 'hgt'), cross)]
    add x0 -> x13, other arithmetic: none -> 0.93 us  [the longest x12 0.92 us: laplace(): (outer_face + inner_face) / radius + 2.0 * arc_weight + faces[:, None, None]]
    select_n x11, other arithmetic: 7.23 us -> 6.48 us  [in_domain(): return jnp.where(radial_mask(width, geometry), x, 0.0)]
    div x8 -> x12, other arithmetic: 0.34 us -> 0.93 us  [the longest x6 0.47 us: laplace(): outward_weight = outer_face / radius]
  transfers between devices with their start and end apart: 8 -> 8, of which waited for: 5 -> 5; matrix products, arithmetic and copies ran while one was open for 9% -> 11% of each run, Pallas kernels for 0% -> 0%
where the time goes in v6:
time: 53.3 us; the launch traced here: 53.1 us
  other arithmetic  19.9 us (37%)
  starting transfers between devices  14.5 us (27%)
  waiting for transfers between devices  10.8 us (20%)
  local copies, waits for them, and re-layouts  6.42 us (12%)
  between operations  1.52 us (3%)
    select_n x11, other arithmetic, in_domain(): return jnp.where(radial_mask(width, geometry), x, 0.0)  6.48 us
    ppermute x2, waiting for transfers between devices, azim_exchange(): after = lax.ppermute(leading, 'azim', down)  4.85 us
    ppermute x1, starting transfers between devices, edge_columns(): lax.ppermute(jnp.where(own == 0, first, last), ('rad', 'hgt'), cross)  4.68 us
    ppermute x2, waiting for transfers between devices, azim_exchange(): before = lax.ppermute(last, 'azim', up)  4.52 us
    reduce_sum x2, other arithmetic, chemical(): cube_sum = jnp.sum(grains * grains * grains, axis=0)  3.17 us
    slice x15, local copies, waits for them, and re-layouts, crop(): return x[..., cut:x.shape[-2] - cut, cut:x.shape[-1] - cut]  2.63 us
    ppermute x2, starting transfers between devices, azim_exchange(): after = lax.ppermute(leading, 'azim', down)  2.59 us
    ppermute x2, starting transfers between devices, azim_exchange(): before = lax.ppermute(last, 'azim', up)  2.53 us
  transfers between devices with their start and end apart: 8, of which 5 were waited for; matrix products, arithmetic and copies ran while one was open for 11% of the time, Pallas kernels for 0%

profile of v6, /device:TPU:9, one launch (start us, length us, event | category | flops | bytes accessed | tf_op | source)
XLA Modules:
  0.0 53.1 jit_solution(16213360522961142674)
XLA Ops:
  0.6 0.9 %convert_bitcast_fusion = (f32[1,4,16,256]{3,2,1,0:T(8,128)S(1)}, f32[1,4,16,256]{3,2,1,0:T(8,128)S(1)}) fusion(s32[4,16,256]{2,1,0:T(8,128)} %param.7, s32[4,16,256]{2,1,0:T(8,128)} %param.5), kind=kLoop, calls=%fused_computation.330 | loop fusion | flops 32768 | bytes 262144 | tf_op jit(solution)/shard_map/stack | solution.py:222
  1.5 0.9 %fusion.184 = (f32[1,4,4,16,256]{4,3,2,1,0:T(8,128)S(1)}, f32[4,4,16,256]{3,2,1,0:T(8,128)S(1)}) fusion(f32[1,4,16,256]{3,2,1,0:T(8,128)S(1)} %get-tuple-element.150, f32[1,4,16,256]{3,2,1,0:T(8,128)} %bitcast.39, f32[1,4,16,256]{3,2,1,0:T(8,128)S(1)} %get-tuple-element.151, f32[1,4,16,256]{3,2,1,0:T(8,128)} %bitcast.40), kind=kLoop, calls=%fused_computation.473 | loop fusion | flops 196608 | bytes 786432 | tf_op jit(solution)/shard_map/stack | solution.py:56
  2.5 0.7 %collective-permute-start.2 = (f32[4,4,16,256]{3,2,1,0:T(8,128)S(1)}, f32[4,4,16,256]{3,2,1,0:T(8,128)S(1)}, u32[]{:S(2)}, u32[]{:S(2)}) collective-permute-start(f32[4,4,16,256]{3,2,1,0:T(8,128)S(1)} %get-tuple-element.85), channel_id=1, source_target_pairs={{0,1},{1,0},{2,3},{3,2},{4,5},{5,4},{6,7},{7,6},{8,9},{9,8},{10,11... | collective-permute-start | bytes 786440 | tf_op jit(solution)/shard_map/ppermute | solution.py:55
  3.2 0.1 slice_select_fusion.1
  3.3 1.9 %collective-permute-start = (f32[4,4,16,12]{3,2,1,0:T(8,128)S(1)}, f32[4,4,16,12]{3,2,1,0:T(8,128)S(1)}, u32[]{:S(2)}, u32[]{:S(2)}) collective-permute-start(f32[4,4,16,12]{3,2,1,0:T(8,128)S(1)} %get-tuple-element.86), channel_id=1, source_target_pairs={{0,2},{3,1},{2,4},{5,3},{4,6},{7,5},{8,10},{11,9},{10,12},{13,11},... | collective-permute-start | bytes 36872 | tf_op jit(solution)/shard_map/ppermute | solution.py:88
  5.2 4.7 %collective-permute-start.1 = (f32[4,4,16,12]{3,2,1,0:T(8,128)S(1)}, f32[4,4,16,12]{3,2,1,0:T(8,128)S(1)}, u32[]{:S(2)}, u32[]{:S(2)}) collective-permute-start(f32[4,4,16,12]{3,2,1,0:T(8,128)S(1)} %get-tuple-element.87), channel_id=1, source_target_pairs={{1,2},{2,1},{3,4},{4,3},{5,6},{6,5},{9,10},{10,9},{11,12},{12,11},... | collective-permute-start | bytes 36872 | tf_op jit(solution)/shard_map/ppermute | solution.py:87
  10.4 0.1 fusion.169
  11.4 0.1 broadcast_add_fusion.4
  12.4 0.3 collective-permute-done.1
  12.8 0.6 %gather_fusion = f32[2,4,4,16,256]{4,3,2,1,0:T(8,128)S(1)} fusion(f32[2,4,4,16,256]{4,3,2,1,0:T(8,128)S(1)} %pad_maximum_fusion, s32[1024]{0:T(1024)S(1)} %pad_clamp_fusion), kind=kCustom, calls=%fused_computation | custom fusion | bytes 1048584 | tf_op jit(solution)/shard_map/jit(_take)/gather | solution.py:58
  13.4 0.1 select_bitcast_fusion
  13.6 0.4 fusion.44
  14.1 1.3 %collective-permute-start.3 = (f32[8,23,152]{2,1,0:T(8,128)S(1)}, f32[8,23,152]{2,1,0:T(8,128)S(1)}, u32[]{:S(2)}, u32[]{:S(2)}) collective-permute-start(f32[8,23,152]{2,1,0:T(8,128)S(1)} %pad_maximum_fusion.11), channel_id=1, source_target_pairs={{0,8},{8,16},{16,24},{24,0},{1,9},{9,17},{17,25},{25,1},{2,10},{10... | collective-permute-start | bytes 335624 | tf_op jit(solution)/shard_map/ppermute | solution.py:39
  15.4 1.2 %collective-permute-start.4 = (f32[8,23,152]{2,1,0:T(8,128)S(1)}, f32[8,23,152]{2,1,0:T(8,128)S(1)}, u32[]{:S(2)}, u32[]{:S(2)}) collective-permute-start(f32[8,23,152]{2,1,0:T(8,128)S(1)} %pad_maximum_fusion.12), channel_id=1, source_target_pairs={{8,0},{16,8},{24,16},{0,24},{9,1},{17,9},{25,17},{1,25},{10,2},{18... | collective-permute-start | bytes 335624 | tf_op jit(solution)/shard_map/ppermute | solution.py:40
  16.6 4.5 %collective-permute-done.3 = f32[8,23,152]{2,1,0:T(8,128)S(1)} collective-permute-done((f32[8,23,152]{2,1,0:T(8,128)S(1)}, f32[8,23,152]{2,1,0:T(8,128)S(1)}, u32[]{:S(2)}, u32[]{:S(2)}) %collective-permute-start.3) | collective-permute-done | bytes 111904 | tf_op jit(solution)/shard_map/ppermute | solution.py:39
  21.1 4.3 %collective-permute-done.4 = f32[8,23,152]{2,1,0:T(8,128)S(1)} collective-permute-done((f32[8,23,152]{2,1,0:T(8,128)S(1)}, f32[8,23,152]{2,1,0:T(8,128)S(1)}, u32[]{:S(2)}, u32[]{:S(2)}) %collective-permute-start.4) | collective-permute-done | bytes 111904 | tf_op jit(solution)/shard_map/ppermute | solution.py:40
  25.5 0.2 pad_maximum_fusion.3
  25.7 0.4 multiply_reduce_fusion.2
  26.1 0.2 slice.947
  26.3 0.6 %fusion.48 = (f32[8,38,150]{2,1,0:T(8,128)S(1)}, f32[8,38,150]{2,1,0:T(8,128)S(1)}, f32[8,38,150]{2,1,0:T(8,128)S(1)}) fusion(f32[8,40,152]{2,1,0:T(8,128)S(1)} %broadcast_select_fusion, f32[8,38,150]{2,1,0:T(8,128)S(1)} %get-tuple-element.17, f32[8,38,150]{2,1,0:T(8,128)S(1)} %get-tuple-element.18, f32[8,150]{1,0:T(8,128)S(1)} %broadcast_add_fusion.10, ...), kind=kLoop, calls=%fused_computation.108 | loop fusion | flops 1048800 | bytes 3179904 | tf_op jit(solution)/shard_map/sub | solution.py:252
  26.9 0.2 slice.944
  27.0 0.2 slice.946
  27.2 0.4 slice.952
  27.6 2.8 %multiply_reduce_fusion.1 = (f32[8,34,146]{2,1,0:T(8,128)S(1)}, f32[8,34,146]{2,1,0:T(8,128)S(1)}, f32[4,8,34,146]{3,2,1,0:T(8,128)S(1)}) fusion(f32[8,146]{1,0:T(8,128)S(1)} %broadcast_add_fusion.8, f32[4,8,36,148]{3,2,1,0:T(8,128)S(1)} %slice.952, f32[4,8,38,150]{3,2,1,0:T(8,128)S(1)} %get-tuple-element.67, f32[146]{0:T(256)S(1)} %get-tuple-element.149, ...), kind=kLoop, calls=%fused_computation.25 | loop fusion | flops 3732928 | bytes 5930538 | tf_op jit(solution)/shard_map/reduce_sum | solution.py:169
  30.4 0.2 mul.1273
  30.6 0.4 slice.974
  31.0 0.1 slice.969
  31.1 0.6 %fusion.54 = f32[8,36,148]{2,1,0:T(8,128)S(1)} fusion(f32[8,38,150]{2,1,0:T(8,128)S(1)} %get-tuple-element.77, f32[8,40,152]{2,1,0:T(8,128)S(1)} %broadcast_select_fusion, f32[8,148]{1,0:T(8,128)S(1)} %broadcast_add_fusion.9, f32[148]{0:T(256)S(1)} %get-tuple-element.141, f32[148]{0:T(256)S(1)} %get-tuple-element.139, f32[148]{0:T(256)S(1)} %get-tuple-element.138, ...), kind=kLoop, calls=%fused_computation.114 | loop fusion | flops 554112 | bytes 2476032 | tf_op jit(solution)/shard_map/jit(_where)/select_n | solution.py:133
  31.8 0.6 %slice_subtract_fusion.1 = (f32[8,34,146]{2,1,0:T(8,128)S(1)}, f32[8,34,146]{2,1,0:T(8,128)S(1)}, f32[8,34,146]{2,1,0:T(8,128)S(1)}) fusion(f32[8,36,148]{2,1,0:T(8,128)S(1)} %fusion.54, f32[8,146]{1,0:T(8,128)S(1)} %broadcast_add_fusion.8, f32[146]{0:T(256)S(1)} %get-tuple-element.149, f32[146]{0:T(256)S(1)} %get-tuple-element.147, ...), kind=kLoop, calls=%fused_computation.142 | loop fusion | flops 913376 | bytes 3109248 | tf_op jit(solution)/shard_map/sub | solution.py:170
  32.3 0.1 slice.966
  32.5 0.1 slice.968
  32.6 0.1 slice-done
  32.8 1.3 %collective-permute-start.5 = (f32[8,12,152]{2,1,0:T(8,128)S(1)}, f32[8,12,152]{2,1,0:T(8,128)S(1)}, u32[]{:S(2)}, u32[]{:S(2)}) collective-permute-start(f32[8,12,152]{2,1,0:T(8,128)S(1)} %pad_maximum_fusion.13), channel_id=1, source_target_pairs={{0,8},{8,16},{16,24},{24,0},{1,9},{9,17},{17,25},{25,1},{2,10},{10... | collective-permute-start | bytes 175112 | tf_op jit(solution)/shard_map/ppermute | solution.py:39
  34.1 1.4 %collective-permute-start.6 = (f32[8,12,152]{2,1,0:T(8,128)S(1)}, f32[8,12,152]{2,1,0:T(8,128)S(1)}, u32[]{:S(2)}, u32[]{:S(2)}) collective-permute-start(f32[8,12,152]{2,1,0:T(8,128)S(1)} %pad_maximum_fusion.14), channel_id=1, source_target_pairs={{8,0},{16,8},{24,16},{0,24},{9,1},{17,9},{25,17},{1,25},{10,2},{18... | collective-permute-start | bytes 175112 | tf_op jit(solution)/shard_map/ppermute | solution.py:40
  35.5 0.5 fusion.87
  36.0 2.3 %multiply_reduce_fusion = (f32[8,30,142]{2,1,0:T(8,128)S(1)}, f32[8,30,142]{2,1,0:T(8,128)S(1)}, f32[4,8,30,142]{3,2,1,0:T(8,128)S(1)}) fusion(f32[8,142]{1,0:T(8,128)S(1)} %broadcast_add_fusion.6, f32[4,8,32,144]{3,2,1,0:T(8,128)S(1)} %slice.974, f32[4,8,34,146]{3,2,1,0:T(8,128)S(1)} %get-tuple-element.51, f32[142]{0:T(256)S(1)} %get-tuple-element.133, ...), kind=kLoop, calls=%fused_computation.5 | loop fusion | flops 3203520 | bytes 5094774 | tf_op jit(solution)/shard_map/reduce_sum | solution.py:168
  38.3 0.5 fusion.71
  38.7 0.3 slice.1014
  39.1 0.6 %collective-permute-done.6 = f32[8,12,152]{2,1,0:T(8,128)S(1)} collective-permute-done((f32[8,12,152]{2,1,0:T(8,128)S(1)}, f32[8,12,152]{2,1,0:T(8,128)S(1)}, u32[]{:S(2)}, u32[]{:S(2)}) %collective-permute-start.6) | collective-permute-done | bytes 58400 | tf_op jit(solution)/shard_map/ppermute | solution.py:40
  39.7 0.8 %fusion.102 = (f32[8,28,140]{2,1,0:T(8,128)S(1)}, f32[8,28,140]{2,1,0:T(8,128)S(1)}) fusion(f32[8,6,152]{2,1,0:T(8,128)S(1)} %get-tuple-element.93, f32[8,16,152]{2,1,0:T(8,128)S(1)} %get-tuple-element.82, f32[8,6,152]{2,1,0:T(8,128)S(1)} %get-tuple-element.91, f32[8,6,152]{2,1,0:T(8,128)S(1)} %get-tuple-element.92, ...), kind=kLoop, calls=%fused_computation.193 | loop fusion | flops 627200 | bytes 2621952 | tf_op jit(solution)/shard_map/jit(_where)/select_n | solution.py:133
  40.4 0.5 broadcast_select_fusion.1
  40.9 0.5 fusion.131
  41.4 0.1 slice.1016
  41.5 0.6 %fusion.192 = (f32[4,8,20,132]{3,2,1,0:T(8,128)S(1)}, f32[4,8,20,132]{3,2,1,0:T(8,128)S(1)}, f32[8,20,132]{2,1,0:T(8,128)S(1)}, f32[8,20,132]{2,1,0:T(8,128)S(1)...) fusion(f32[4,8,34,146]{3,2,1,0:T(8,128)S(1)} %get-tuple-element.51, f32[8,20,132]{2,1,0:T(8,128)S(1)} %slice.1016, ...), kind=kLoop, calls=%fused_computation.474 | loop fusion | flops 1034880 | bytes 2027652 | tf_op jit(solution)/shard_map/slice | solution.py:123
  42.2 0.4 broadcast_select_fusion.3
  42.5 0.5 fusion.120
  43.1 0.1 slice.1033
  43.2 0.1 slice.1034
  43.3 0.1 slice.1038
  43.4 0.1 slice.1039
  43.6 0.1 slice.1036
  43.7 1.7 %fusion.34 = f32[4,8,18,130]{3,2,1,0:T(8,128)S(1)} fusion(f32[4,8,20,132]{3,2,1,0:T(8,128)S(1)} %get-tuple-element.59, f32[4,8,20,132]{3,2,1,0:T(8,128)S(1)} %get-tuple-element.55, f32[4,8,20,132]{3,2,1,0:T(8,128)S(1)} %get-tuple-element.54, f32[8,18,130]{2,1,0:T(8,128)S(1)} %slice.1039, f32[8,18,130]{2,1,0:T(8,128)S(1)} %slice.1038, ...), kind=kLoop, calls=%fused_computation.61 | loop fusion | flops 1722240 | bytes 7585792 | tf_op jit(solution)/shard_map/jit(_where)/select_n | solution.py:133
  45.4 0.2 multiply_reduce_fusion.9
  45.6 0.4 broadcast_select_fusion.2
  46.0 0.1 slice_bitcast_fusion.5
  46.1 0.2 fusion.161
  46.4 0.6 %fusion.93 = f32[4,8,16,128]{3,2,1,0:T(8,128)S(1)} fusion(f32[4,8,18,130]{3,2,1,0:T(8,128)S(1)} %fusion.34, f32[4,8,38,150]{3,2,1,0:T(8,128)S(1)} %get-tuple-element.67, f32[8,128]{1,0:T(8,128)S(1)} %broadcast_add_fusion.11, f32[128]{0:T(128)S(1)} %get-tuple-element.109, f32[128]{0:T(128)S(1)} %get-tuple-element.107, f32[128]{0:T(128)S(1)} %get-tuple-element.106, ...), kind=kLoop, calls=%fused_computation.174 | loop fusion | flops 1638400 | bytes 2955264 | tf_op jit(solution)/shard_map/jit(_where)/select_n | solution.py:133
  47.0 2.0 %collective-permute-start.7 = (f32[6,4,16,128]{3,2,1,0:T(8,128)S(1)}, f32[6,4,16,128]{3,2,1,0:T(8,128)S(1)}, u32[]{:S(2)}, u32[]{:S(2)}) collective-permute-start(f32[6,4,16,128]{3,2,1,0:T(8,128)S(1)} %get-tuple-element.65), channel_id=1, source_target_pairs={{0,1},{1,0},{2,3},{3,2},{4,5},{5,4},{6,7},{7,6},{8,9},{9,8},{10,11... | collective-permute-start | bytes 589832 | tf_op jit(solution)/shard_map/ppermute | solution.py:110
  49.1 1.1 %collective-permute-done.7 = f32[6,4,16,128]{3,2,1,0:T(8,128)S(1)} collective-permute-done((f32[6,4,16,128]{3,2,1,0:T(8,128)S(1)}, f32[6,4,16,128]{3,2,1,0:T(8,128)S(1)}, u32[]{:S(2)}, u32[]{:S(2)}) %collective-permute-start.7) | collective-permute-done | bytes 196640 | tf_op jit(solution)/shard_map/ppermute | solution.py:110
  50.2 0.6 %gather_fusion.1 = f32[2,6,4,16,128]{4,3,2,1,0:T(8,128)S(1)} fusion(f32[2,6,4,16,128]{4,3,2,1,0:T(8,128)S(1)} %pad_maximum_fusion.2, s32[1024]{0:T(1024)S(1)} %pad_clamp_fusion), kind=kCustom, calls=%fused_computation.1 | custom fusion | bytes 786440 | tf_op jit(solution)/shard_map/jit(_take)/gather | solution.py:114
  50.7 0.1 select_bitcast_fusion.1
  50.9 0.7 %copy_bitcast_fusion = f32[4,4,16,256]{3,2,1,0:T(8,128)} fusion(f32[6,4,16,2,128]{4,2,1,0,3:T(8,128)S(1)} %select_bitcast_fusion.1), kind=kLoop, calls=%fused_computation.175 | loop fusion | bytes 524288 | tf_op jit(solution)/shard_map/slice | solution.py:310
  51.6 0.7 %squeeze.22 = f32[4,16,256]{2,1,0:T(8,128)} reshape(f32[1,4,16,2,128]{4,3,2,1,0:T(2,128)S(1)} %copy.9) | data formatting | bytes 131072 | tf_op jit(solution)/shard_map/squeeze | solution.py:310
  52.4 0.7 %squeeze.23 = f32[4,16,256]{2,1,0:T(8,128)} reshape(f32[1,4,16,2,128]{4,3,2,1,0:T(2,128)S(1)} %copy.10) | data formatting | bytes 131072 | tf_op jit(solution)/shard_map/squeeze | solution.py:310
  (98 shorter events, 2.6 us)
Async XLA Ops:
  2.5 10.3 %collective-permute-start.2 = (f32[4,4,16,256]{3,2,1,0:T(8,128)S(1)}, f32[4,4,16,256]{3,2,1,0:T(8,128)S(1)}, u32[]{:S(2)}, u32[]{:S(2)}) collective-permute-start(f32[4,4,16,256]{3,2,1,0:T(8,128)S(1)} %get-tuple-element.85), channel_id=1, source_target_pairs={{0,1},{1,0},{2,3},{3,2},{4,5},{5,4},{6,7},{7,6},{8,9},{9,8},{10,11... | collective-permute-start | bytes 786440 | tf_op jit(solution)/shard_map/ppermute | solution.py:55
  3.3 9.1 %collective-permute-start = (f32[4,4,16,12]{3,2,1,0:T(8,128)S(1)}, f32[4,4,16,12]{3,2,1,0:T(8,128)S(1)}, u32[]{:S(2)}, u32[]{:S(2)}) collective-permute-start(f32[4,4,16,12]{3,2,1,0:T(8,128)S(1)} %get-tuple-element.86), channel_id=1, source_target_pairs={{0,2},{3,1},{2,4},{5,3},{4,6},{7,5},{8,10},{11,9},{10,12},{13,11},... | collective-permute-start | bytes 36872 | tf_op jit(solution)/shard_map/ppermute | solution.py:88
  5.2 7.5 %collective-permute-start.1 = (f32[4,4,16,12]{3,2,1,0:T(8,128)S(1)}, f32[4,4,16,12]{3,2,1,0:T(8,128)S(1)}, u32[]{:S(2)}, u32[]{:S(2)}) collective-permute-start(f32[4,4,16,12]{3,2,1,0:T(8,128)S(1)} %get-tuple-element.87), channel_id=1, source_target_pairs={{1,2},{2,1},{3,4},{4,3},{5,6},{6,5},{9,10},{10,9},{11,12},{12,11},... | collective-permute-start | bytes 36872 | tf_op jit(solution)/shard_map/ppermute | solution.py:87
  14.0 2.6 %copy-start = (f32[4,8,16,152]{3,2,1,0:T(8,128)}, f32[4,8,16,152]{3,2,1,0:T(8,128)S(1)}, u32[]{:S(2)}) copy-start(f32[4,8,16,152]{3,2,1,0:T(8,128)S(1)} %fusion.44) | copy-start | bytes 933892
  14.1 7.0 %collective-permute-start.3 = (f32[8,23,152]{2,1,0:T(8,128)S(1)}, f32[8,23,152]{2,1,0:T(8,128)S(1)}, u32[]{:S(2)}, u32[]{:S(2)}) collective-permute-start(f32[8,23,152]{2,1,0:T(8,128)S(1)} %pad_maximum_fusion.11), channel_id=1, source_target_pairs={{0,8},{8,16},{16,24},{24,0},{1,9},{9,17},{17,25},{25,1},{2,10},{10... | collective-permute-start | bytes 335624 | tf_op jit(solution)/shard_map/ppermute | solution.py:39
  15.4 10.0 %collective-permute-start.4 = (f32[8,23,152]{2,1,0:T(8,128)S(1)}, f32[8,23,152]{2,1,0:T(8,128)S(1)}, u32[]{:S(2)}, u32[]{:S(2)}) collective-permute-start(f32[8,23,152]{2,1,0:T(8,128)S(1)} %pad_maximum_fusion.12), channel_id=1, source_target_pairs={{8,0},{16,8},{24,16},{0,24},{9,1},{17,9},{25,17},{1,25},{10,2},{18... | collective-permute-start | bytes 335624 | tf_op jit(solution)/shard_map/ppermute | solution.py:40
  31.7 1.0 %slice-start = ((f32[4,8,16,152]{3,2,1,0:T(8,128)}), f32[2,8,16,152]{3,2,1,0:T(8,128)S(1)}, s32[]{:S(2)}) async-start(f32[4,8,16,152]{3,2,1,0:T(8,128)} %copy-done), calls=%async_computation | async-start | bytes 524288 | tf_op jit(solution)/shard_map/slice | solution.py:234
  32.8 6.2 %collective-permute-start.5 = (f32[8,12,152]{2,1,0:T(8,128)S(1)}, f32[8,12,152]{2,1,0:T(8,128)S(1)}, u32[]{:S(2)}, u32[]{:S(2)}) collective-permute-start(f32[8,12,152]{2,1,0:T(8,128)S(1)} %pad_maximum_fusion.13), channel_id=1, source_target_pairs={{0,8},{8,16},{16,24},{24,0},{1,9},{9,17},{17,25},{25,1},{2,10},{10... | collective-permute-start | bytes 175112 | tf_op jit(solution)/shard_map/ppermute | solution.py:39
  34.1 5.6 %collective-permute-start.6 = (f32[8,12,152]{2,1,0:T(8,128)S(1)}, f32[8,12,152]{2,1,0:T(8,128)S(1)}, u32[]{:S(2)}, u32[]{:S(2)}) collective-permute-start(f32[8,12,152]{2,1,0:T(8,128)S(1)} %pad_maximum_fusion.14), channel_id=1, source_target_pairs={{8,0},{16,8},{24,16},{0,24},{9,1},{17,9},{25,17},{1,25},{10,2},{18... | collective-permute-start | bytes 175112 | tf_op jit(solution)/shard_map/ppermute | solution.py:40
  47.0 3.1 %collective-permute-start.7 = (f32[6,4,16,128]{3,2,1,0:T(8,128)S(1)}, f32[6,4,16,128]{3,2,1,0:T(8,128)S(1)}, u32[]{:S(2)}, u32[]{:S(2)}) collective-permute-start(f32[6,4,16,128]{3,2,1,0:T(8,128)S(1)} %get-tuple-element.65), channel_id=1, source_target_pairs={{0,1},{1,0},{2,3},{3,2},{4,5},{5,4},{6,7},{7,6},{8,9},{9,8},{10,11... | collective-permute-start | bytes 589832 | tf_op jit(solution)/shard_map/ppermute | solution.py:110

commit v7 on v6

--- a/solution.py
+++ b/solution.py
@@ -53,6 +53,12 @@
     parts = [block]
     for shift in range(1, peers):
         parts.append(lax.ppermute(block, axis, [(i, (i + shift) % peers) for i in range(peers)]))
+    if peers == 2:
+        return jnp.where(
+            own == 0,
+            jnp.concatenate([parts[0], parts[1]], axis=dim),
+            jnp.concatenate([parts[1], parts[0]], axis=dim),
+        )
     stacked = jnp.stack(parts)
     order = (own - jnp.arange(peers, dtype=jnp.int32)) % peers
     ordered = jnp.take(stacked, order, axis=0)
@@ -109,6 +115,12 @@
         if shift:
             piece = lax.ppermute(piece, "hgt", [(i, (i + shift) % peers) for i in range(peers)])
         parts.append(piece)
+    if peers == 2:
+        return jnp.where(
+            own == 0,
+            jnp.concatenate([parts[0], parts[1]], axis=-1),
+            jnp.concatenate([parts[1], parts[0]], axis=-1),
+        )
     stacked = jnp.stack(parts)
     order = (own - jnp.arange(peers, dtype=jnp.int32)) % peers
     ordered = jnp.moveaxis(jnp.take(stacked, order, axis=0), 0, -2)

time: 53.3 us -> 51.1 us (0.959)
  local copies, waits for them, and re-layouts: 6.42 us -> 4.41 us
    gather x2 -> x0, local copies, waits for them, and re-layouts: 1.16 us -> none  [the longest x1 0.58 us: gather_axis(): ordered = jnp.take(stacked, order, axis=0)]
    another operation x3 -> x0, other arithmetic: 0.99 us -> none  [the longest x2 0.96 us: gather_axis(): stacked = jnp.stack(parts)]
    another operation x1 -> x2, other arithmetic: 0.88 us -> 1.81 us  [shards(): jnp.stack([density, labels.astype(jnp.float32), observed, measured.astype...]
    squeeze x2 -> x1, local copies, waits for them, and re-layouts: 1.37 us -> 0.66 us  [shards(): return (result[0], result[1], result[2:])]
where the time goes in v7:
time: 51.1 us; the launch traced here: 50.8 us
  other arithmetic  19.6 us (38%)
  starting transfers between devices  14.5 us (28%)
  waiting for transfers between devices  10.8 us (21%)
  local copies, waits for them, and re-layouts  4.41 us (9%)
  between operations  1.48 us (3%)
    select_n x11, other arithmetic, in_domain(): return jnp.where(radial_mask(width, geometry), x, 0.0)  6.49 us
    ppermute x2, waiting for transfers between devices, azim_exchange(): after = lax.ppermute(leading, 'azim', down)  4.85 us
    ppermute x1, starting transfers between devices, edge_columns(): lax.ppermute(jnp.where(own == 0, first, last), ('rad', 'hgt'), cross)  4.68 us
    ppermute x2, waiting for transfers between devices, azim_exchange(): before = lax.ppermute(last, 'azim', up)  4.52 us
    reduce_sum x2, other arithmetic, chemical(): cube_sum = jnp.sum(grains * grains * grains, axis=0)  3.17 us
    slice x15, local copies, waits for them, and re-layouts, crop(): return x[..., cut:x.shape[-2] - cut, cut:x.shape[-1] - cut]  2.63 us
    ppermute x2, starting transfers between devices, azim_exchange(): after = lax.ppermute(leading, 'azim', down)  2.59 us
    ppermute x2, starting transfers between devices, azim_exchange(): before = lax.ppermute(last, 'azim', up)  2.53 us
  transfers between devices with their start and end apart: 8, of which 5 were waited for; matrix products, arithmetic and copies ran while one was open for 11% of the time, Pallas kernels for 0%

profile of v7, /device:TPU:9, one launch (start us, length us, event | category | flops | bytes accessed | tf_op | source)
XLA Modules:
  0.0 50.8 jit_solution(15115349571994238612)
XLA Ops:
  0.7 0.9 %convert_bitcast_fusion = (f32[1,4,16,256]{3,2,1,0:T(8,128)S(1)}, f32[1,4,16,256]{3,2,1,0:T(8,128)S(1)}) fusion(s32[4,16,256]{2,1,0:T(8,128)} %param.7, s32[4,16,256]{2,1,0:T(8,128)} %param.5), kind=kLoop, calls=%fused_computation.325 | loop fusion | flops 32768 | bytes 262144 | tf_op jit(solution)/shard_map/stack | solution.py:234
  1.6 0.9 %pad_maximum_fusion.8 = f32[4,4,16,256]{3,2,1,0:T(8,128)S(1)} fusion(f32[1,4,16,256]{3,2,1,0:T(8,128)S(1)} %get-tuple-element.148, f32[1,4,16,256]{3,2,1,0:T(8,128)} %bitcast.22, f32[1,4,16,256]{3,2,1,0:T(8,128)S(1)} %get-tuple-element.149, f32[1,4,16,256]{3,2,1,0:T(8,128)} %bitcast.24), kind=kLoop, calls=%fused_computation.211 | loop fusion | flops 196608 | bytes 524288 | tf_op jit(solution)/shard_map/stack | solution.py:234
  2.5 0.7 %collective-permute-start.2 = (f32[4,4,16,256]{3,2,1,0:T(8,128)S(1)}, f32[4,4,16,256]{3,2,1,0:T(8,128)S(1)}, u32[]{:S(2)}, u32[]{:S(2)}) collective-permute-start(f32[4,4,16,256]{3,2,1,0:T(8,128)S(1)} %pad_maximum_fusion.8), channel_id=1, source_target_pairs={{0,1},{1,0},{2,3},{3,2},{4,5},{5,4},{6,7},{7,6},{8,9},{9,8},{10,11... | collective-permute-start | bytes 786440 | tf_op jit(solution)/shard_map/ppermute | solution.py:55
  3.2 0.1 slice_select_fusion.1
  3.3 1.9 %collective-permute-start = (f32[4,4,16,12]{3,2,1,0:T(8,128)S(1)}, f32[4,4,16,12]{3,2,1,0:T(8,128)S(1)}, u32[]{:S(2)}, u32[]{:S(2)}) collective-permute-start(f32[4,4,16,12]{3,2,1,0:T(8,128)S(1)} %get-tuple-element.84), channel_id=1, source_target_pairs={{0,2},{3,1},{2,4},{5,3},{4,6},{7,5},{8,10},{11,9},{10,12},{13,11},... | collective-permute-start | bytes 36872 | tf_op jit(solution)/shard_map/ppermute | solution.py:94
  5.2 4.7 %collective-permute-start.1 = (f32[4,4,16,12]{3,2,1,0:T(8,128)S(1)}, f32[4,4,16,12]{3,2,1,0:T(8,128)S(1)}, u32[]{:S(2)}, u32[]{:S(2)}) collective-permute-start(f32[4,4,16,12]{3,2,1,0:T(8,128)S(1)} %get-tuple-element.85), channel_id=1, source_target_pairs={{1,2},{2,1},{3,4},{4,3},{5,6},{6,5},{9,10},{10,9},{11,12},{12,11},... | collective-permute-start | bytes 36872 | tf_op jit(solution)/shard_map/ppermute | solution.py:93
  10.4 0.1 fusion.169
  10.6 0.1 fusion.168
  10.7 0.1 fusion.173
  10.9 0.1 fusion.177
  11.0 0.1 fusion.172
  11.2 0.1 fusion.176
  11.4 0.1 broadcast_add_fusion.4
  12.3 0.4 collective-permute-done.1
  12.8 0.4 fusion.44
  13.4 1.3 %collective-permute-start.3 = (f32[8,23,152]{2,1,0:T(8,128)S(1)}, f32[8,23,152]{2,1,0:T(8,128)S(1)}, u32[]{:S(2)}, u32[]{:S(2)}) collective-permute-start(f32[8,23,152]{2,1,0:T(8,128)S(1)} %pad_maximum_fusion.9), channel_id=1, source_target_pairs={{0,8},{8,16},{16,24},{24,0},{1,9},{9,17},{17,25},{25,1},{2,10},{10... | collective-permute-start | bytes 335624 | tf_op jit(solution)/shard_map/ppermute | solution.py:39
  14.7 1.2 %collective-permute-start.4 = (f32[8,23,152]{2,1,0:T(8,128)S(1)}, f32[8,23,152]{2,1,0:T(8,128)S(1)}, u32[]{:S(2)}, u32[]{:S(2)}) collective-permute-start(f32[8,23,152]{2,1,0:T(8,128)S(1)} %pad_maximum_fusion.10), channel_id=1, source_target_pairs={{8,0},{16,8},{24,16},{0,24},{9,1},{17,9},{25,17},{1,25},{10,2},{18... | collective-permute-start | bytes 335624 | tf_op jit(solution)/shard_map/ppermute | solution.py:40
  15.9 4.5 %collective-permute-done.3 = f32[8,23,152]{2,1,0:T(8,128)S(1)} collective-permute-done((f32[8,23,152]{2,1,0:T(8,128)S(1)}, f32[8,23,152]{2,1,0:T(8,128)S(1)}, u32[]{:S(2)}, u32[]{:S(2)}) %collective-permute-start.3) | collective-permute-done | bytes 111904 | tf_op jit(solution)/shard_map/ppermute | solution.py:39
  20.4 4.3 %collective-permute-done.4 = f32[8,23,152]{2,1,0:T(8,128)S(1)} collective-permute-done((f32[8,23,152]{2,1,0:T(8,128)S(1)}, f32[8,23,152]{2,1,0:T(8,128)S(1)}, u32[]{:S(2)}, u32[]{:S(2)}) %collective-permute-start.4) | collective-permute-done | bytes 111904 | tf_op jit(solution)/shard_map/ppermute | solution.py:40
  24.8 0.2 pad_maximum_fusion.1
  25.0 0.4 multiply_reduce_fusion.2
  25.4 0.2 slice.937
  25.6 0.6 %fusion.48 = (f32[8,38,150]{2,1,0:T(8,128)S(1)}, f32[8,38,150]{2,1,0:T(8,128)S(1)}, f32[8,38,150]{2,1,0:T(8,128)S(1)}) fusion(f32[8,40,152]{2,1,0:T(8,128)S(1)} %broadcast_select_fusion, f32[8,38,150]{2,1,0:T(8,128)S(1)} %get-tuple-element.17, f32[8,38,150]{2,1,0:T(8,128)S(1)} %get-tuple-element.18, f32[8,150]{1,0:T(8,128)S(1)} %broadcast_add_fusion.10, ...), kind=kLoop, calls=%fused_computation.104 | loop fusion | flops 1048800 | bytes 3179904 | tf_op jit(solution)/shard_map/sub | solution.py:264
  26.2 0.2 slice.934
  26.3 0.2 slice.936
  26.5 0.4 slice.942
  26.9 2.8 %multiply_reduce_fusion.1 = (f32[8,34,146]{2,1,0:T(8,128)S(1)}, f32[8,34,146]{2,1,0:T(8,128)S(1)}, f32[4,8,34,146]{3,2,1,0:T(8,128)S(1)}) fusion(f32[8,146]{1,0:T(8,128)S(1)} %broadcast_add_fusion.8, f32[4,8,36,148]{3,2,1,0:T(8,128)S(1)} %slice.942, f32[4,8,38,150]{3,2,1,0:T(8,128)S(1)} %get-tuple-element.67, f32[146]{0:T(256)S(1)} %get-tuple-element.147, ...), kind=kLoop, calls=%fused_computation.23 | loop fusion | flops 3732928 | bytes 5930538 | tf_op jit(solution)/shard_map/reduce_sum | solution.py:181
  29.7 0.2 mul.1273
  29.9 0.4 slice.964
  30.2 0.1 slice.959
  30.4 0.6 %fusion.54 = f32[8,36,148]{2,1,0:T(8,128)S(1)} fusion(f32[8,38,150]{2,1,0:T(8,128)S(1)} %get-tuple-element.77, f32[8,40,152]{2,1,0:T(8,128)S(1)} %broadcast_select_fusion, f32[8,148]{1,0:T(8,128)S(1)} %broadcast_add_fusion.9, f32[148]{0:T(256)S(1)} %get-tuple-element.139, f32[148]{0:T(256)S(1)} %get-tuple-element.137, f32[148]{0:T(256)S(1)} %get-tuple-element.136, ...), kind=kLoop, calls=%fused_computation.110 | loop fusion | flops 554112 | bytes 2476032 | tf_op jit(solution)/shard_map/jit(_where)/select_n | solution.py:145
  31.0 0.6 %slice_subtract_fusion.1 = (f32[8,34,146]{2,1,0:T(8,128)S(1)}, f32[8,34,146]{2,1,0:T(8,128)S(1)}, f32[8,34,146]{2,1,0:T(8,128)S(1)}) fusion(f32[8,36,148]{2,1,0:T(8,128)S(1)} %fusion.54, f32[8,146]{1,0:T(8,128)S(1)} %broadcast_add_fusion.8, f32[146]{0:T(256)S(1)} %get-tuple-element.147, f32[146]{0:T(256)S(1)} %get-tuple-element.145, ...), kind=kLoop, calls=%fused_computation.138 | loop fusion | flops 913376 | bytes 3109248 | tf_op jit(solution)/shard_map/sub | solution.py:182
  31.6 0.1 slice.956
  31.8 0.1 slice.958
  31.9 0.1 slice-done
  32.1 1.3 %collective-permute-start.5 = (f32[8,12,152]{2,1,0:T(8,128)S(1)}, f32[8,12,152]{2,1,0:T(8,128)S(1)}, u32[]{:S(2)}, u32[]{:S(2)}) collective-permute-start(f32[8,12,152]{2,1,0:T(8,128)S(1)} %pad_maximum_fusion.11), channel_id=1, source_target_pairs={{0,8},{8,16},{16,24},{24,0},{1,9},{9,17},{17,25},{25,1},{2,10},{10... | collective-permute-start | bytes 175112 | tf_op jit(solution)/shard_map/ppermute | solution.py:39
  33.4 1.4 %collective-permute-start.6 = (f32[8,12,152]{2,1,0:T(8,128)S(1)}, f32[8,12,152]{2,1,0:T(8,128)S(1)}, u32[]{:S(2)}, u32[]{:S(2)}) collective-permute-start(f32[8,12,152]{2,1,0:T(8,128)S(1)} %pad_maximum_fusion.12), channel_id=1, source_target_pairs={{8,0},{16,8},{24,16},{0,24},{9,1},{17,9},{25,17},{1,25},{10,2},{18... | collective-permute-start | bytes 175112 | tf_op jit(solution)/shard_map/ppermute | solution.py:40
  34.8 0.5 %fusion.87 = f32[8,32,144]{2,1,0:T(8,128)S(1)} fusion(f32[8,34,146]{2,1,0:T(8,128)S(1)} %get-tuple-element.76, f32[8,36,148]{2,1,0:T(8,128)S(1)} %fusion.54, f32[8,144]{1,0:T(8,128)S(1)} %broadcast_add_fusion.7, f32[144]{0:T(256)S(1)} %get-tuple-element.135, f32[144]{0:T(256)S(1)} %get-tuple-element.133, f32[144]{0:T(256)S(1)} %get-tuple-element.132, ...), kind=kLoop, calls=%fused_computation.164 | loop fusion | flops 479232 | bytes 2059776 | tf_op jit(solution)/shard_map/jit(_where)/select_n | solution.py:145
  35.3 2.3 %multiply_reduce_fusion = (f32[8,30,142]{2,1,0:T(8,128)S(1)}, f32[8,30,142]{2,1,0:T(8,128)S(1)}, f32[4,8,30,142]{3,2,1,0:T(8,128)S(1)}) fusion(f32[8,142]{1,0:T(8,128)S(1)} %broadcast_add_fusion.6, f32[4,8,32,144]{3,2,1,0:T(8,128)S(1)} %slice.964, f32[4,8,34,146]{3,2,1,0:T(8,128)S(1)} %get-tuple-element.51, f32[142]{0:T(256)S(1)} %get-tuple-element.131, ...), kind=kLoop, calls=%fused_computation.3 | loop fusion | flops 3203520 | bytes 5094774 | tf_op jit(solution)/shard_map/reduce_sum | solution.py:180
  37.5 0.5 fusion.71
  38.0 0.3 slice.1004
  38.3 0.6 %collective-permute-done.6 = f32[8,12,152]{2,1,0:T(8,128)S(1)} collective-permute-done((f32[8,12,152]{2,1,0:T(8,128)S(1)}, f32[8,12,152]{2,1,0:T(8,128)S(1)}, u32[]{:S(2)}, u32[]{:S(2)}) %collective-permute-start.6) | collective-permute-done | bytes 58400 | tf_op jit(solution)/shard_map/ppermute | solution.py:40
  39.0 0.8 %fusion.102 = (f32[8,28,140]{2,1,0:T(8,128)S(1)}, f32[8,28,140]{2,1,0:T(8,128)S(1)}) fusion(f32[8,6,152]{2,1,0:T(8,128)S(1)} %get-tuple-element.91, f32[8,16,152]{2,1,0:T(8,128)S(1)} %get-tuple-element.82, f32[8,6,152]{2,1,0:T(8,128)S(1)} %get-tuple-element.89, f32[8,6,152]{2,1,0:T(8,128)S(1)} %get-tuple-element.90, ...), kind=kLoop, calls=%fused_computation.187 | loop fusion | flops 627200 | bytes 2621952 | tf_op jit(solution)/shard_map/jit(_where)/select_n | solution.py:145
  39.7 0.5 broadcast_select_fusion.1
  40.2 0.5 %fusion.131 = (f32[8,24,136]{2,1,0:T(8,128)S(1)}, f32[8,24,136]{2,1,0:T(8,128)S(1)}) fusion(f32[8,26,138]{2,1,0:T(8,128)S(1)} %get-tuple-element.33, f32[8,32,144]{2,1,0:T(8,128)S(1)} %fusion.87, f32[8,28,140]{2,1,0:T(8,128)S(1)} %get-tuple-element.38, f32[8,26,138]{2,1,0:T(8,128)S(1)} %get-tuple-element.34, f32[8,136]{1,0:T(8,128)S(1)} %broadcast_add_fusion.3, ...), kind=kLoop, calls=%fused_computation.243 | loop fusion | flops 548352 | bytes 2055680 | tf_op jit(solution)/shard_map/jit(_where)/select_n | solution.py:145
  40.7 0.1 slice.1006
  40.8 0.6 %fusion.188 = (f32[4,8,20,132]{3,2,1,0:T(8,128)S(1)}, f32[4,8,20,132]{3,2,1,0:T(8,128)S(1)}, f32[8,20,132]{2,1,0:T(8,128)S(1)}, f32[8,20,132]{2,1,0:T(8,128)S(1)...) fusion(f32[4,8,34,146]{3,2,1,0:T(8,128)S(1)} %get-tuple-element.51, f32[8,20,132]{2,1,0:T(8,128)S(1)} %slice.1006, ...), kind=kLoop, calls=%fused_computation.456 | loop fusion | flops 1034880 | bytes 2027652 | tf_op jit(solution)/shard_map/slice | solution.py:135
  41.4 0.4 broadcast_select_fusion.3
  41.8 0.5 %fusion.120 = (f32[8,20,132]{2,1,0:T(8,128)S(1)}, f32[8,20,132]{2,1,0:T(8,128)S(1)}, f32[8,20,132]{2,1,0:T(8,128)S(1)}, f32[8,20,132]{2,1,0:T(8,128)S(1)}) fusion(f32[8,22,134]{2,1,0:T(8,128)S(1)} %get-tuple-element.23, f32[8,20,132]{2,1,0:T(8,128)S(1)} %get-tuple-element.58, f32[8,24,136]{2,1,0:T(8,128)S(1)} %get-tuple-element.80, ...), kind=kLoop, calls=%fused_computation.232 | loop fusion | flops 528000 | bytes 2315776 | tf_op jit(solution)/shard_map/jit(_where)/select_n | solution.py:145
  42.3 0.1 slice.1023
  42.5 0.1 slice.1024
  42.6 0.1 slice.1028
  42.7 0.1 slice.1029
  42.9 0.1 slice.1026
  43.0 1.7 %fusion.34 = f32[4,8,18,130]{3,2,1,0:T(8,128)S(1)} fusion(f32[4,8,20,132]{3,2,1,0:T(8,128)S(1)} %get-tuple-element.59, f32[4,8,20,132]{3,2,1,0:T(8,128)S(1)} %get-tuple-element.55, f32[4,8,20,132]{3,2,1,0:T(8,128)S(1)} %get-tuple-element.54, f32[8,18,130]{2,1,0:T(8,128)S(1)} %slice.1029, f32[8,18,130]{2,1,0:T(8,128)S(1)} %slice.1028, ...), kind=kLoop, calls=%fused_computation.59 | loop fusion | flops 1722240 | bytes 7585792 | tf_op jit(solution)/shard_map/jit(_where)/select_n | solution.py:145
  44.7 0.2 multiply_reduce_fusion.9
  44.9 0.4 broadcast_select_fusion.2
  45.3 0.1 slice_bitcast_fusion.6
  45.4 0.2 fusion.161
  45.7 0.6 %fusion.93 = f32[4,8,16,128]{3,2,1,0:T(8,128)S(1)} fusion(f32[4,8,18,130]{3,2,1,0:T(8,128)S(1)} %fusion.34, f32[4,8,38,150]{3,2,1,0:T(8,128)S(1)} %get-tuple-element.67, f32[8,128]{1,0:T(8,128)S(1)} %broadcast_add_fusion.11, f32[128]{0:T(128)S(1)} %get-tuple-element.107, f32[128]{0:T(128)S(1)} %get-tuple-element.105, f32[128]{0:T(128)S(1)} %get-tuple-element.104, ...), kind=kLoop, calls=%fused_computation.170 | loop fusion | flops 1638400 | bytes 2955264 | tf_op jit(solution)/shard_map/jit(_where)/select_n | solution.py:145
  46.3 2.0 %collective-permute-start.7 = (f32[6,4,16,128]{3,2,1,0:T(8,128)S(1)}, f32[6,4,16,128]{3,2,1,0:T(8,128)S(1)}, u32[]{:S(2)}, u32[]{:S(2)}) collective-permute-start(f32[6,4,16,128]{3,2,1,0:T(8,128)S(1)} %get-tuple-element.65), channel_id=1, source_target_pairs={{0,1},{1,0},{2,3},{3,2},{4,5},{5,4},{6,7},{7,6},{8,9},{9,8},{10,11... | collective-permute-start | bytes 589832 | tf_op jit(solution)/shard_map/ppermute | solution.py:116
  48.3 1.1 %collective-permute-done.7 = f32[6,4,16,128]{3,2,1,0:T(8,128)S(1)} collective-permute-done((f32[6,4,16,128]{3,2,1,0:T(8,128)S(1)}, f32[6,4,16,128]{3,2,1,0:T(8,128)S(1)}, u32[]{:S(2)}, u32[]{:S(2)}) %collective-permute-start.7) | collective-permute-done | bytes 196640 | tf_op jit(solution)/shard_map/ppermute | solution.py:116
  49.5 0.7 %slice.1047 = f32[4,4,16,256]{3,2,1,0:T(8,128)} slice(f32[6,4,16,256]{3,2,1,0:T(8,128)S(1)} %maximum_select_fusion.1), slice={[2:6], [0:4], [0:16], [0:256]} | slice | bytes 524288 | tf_op jit(solution)/shard_map/slice | solution.py:322
  50.2 0.7 %slice_bitcast_fusion.4 = (f32[4,16,256]{2,1,0:T(8,128)}, f32[4,16,256]{2,1,0:T(8,128)}) fusion(f32[6,4,16,256]{3,2,1,0:T(8,128)S(1)} %maximum_select_fusion.1), kind=kLoop, calls=%fused_computation.314 | loop fusion | bytes 262144 | tf_op jit(solution)/shard_map/squeeze | solution.py:322
  (90 shorter events, 2.1 us)
Async XLA Ops:
  0.6 12.1 %copy-start.2 = (f32[4,16,256]{2,1,0:T(8,128)S(1)}, f32[4,16,256]{2,1,0:T(8,128)}, u32[]{:S(2)}) copy-start(f32[4,16,256]{2,1,0:T(8,128)} %param.4) | copy-start | bytes 196612
  0.6 12.1 %copy-start.1 = (f32[4,16,256]{2,1,0:T(8,128)S(1)}, f32[4,16,256]{2,1,0:T(8,128)}, u32[]{:S(2)}) copy-start(f32[4,16,256]{2,1,0:T(8,128)} %param.6) | copy-start | bytes 196612
  2.5 10.3 %collective-permute-start.2 = (f32[4,4,16,256]{3,2,1,0:T(8,128)S(1)}, f32[4,4,16,256]{3,2,1,0:T(8,128)S(1)}, u32[]{:S(2)}, u32[]{:S(2)}) collective-permute-start(f32[4,4,16,256]{3,2,1,0:T(8,128)S(1)} %pad_maximum_fusion.8), channel_id=1, source_target_pairs={{0,1},{1,0},{2,3},{3,2},{4,5},{5,4},{6,7},{7,6},{8,9},{9,8},{10,11... | collective-permute-start | bytes 786440 | tf_op jit(solution)/shard_map/ppermute | solution.py:55
  3.3 9.0 %collective-permute-start = (f32[4,4,16,12]{3,2,1,0:T(8,128)S(1)}, f32[4,4,16,12]{3,2,1,0:T(8,128)S(1)}, u32[]{:S(2)}, u32[]{:S(2)}) collective-permute-start(f32[4,4,16,12]{3,2,1,0:T(8,128)S(1)} %get-tuple-element.84), channel_id=1, source_target_pairs={{0,2},{3,1},{2,4},{5,3},{4,6},{7,5},{8,10},{11,9},{10,12},{13,11},... | collective-permute-start | bytes 36872 | tf_op jit(solution)/shard_map/ppermute | solution.py:94
  5.2 7.5 %collective-permute-start.1 = (f32[4,4,16,12]{3,2,1,0:T(8,128)S(1)}, f32[4,4,16,12]{3,2,1,0:T(8,128)S(1)}, u32[]{:S(2)}, u32[]{:S(2)}) collective-permute-start(f32[4,4,16,12]{3,2,1,0:T(8,128)S(1)} %get-tuple-element.85), channel_id=1, source_target_pairs={{1,2},{2,1},{3,4},{4,3},{5,6},{6,5},{9,10},{10,9},{11,12},{12,11},... | collective-permute-start | bytes 36872 | tf_op jit(solution)/shard_map/ppermute | solution.py:93
  13.3 2.6 %copy-start = (f32[4,8,16,152]{3,2,1,0:T(8,128)}, f32[4,8,16,152]{3,2,1,0:T(8,128)S(1)}, u32[]{:S(2)}) copy-start(f32[4,8,16,152]{3,2,1,0:T(8,128)S(1)} %fusion.44) | copy-start | bytes 933892
  13.4 7.0 %collective-permute-start.3 = (f32[8,23,152]{2,1,0:T(8,128)S(1)}, f32[8,23,152]{2,1,0:T(8,128)S(1)}, u32[]{:S(2)}, u32[]{:S(2)}) collective-permute-start(f32[8,23,152]{2,1,0:T(8,128)S(1)} %pad_maximum_fusion.9), channel_id=1, source_target_pairs={{0,8},{8,16},{16,24},{24,0},{1,9},{9,17},{17,25},{25,1},{2,10},{10... | collective-permute-start | bytes 335624 | tf_op jit(solution)/shard_map/ppermute | solution.py:39
  14.7 10.0 %collective-permute-start.4 = (f32[8,23,152]{2,1,0:T(8,128)S(1)}, f32[8,23,152]{2,1,0:T(8,128)S(1)}, u32[]{:S(2)}, u32[]{:S(2)}) collective-permute-start(f32[8,23,152]{2,1,0:T(8,128)S(1)} %pad_maximum_fusion.10), channel_id=1, source_target_pairs={{8,0},{16,8},{24,16},{0,24},{9,1},{17,9},{25,17},{1,25},{10,2},{18... | collective-permute-start | bytes 335624 | tf_op jit(solution)/shard_map/ppermute | solution.py:40
  31.0 1.0 %slice-start = ((f32[4,8,16,152]{3,2,1,0:T(8,128)}), f32[2,8,16,152]{3,2,1,0:T(8,128)S(1)}, s32[]{:S(2)}) async-start(f32[4,8,16,152]{3,2,1,0:T(8,128)} %copy-done), calls=%async_computation | async-start | bytes 524288 | tf_op jit(solution)/shard_map/slice | solution.py:246
  32.1 6.2 %collective-permute-start.5 = (f32[8,12,152]{2,1,0:T(8,128)S(1)}, f32[8,12,152]{2,1,0:T(8,128)S(1)}, u32[]{:S(2)}, u32[]{:S(2)}) collective-permute-start(f32[8,12,152]{2,1,0:T(8,128)S(1)} %pad_maximum_fusion.11), channel_id=1, source_target_pairs={{0,8},{8,16},{16,24},{24,0},{1,9},{9,17},{17,25},{25,1},{2,10},{10... | collective-permute-start | bytes 175112 | tf_op jit(solution)/shard_map/ppermute | solution.py:39
  33.4 5.6 %collective-permute-start.6 = (f32[8,12,152]{2,1,0:T(8,128)S(1)}, f32[8,12,152]{2,1,0:T(8,128)S(1)}, u32[]{:S(2)}, u32[]{:S(2)}) collective-permute-start(f32[8,12,152]{2,1,0:T(8,128)S(1)} %pad_maximum_fusion.12), channel_id=1, source_target_pairs={{8,0},{16,8},{24,16},{0,24},{9,1},{17,9},{25,17},{1,25},{10,2},{18... | collective-permute-start | bytes 175112 | tf_op jit(solution)/shard_map/ppermute | solution.py:40
  46.3 3.1 %collective-permute-start.7 = (f32[6,4,16,128]{3,2,1,0:T(8,128)S(1)}, f32[6,4,16,128]{3,2,1,0:T(8,128)S(1)}, u32[]{:S(2)}, u32[]{:S(2)}) collective-permute-start(f32[6,4,16,128]{3,2,1,0:T(8,128)S(1)} %get-tuple-element.65), channel_id=1, source_target_pairs={{0,1},{1,0},{2,3},{3,2},{4,5},{5,4},{6,7},{7,6},{8,9},{9,8},{10,11... | collective-permute-start | bytes 589832 | tf_op jit(solution)/shard_map/ppermute | solution.py:116

commit v8 on v7

--- a/solution.py
+++ b/solution.py
@@ -78,30 +78,6 @@
         pairs.append((r * peers + peers - 1, (r + 1) * peers))
         pairs.append(((r + 1) * peers, r * peers + peers - 1))
     received = lax.ppermute(piece, ("rad", "hgt"), pairs)
-    padded = jnp.concatenate([received, block, received], axis=-1)
-    return lax.dynamic_slice_in_dim(padded, own * part, part + 2 * width, axis=padded.ndim - 1)
-
-
-def edge_columns(block, width):
-    own, rad_peers = (lax.axis_index("hgt"), lax.axis_size("rad"))
-    cols = block.shape[-1]
-    first, last = (block[..., :width], block[..., cols - width :])
-    cross, same = ([], [])
-    for r in range(rad_peers - 1):
-        cross += [(2 * r + 1, 2 * r + 2), (2 * r + 2, 2 * r + 1)]
-        same += [(2 * r, 2 * r + 2), (2 * r + 3, 2 * r + 1)]
-    from_cross = lax.ppermute(jnp.where(own == 0, first, last), ("rad", "hgt"), cross)
-    from_same = lax.ppermute(jnp.where(own == 0, last, first), ("rad", "hgt"), same)
-    return jnp.where(
-        own == 0,
-        jnp.concatenate([from_same, from_cross], axis=1),
-        jnp.concatenate([from_cross, from_same], axis=1),
-    )
-
-
-def two_core_window(block, received, width):
-    own = lax.axis_index("hgt")
-    part = block.shape[-1] // 2
     padded = jnp.concatenate([received, block, received], axis=-1)
     return lax.dynamic_slice_in_dim(padded, own * part, part + 2 * width, axis=padded.ndim - 1)
 
@@ -232,11 +208,7 @@
         part,
     )
     packed = jnp.stack([density, labels.astype(jnp.float32), observed, measured.astype(jnp.float32)])
-    if lax.axis_size("hgt") == 2:
-        received = edge_columns(packed, HALO)
-        packed = two_core_window(gather_axis(packed, "hgt", 1), received, HALO)
-    else:
-        packed = chip_window(gather_axis(packed, "hgt", 1), HALO)
+    packed = chip_window(gather_axis(packed, "hgt", 1), HALO)
     need_d, need_e, need_lc, need_lg = reach()
     widths = (need_d[0], need_e[0], need_lc[STEPS], need_lc[STEPS])
     trim = lambda f, w: f[..., HALO - w : f.shape[-1] - (HALO - w)]

time: 51.1 us -> 52.9 us (1.035)
  waiting for transfers between devices: 10.8 us -> 15.5 us
  starting transfers between devices: 14.5 us -> 10.7 us
  other arithmetic: 19.6 us -> 20.5 us
    ppermute x2 -> x1, waiting for transfers between devices: 0.38 us -> 4.52 us  [chip_window(): received = lax.ppermute(piece, ('rad', 'hgt'), pairs)]
    ppermute x2 -> x1, starting transfers between devices: 6.6 us -> 3.13 us  [chip_window(): received = lax.ppermute(piece, ('rad', 'hgt'), pairs)]
    select_n x1, other arithmetic: 0.05 us -> 0.99 us  [gather_axis(): jnp.where(own == 0, jnp.concatenate([parts[0], parts[1]], axis=dim), jnp....]
  transfers between devices with their start and end apart: 8 -> 7, of which waited for: 5 -> 5; matrix products, arithmetic and copies ran while one was open for 11% -> 11% of each run, Pallas kernels for 0% -> 0%
where the time goes in v8:
time: 52.9 us; the launch traced here: 52.6 us
  other arithmetic  20.5 us (39%)
  waiting for transfers between devices  15.5 us (29%)
  starting transfers between devices  10.7 us (20%)
  local copies, waits for them, and re-layouts  4.39 us (8%)
  between operations  1.41 us (3%)
    select_n x11, other arithmetic, in_domain(): return jnp.where(radial_mask(width, geometry), x, 0.0)  6.48 us
    ppermute x2, waiting for transfers between devices, azim_exchange(): after = lax.ppermute(leading, 'azim', down)  5.02 us
    ppermute x2, waiting for transfers between devices, azim_exchange(): before = lax.ppermute(last, 'azim', up)  4.93 us
    ppermute x1, waiting for transfers between devices, chip_window(): received = lax.ppermute(piece, ('rad', 'hgt'), pairs)  4.52 us
    reduce_sum x2, other arithmetic, chemical(): cube_sum = jnp.sum(grains * grains * grains, axis=0)  3.17 us
    ppermute x1, starting transfers between devices, chip_window(): received = lax.ppermute(piece, ('rad', 'hgt'), pairs)  3.13 us
    slice x15, local copies, waits for them, and re-layouts, crop(): return x[..., cut:x.shape[-2] - cut, cut:x.shape[-1] - cut]  2.63 us
    ppermute x2, starting transfers between devices, azim_exchange(): after = lax.ppermute(leading, 'azim', down)  2.59 us
  transfers between devices with their start and end apart: 7, of which 5 were waited for; matrix products, arithmetic and copies ran while one was open for 11% of the time, Pallas kernels for 0%

profile of v8, /device:TPU:9, one launch (start us, length us, event | category | flops | bytes accessed | tf_op | source)
XLA Modules:
  0.0 52.6 jit_solution(1286531053082269331)
XLA Ops:
  0.6 0.9 %convert_bitcast_fusion = (f32[1,4,16,256]{3,2,1,0:T(8,128)S(1)}, f32[1,4,16,256]{3,2,1,0:T(8,128)S(1)}) fusion(s32[4,16,256]{2,1,0:T(8,128)} %param.7, s32[4,16,256]{2,1,0:T(8,128)} %param.5), kind=kLoop, calls=%fused_computation.323 | loop fusion | flops 32768 | bytes 262144 | tf_op jit(solution)/shard_map/stack | solution.py:210
  1.5 0.9 %pad_maximum_fusion.8 = f32[4,4,16,256]{3,2,1,0:T(8,128)S(1)} fusion(f32[1,4,16,256]{3,2,1,0:T(8,128)S(1)} %get-tuple-element.146, f32[1,4,16,256]{3,2,1,0:T(8,128)} %bitcast.22, f32[1,4,16,256]{3,2,1,0:T(8,128)S(1)} %get-tuple-element.147, f32[1,4,16,256]{3,2,1,0:T(8,128)} %bitcast.24), kind=kLoop, calls=%fused_computation.212 | loop fusion | flops 196608 | bytes 524288 | tf_op jit(solution)/shard_map/stack | solution.py:210
  2.4 0.7 %collective-permute-start = (f32[4,4,16,256]{3,2,1,0:T(8,128)S(1)}, f32[4,4,16,256]{3,2,1,0:T(8,128)S(1)}, u32[]{:S(2)}, u32[]{:S(2)}) collective-permute-start(f32[4,4,16,256]{3,2,1,0:T(8,128)S(1)} %pad_maximum_fusion.8), channel_id=1, source_target_pairs={{0,1},{1,0},{2,3},{3,2},{4,5},{5,4},{6,7},{7,6},{8,9},{9,8},{10,11... | collective-permute-start | bytes 786440 | tf_op jit(solution)/shard_map/ppermute | solution.py:55
  3.6 0.1 fusion.169
  3.8 0.1 fusion.168
  3.9 0.1 fusion.173
  4.1 0.1 fusion.177
  4.2 0.1 fusion.172
  4.6 0.1 broadcast_add_fusion.4
  5.2 0.1 broadcast_add_fusion.11
  5.5 1.0 %maximum_select_fusion = f32[4,8,16,256]{3,2,1,0:T(8,128)S(1)} fusion(f32[4,4,16,256]{3,2,1,0:T(8,128)S(1)} %collective-permute-done, f32[1,4,16,256]{3,2,1,0:T(8,128)S(1)} %get-tuple-element.146, f32[1,4,16,256]{3,2,1,0:T(8,128)} %bitcast.23, f32[1,4,16,256]{3,2,1,0:T(8,128)S(1)} %get-tuple-element.147, f32[1,4,16,256]{3,2,1,0:T(8,128)} %bitcast.25, pred[]{:T(512)S(6)} %eq.11), kind=kLoop, calls=%fused_computation.79 | loop fusion | flops 1179648 | bytes 1048577 | tf_op jit(solution)/shard_map/jit(_where)/select_n | solution.py:57
  6.5 0.1 slice_select_fusion
  6.6 3.1 %collective-permute-start.1 = (f32[4,8,16,12]{3,2,1,0:T(8,128)S(1)}, f32[4,8,16,12]{3,2,1,0:T(8,128)S(1)}, u32[]{:S(2)}, u32[]{:S(2)}) collective-permute-start(f32[4,8,16,12]{3,2,1,0:T(8,128)S(1)} %slice_select_fusion), channel_id=1, source_target_pairs={{1,2},{2,1},{3,4},{4,3},{5,6},{6,5},{9,10},{10,9},{11,12},{12,11},... | collective-permute-start | bytes 73736 | tf_op jit(solution)/shard_map/ppermute | solution.py:80
  9.8 4.5 %collective-permute-done.1 = f32[4,8,16,12]{3,2,1,0:T(8,128)S(1)} collective-permute-done((f32[4,8,16,12]{3,2,1,0:T(8,128)S(1)}, f32[4,8,16,12]{3,2,1,0:T(8,128)S(1)}, u32[]{:S(2)}, u32[]{:S(2)}) %collective-permute-start.1) | collective-permute-done | bytes 24608 | tf_op jit(solution)/shard_map/ppermute | solution.py:80
  14.3 0.4 fusion.44
  14.9 1.3 %collective-permute-start.2 = (f32[8,23,152]{2,1,0:T(8,128)S(1)}, f32[8,23,152]{2,1,0:T(8,128)S(1)}, u32[]{:S(2)}, u32[]{:S(2)}) collective-permute-start(f32[8,23,152]{2,1,0:T(8,128)S(1)} %pad_maximum_fusion.9), channel_id=1, source_target_pairs={{0,8},{8,16},{16,24},{24,0},{1,9},{9,17},{17,25},{25,1},{2,10},{10... | collective-permute-start | bytes 335624 | tf_op jit(solution)/shard_map/ppermute | solution.py:39
  16.2 1.2 %collective-permute-start.3 = (f32[8,23,152]{2,1,0:T(8,128)S(1)}, f32[8,23,152]{2,1,0:T(8,128)S(1)}, u32[]{:S(2)}, u32[]{:S(2)}) collective-permute-start(f32[8,23,152]{2,1,0:T(8,128)S(1)} %pad_maximum_fusion.10), channel_id=1, source_target_pairs={{8,0},{16,8},{24,16},{0,24},{9,1},{17,9},{25,17},{1,25},{10,2},{18... | collective-permute-start | bytes 335624 | tf_op jit(solution)/shard_map/ppermute | solution.py:40
  17.4 4.9 %collective-permute-done.2 = f32[8,23,152]{2,1,0:T(8,128)S(1)} collective-permute-done((f32[8,23,152]{2,1,0:T(8,128)S(1)}, f32[8,23,152]{2,1,0:T(8,128)S(1)}, u32[]{:S(2)}, u32[]{:S(2)}) %collective-permute-start.2) | collective-permute-done | bytes 111904 | tf_op jit(solution)/shard_map/ppermute | solution.py:39
  22.3 4.3 %collective-permute-done.3 = f32[8,23,152]{2,1,0:T(8,128)S(1)} collective-permute-done((f32[8,23,152]{2,1,0:T(8,128)S(1)}, f32[8,23,152]{2,1,0:T(8,128)S(1)}, u32[]{:S(2)}, u32[]{:S(2)}) %collective-permute-start.3) | collective-permute-done | bytes 111904 | tf_op jit(solution)/shard_map/ppermute | solution.py:40
  26.7 0.2 pad_maximum_fusion.1
  26.9 0.4 multiply_reduce_fusion.2
  27.3 0.2 slice.937
  27.5 0.6 %fusion.48 = (f32[8,38,150]{2,1,0:T(8,128)S(1)}, f32[8,38,150]{2,1,0:T(8,128)S(1)}, f32[8,38,150]{2,1,0:T(8,128)S(1)}) fusion(f32[8,40,152]{2,1,0:T(8,128)S(1)} %broadcast_select_fusion, f32[8,38,150]{2,1,0:T(8,128)S(1)} %get-tuple-element.17, f32[8,38,150]{2,1,0:T(8,128)S(1)} %get-tuple-element.18, f32[8,150]{1,0:T(8,128)S(1)} %broadcast_add_fusion.10, ...), kind=kLoop, calls=%fused_computation.104 | loop fusion | flops 1048800 | bytes 3179904 | tf_op jit(solution)/shard_map/sub | solution.py:236
  28.1 0.2 slice.934
  28.2 0.2 slice.936
  28.4 0.4 slice.942
  28.8 2.8 %multiply_reduce_fusion.1 = (f32[8,34,146]{2,1,0:T(8,128)S(1)}, f32[8,34,146]{2,1,0:T(8,128)S(1)}, f32[4,8,34,146]{3,2,1,0:T(8,128)S(1)}) fusion(f32[8,146]{1,0:T(8,128)S(1)} %broadcast_add_fusion.8, f32[4,8,36,148]{3,2,1,0:T(8,128)S(1)} %slice.942, f32[4,8,38,150]{3,2,1,0:T(8,128)S(1)} %get-tuple-element.67, f32[146]{0:T(256)S(1)} %get-tuple-element.145, ...), kind=kLoop, calls=%fused_computation.23 | loop fusion | flops 3732928 | bytes 5930538 | tf_op jit(solution)/shard_map/reduce_sum | solution.py:157
  31.6 0.2 mul.1273
  31.8 0.4 slice.964
  32.1 0.1 slice.959
  32.3 0.6 %fusion.54 = f32[8,36,148]{2,1,0:T(8,128)S(1)} fusion(f32[8,38,150]{2,1,0:T(8,128)S(1)} %get-tuple-element.77, f32[8,40,152]{2,1,0:T(8,128)S(1)} %broadcast_select_fusion, f32[8,148]{1,0:T(8,128)S(1)} %broadcast_add_fusion.9, f32[148]{0:T(256)S(1)} %get-tuple-element.137, f32[148]{0:T(256)S(1)} %get-tuple-element.135, f32[148]{0:T(256)S(1)} %get-tuple-element.134, ...), kind=kLoop, calls=%fused_computation.110 | loop fusion | flops 554112 | bytes 2476032 | tf_op jit(solution)/shard_map/jit(_where)/select_n | solution.py:121
  32.9 0.6 %slice_subtract_fusion.1 = (f32[8,34,146]{2,1,0:T(8,128)S(1)}, f32[8,34,146]{2,1,0:T(8,128)S(1)}, f32[8,34,146]{2,1,0:T(8,128)S(1)}) fusion(f32[8,36,148]{2,1,0:T(8,128)S(1)} %fusion.54, f32[8,146]{1,0:T(8,128)S(1)} %broadcast_add_fusion.8, f32[146]{0:T(256)S(1)} %get-tuple-element.145, f32[146]{0:T(256)S(1)} %get-tuple-element.143, ...), kind=kLoop, calls=%fused_computation.138 | loop fusion | flops 913376 | bytes 3109248 | tf_op jit(solution)/shard_map/sub | solution.py:158
  33.5 0.1 slice.956
  33.7 0.1 slice.958
  33.8 0.1 slice-done
  34.0 1.3 %collective-permute-start.4 = (f32[8,12,152]{2,1,0:T(8,128)S(1)}, f32[8,12,152]{2,1,0:T(8,128)S(1)}, u32[]{:S(2)}, u32[]{:S(2)}) collective-permute-start(f32[8,12,152]{2,1,0:T(8,128)S(1)} %pad_maximum_fusion.11), channel_id=1, source_target_pairs={{0,8},{8,16},{16,24},{24,0},{1,9},{9,17},{17,25},{25,1},{2,10},{10... | collective-permute-start | bytes 175112 | tf_op jit(solution)/shard_map/ppermute | solution.py:39
  35.3 1.4 %collective-permute-start.5 = (f32[8,12,152]{2,1,0:T(8,128)S(1)}, f32[8,12,152]{2,1,0:T(8,128)S(1)}, u32[]{:S(2)}, u32[]{:S(2)}) collective-permute-start(f32[8,12,152]{2,1,0:T(8,128)S(1)} %pad_maximum_fusion.12), channel_id=1, source_target_pairs={{8,0},{16,8},{24,16},{0,24},{9,1},{17,9},{25,17},{1,25},{10,2},{18... | collective-permute-start | bytes 175112 | tf_op jit(solution)/shard_map/ppermute | solution.py:40
  36.7 0.5 %fusion.87 = f32[8,32,144]{2,1,0:T(8,128)S(1)} fusion(f32[8,34,146]{2,1,0:T(8,128)S(1)} %get-tuple-element.76, f32[8,36,148]{2,1,0:T(8,128)S(1)} %fusion.54, f32[8,144]{1,0:T(8,128)S(1)} %broadcast_add_fusion.7, f32[144]{0:T(256)S(1)} %get-tuple-element.133, f32[144]{0:T(256)S(1)} %get-tuple-element.131, f32[144]{0:T(256)S(1)} %get-tuple-element.130, ...), kind=kLoop, calls=%fused_computation.164 | loop fusion | flops 479232 | bytes 2059776 | tf_op jit(solution)/shard_map/jit(_where)/select_n | solution.py:121
  37.2 2.3 %multiply_reduce_fusion = (f32[8,30,142]{2,1,0:T(8,128)S(1)}, f32[8,30,142]{2,1,0:T(8,128)S(1)}, f32[4,8,30,142]{3,2,1,0:T(8,128)S(1)}) fusion(f32[8,142]{1,0:T(8,128)S(1)} %broadcast_add_fusion.6, f32[4,8,32,144]{3,2,1,0:T(8,128)S(1)} %slice.964, f32[4,8,34,146]{3,2,1,0:T(8,128)S(1)} %get-tuple-element.51, f32[142]{0:T(256)S(1)} %get-tuple-element.129, ...), kind=kLoop, calls=%fused_computation.3 | loop fusion | flops 3203520 | bytes 5094774 | tf_op jit(solution)/shard_map/reduce_sum | solution.py:156
  39.4 0.5 fusion.71
  39.9 0.3 slice.1004
  40.2 0.8 %collective-permute-done.5 = f32[8,12,152]{2,1,0:T(8,128)S(1)} collective-permute-done((f32[8,12,152]{2,1,0:T(8,128)S(1)}, f32[8,12,152]{2,1,0:T(8,128)S(1)}, u32[]{:S(2)}, u32[]{:S(2)}) %collective-permute-start.5) | collective-permute-done | bytes 58400 | tf_op jit(solution)/shard_map/ppermute | solution.py:40
  41.0 0.8 %fusion.102 = (f32[8,28,140]{2,1,0:T(8,128)S(1)}, f32[8,28,140]{2,1,0:T(8,128)S(1)}) fusion(f32[8,6,152]{2,1,0:T(8,128)S(1)} %get-tuple-element.89, f32[8,16,152]{2,1,0:T(8,128)S(1)} %get-tuple-element.82, f32[8,6,152]{2,1,0:T(8,128)S(1)} %get-tuple-element.87, f32[8,6,152]{2,1,0:T(8,128)S(1)} %get-tuple-element.88, ...), kind=kLoop, calls=%fused_computation.187 | loop fusion | flops 627200 | bytes 2621952 | tf_op jit(solution)/shard_map/jit(_where)/select_n | solution.py:121
  41.8 0.5 broadcast_select_fusion.1
  42.3 0.5 %fusion.131 = (f32[8,24,136]{2,1,0:T(8,128)S(1)}, f32[8,24,136]{2,1,0:T(8,128)S(1)}) fusion(f32[8,26,138]{2,1,0:T(8,128)S(1)} %get-tuple-element.33, f32[8,32,144]{2,1,0:T(8,128)S(1)} %fusion.87, f32[8,28,140]{2,1,0:T(8,128)S(1)} %get-tuple-element.38, f32[8,26,138]{2,1,0:T(8,128)S(1)} %get-tuple-element.34, f32[8,136]{1,0:T(8,128)S(1)} %broadcast_add_fusion.3, ...), kind=kLoop, calls=%fused_computation.243 | loop fusion | flops 548352 | bytes 2055680 | tf_op jit(solution)/shard_map/jit(_where)/select_n | solution.py:121
  42.8 0.1 slice.1006
  42.9 0.6 %fusion.188 = (f32[4,8,20,132]{3,2,1,0:T(8,128)S(1)}, f32[4,8,20,132]{3,2,1,0:T(8,128)S(1)}, f32[8,20,132]{2,1,0:T(8,128)S(1)}, f32[8,20,132]{2,1,0:T(8,128)S(1)...) fusion(f32[4,8,34,146]{3,2,1,0:T(8,128)S(1)} %get-tuple-element.51, f32[8,20,132]{2,1,0:T(8,128)S(1)} %slice.1006, ...), kind=kLoop, calls=%fused_computation.454 | loop fusion | flops 1034880 | bytes 2027652 | tf_op jit(solution)/shard_map/slice | solution.py:111
  43.5 0.4 broadcast_select_fusion.3
  43.9 0.5 fusion.120
  44.4 0.1 slice.1023
  44.5 0.1 slice.1024
  44.7 0.1 slice.1028
  44.8 0.1 slice.1029
  44.9 0.1 slice.1026
  45.0 1.7 %fusion.34 = f32[4,8,18,130]{3,2,1,0:T(8,128)S(1)} fusion(f32[4,8,20,132]{3,2,1,0:T(8,128)S(1)} %get-tuple-element.59, f32[4,8,20,132]{3,2,1,0:T(8,128)S(1)} %get-tuple-element.55, f32[4,8,20,132]{3,2,1,0:T(8,128)S(1)} %get-tuple-element.54, f32[8,18,130]{2,1,0:T(8,128)S(1)} %slice.1029, f32[8,18,130]{2,1,0:T(8,128)S(1)} %slice.1028, ...), kind=kLoop, calls=%fused_computation.59 | loop fusion | flops 1722240 | bytes 7585792 | tf_op jit(solution)/shard_map/jit(_where)/select_n | solution.py:121
  46.8 0.2 multiply_reduce_fusion.9
  47.0 0.4 broadcast_select_fusion.2
  47.4 0.1 slice_bitcast_fusion.6
  47.5 0.2 fusion.161
  47.7 0.6 %fusion.93 = f32[4,8,16,128]{3,2,1,0:T(8,128)S(1)} fusion(f32[4,8,18,130]{3,2,1,0:T(8,128)S(1)} %fusion.34, f32[4,8,38,150]{3,2,1,0:T(8,128)S(1)} %get-tuple-element.67, f32[8,128]{1,0:T(8,128)S(1)} %broadcast_add_fusion.11, f32[128]{0:T(128)S(1)} %get-tuple-element.105, f32[128]{0:T(128)S(1)} %get-tuple-element.103, f32[128]{0:T(128)S(1)} %get-tuple-element.102, ...), kind=kLoop, calls=%fused_computation.170 | loop fusion | flops 1638400 | bytes 2955264 | tf_op jit(solution)/shard_map/jit(_where)/select_n | solution.py:121
  48.4 1.7 %collective-permute-start.6 = (f32[6,4,16,128]{3,2,1,0:T(8,128)S(1)}, f32[6,4,16,128]{3,2,1,0:T(8,128)S(1)}, u32[]{:S(2)}, u32[]{:S(2)}) collective-permute-start(f32[6,4,16,128]{3,2,1,0:T(8,128)S(1)} %get-tuple-element.65), channel_id=1, source_target_pairs={{0,1},{1,0},{2,3},{3,2},{4,5},{5,4},{6,7},{7,6},{8,9},{9,8},{10,11... | collective-permute-start | bytes 589832 | tf_op jit(solution)/shard_map/ppermute | solution.py:92
  50.1 1.1 %collective-permute-done.6 = f32[6,4,16,128]{3,2,1,0:T(8,128)S(1)} collective-permute-done((f32[6,4,16,128]{3,2,1,0:T(8,128)S(1)}, f32[6,4,16,128]{3,2,1,0:T(8,128)S(1)}, u32[]{:S(2)}, u32[]{:S(2)}) %collective-permute-start.6) | collective-permute-done | bytes 196640 | tf_op jit(solution)/shard_map/ppermute | solution.py:92
  51.2 0.7 %slice.1047 = f32[4,4,16,256]{3,2,1,0:T(8,128)} slice(f32[6,4,16,256]{3,2,1,0:T(8,128)S(1)} %maximum_select_fusion.1), slice={[2:6], [0:4], [0:16], [0:256]} | slice | bytes 524288 | tf_op jit(solution)/shard_map/slice | solution.py:294
  51.9 0.7 %slice_bitcast_fusion.4 = (f32[4,16,256]{2,1,0:T(8,128)}, f32[4,16,256]{2,1,0:T(8,128)}) fusion(f32[6,4,16,256]{3,2,1,0:T(8,128)S(1)} %maximum_select_fusion.1), kind=kLoop, calls=%fused_computation.312 | loop fusion | bytes 262144 | tf_op jit(solution)/shard_map/squeeze | solution.py:294
  (83 shorter events, 2.0 us)
Async XLA Ops:
  2.4 3.1 %collective-permute-start = (f32[4,4,16,256]{3,2,1,0:T(8,128)S(1)}, f32[4,4,16,256]{3,2,1,0:T(8,128)S(1)}, u32[]{:S(2)}, u32[]{:S(2)}) collective-permute-start(f32[4,4,16,256]{3,2,1,0:T(8,128)S(1)} %pad_maximum_fusion.8), channel_id=1, source_target_pairs={{0,1},{1,0},{2,3},{3,2},{4,5},{5,4},{6,7},{7,6},{8,9},{9,8},{10,11... | collective-permute-start | bytes 786440 | tf_op jit(solution)/shard_map/ppermute | solution.py:55
  6.6 7.7 %collective-permute-start.1 = (f32[4,8,16,12]{3,2,1,0:T(8,128)S(1)}, f32[4,8,16,12]{3,2,1,0:T(8,128)S(1)}, u32[]{:S(2)}, u32[]{:S(2)}) collective-permute-start(f32[4,8,16,12]{3,2,1,0:T(8,128)S(1)} %slice_select_fusion), channel_id=1, source_target_pairs={{1,2},{2,1},{3,4},{4,3},{5,6},{6,5},{9,10},{10,9},{11,12},{12,11},... | collective-permute-start | bytes 73736 | tf_op jit(solution)/shard_map/ppermute | solution.py:80
  14.8 2.6 %copy-start = (f32[4,8,16,152]{3,2,1,0:T(8,128)}, f32[4,8,16,152]{3,2,1,0:T(8,128)S(1)}, u32[]{:S(2)}) copy-start(f32[4,8,16,152]{3,2,1,0:T(8,128)S(1)} %fusion.44) | copy-start | bytes 933892
  14.9 7.4 %collective-permute-start.2 = (f32[8,23,152]{2,1,0:T(8,128)S(1)}, f32[8,23,152]{2,1,0:T(8,128)S(1)}, u32[]{:S(2)}, u32[]{:S(2)}) collective-permute-start(f32[8,23,152]{2,1,0:T(8,128)S(1)} %pad_maximum_fusion.9), channel_id=1, source_target_pairs={{0,8},{8,16},{16,24},{24,0},{1,9},{9,17},{17,25},{25,1},{2,10},{10... | collective-permute-start | bytes 335624 | tf_op jit(solution)/shard_map/ppermute | solution.py:39
  16.2 10.4 %collective-permute-start.3 = (f32[8,23,152]{2,1,0:T(8,128)S(1)}, f32[8,23,152]{2,1,0:T(8,128)S(1)}, u32[]{:S(2)}, u32[]{:S(2)}) collective-permute-start(f32[8,23,152]{2,1,0:T(8,128)S(1)} %pad_maximum_fusion.10), channel_id=1, source_target_pairs={{8,0},{16,8},{24,16},{0,24},{9,1},{17,9},{25,17},{1,25},{10,2},{18... | collective-permute-start | bytes 335624 | tf_op jit(solution)/shard_map/ppermute | solution.py:40
  32.9 1.0 %slice-start = ((f32[4,8,16,152]{3,2,1,0:T(8,128)}), f32[2,8,16,152]{3,2,1,0:T(8,128)S(1)}, s32[]{:S(2)}) async-start(f32[4,8,16,152]{3,2,1,0:T(8,128)} %copy-done), calls=%async_computation | async-start | bytes 524288 | tf_op jit(solution)/shard_map/slice | solution.py:218
  34.0 6.2 %collective-permute-start.4 = (f32[8,12,152]{2,1,0:T(8,128)S(1)}, f32[8,12,152]{2,1,0:T(8,128)S(1)}, u32[]{:S(2)}, u32[]{:S(2)}) collective-permute-start(f32[8,12,152]{2,1,0:T(8,128)S(1)} %pad_maximum_fusion.11), channel_id=1, source_target_pairs={{0,8},{8,16},{16,24},{24,0},{1,9},{9,17},{17,25},{25,1},{2,10},{10... | collective-permute-start | bytes 175112 | tf_op jit(solution)/shard_map/ppermute | solution.py:39
  35.3 5.7 %collective-permute-start.5 = (f32[8,12,152]{2,1,0:T(8,128)S(1)}, f32[8,12,152]{2,1,0:T(8,128)S(1)}, u32[]{:S(2)}, u32[]{:S(2)}) collective-permute-start(f32[8,12,152]{2,1,0:T(8,128)S(1)} %pad_maximum_fusion.12), channel_id=1, source_target_pairs={{8,0},{16,8},{24,16},{0,24},{9,1},{17,9},{25,17},{1,25},{10,2},{18... | collective-permute-start | bytes 175112 | tf_op jit(solution)/shard_map/ppermute | solution.py:40
  48.4 2.8 %collective-permute-start.6 = (f32[6,4,16,128]{3,2,1,0:T(8,128)S(1)}, f32[6,4,16,128]{3,2,1,0:T(8,128)S(1)}, u32[]{:S(2)}, u32[]{:S(2)}) collective-permute-start(f32[6,4,16,128]{3,2,1,0:T(8,128)S(1)} %get-tuple-element.65), channel_id=1, source_target_pairs={{0,1},{1,0},{2,3},{3,2},{4,5},{5,4},{6,7},{7,6},{8,9},{9,8},{10,11... | collective-permute-start | bytes 589832 | tf_op jit(solution)/shard_map/ppermute | solution.py:92

commit v9 on v7

--- a/solution.py
+++ b/solution.py
@@ -136,7 +136,7 @@
 
 
 def radial_mask(width, geometry):
-    rad_start, total_hgt, total_azim, total_rad, cols = geometry
+    rad_start, total_hgt, total_azim, total_rad, cols, weights = geometry
     rad_index = rad_start - width + jnp.arange(cols + 2 * width, dtype=jnp.int32)
     return (rad_index >= 0) & (rad_index < total_rad)
 
@@ -145,28 +145,34 @@
     return jnp.where(radial_mask(width, geometry), x, 0.0)
 
 
-def laplace(x, width, geometry, transpose):
-    rad_start, total_hgt, total_azim, total_rad, cols = geometry
-    margin = width - 1
-    height_rows = x.shape[-3]
-    radius_rows = x.shape[-1] - 2
-    rad_index_all = rad_start - margin - 1 + jnp.arange(radius_rows + 2, dtype=jnp.int32)
+def stencil_weights(rad_start, total_azim, total_rad, cols):
+    rad_index_all = rad_start - HALO - 1 + jnp.arange(cols + 2 * HALO + 2, dtype=jnp.int32)
     radius_all = total_azim / full_turn + rad_index_all.astype(jnp.float32) + 0.5
     rad_index = rad_index_all[1:-1]
     radius = radius_all[1:-1]
     outer_face = (radius + 0.5) * (rad_index < total_rad - 1).astype(jnp.float32)
     inner_face = (radius - 0.5) * (rad_index > 0).astype(jnp.float32)
-    if transpose:
-        outward_weight = outer_face / radius_all[2:]
-        inward_weight = inner_face / radius_all[:-2]
-    else:
-        outward_weight = outer_face / radius
-        inward_weight = inner_face / radius
     arc_length = radius * (full_turn / total_azim)
     arc_weight = 1.0 / (arc_length * arc_length)
+    radial_center = (outer_face + inner_face) / radius
+    forward = (outer_face / radius, inner_face / radius)
+    transposed = (outer_face / radius_all[2:], inner_face / radius_all[:-2])
+    return forward, transposed, arc_weight, radial_center
+
+
+def laplace(x, width, geometry, transpose):
+    rad_start, total_hgt, total_azim, total_rad, cols, weights = geometry
+    forward, transposed, arc_weight, radial_center = weights
+    outward_weight, inward_weight = transposed if transpose else forward
+    height_rows = x.shape[-3]
+    out_cols = x.shape[-1] - 2
+    at = HALO - (width - 1)
+    cut = lambda w: w[at : at + out_cols]
+    outward_weight, inward_weight = cut(outward_weight), cut(inward_weight)
+    arc_weight, radial_center = cut(arc_weight), cut(radial_center)
     hgt_index = jnp.arange(height_rows, dtype=jnp.int32)
     faces = (hgt_index < total_hgt - 1).astype(jnp.float32) + (hgt_index > 0).astype(jnp.float32)
-    center_weight = (outer_face + inner_face) / radius + 2.0 * arc_weight + faces[:, None, None]
+    center_weight = radial_center + 2.0 * arc_weight + faces[:, None, None]
     leading = x.ndim - 3
     padded = jnp.pad(x, [(0, 0)] * leading + [(1, 1), (0, 0), (0, 0)])
     center = padded[..., 1:-1, 1:-1, 1:-1]
@@ -224,12 +230,16 @@
     height_rows, azim_rows, radius_rows = density.shape
     total_hgt = height_rows * lax.axis_size("hgt")
     part = radius_rows // lax.axis_size("hgt")
+    rad_start = lax.axis_index("rad") * radius_rows + lax.axis_index("hgt") * part
+    total_azim = azim_rows * lax.axis_size("azim")
+    total_rad = radius_rows * lax.axis_size("rad")
     geometry = (
-        lax.axis_index("rad") * radius_rows + lax.axis_index("hgt") * part,
+        rad_start,
         total_hgt,
-        azim_rows * lax.axis_size("azim"),
-        radius_rows * lax.axis_size("rad"),
+        total_azim,
+        total_rad,
         part,
+        stencil_weights(rad_start, total_azim, total_rad, part),
     )
     packed = jnp.stack([density, labels.astype(jnp.float32), observed, measured.astype(jnp.float32)])
     if lax.axis_size("hgt") == 2:

time: 51.1 us -> 52.6 us (1.029)
  local copies, waits for them, and re-layouts: 4.41 us -> 6.13 us
  waiting for transfers between devices: 10.8 us -> 11.8 us
  starting transfers between devices: 14.5 us -> 13.7 us
    slice x0 -> x24, local copies, waits for them, and re-layouts: none -> 1.72 us  [laplace(): cut = lambda w: w[at:at + out_cols]]
    slice x0 -> x12, other arithmetic: none -> 0.88 us  [laplace(): cut = lambda w: w[at:at + out_cols]]
    div x12 -> x1, other arithmetic: 0.93 us -> 0.08 us  [stencil_weights(): transposed = (outer_face / radius_all[2:], inner_face / radius_all[:-2])]
    ppermute x1, starting transfers between devices: 2.04 us -> 1.29 us  [scatter_heights(): lax.ppermute(piece, 'hgt', [(i, (i + shift) % peers) for i in range(peers)])]
    ppermute x2, waiting for transfers between devices: 4.52 us -> 5.24 us  [azim_exchange(): before = lax.ppermute(last, 'azim', up)]
    ppermute x2, waiting for transfers between devices: 4.85 us -> 5.48 us  [azim_exchange(): after = lax.ppermute(leading, 'azim', down)]
  transfers between devices with their start and end apart: 8 -> 8, of which waited for: 5 -> 4; matrix products, arithmetic and copies ran while one was open for 11% -> 14% of each run, Pallas kernels for 0% -> 0%
where the time goes in v9:
time: 52.6 us; the launch traced here: 52.3 us
  other arithmetic  19.5 us (37%)
  starting transfers between devices  13.7 us (26%)
  waiting for transfers between devices  11.8 us (22%)
  local copies, waits for them, and re-layouts  6.13 us (12%)
  between operations  1.21 us (2%)
    select_n x11, other arithmetic, in_domain(): return jnp.where(radial_mask(width, geometry), x, 0.0)  6.48 us
    ppermute x2, waiting for transfers between devices, azim_exchange(): after = lax.ppermute(leading, 'azim', down)  5.48 us
    ppermute x2, waiting for transfers between devices, azim_exchange(): before = lax.ppermute(last, 'azim', up)  5.24 us
    ppermute x1, starting transfers between devices, edge_columns(): lax.ppermute(jnp.where(own == 0, first, last), ('rad', 'hgt'), cross)  4.68 us
    reduce_sum x2, other arithmetic, chemical(): cube_sum = jnp.sum(grains * grains * grains, axis=0)  3.16 us
    slice x15, local copies, waits for them, and re-layouts, crop(): return x[..., cut:x.shape[-2] - cut, cut:x.shape[-1] - cut]  2.63 us
    ppermute x2, starting transfers between devices, azim_exchange(): after = lax.ppermute(leading, 'azim', down)  2.59 us
    ppermute x2, starting transfers between devices, azim_exchange(): before = lax.ppermute(last, 'azim', up)  2.53 us
  transfers between devices with their start and end apart: 8, of which 4 were waited for; matrix products, arithmetic and copies ran while one was open for 14% of the time, Pallas kernels for 0%

profile of v9, /device:TPU:9, one launch (start us, length us, event | category | flops | bytes accessed | tf_op | source)
XLA Modules:
  0.0 52.3 jit_solution(1884128266488027880)
XLA Ops:
  0.7 0.9 %convert_bitcast_fusion = (f32[1,4,16,256]{3,2,1,0:T(8,128)S(1)}, f32[1,4,16,256]{3,2,1,0:T(8,128)S(1)}) fusion(s32[4,16,256]{2,1,0:T(8,128)} %param.7, s32[4,16,256]{2,1,0:T(8,128)} %param.5), kind=kLoop, calls=%fused_computation.325 | loop fusion | flops 32768 | bytes 262144 | tf_op jit(solution)/shard_map/stack | solution.py:244
  1.6 0.9 %pad_maximum_fusion.8 = f32[4,4,16,256]{3,2,1,0:T(8,128)S(1)} fusion(f32[1,4,16,256]{3,2,1,0:T(8,128)S(1)} %get-tuple-element.106, f32[1,4,16,256]{3,2,1,0:T(8,128)} %bitcast.22, f32[1,4,16,256]{3,2,1,0:T(8,128)S(1)} %get-tuple-element.107, f32[1,4,16,256]{3,2,1,0:T(8,128)} %bitcast.24), kind=kLoop, calls=%fused_computation.211 | loop fusion | flops 196608 | bytes 524288 | tf_op jit(solution)/shard_map/stack | solution.py:244
  2.5 0.7 %collective-permute-start.2 = (f32[4,4,16,256]{3,2,1,0:T(8,128)S(1)}, f32[4,4,16,256]{3,2,1,0:T(8,128)S(1)}, u32[]{:S(2)}, u32[]{:S(2)}) collective-permute-start(f32[4,4,16,256]{3,2,1,0:T(8,128)S(1)} %pad_maximum_fusion.8), channel_id=1, source_target_pairs={{0,1},{1,0},{2,3},{3,2},{4,5},{5,4},{6,7},{7,6},{8,9},{9,8},{10,11... | collective-permute-start | bytes 786440 | tf_op jit(solution)/shard_map/ppermute | solution.py:55
  3.2 0.1 slice_select_fusion.1
  3.3 1.9 %collective-permute-start = (f32[4,4,16,12]{3,2,1,0:T(8,128)S(1)}, f32[4,4,16,12]{3,2,1,0:T(8,128)S(1)}, u32[]{:S(2)}, u32[]{:S(2)}) collective-permute-start(f32[4,4,16,12]{3,2,1,0:T(8,128)S(1)} %get-tuple-element.60), channel_id=1, source_target_pairs={{0,2},{3,1},{2,4},{5,3},{4,6},{7,5},{8,10},{11,9},{10,12},{13,11},... | collective-permute-start | bytes 36872 | tf_op jit(solution)/shard_map/ppermute | solution.py:94
  5.2 4.7 %collective-permute-start.1 = (f32[4,4,16,12]{3,2,1,0:T(8,128)S(1)}, f32[4,4,16,12]{3,2,1,0:T(8,128)S(1)}, u32[]{:S(2)}, u32[]{:S(2)}) collective-permute-start(f32[4,4,16,12]{3,2,1,0:T(8,128)S(1)} %get-tuple-element.61), channel_id=1, source_target_pairs={{1,2},{2,1},{3,4},{4,3},{5,6},{6,5},{9,10},{10,9},{11,12},{12,11},... | collective-permute-start | bytes 36872 | tf_op jit(solution)/shard_map/ppermute | solution.py:93
  10.0 0.1 slice_divide_fusion.1
  10.1 0.1 fusion.193
  10.1 0.1 fusion.192
  10.2 0.1 fusion.194
  10.3 0.1 fusion.190
  10.4 0.1 fusion.191
  10.4 0.1 fusion.189
  10.5 0.1 fusion.188
  13.8 0.4 fusion.44
  14.3 1.3 %collective-permute-start.3 = (f32[8,23,152]{2,1,0:T(8,128)S(1)}, f32[8,23,152]{2,1,0:T(8,128)S(1)}, u32[]{:S(2)}, u32[]{:S(2)}) collective-permute-start(f32[8,23,152]{2,1,0:T(8,128)S(1)} %pad_maximum_fusion.9), channel_id=1, source_target_pairs={{0,8},{8,16},{16,24},{24,0},{1,9},{9,17},{17,25},{25,1},{2,10},{10... | collective-permute-start | bytes 335624 | tf_op jit(solution)/shard_map/ppermute | solution.py:39
  15.6 1.2 %collective-permute-start.4 = (f32[8,23,152]{2,1,0:T(8,128)S(1)}, f32[8,23,152]{2,1,0:T(8,128)S(1)}, u32[]{:S(2)}, u32[]{:S(2)}) collective-permute-start(f32[8,23,152]{2,1,0:T(8,128)S(1)} %pad_maximum_fusion.10), channel_id=1, source_target_pairs={{8,0},{16,8},{24,16},{0,24},{9,1},{17,9},{25,17},{1,25},{10,2},{18... | collective-permute-start | bytes 335624 | tf_op jit(solution)/shard_map/ppermute | solution.py:40
  16.8 5.2 %collective-permute-done.3 = f32[8,23,152]{2,1,0:T(8,128)S(1)} collective-permute-done((f32[8,23,152]{2,1,0:T(8,128)S(1)}, f32[8,23,152]{2,1,0:T(8,128)S(1)}, u32[]{:S(2)}, u32[]{:S(2)}) %collective-permute-start.3) | collective-permute-done | bytes 111904 | tf_op jit(solution)/shard_map/ppermute | solution.py:39
  22.1 4.3 %collective-permute-done.4 = f32[8,23,152]{2,1,0:T(8,128)S(1)} collective-permute-done((f32[8,23,152]{2,1,0:T(8,128)S(1)}, f32[8,23,152]{2,1,0:T(8,128)S(1)}, u32[]{:S(2)}, u32[]{:S(2)}) %collective-permute-start.4) | collective-permute-done | bytes 111904 | tf_op jit(solution)/shard_map/ppermute | solution.py:40
  26.4 0.2 pad_maximum_fusion.1
  26.6 0.4 multiply_reduce_fusion.2
  27.0 0.2 slice.1005
  27.2 0.6 %fusion.48 = (f32[8,38,150]{2,1,0:T(8,128)S(1)}, f32[8,38,150]{2,1,0:T(8,128)S(1)}, f32[8,38,150]{2,1,0:T(8,128)S(1)}) fusion(f32[8,40,152]{2,1,0:T(8,128)S(1)} %broadcast_select_fusion, f32[8,38,150]{2,1,0:T(8,128)S(1)} %get-tuple-element.17, f32[8,38,150]{2,1,0:T(8,128)S(1)} %get-tuple-element.18, f32[8,150]{1,0:T(8,128)S(1)} %broadcast_add_fusion.10, ...), kind=kLoop, calls=%fused_computation.104 | loop fusion | flops 1048800 | bytes 3179904 | tf_op jit(solution)/shard_map/sub | solution.py:274
  27.8 0.2 slice.1002
  28.0 0.2 slice.1004
  28.1 0.4 slice.1010
  28.6 2.8 %multiply_reduce_fusion.1 = (f32[8,34,146]{2,1,0:T(8,128)S(1)}, f32[8,34,146]{2,1,0:T(8,128)S(1)}, f32[4,8,34,146]{3,2,1,0:T(8,128)S(1)}) fusion(f32[8,146]{1,0:T(8,128)S(1)} %broadcast_add_fusion.8, f32[4,8,36,148]{3,2,1,0:T(8,128)S(1)} %slice.1010, f32[4,8,38,150]{3,2,1,0:T(8,128)S(1)} %get-tuple-element.43, f32[146]{0:T(256)S(1)} %get-tuple-element.104, ...), kind=kLoop, calls=%fused_computation.23 | loop fusion | flops 3732928 | bytes 5930538 | tf_op jit(solution)/shard_map/reduce_sum | solution.py:187
  31.3 0.2 mul.1094
  31.5 0.4 slice.1032
  31.9 0.1 slice.1027
  32.0 0.6 %fusion.54 = f32[8,36,148]{2,1,0:T(8,128)S(1)} fusion(f32[8,38,150]{2,1,0:T(8,128)S(1)} %get-tuple-element.53, f32[8,40,152]{2,1,0:T(8,128)S(1)} %broadcast_select_fusion, f32[8,148]{1,0:T(8,128)S(1)} %broadcast_add_fusion.9, f32[148]{0:T(256)S(1)} %get-tuple-element.100, f32[148]{0:T(256)S(1)} %slice.789, f32[148]{0:T(256)S(1)} %slice.773, ...), kind=kLoop, calls=%fused_computation.110 | loop fusion | flops 554112 | bytes 2476032 | tf_op jit(solution)/shard_map/jit(_where)/select_n | solution.py:145
  32.7 0.6 %slice_subtract_fusion.1 = (f32[8,34,146]{2,1,0:T(8,128)S(1)}, f32[8,34,146]{2,1,0:T(8,128)S(1)}, f32[8,34,146]{2,1,0:T(8,128)S(1)}) fusion(f32[8,36,148]{2,1,0:T(8,128)S(1)} %fusion.54, f32[8,146]{1,0:T(8,128)S(1)} %broadcast_add_fusion.8, f32[146]{0:T(256)S(1)} %get-tuple-element.104, f32[146]{0:T(256)S(1)} %slice.805, f32[146]{0:T(256)S(1)} %slice.803, ...), kind=kLoop, calls=%fused_computation.138 | loop fusion | flops 913376 | bytes 3109248 | tf_op jit(solution)/shard_map/sub | solution.py:188
  33.3 0.1 slice.1024
  33.4 0.1 slice.1026
  33.5 0.1 slice-done
  33.7 1.3 %collective-permute-start.5 = (f32[8,12,152]{2,1,0:T(8,128)S(1)}, f32[8,12,152]{2,1,0:T(8,128)S(1)}, u32[]{:S(2)}, u32[]{:S(2)}) collective-permute-start(f32[8,12,152]{2,1,0:T(8,128)S(1)} %pad_maximum_fusion.11), channel_id=1, source_target_pairs={{0,8},{8,16},{16,24},{24,0},{1,9},{9,17},{17,25},{25,1},{2,10},{10... | collective-permute-start | bytes 175112 | tf_op jit(solution)/shard_map/ppermute | solution.py:39
  35.0 1.4 %collective-permute-start.6 = (f32[8,12,152]{2,1,0:T(8,128)S(1)}, f32[8,12,152]{2,1,0:T(8,128)S(1)}, u32[]{:S(2)}, u32[]{:S(2)}) collective-permute-start(f32[8,12,152]{2,1,0:T(8,128)S(1)} %pad_maximum_fusion.12), channel_id=1, source_target_pairs={{8,0},{16,8},{24,16},{0,24},{9,1},{17,9},{25,17},{1,25},{10,2},{18... | collective-permute-start | bytes 175112 | tf_op jit(solution)/shard_map/ppermute | solution.py:40
  36.4 0.5 %fusion.87 = f32[8,32,144]{2,1,0:T(8,128)S(1)} fusion(f32[8,34,146]{2,1,0:T(8,128)S(1)} %get-tuple-element.52, f32[8,36,148]{2,1,0:T(8,128)S(1)} %fusion.54, f32[8,144]{1,0:T(8,128)S(1)} %broadcast_add_fusion.7, f32[144]{0:T(256)S(1)} %get-tuple-element.98, f32[144]{0:T(256)S(1)} %slice.821, f32[144]{0:T(256)S(1)} %slice.799, ...), kind=kLoop, calls=%fused_computation.164 | loop fusion | flops 479232 | bytes 2059776 | tf_op jit(solution)/shard_map/jit(_where)/select_n | solution.py:145
  36.9 2.2 %multiply_reduce_fusion = (f32[8,30,142]{2,1,0:T(8,128)S(1)}, f32[8,30,142]{2,1,0:T(8,128)S(1)}, f32[4,8,30,142]{3,2,1,0:T(8,128)S(1)}) fusion(f32[8,142]{1,0:T(8,128)S(1)} %broadcast_add_fusion.6, f32[4,8,32,144]{3,2,1,0:T(8,128)S(1)} %slice.1032, f32[4,8,34,146]{3,2,1,0:T(8,128)S(1)} %get-tuple-element.29, f32[142]{0:T(256)S(1)} %get-tuple-element.96, ...), kind=kLoop, calls=%fused_computation.3 | loop fusion | flops 3203520 | bytes 5094774 | tf_op jit(solution)/shard_map/reduce_sum | solution.py:186
  39.2 0.5 fusion.71
  39.7 0.3 slice.1072
  40.0 1.2 %collective-permute-done.6 = f32[8,12,152]{2,1,0:T(8,128)S(1)} collective-permute-done((f32[8,12,152]{2,1,0:T(8,128)S(1)}, f32[8,12,152]{2,1,0:T(8,128)S(1)}, u32[]{:S(2)}, u32[]{:S(2)}) %collective-permute-start.6) | collective-permute-done | bytes 58400 | tf_op jit(solution)/shard_map/ppermute | solution.py:40
  41.2 0.8 %fusion.102 = (f32[8,28,140]{2,1,0:T(8,128)S(1)}, f32[8,28,140]{2,1,0:T(8,128)S(1)}) fusion(f32[8,6,152]{2,1,0:T(8,128)S(1)} %get-tuple-element.67, f32[8,16,152]{2,1,0:T(8,128)S(1)} %get-tuple-element.58, f32[8,6,152]{2,1,0:T(8,128)S(1)} %get-tuple-element.65, f32[8,6,152]{2,1,0:T(8,128)S(1)} %get-tuple-element.66, ...), kind=kLoop, calls=%fused_computation.187 | loop fusion | flops 627200 | bytes 2621952 | tf_op jit(solution)/shard_map/jit(_where)/select_n | solution.py:145
  42.0 0.5 broadcast_select_fusion.1
  42.4 0.5 %fusion.131 = (f32[8,24,136]{2,1,0:T(8,128)S(1)}, f32[8,24,136]{2,1,0:T(8,128)S(1)}) fusion(f32[8,26,138]{2,1,0:T(8,128)S(1)} %get-tuple-element.23, f32[8,32,144]{2,1,0:T(8,128)S(1)} %fusion.87, f32[8,28,140]{2,1,0:T(8,128)S(1)} %get-tuple-element.26, f32[8,26,138]{2,1,0:T(8,128)S(1)} %get-tuple-element.24, f32[8,136]{1,0:T(8,128)S(1)} %broadcast_add_fusion.3, ...), kind=kLoop, calls=%fused_computation.243 | loop fusion | flops 548352 | bytes 2055680 | tf_op jit(solution)/shard_map/jit(_where)/select_n | solution.py:145
  43.0 0.1 slice.1074
  43.1 0.6 %fusion.176 = (f32[4,8,20,132]{3,2,1,0:T(8,128)S(1)}, f32[4,8,20,132]{3,2,1,0:T(8,128)S(1)}, f32[8,20,132]{2,1,0:T(8,128)S(1)}, f32[8,20,132]{2,1,0:T(8,128)S(1)...) fusion(f32[4,8,34,146]{3,2,1,0:T(8,128)S(1)} %get-tuple-element.29, f32[8,20,132]{2,1,0:T(8,128)S(1)} %slice.1074, ...), kind=kLoop, calls=%fused_computation.382 | loop fusion | flops 1034880 | bytes 2027652 | tf_op jit(solution)/shard_map/slice | solution.py:135
  43.7 0.4 broadcast_select_fusion.3
  44.1 0.5 %fusion.120 = (f32[8,20,132]{2,1,0:T(8,128)S(1)}, f32[8,20,132]{2,1,0:T(8,128)S(1)}, f32[8,20,132]{2,1,0:T(8,128)S(1)}, f32[8,20,132]{2,1,0:T(8,128)S(1)}) fusion(f32[8,22,134]{2,1,0:T(8,128)S(1)} %get-tuple-element.21, f32[8,20,132]{2,1,0:T(8,128)S(1)} %get-tuple-element.34, f32[8,24,136]{2,1,0:T(8,128)S(1)} %get-tuple-element.56, ...), kind=kLoop, calls=%fused_computation.232 | loop fusion | flops 528000 | bytes 2315776 | tf_op jit(solution)/shard_map/jit(_where)/select_n | solution.py:145
  44.6 0.1 slice.1091
  44.7 0.1 slice.1092
  44.8 0.1 slice.1096
  45.0 0.1 slice.1097
  45.1 0.1 slice.1094
  45.2 1.7 %fusion.34 = f32[4,8,18,130]{3,2,1,0:T(8,128)S(1)} fusion(f32[4,8,20,132]{3,2,1,0:T(8,128)S(1)} %get-tuple-element.35, f32[4,8,20,132]{3,2,1,0:T(8,128)S(1)} %get-tuple-element.31, f32[4,8,20,132]{3,2,1,0:T(8,128)S(1)} %get-tuple-element.30, f32[8,18,130]{2,1,0:T(8,128)S(1)} %slice.1097, f32[8,18,130]{2,1,0:T(8,128)S(1)} %slice.1096, ...), kind=kLoop, calls=%fused_computation.59 | loop fusion | flops 1722240 | bytes 7585792 | tf_op jit(solution)/shard_map/jit(_where)/select_n | solution.py:145
  47.0 0.2 multiply_reduce_fusion.9
  47.2 0.4 broadcast_select_fusion.2
  47.6 0.1 slice_bitcast_fusion.6
  47.7 0.2 fusion.161
  47.9 0.6 %fusion.93 = f32[4,8,16,128]{3,2,1,0:T(8,128)S(1)} fusion(f32[4,8,18,130]{3,2,1,0:T(8,128)S(1)} %fusion.34, f32[4,8,38,150]{3,2,1,0:T(8,128)S(1)} %get-tuple-element.43, f32[8,128]{1,0:T(8,128)S(1)} %broadcast_add_fusion.11, f32[128]{0:T(128)S(1)} %get-tuple-element.83, f32[128]{0:T(128)S(1)} %slice.956, f32[128]{0:T(128)S(1)} %slice.954, ...), kind=kLoop, calls=%fused_computation.170 | loop fusion | flops 1638400 | bytes 2955264 | tf_op jit(solution)/shard_map/jit(_where)/select_n | solution.py:145
  48.6 1.3 %collective-permute-start.7 = (f32[6,4,16,128]{3,2,1,0:T(8,128)S(1)}, f32[6,4,16,128]{3,2,1,0:T(8,128)S(1)}, u32[]{:S(2)}, u32[]{:S(2)}) collective-permute-start(f32[6,4,16,128]{3,2,1,0:T(8,128)S(1)} %get-tuple-element.41), channel_id=1, source_target_pairs={{0,1},{1,0},{2,3},{3,2},{4,5},{5,4},{6,7},{7,6},{8,9},{9,8},{10,11... | collective-permute-start | bytes 589832 | tf_op jit(solution)/shard_map/ppermute | solution.py:116
  49.9 1.1 %collective-permute-done.7 = f32[6,4,16,128]{3,2,1,0:T(8,128)S(1)} collective-permute-done((f32[6,4,16,128]{3,2,1,0:T(8,128)S(1)}, f32[6,4,16,128]{3,2,1,0:T(8,128)S(1)}, u32[]{:S(2)}, u32[]{:S(2)}) %collective-permute-start.7) | collective-permute-done | bytes 196640 | tf_op jit(solution)/shard_map/ppermute | solution.py:116
  51.0 0.7 %slice.1115 = f32[4,4,16,256]{3,2,1,0:T(8,128)} slice(f32[6,4,16,256]{3,2,1,0:T(8,128)S(1)} %maximum_select_fusion.1), slice={[2:6], [0:4], [0:16], [0:256]} | slice | bytes 524288 | tf_op jit(solution)/shard_map/slice | solution.py:332
  51.7 0.7 %slice_bitcast_fusion.4 = (f32[4,16,256]{2,1,0:T(8,128)}, f32[4,16,256]{2,1,0:T(8,128)}) fusion(f32[6,4,16,256]{3,2,1,0:T(8,128)S(1)} %maximum_select_fusion.1), kind=kLoop, calls=%fused_computation.314 | loop fusion | bytes 262144 | tf_op jit(solution)/shard_map/squeeze | solution.py:332
  (93 shorter events, 3.6 us)
Async XLA Ops:
  0.6 13.1 %copy-start.2 = (f32[4,16,256]{2,1,0:T(8,128)S(1)}, f32[4,16,256]{2,1,0:T(8,128)}, u32[]{:S(2)}) copy-start(f32[4,16,256]{2,1,0:T(8,128)} %param.4) | copy-start | bytes 196612
  0.6 13.1 %copy-start.1 = (f32[4,16,256]{2,1,0:T(8,128)S(1)}, f32[4,16,256]{2,1,0:T(8,128)}, u32[]{:S(2)}) copy-start(f32[4,16,256]{2,1,0:T(8,128)} %param.6) | copy-start | bytes 196612
  2.5 11.2 %collective-permute-start.2 = (f32[4,4,16,256]{3,2,1,0:T(8,128)S(1)}, f32[4,4,16,256]{3,2,1,0:T(8,128)S(1)}, u32[]{:S(2)}, u32[]{:S(2)}) collective-permute-start(f32[4,4,16,256]{3,2,1,0:T(8,128)S(1)} %pad_maximum_fusion.8), channel_id=1, source_target_pairs={{0,1},{1,0},{2,3},{3,2},{4,5},{5,4},{6,7},{7,6},{8,9},{9,8},{10,11... | collective-permute-start | bytes 786440 | tf_op jit(solution)/shard_map/ppermute | solution.py:55
  3.3 10.3 %collective-permute-start = (f32[4,4,16,12]{3,2,1,0:T(8,128)S(1)}, f32[4,4,16,12]{3,2,1,0:T(8,128)S(1)}, u32[]{:S(2)}, u32[]{:S(2)}) collective-permute-start(f32[4,4,16,12]{3,2,1,0:T(8,128)S(1)} %get-tuple-element.60), channel_id=1, source_target_pairs={{0,2},{3,1},{2,4},{5,3},{4,6},{7,5},{8,10},{11,9},{10,12},{13,11},... | collective-permute-start | bytes 36872 | tf_op jit(solution)/shard_map/ppermute | solution.py:94
  5.2 8.4 %collective-permute-start.1 = (f32[4,4,16,12]{3,2,1,0:T(8,128)S(1)}, f32[4,4,16,12]{3,2,1,0:T(8,128)S(1)}, u32[]{:S(2)}, u32[]{:S(2)}) collective-permute-start(f32[4,4,16,12]{3,2,1,0:T(8,128)S(1)} %get-tuple-element.61), channel_id=1, source_target_pairs={{1,2},{2,1},{3,4},{4,3},{5,6},{6,5},{9,10},{10,9},{11,12},{12,11},... | collective-permute-start | bytes 36872 | tf_op jit(solution)/shard_map/ppermute | solution.py:93
  14.2 2.6 %copy-start = (f32[4,8,16,152]{3,2,1,0:T(8,128)}, f32[4,8,16,152]{3,2,1,0:T(8,128)S(1)}, u32[]{:S(2)}) copy-start(f32[4,8,16,152]{3,2,1,0:T(8,128)S(1)} %fusion.44) | copy-start | bytes 933892
  14.3 7.7 %collective-permute-start.3 = (f32[8,23,152]{2,1,0:T(8,128)S(1)}, f32[8,23,152]{2,1,0:T(8,128)S(1)}, u32[]{:S(2)}, u32[]{:S(2)}) collective-permute-start(f32[8,23,152]{2,1,0:T(8,128)S(1)} %pad_maximum_fusion.9), channel_id=1, source_target_pairs={{0,8},{8,16},{16,24},{24,0},{1,9},{9,17},{17,25},{25,1},{2,10},{10... | collective-permute-start | bytes 335624 | tf_op jit(solution)/shard_map/ppermute | solution.py:39
  15.6 10.7 %collective-permute-start.4 = (f32[8,23,152]{2,1,0:T(8,128)S(1)}, f32[8,23,152]{2,1,0:T(8,128)S(1)}, u32[]{:S(2)}, u32[]{:S(2)}) collective-permute-start(f32[8,23,152]{2,1,0:T(8,128)S(1)} %pad_maximum_fusion.10), channel_id=1, source_target_pairs={{8,0},{16,8},{24,16},{0,24},{9,1},{17,9},{25,17},{1,25},{10,2},{18... | collective-permute-start | bytes 335624 | tf_op jit(solution)/shard_map/ppermute | solution.py:40
  32.7 1.0 %slice-start = ((f32[4,8,16,152]{3,2,1,0:T(8,128)}), f32[2,8,16,152]{3,2,1,0:T(8,128)S(1)}, s32[]{:S(2)}) async-start(f32[4,8,16,152]{3,2,1,0:T(8,128)} %copy-done), calls=%async_computation | async-start | bytes 524288 | tf_op jit(solution)/shard_map/slice | solution.py:256
  33.7 6.2 %collective-permute-start.5 = (f32[8,12,152]{2,1,0:T(8,128)S(1)}, f32[8,12,152]{2,1,0:T(8,128)S(1)}, u32[]{:S(2)}, u32[]{:S(2)}) collective-permute-start(f32[8,12,152]{2,1,0:T(8,128)S(1)} %pad_maximum_fusion.11), channel_id=1, source_target_pairs={{0,8},{8,16},{16,24},{24,0},{1,9},{9,17},{17,25},{25,1},{2,10},{10... | collective-permute-start | bytes 175112 | tf_op jit(solution)/shard_map/ppermute | solution.py:39
  35.0 6.2 %collective-permute-start.6 = (f32[8,12,152]{2,1,0:T(8,128)S(1)}, f32[8,12,152]{2,1,0:T(8,128)S(1)}, u32[]{:S(2)}, u32[]{:S(2)}) collective-permute-start(f32[8,12,152]{2,1,0:T(8,128)S(1)} %pad_maximum_fusion.12), channel_id=1, source_target_pairs={{8,0},{16,8},{24,16},{0,24},{9,1},{17,9},{25,17},{1,25},{10,2},{18... | collective-permute-start | bytes 175112 | tf_op jit(solution)/shard_map/ppermute | solution.py:40
  48.6 2.4 %collective-permute-start.7 = (f32[6,4,16,128]{3,2,1,0:T(8,128)S(1)}, f32[6,4,16,128]{3,2,1,0:T(8,128)S(1)}, u32[]{:S(2)}, u32[]{:S(2)}) collective-permute-start(f32[6,4,16,128]{3,2,1,0:T(8,128)S(1)} %get-tuple-element.41), channel_id=1, source_target_pairs={{0,1},{1,0},{2,3},{3,2},{4,5},{5,4},{6,7},{7,6},{8,9},{9,8},{10,11... | collective-permute-start | bytes 589832 | tf_op jit(solution)/shard_map/ppermute | solution.py:116

commit v10 on v7

--- a/solution.py
+++ b/solution.py
@@ -243,7 +243,7 @@
     density, grain_label = [
         trim(f, w) for f, w in zip(azim_exchange([packed[0], packed[1]], widths[:2]), widths[:2])
     ]
-    misfit_terms, density = lax.optimization_barrier((packed[2:], density))
+    misfit_terms = packed[2:]
     observed, measured = [
         trim(f, w) for f, w in zip(azim_exchange([misfit_terms[0], misfit_terms[1]], widths[2:]), widths[2:])
     ]

time: 51.1 us -> 52.7 us (1.031)
  waiting for transfers between devices: 10.8 us -> 13.3 us
  starting transfers between devices: 14.5 us -> 13.6 us
    ppermute x2, waiting for transfers between devices: 4.52 us -> 8.99 us  [azim_exchange(): before = lax.ppermute(last, 'azim', up)]
    ppermute x2, waiting for transfers between devices: 4.85 us -> 2.85 us  [azim_exchange(): after = lax.ppermute(leading, 'azim', down)]
    ppermute x2, starting transfers between devices: 2.53 us -> 1.63 us  [azim_exchange(): before = lax.ppermute(last, 'azim', up)]
    ppermute x1, starting transfers between devices: 2.04 us -> 1.31 us  [scatter_heights(): lax.ppermute(piece, 'hgt', [(i, (i + shift) % peers) for i in range(peers)])]
    ppermute x2, starting transfers between devices: 2.59 us -> 3.31 us  [azim_exchange(): after = lax.ppermute(leading, 'azim', down)]
  transfers between devices with their start and end apart: 8 -> 8, of which waited for: 5 -> 4; matrix products, arithmetic and copies ran while one was open for 11% -> 4% of each run, Pallas kernels for 0% -> 0%
where the time goes in v10:
time: 52.7 us; the launch traced here: 52.5 us
  other arithmetic  19.6 us (37%)
  starting transfers between devices  13.6 us (26%)
  waiting for transfers between devices  13.3 us (25%)
  local copies, waits for them, and re-layouts  4.49 us (9%)
  between operations  1.47 us (3%)
    ppermute x2, waiting for transfers between devices, azim_exchange(): before = lax.ppermute(last, 'azim', up)  8.99 us
    select_n x11, other arithmetic, in_domain(): return jnp.where(radial_mask(width, geometry), x, 0.0)  6.54 us
    ppermute x1, starting transfers between devices, edge_columns(): lax.ppermute(jnp.where(own == 0, first, last), ('rad', 'hgt'), cross)  4.68 us
    ppermute x2, starting transfers between devices, azim_exchange(): after = lax.ppermute(leading, 'azim', down)  3.31 us
    reduce_sum x2, other arithmetic, chemical(): cube_sum = jnp.sum(grains * grains * grains, axis=0)  3.17 us
    ppermute x2, waiting for transfers between devices, azim_exchange(): after = lax.ppermute(leading, 'azim', down)  2.85 us
    slice x15, local copies, waits for them, and re-layouts, crop(): return x[..., cut:x.shape[-2] - cut, cut:x.shape[-1] - cut]  2.81 us
    reduce_sum x1, other arithmetic, chemical(): square_sum = jnp.sum(grains * grains, axis=0)  2.25 us
  transfers between devices with their start and end apart: 8, of which 4 were waited for; matrix products, arithmetic and copies ran while one was open for 4% of the time, Pallas kernels for 0%

profile of v10, /device:TPU:9, one launch (start us, length us, event | category | flops | bytes accessed | tf_op | source)
XLA Modules:
  0.0 52.5 jit_solution(6401471993669019509)
XLA Ops:
  0.7 0.9 %convert_bitcast_fusion = (f32[1,4,16,256]{3,2,1,0:T(8,128)S(1)}, f32[1,4,16,256]{3,2,1,0:T(8,128)S(1)}) fusion(s32[4,16,256]{2,1,0:T(8,128)} %param.7, s32[4,16,256]{2,1,0:T(8,128)} %param.5), kind=kLoop, calls=%fused_computation.324 | loop fusion | flops 32768 | bytes 262144 | tf_op jit(solution)/shard_map/stack | solution.py:234
  1.6 0.9 %pad_maximum_fusion.7 = f32[4,4,16,256]{3,2,1,0:T(8,128)S(1)} fusion(f32[1,4,16,256]{3,2,1,0:T(8,128)S(1)} %get-tuple-element.144, f32[1,4,16,256]{3,2,1,0:T(8,128)} %bitcast.22, f32[1,4,16,256]{3,2,1,0:T(8,128)S(1)} %get-tuple-element.145, f32[1,4,16,256]{3,2,1,0:T(8,128)} %bitcast.24), kind=kLoop, calls=%fused_computation.211 | loop fusion | flops 196608 | bytes 524288 | tf_op jit(solution)/shard_map/stack | solution.py:234
  2.5 0.7 %collective-permute-start.2 = (f32[4,4,16,256]{3,2,1,0:T(8,128)S(1)}, f32[4,4,16,256]{3,2,1,0:T(8,128)S(1)}, u32[]{:S(2)}, u32[]{:S(2)}) collective-permute-start(f32[4,4,16,256]{3,2,1,0:T(8,128)S(1)} %pad_maximum_fusion.7), channel_id=1, source_target_pairs={{0,1},{1,0},{2,3},{3,2},{4,5},{5,4},{6,7},{7,6},{8,9},{9,8},{10,11... | collective-permute-start | bytes 786440 | tf_op jit(solution)/shard_map/ppermute | solution.py:55
  3.2 0.1 slice_select_fusion.1
  3.3 1.9 %collective-permute-start = (f32[4,4,16,12]{3,2,1,0:T(8,128)S(1)}, f32[4,4,16,12]{3,2,1,0:T(8,128)S(1)}, u32[]{:S(2)}, u32[]{:S(2)}) collective-permute-start(f32[4,4,16,12]{3,2,1,0:T(8,128)S(1)} %get-tuple-element.80), channel_id=1, source_target_pairs={{0,2},{3,1},{2,4},{5,3},{4,6},{7,5},{8,10},{11,9},{10,12},{13,11},... | collective-permute-start | bytes 36872 | tf_op jit(solution)/shard_map/ppermute | solution.py:94
  5.2 4.7 %collective-permute-start.1 = (f32[4,4,16,12]{3,2,1,0:T(8,128)S(1)}, f32[4,4,16,12]{3,2,1,0:T(8,128)S(1)}, u32[]{:S(2)}, u32[]{:S(2)}) collective-permute-start(f32[4,4,16,12]{3,2,1,0:T(8,128)S(1)} %get-tuple-element.81), channel_id=1, source_target_pairs={{1,2},{2,1},{3,4},{4,3},{5,6},{6,5},{9,10},{10,9},{11,12},{12,11},... | collective-permute-start | bytes 36872 | tf_op jit(solution)/shard_map/ppermute | solution.py:93
  10.4 0.1 fusion.169
  10.6 0.1 fusion.168
  10.7 0.1 fusion.173
  10.9 0.1 fusion.177
  11.0 0.1 fusion.172
  11.2 0.1 fusion.176
  11.4 0.1 broadcast_add_fusion.4
  11.6 0.1 broadcast_add_fusion.3
  11.7 0.1 broadcast_add_fusion.2
  12.4 0.4 collective-permute-done.1
  12.8 0.4 fusion.44
  13.4 1.3 %collective-permute-start.3 = (f32[8,23,152]{2,1,0:T(8,128)S(1)}, f32[8,23,152]{2,1,0:T(8,128)S(1)}, u32[]{:S(2)}, u32[]{:S(2)}) collective-permute-start(f32[8,23,152]{2,1,0:T(8,128)S(1)} %pad_maximum_fusion.8), channel_id=1, source_target_pairs={{0,8},{8,16},{16,24},{24,0},{1,9},{9,17},{17,25},{25,1},{2,10},{10... | collective-permute-start | bytes 335624 | tf_op jit(solution)/shard_map/ppermute | solution.py:39
  14.7 1.2 %collective-permute-start.4 = (f32[8,23,152]{2,1,0:T(8,128)S(1)}, f32[8,23,152]{2,1,0:T(8,128)S(1)}, u32[]{:S(2)}, u32[]{:S(2)}) collective-permute-start(f32[8,23,152]{2,1,0:T(8,128)S(1)} %pad_maximum_fusion.9), channel_id=1, source_target_pairs={{8,0},{16,8},{24,16},{0,24},{9,1},{17,9},{25,17},{1,25},{10,2},{18... | collective-permute-start | bytes 335624 | tf_op jit(solution)/shard_map/ppermute | solution.py:40
  16.0 0.4 collective-permute-start.5
  16.4 2.1 %collective-permute-start.6 = (f32[8,12,152]{2,1,0:T(8,128)S(1)}, f32[8,12,152]{2,1,0:T(8,128)S(1)}, u32[]{:S(2)}, u32[]{:S(2)}) collective-permute-start(f32[8,12,152]{2,1,0:T(8,128)S(1)} %pad_maximum_fusion.11), channel_id=1, source_target_pairs={{8,0},{16,8},{24,16},{0,24},{9,1},{17,9},{25,17},{1,25},{10,2},{18... | collective-permute-start | bytes 175112 | tf_op jit(solution)/shard_map/ppermute | solution.py:40
  18.5 9.0 %collective-permute-done.5 = f32[8,12,152]{2,1,0:T(8,128)S(1)} collective-permute-done((f32[8,12,152]{2,1,0:T(8,128)S(1)}, f32[8,12,152]{2,1,0:T(8,128)S(1)}, u32[]{:S(2)}, u32[]{:S(2)}) %collective-permute-start.5) | collective-permute-done | bytes 58400 | tf_op jit(solution)/shard_map/ppermute | solution.py:39
  27.5 2.9 %collective-permute-done.6 = f32[8,12,152]{2,1,0:T(8,128)S(1)} collective-permute-done((f32[8,12,152]{2,1,0:T(8,128)S(1)}, f32[8,12,152]{2,1,0:T(8,128)S(1)}, u32[]{:S(2)}, u32[]{:S(2)}) %collective-permute-start.6) | collective-permute-done | bytes 58400 | tf_op jit(solution)/shard_map/ppermute | solution.py:40
  30.4 0.2 pad_maximum_fusion.1
  30.6 0.4 multiply_reduce_fusion.2
  31.0 0.2 slice.935
  31.3 0.6 %fusion.48 = (f32[8,38,150]{2,1,0:T(8,128)S(1)}, f32[8,38,150]{2,1,0:T(8,128)S(1)}, f32[8,38,150]{2,1,0:T(8,128)S(1)}) fusion(f32[8,40,152]{2,1,0:T(8,128)S(1)} %maximum_select_fusion.2, f32[8,38,150]{2,1,0:T(8,128)S(1)} %get-tuple-element.13, f32[8,38,150]{2,1,0:T(8,128)S(1)} %get-tuple-element.14, f32[8,150]{1,0:T(8,128)S(1)} %broadcast_add_fusion.10, ...), kind=kLoop, calls=%fused_computation.104 | loop fusion | flops 1048800 | bytes 3179904 | tf_op jit(solution)/shard_map/sub | solution.py:264
  31.8 0.2 slice.932
  32.0 0.2 slice.934
  32.1 0.4 slice.940
  32.6 2.8 %multiply_reduce_fusion.1 = (f32[8,34,146]{2,1,0:T(8,128)S(1)}, f32[8,34,146]{2,1,0:T(8,128)S(1)}, f32[4,8,34,146]{3,2,1,0:T(8,128)S(1)}) fusion(f32[8,146]{1,0:T(8,128)S(1)} %broadcast_add_fusion.8, f32[4,8,36,148]{3,2,1,0:T(8,128)S(1)} %slice.940, f32[4,8,38,150]{3,2,1,0:T(8,128)S(1)} %get-tuple-element.65, f32[146]{0:T(256)S(1)} %get-tuple-element.143, ...), kind=kLoop, calls=%fused_computation.23 | loop fusion | flops 3732928 | bytes 5930538 | tf_op jit(solution)/shard_map/reduce_sum | solution.py:181
  35.4 0.2 mul.1273
  35.5 0.4 slice.962
  35.9 0.1 slice.957
  36.0 0.6 %fusion.54 = f32[8,36,148]{2,1,0:T(8,128)S(1)} fusion(f32[8,38,150]{2,1,0:T(8,128)S(1)} %get-tuple-element.75, f32[8,40,152]{2,1,0:T(8,128)S(1)} %maximum_select_fusion.2, f32[8,148]{1,0:T(8,128)S(1)} %broadcast_add_fusion.9, f32[148]{0:T(256)S(1)} %get-tuple-element.135, f32[148]{0:T(256)S(1)} %get-tuple-element.133, f32[148]{0:T(256)S(1)} %get-tuple-element.132, ...), kind=kLoop, calls=%fused_computation.110 | loop fusion | flops 554112 | bytes 2476032 | tf_op jit(solution)/shard_map/jit(_where)/select_n | solution.py:145
  36.7 0.6 %slice_subtract_fusion.1 = (f32[8,34,146]{2,1,0:T(8,128)S(1)}, f32[8,34,146]{2,1,0:T(8,128)S(1)}, f32[8,34,146]{2,1,0:T(8,128)S(1)}) fusion(f32[8,36,148]{2,1,0:T(8,128)S(1)} %fusion.54, f32[8,146]{1,0:T(8,128)S(1)} %broadcast_add_fusion.8, f32[146]{0:T(256)S(1)} %get-tuple-element.143, f32[146]{0:T(256)S(1)} %get-tuple-element.141, ...), kind=kLoop, calls=%fused_computation.138 | loop fusion | flops 913376 | bytes 3109248 | tf_op jit(solution)/shard_map/sub | solution.py:182
  37.3 0.1 slice.954
  37.4 0.1 slice.956
  37.5 0.5 %fusion.87 = f32[8,32,144]{2,1,0:T(8,128)S(1)} fusion(f32[8,34,146]{2,1,0:T(8,128)S(1)} %get-tuple-element.74, f32[8,36,148]{2,1,0:T(8,128)S(1)} %fusion.54, f32[8,144]{1,0:T(8,128)S(1)} %broadcast_add_fusion.7, f32[144]{0:T(256)S(1)} %get-tuple-element.131, f32[144]{0:T(256)S(1)} %get-tuple-element.129, f32[144]{0:T(256)S(1)} %get-tuple-element.128, ...), kind=kLoop, calls=%fused_computation.164 | loop fusion | flops 479232 | bytes 2059776 | tf_op jit(solution)/shard_map/jit(_where)/select_n | solution.py:145
  38.1 2.3 %multiply_reduce_fusion = (f32[8,30,142]{2,1,0:T(8,128)S(1)}, f32[8,30,142]{2,1,0:T(8,128)S(1)}, f32[4,8,30,142]{3,2,1,0:T(8,128)S(1)}) fusion(f32[8,142]{1,0:T(8,128)S(1)} %broadcast_add_fusion.6, f32[4,8,32,144]{3,2,1,0:T(8,128)S(1)} %slice.962, f32[4,8,34,146]{3,2,1,0:T(8,128)S(1)} %get-tuple-element.47, f32[142]{0:T(256)S(1)} %get-tuple-element.127, ...), kind=kLoop, calls=%fused_computation.3 | loop fusion | flops 3203520 | bytes 5094774 | tf_op jit(solution)/shard_map/reduce_sum | solution.py:180
  40.3 0.5 fusion.71
  40.8 0.8 %fusion.102 = (f32[8,28,140]{2,1,0:T(8,128)S(1)}, f32[8,28,140]{2,1,0:T(8,128)S(1)}) fusion(f32[8,6,152]{2,1,0:T(8,128)S(1)} %get-tuple-element.87, f32[8,16,152]{2,1,0:T(8,128)S(1)} %get-tuple-element.56, f32[8,6,152]{2,1,0:T(8,128)S(1)} %get-tuple-element.85, f32[8,6,152]{2,1,0:T(8,128)S(1)} %get-tuple-element.86, ...), kind=kLoop, calls=%fused_computation.187 | loop fusion | flops 627200 | bytes 2621952 | tf_op jit(solution)/shard_map/jit(_where)/select_n | solution.py:145
  41.6 0.5 broadcast_select_fusion
  42.0 0.5 %fusion.131 = (f32[8,24,136]{2,1,0:T(8,128)S(1)}, f32[8,24,136]{2,1,0:T(8,128)S(1)}) fusion(f32[8,26,138]{2,1,0:T(8,128)S(1)} %get-tuple-element.29, f32[8,32,144]{2,1,0:T(8,128)S(1)} %fusion.87, f32[8,28,140]{2,1,0:T(8,128)S(1)} %get-tuple-element.34, f32[8,26,138]{2,1,0:T(8,128)S(1)} %get-tuple-element.30, f32[8,136]{1,0:T(8,128)S(1)} %broadcast_add_fusion.3, ...), kind=kLoop, calls=%fused_computation.243 | loop fusion | flops 548352 | bytes 2055680 | tf_op jit(solution)/shard_map/jit(_where)/select_n | solution.py:145
  42.6 0.3 slice.1006
  42.9 0.3 slice.1004
  43.2 0.6 %fusion.188 = (f32[4,8,20,132]{3,2,1,0:T(8,128)S(1)}, f32[4,8,20,132]{3,2,1,0:T(8,128)S(1)}, f32[8,20,132]{2,1,0:T(8,128)S(1)}, f32[8,20,132]{2,1,0:T(8,128)S(1)...) fusion(f32[4,8,34,146]{3,2,1,0:T(8,128)S(1)} %get-tuple-element.47, f32[8,20,132]{2,1,0:T(8,128)S(1)} %slice.1006, ...), kind=kLoop, calls=%fused_computation.455 | loop fusion | flops 1034880 | bytes 2027652 | tf_op jit(solution)/shard_map/slice | solution.py:135
  43.8 0.4 broadcast_select_fusion.2
  44.2 0.5 %fusion.120 = (f32[8,20,132]{2,1,0:T(8,128)S(1)}, f32[8,20,132]{2,1,0:T(8,128)S(1)}, f32[8,20,132]{2,1,0:T(8,128)S(1)}, f32[8,20,132]{2,1,0:T(8,128)S(1)}) fusion(f32[8,22,134]{2,1,0:T(8,128)S(1)} %get-tuple-element.19, f32[8,20,132]{2,1,0:T(8,128)S(1)} %get-tuple-element.54, f32[8,24,136]{2,1,0:T(8,128)S(1)} %get-tuple-element.78, ...), kind=kLoop, calls=%fused_computation.232 | loop fusion | flops 528000 | bytes 2315776 | tf_op jit(solution)/shard_map/jit(_where)/select_n | solution.py:145
  44.7 0.1 slice.1023
  44.8 0.1 slice.1024
  44.9 0.1 slice.1028
  45.1 0.1 slice.1029
  45.2 0.1 slice.1026
  45.3 1.7 %fusion.34 = f32[4,8,18,130]{3,2,1,0:T(8,128)S(1)} fusion(f32[4,8,20,132]{3,2,1,0:T(8,128)S(1)} %get-tuple-element.55, f32[4,8,20,132]{3,2,1,0:T(8,128)S(1)} %get-tuple-element.51, f32[4,8,20,132]{3,2,1,0:T(8,128)S(1)} %get-tuple-element.50, f32[8,18,130]{2,1,0:T(8,128)S(1)} %slice.1029, f32[8,18,130]{2,1,0:T(8,128)S(1)} %slice.1028, ...), kind=kLoop, calls=%fused_computation.59 | loop fusion | flops 1722240 | bytes 7585792 | tf_op jit(solution)/shard_map/jit(_where)/select_n | solution.py:145
  47.1 0.2 multiply_reduce_fusion.9
  47.3 0.4 broadcast_select_fusion.1
  47.7 0.1 slice_bitcast_fusion.6
  47.8 0.2 fusion.161
  48.0 0.6 %fusion.93 = f32[4,8,16,128]{3,2,1,0:T(8,128)S(1)} fusion(f32[4,8,18,130]{3,2,1,0:T(8,128)S(1)} %fusion.34, f32[4,8,38,150]{3,2,1,0:T(8,128)S(1)} %get-tuple-element.65, f32[8,128]{1,0:T(8,128)S(1)} %broadcast_add_fusion.11, f32[128]{0:T(128)S(1)} %get-tuple-element.103, f32[128]{0:T(128)S(1)} %get-tuple-element.101, f32[128]{0:T(128)S(1)} %get-tuple-element.100, ...), kind=kLoop, calls=%fused_computation.170 | loop fusion | flops 1638400 | bytes 2955264 | tf_op jit(solution)/shard_map/jit(_where)/select_n | solution.py:145
  48.7 1.3 %collective-permute-start.7 = (f32[6,4,16,128]{3,2,1,0:T(8,128)S(1)}, f32[6,4,16,128]{3,2,1,0:T(8,128)S(1)}, u32[]{:S(2)}, u32[]{:S(2)}) collective-permute-start(f32[6,4,16,128]{3,2,1,0:T(8,128)S(1)} %get-tuple-element.63), channel_id=1, source_target_pairs={{0,1},{1,0},{2,3},{3,2},{4,5},{5,4},{6,7},{7,6},{8,9},{9,8},{10,11... | collective-permute-start | bytes 589832 | tf_op jit(solution)/shard_map/ppermute | solution.py:116
  50.0 1.1 %collective-permute-done.7 = f32[6,4,16,128]{3,2,1,0:T(8,128)S(1)} collective-permute-done((f32[6,4,16,128]{3,2,1,0:T(8,128)S(1)}, f32[6,4,16,128]{3,2,1,0:T(8,128)S(1)}, u32[]{:S(2)}, u32[]{:S(2)}) %collective-permute-start.7) | collective-permute-done | bytes 196640 | tf_op jit(solution)/shard_map/ppermute | solution.py:116
  51.1 0.7 %slice.1047 = f32[4,4,16,256]{3,2,1,0:T(8,128)} slice(f32[6,4,16,256]{3,2,1,0:T(8,128)S(1)} %maximum_select_fusion.1), slice={[2:6], [0:4], [0:16], [0:256]} | slice | bytes 524288 | tf_op jit(solution)/shard_map/slice | solution.py:322
  51.8 0.7 %slice_bitcast_fusion.4 = (f32[4,16,256]{2,1,0:T(8,128)}, f32[4,16,256]{2,1,0:T(8,128)}) fusion(f32[6,4,16,256]{3,2,1,0:T(8,128)S(1)} %maximum_select_fusion.1), kind=kLoop, calls=%fused_computation.313 | loop fusion | bytes 262144 | tf_op jit(solution)/shard_map/squeeze | solution.py:322
  (84 shorter events, 1.9 us)
Async XLA Ops:
  0.6 12.1 %copy-start.1 = (f32[4,16,256]{2,1,0:T(8,128)S(1)}, f32[4,16,256]{2,1,0:T(8,128)}, u32[]{:S(2)}) copy-start(f32[4,16,256]{2,1,0:T(8,128)} %param.4) | copy-start | bytes 196612
  0.6 12.1 %copy-start = (f32[4,16,256]{2,1,0:T(8,128)S(1)}, f32[4,16,256]{2,1,0:T(8,128)}, u32[]{:S(2)}) copy-start(f32[4,16,256]{2,1,0:T(8,128)} %param.6) | copy-start | bytes 196612
  2.5 10.3 %collective-permute-start.2 = (f32[4,4,16,256]{3,2,1,0:T(8,128)S(1)}, f32[4,4,16,256]{3,2,1,0:T(8,128)S(1)}, u32[]{:S(2)}, u32[]{:S(2)}) collective-permute-start(f32[4,4,16,256]{3,2,1,0:T(8,128)S(1)} %pad_maximum_fusion.7), channel_id=1, source_target_pairs={{0,1},{1,0},{2,3},{3,2},{4,5},{5,4},{6,7},{7,6},{8,9},{9,8},{10,11... | collective-permute-start | bytes 786440 | tf_op jit(solution)/shard_map/ppermute | solution.py:55
  3.3 9.0 %collective-permute-start = (f32[4,4,16,12]{3,2,1,0:T(8,128)S(1)}, f32[4,4,16,12]{3,2,1,0:T(8,128)S(1)}, u32[]{:S(2)}, u32[]{:S(2)}) collective-permute-start(f32[4,4,16,12]{3,2,1,0:T(8,128)S(1)} %get-tuple-element.80), channel_id=1, source_target_pairs={{0,2},{3,1},{2,4},{5,3},{4,6},{7,5},{8,10},{11,9},{10,12},{13,11},... | collective-permute-start | bytes 36872 | tf_op jit(solution)/shard_map/ppermute | solution.py:94
  5.2 7.5 %collective-permute-start.1 = (f32[4,4,16,12]{3,2,1,0:T(8,128)S(1)}, f32[4,4,16,12]{3,2,1,0:T(8,128)S(1)}, u32[]{:S(2)}, u32[]{:S(2)}) collective-permute-start(f32[4,4,16,12]{3,2,1,0:T(8,128)S(1)} %get-tuple-element.81), channel_id=1, source_target_pairs={{1,2},{2,1},{3,4},{4,3},{5,6},{6,5},{9,10},{10,9},{11,12},{12,11},... | collective-permute-start | bytes 36872 | tf_op jit(solution)/shard_map/ppermute | solution.py:93
  13.4 16.9 %collective-permute-start.3 = (f32[8,23,152]{2,1,0:T(8,128)S(1)}, f32[8,23,152]{2,1,0:T(8,128)S(1)}, u32[]{:S(2)}, u32[]{:S(2)}) collective-permute-start(f32[8,23,152]{2,1,0:T(8,128)S(1)} %pad_maximum_fusion.8), channel_id=1, source_target_pairs={{0,8},{8,16},{16,24},{24,0},{1,9},{9,17},{17,25},{25,1},{2,10},{10... | collective-permute-start | bytes 335624 | tf_op jit(solution)/shard_map/ppermute | solution.py:39
  14.7 15.7 %collective-permute-start.4 = (f32[8,23,152]{2,1,0:T(8,128)S(1)}, f32[8,23,152]{2,1,0:T(8,128)S(1)}, u32[]{:S(2)}, u32[]{:S(2)}) collective-permute-start(f32[8,23,152]{2,1,0:T(8,128)S(1)} %pad_maximum_fusion.9), channel_id=1, source_target_pairs={{8,0},{16,8},{24,16},{0,24},{9,1},{17,9},{25,17},{1,25},{10,2},{18... | collective-permute-start | bytes 335624 | tf_op jit(solution)/shard_map/ppermute | solution.py:40
  16.0 11.5 %collective-permute-start.5 = (f32[8,12,152]{2,1,0:T(8,128)S(1)}, f32[8,12,152]{2,1,0:T(8,128)S(1)}, u32[]{:S(2)}, u32[]{:S(2)}) collective-permute-start(f32[8,12,152]{2,1,0:T(8,128)S(1)} %pad_maximum_fusion.10), channel_id=1, source_target_pairs={{0,8},{8,16},{16,24},{24,0},{1,9},{9,17},{17,25},{25,1},{2,10},{10... | collective-permute-start | bytes 175112 | tf_op jit(solution)/shard_map/ppermute | solution.py:39
  16.4 14.0 %collective-permute-start.6 = (f32[8,12,152]{2,1,0:T(8,128)S(1)}, f32[8,12,152]{2,1,0:T(8,128)S(1)}, u32[]{:S(2)}, u32[]{:S(2)}) collective-permute-start(f32[8,12,152]{2,1,0:T(8,128)S(1)} %pad_maximum_fusion.11), channel_id=1, source_target_pairs={{8,0},{16,8},{24,16},{0,24},{9,1},{17,9},{25,17},{1,25},{10,2},{18... | collective-permute-start | bytes 175112 | tf_op jit(solution)/shard_map/ppermute | solution.py:40
  48.7 2.4 %collective-permute-start.7 = (f32[6,4,16,128]{3,2,1,0:T(8,128)S(1)}, f32[6,4,16,128]{3,2,1,0:T(8,128)S(1)}, u32[]{:S(2)}, u32[]{:S(2)}) collective-permute-start(f32[6,4,16,128]{3,2,1,0:T(8,128)S(1)} %get-tuple-element.63), channel_id=1, source_target_pairs={{0,1},{1,0},{2,3},{3,2},{4,5},{5,4},{6,7},{7,6},{8,9},{9,8},{10,11... | collective-permute-start | bytes 589832 | tf_op jit(solution)/shard_map/ppermute | solution.py:116

commit v11 on v7

--- a/solution.py
+++ b/solution.py
@@ -106,7 +106,7 @@
     return lax.dynamic_slice_in_dim(padded, own * part, part + 2 * width, axis=padded.ndim - 1)
 
 
-def scatter_heights(x, height_rows):
+def scatter_heights(x, height_rows, splits):
     peers, own = (lax.axis_size("hgt"), lax.axis_index("hgt"))
     parts = []
     for shift in range(peers):
@@ -116,16 +116,20 @@
             piece = lax.ppermute(piece, "hgt", [(i, (i + shift) % peers) for i in range(peers)])
         parts.append(piece)
     if peers == 2:
-        return jnp.where(
-            own == 0,
-            jnp.concatenate([parts[0], parts[1]], axis=-1),
-            jnp.concatenate([parts[1], parts[0]], axis=-1),
-        )
+        return [
+            jnp.where(
+                own == 0,
+                jnp.concatenate([parts[0][lo:hi], parts[1][lo:hi]], axis=-1),
+                jnp.concatenate([parts[1][lo:hi], parts[0][lo:hi]], axis=-1),
+            )
+            for lo, hi in splits
+        ]
     stacked = jnp.stack(parts)
     order = (own - jnp.arange(peers, dtype=jnp.int32)) % peers
     ordered = jnp.moveaxis(jnp.take(stacked, order, axis=0), 0, -2)
     shape = ordered.shape
-    return ordered.reshape(shape[:-2] + (shape[-2] * shape[-1],))
+    ordered = ordered.reshape(shape[:-2] + (shape[-2] * shape[-1],))
+    return [ordered[lo:hi] for lo, hi in splits]
 
 
 def crop(x, width, new_width):
@@ -231,7 +235,16 @@
         radius_rows * lax.axis_size("rad"),
         part,
     )
-    packed = jnp.stack([density, labels.astype(jnp.float32), observed, measured.astype(jnp.float32)])
+    field = lax.broadcasted_iota(jnp.int32, (4,) + density.shape, 0)
+    packed = jnp.where(
+        field == 0,
+        density[None],
+        jnp.where(
+            field == 1,
+            labels[None].astype(jnp.float32),
+            jnp.where(field == 2, observed[None], measured[None].astype(jnp.float32)),
+        ),
+    )
     if lax.axis_size("hgt") == 2:
         received = edge_columns(packed, HALO)
         packed = two_core_window(gather_axis(packed, "hgt", 1), received, HALO)
@@ -316,10 +329,12 @@
 
     costate = crop(costate, c_width, 0)
     cograins = crop(cograins, cg_width, 0)
-    result = scatter_heights(
-        jnp.concatenate([last_density[None], costate[None], cograins], axis=0), height_rows
-    )
-    return (result[0], result[1], result[2:])
+    last_density, costate, cograins = scatter_heights(
+        jnp.concatenate([last_density[None], costate[None], cograins], axis=0),
+        height_rows,
+        ((0, 1), (1, 2), (2, 2 + GRAINS)),
+    )
+    return (last_density[0], costate[0], cograins)
 
 
 def solution(mesh):

time: 51.1 us -> 52.6 us (1.029)
  other arithmetic: 19.6 us -> 22.5 us
  local copies, waits for them, and re-layouts: 4.41 us -> 3.03 us
    select_n x1 -> x4, other arithmetic: 0.03 us -> 2.98 us  [the longest x3 2 us: scatter_heights(): jnp.where(own == 0, jnp.concatenate([parts[0][lo:hi], parts[1][lo:hi]], a...]
    another operation x2 -> x0, other arithmetic: 1.81 us -> none  [shards(): jnp.stack([density, labels.astype(jnp.float32), observed, measured.astype...]
    convert_element_type x0 -> x2, other arithmetic: none -> 1.69 us  [the longest x1 0.85 us: shards(): labels[None].astype(jnp.float32)]
    slice x1 -> x2, local copies, waits for them, and re-layouts: 0.72 us -> 0.02 us  [the longest x1 0.01 us: scatter_heights(): parts[0][lo:hi]]
    squeeze x1 -> x0, local copies, waits for them, and re-layouts: 0.66 us -> none  [shards(): return (result[0], result[1], result[2:])]
where the time goes in v11:
time: 52.6 us; the launch traced here: 52.3 us
  other arithmetic  22.5 us (43%)
  starting transfers between devices  14.5 us (28%)
  waiting for transfers between devices  10.8 us (21%)
  local copies, waits for them, and re-layouts  3.03 us (6%)
  between operations  1.47 us (3%)
    select_n x11, other arithmetic, in_domain(): return jnp.where(radial_mask(width, geometry), x, 0.0)  6.49 us
    ppermute x2, waiting for transfers between devices, azim_exchange(): after = lax.ppermute(leading, 'azim', down)  4.86 us
    ppermute x1, starting transfers between devices, edge_columns(): lax.ppermute(jnp.where(own == 0, first, last), ('rad', 'hgt'), cross)  4.68 us
    ppermute x2, waiting for transfers between devices, azim_exchange(): before = lax.ppermute(last, 'azim', up)  4.53 us
    reduce_sum x2, other arithmetic, chemical(): cube_sum = jnp.sum(grains * grains * grains, axis=0)  3.17 us
    slice x15, local copies, waits for them, and re-layouts, crop(): return x[..., cut:x.shape[-2] - cut, cut:x.shape[-1] - cut]  2.63 us
    ppermute x2, starting transfers between devices, azim_exchange(): after = lax.ppermute(leading, 'azim', down)  2.59 us
    ppermute x2, starting transfers between devices, azim_exchange(): before = lax.ppermute(last, 'azim', up)  2.53 us
  transfers between devices with their start and end apart: 8, of which 5 were waited for; matrix products, arithmetic and copies ran while one was open for 11% of the time, Pallas kernels for 0%

profile of v11, /device:TPU:9, one launch (start us, length us, event | category | flops | bytes accessed | tf_op | source)
XLA Modules:
  0.0 52.3 jit_solution(10939041504916726077)
XLA Ops:
  0.7 0.8 %convert_element_type.203 = f32[4,16,256]{2,1,0:T(8,128)S(1)} convert(s32[4,16,256]{2,1,0:T(8,128)} %param.5) | non-fusion elementwise | flops 16384 | bytes 131072 | tf_op jit(solution)/shard_map/convert_element_type | solution.py:244
  1.5 0.8 %convert_element_type.204 = f32[4,16,256]{2,1,0:T(8,128)S(1)} convert(s32[4,16,256]{2,1,0:T(8,128)} %param.7) | non-fusion elementwise | flops 16384 | bytes 131072 | tf_op jit(solution)/shard_map/convert_element_type | solution.py:245
  2.3 1.0 %select_select_fusion = f32[4,4,16,256]{3,2,1,0:T(8,128)S(1)} fusion(f32[4,16,256]{2,1,0:T(8,128)S(1)} %convert_element_type.204, f32[4,16,256]{2,1,0:T(8,128)} %param.6, f32[4,16,256]{2,1,0:T(8,128)S(1)} %convert_element_type.203, f32[4,16,256]{2,1,0:T(8,128)} %param.4, pred[4]{0:T(512)(128)(4,1)S(1)} %get-tuple-element.148, ...), kind=kLoop, calls=%fused_computation.214 | loop fusion | flops 196608 | bytes 524300 | tf_op jit(solution)/shard_map/jit(_where)/select_n | solution.py:239
  3.3 0.7 %collective-permute-start.2 = (f32[4,4,16,256]{3,2,1,0:T(8,128)S(1)}, f32[4,4,16,256]{3,2,1,0:T(8,128)S(1)}, u32[]{:S(2)}, u32[]{:S(2)}) collective-permute-start(f32[4,4,16,256]{3,2,1,0:T(8,128)S(1)} %select_select_fusion), channel_id=1, source_target_pairs={{0,1},{1,0},{2,3},{3,2},{4,5},{5,4},{6,7},{7,6},{8,9},{9,8},{10,11... | collective-permute-start | bytes 786440 | tf_op jit(solution)/shard_map/ppermute | solution.py:55
  4.1 0.1 slice_select_fusion.1
  4.2 1.9 %collective-permute-start = (f32[4,4,16,12]{3,2,1,0:T(8,128)S(1)}, f32[4,4,16,12]{3,2,1,0:T(8,128)S(1)}, u32[]{:S(2)}, u32[]{:S(2)}) collective-permute-start(f32[4,4,16,12]{3,2,1,0:T(8,128)S(1)} %get-tuple-element.82), channel_id=1, source_target_pairs={{0,2},{3,1},{2,4},{5,3},{4,6},{7,5},{8,10},{11,9},{10,12},{13,11},... | collective-permute-start | bytes 36872 | tf_op jit(solution)/shard_map/ppermute | solution.py:94
  6.1 4.7 %collective-permute-start.1 = (f32[4,4,16,12]{3,2,1,0:T(8,128)S(1)}, f32[4,4,16,12]{3,2,1,0:T(8,128)S(1)}, u32[]{:S(2)}, u32[]{:S(2)}) collective-permute-start(f32[4,4,16,12]{3,2,1,0:T(8,128)S(1)} %get-tuple-element.83), channel_id=1, source_target_pairs={{1,2},{2,1},{3,4},{4,3},{5,6},{6,5},{9,10},{10,9},{11,12},{12,11},... | collective-permute-start | bytes 36872 | tf_op jit(solution)/shard_map/ppermute | solution.py:93
  11.3 0.1 fusion.169
  11.4 0.1 fusion.168
  11.6 0.1 fusion.173
  11.7 0.1 fusion.177
  12.3 0.1 broadcast_add_fusion.4
  13.2 0.4 collective-permute-done.1
  13.7 0.4 fusion.44
  14.2 1.3 %collective-permute-start.3 = (f32[8,23,152]{2,1,0:T(8,128)S(1)}, f32[8,23,152]{2,1,0:T(8,128)S(1)}, u32[]{:S(2)}, u32[]{:S(2)}) collective-permute-start(f32[8,23,152]{2,1,0:T(8,128)S(1)} %pad_maximum_fusion.8), channel_id=1, source_target_pairs={{0,8},{8,16},{16,24},{24,0},{1,9},{9,17},{17,25},{25,1},{2,10},{10... | collective-permute-start | bytes 335624 | tf_op jit(solution)/shard_map/ppermute | solution.py:39
  15.5 1.2 %collective-permute-start.4 = (f32[8,23,152]{2,1,0:T(8,128)S(1)}, f32[8,23,152]{2,1,0:T(8,128)S(1)}, u32[]{:S(2)}, u32[]{:S(2)}) collective-permute-start(f32[8,23,152]{2,1,0:T(8,128)S(1)} %pad_maximum_fusion.9), channel_id=1, source_target_pairs={{8,0},{16,8},{24,16},{0,24},{9,1},{17,9},{25,17},{1,25},{10,2},{18... | collective-permute-start | bytes 335624 | tf_op jit(solution)/shard_map/ppermute | solution.py:40
  16.7 4.5 %collective-permute-done.3 = f32[8,23,152]{2,1,0:T(8,128)S(1)} collective-permute-done((f32[8,23,152]{2,1,0:T(8,128)S(1)}, f32[8,23,152]{2,1,0:T(8,128)S(1)}, u32[]{:S(2)}, u32[]{:S(2)}) %collective-permute-start.3) | collective-permute-done | bytes 111904 | tf_op jit(solution)/shard_map/ppermute | solution.py:39
  21.3 4.3 %collective-permute-done.4 = f32[8,23,152]{2,1,0:T(8,128)S(1)} collective-permute-done((f32[8,23,152]{2,1,0:T(8,128)S(1)}, f32[8,23,152]{2,1,0:T(8,128)S(1)}, u32[]{:S(2)}, u32[]{:S(2)}) %collective-permute-start.4) | collective-permute-done | bytes 111904 | tf_op jit(solution)/shard_map/ppermute | solution.py:40
  25.6 0.2 pad_maximum_fusion.1
  25.8 0.4 multiply_reduce_fusion.2
  26.3 0.2 slice.955
  26.4 0.6 %fusion.48 = (f32[8,38,150]{2,1,0:T(8,128)S(1)}, f32[8,38,150]{2,1,0:T(8,128)S(1)}, f32[8,38,150]{2,1,0:T(8,128)S(1)}) fusion(f32[8,40,152]{2,1,0:T(8,128)S(1)} %broadcast_select_fusion, f32[8,38,150]{2,1,0:T(8,128)S(1)} %get-tuple-element.17, f32[8,38,150]{2,1,0:T(8,128)S(1)} %get-tuple-element.18, f32[8,150]{1,0:T(8,128)S(1)} %broadcast_add_fusion.10, ...), kind=kLoop, calls=%fused_computation.103 | loop fusion | flops 1048800 | bytes 3179904 | tf_op jit(solution)/shard_map/sub | solution.py:277
  27.0 0.2 slice.952
  27.2 0.2 slice.954
  27.3 0.4 slice.960
  27.8 2.8 %multiply_reduce_fusion.1 = (f32[8,34,146]{2,1,0:T(8,128)S(1)}, f32[8,34,146]{2,1,0:T(8,128)S(1)}, f32[4,8,34,146]{3,2,1,0:T(8,128)S(1)}) fusion(f32[8,146]{1,0:T(8,128)S(1)} %broadcast_add_fusion.8, f32[4,8,36,148]{3,2,1,0:T(8,128)S(1)} %slice.960, f32[4,8,38,150]{3,2,1,0:T(8,128)S(1)} %get-tuple-element.65, f32[146]{0:T(256)S(1)} %get-tuple-element.147, ...), kind=kLoop, calls=%fused_computation.23 | loop fusion | flops 3732928 | bytes 5930538 | tf_op jit(solution)/shard_map/reduce_sum | solution.py:185
  30.5 0.2 mul.1273
  30.7 0.4 slice.982
  31.1 0.1 slice.977
  31.2 0.6 %fusion.54 = f32[8,36,148]{2,1,0:T(8,128)S(1)} fusion(f32[8,38,150]{2,1,0:T(8,128)S(1)} %get-tuple-element.75, f32[8,40,152]{2,1,0:T(8,128)S(1)} %broadcast_select_fusion, f32[8,148]{1,0:T(8,128)S(1)} %broadcast_add_fusion.9, f32[148]{0:T(256)S(1)} %get-tuple-element.139, f32[148]{0:T(256)S(1)} %get-tuple-element.137, f32[148]{0:T(256)S(1)} %get-tuple-element.136, ...), kind=kLoop, calls=%fused_computation.109 | loop fusion | flops 554112 | bytes 2476032 | tf_op jit(solution)/shard_map/jit(_where)/select_n | solution.py:149
  31.9 0.6 %slice_subtract_fusion.1 = (f32[8,34,146]{2,1,0:T(8,128)S(1)}, f32[8,34,146]{2,1,0:T(8,128)S(1)}, f32[8,34,146]{2,1,0:T(8,128)S(1)}) fusion(f32[8,36,148]{2,1,0:T(8,128)S(1)} %fusion.54, f32[8,146]{1,0:T(8,128)S(1)} %broadcast_add_fusion.8, f32[146]{0:T(256)S(1)} %get-tuple-element.147, f32[146]{0:T(256)S(1)} %get-tuple-element.145, ...), kind=kLoop, calls=%fused_computation.137 | loop fusion | flops 913376 | bytes 3109248 | tf_op jit(solution)/shard_map/sub | solution.py:186
  32.5 0.1 slice.974
  32.6 0.1 slice.976
  32.7 0.1 slice-done
  32.9 1.3 %collective-permute-start.5 = (f32[8,12,152]{2,1,0:T(8,128)S(1)}, f32[8,12,152]{2,1,0:T(8,128)S(1)}, u32[]{:S(2)}, u32[]{:S(2)}) collective-permute-start(f32[8,12,152]{2,1,0:T(8,128)S(1)} %pad_maximum_fusion.10), channel_id=1, source_target_pairs={{0,8},{8,16},{16,24},{24,0},{1,9},{9,17},{17,25},{25,1},{2,10},{10... | collective-permute-start | bytes 175112 | tf_op jit(solution)/shard_map/ppermute | solution.py:39
  34.2 1.4 %collective-permute-start.6 = (f32[8,12,152]{2,1,0:T(8,128)S(1)}, f32[8,12,152]{2,1,0:T(8,128)S(1)}, u32[]{:S(2)}, u32[]{:S(2)}) collective-permute-start(f32[8,12,152]{2,1,0:T(8,128)S(1)} %pad_maximum_fusion.11), channel_id=1, source_target_pairs={{8,0},{16,8},{24,16},{0,24},{9,1},{17,9},{25,17},{1,25},{10,2},{18... | collective-permute-start | bytes 175112 | tf_op jit(solution)/shard_map/ppermute | solution.py:40
  35.6 0.5 %fusion.87 = f32[8,32,144]{2,1,0:T(8,128)S(1)} fusion(f32[8,34,146]{2,1,0:T(8,128)S(1)} %get-tuple-element.74, f32[8,36,148]{2,1,0:T(8,128)S(1)} %fusion.54, f32[8,144]{1,0:T(8,128)S(1)} %broadcast_add_fusion.7, f32[144]{0:T(256)S(1)} %get-tuple-element.135, f32[144]{0:T(256)S(1)} %get-tuple-element.133, f32[144]{0:T(256)S(1)} %get-tuple-element.132, ...), kind=kLoop, calls=%fused_computation.163 | loop fusion | flops 479232 | bytes 2059776 | tf_op jit(solution)/shard_map/jit(_where)/select_n | solution.py:149
  36.1 2.3 %multiply_reduce_fusion = (f32[8,30,142]{2,1,0:T(8,128)S(1)}, f32[8,30,142]{2,1,0:T(8,128)S(1)}, f32[4,8,30,142]{3,2,1,0:T(8,128)S(1)}) fusion(f32[8,142]{1,0:T(8,128)S(1)} %broadcast_add_fusion.6, f32[4,8,32,144]{3,2,1,0:T(8,128)S(1)} %slice.982, f32[4,8,34,146]{3,2,1,0:T(8,128)S(1)} %get-tuple-element.51, f32[142]{0:T(256)S(1)} %get-tuple-element.131, ...), kind=kLoop, calls=%fused_computation.3 | loop fusion | flops 3203520 | bytes 5094774 | tf_op jit(solution)/shard_map/reduce_sum | solution.py:184
  38.4 0.5 fusion.71
  38.9 0.3 slice.1022
  39.2 0.6 %collective-permute-done.6 = f32[8,12,152]{2,1,0:T(8,128)S(1)} collective-permute-done((f32[8,12,152]{2,1,0:T(8,128)S(1)}, f32[8,12,152]{2,1,0:T(8,128)S(1)}, u32[]{:S(2)}, u32[]{:S(2)}) %collective-permute-start.6) | collective-permute-done | bytes 58400 | tf_op jit(solution)/shard_map/ppermute | solution.py:40
  39.8 0.8 %fusion.102 = (f32[8,28,140]{2,1,0:T(8,128)S(1)}, f32[8,28,140]{2,1,0:T(8,128)S(1)}) fusion(f32[8,6,152]{2,1,0:T(8,128)S(1)} %get-tuple-element.91, f32[8,16,152]{2,1,0:T(8,128)S(1)} %get-tuple-element.80, f32[8,6,152]{2,1,0:T(8,128)S(1)} %get-tuple-element.89, f32[8,6,152]{2,1,0:T(8,128)S(1)} %get-tuple-element.90, ...), kind=kLoop, calls=%fused_computation.186 | loop fusion | flops 627200 | bytes 2621952 | tf_op jit(solution)/shard_map/jit(_where)/select_n | solution.py:149
  40.6 0.5 broadcast_select_fusion.1
  41.0 0.5 %fusion.131 = (f32[8,24,136]{2,1,0:T(8,128)S(1)}, f32[8,24,136]{2,1,0:T(8,128)S(1)}) fusion(f32[8,26,138]{2,1,0:T(8,128)S(1)} %get-tuple-element.33, f32[8,32,144]{2,1,0:T(8,128)S(1)} %fusion.87, f32[8,28,140]{2,1,0:T(8,128)S(1)} %get-tuple-element.38, f32[8,26,138]{2,1,0:T(8,128)S(1)} %get-tuple-element.34, f32[8,136]{1,0:T(8,128)S(1)} %broadcast_add_fusion.3, ...), kind=kLoop, calls=%fused_computation.243 | loop fusion | flops 548352 | bytes 2055680 | tf_op jit(solution)/shard_map/jit(_where)/select_n | solution.py:149
  41.6 0.1 slice.1024
  41.7 0.6 %fusion.188 = (f32[4,8,20,132]{3,2,1,0:T(8,128)S(1)}, f32[4,8,20,132]{3,2,1,0:T(8,128)S(1)}, f32[8,20,132]{2,1,0:T(8,128)S(1)}, f32[8,20,132]{2,1,0:T(8,128)S(1)...) fusion(f32[4,8,34,146]{3,2,1,0:T(8,128)S(1)} %get-tuple-element.51, f32[8,20,132]{2,1,0:T(8,128)S(1)} %slice.1024, ...), kind=kLoop, calls=%fused_computation.461 | loop fusion | flops 1034880 | bytes 2027652 | tf_op jit(solution)/shard_map/slice | solution.py:139
  42.3 0.4 broadcast_select_fusion.3
  42.7 0.5 %fusion.120 = (f32[8,20,132]{2,1,0:T(8,128)S(1)}, f32[8,20,132]{2,1,0:T(8,128)S(1)}, f32[8,20,132]{2,1,0:T(8,128)S(1)}, f32[8,20,132]{2,1,0:T(8,128)S(1)}) fusion(f32[8,22,134]{2,1,0:T(8,128)S(1)} %get-tuple-element.23, f32[8,20,132]{2,1,0:T(8,128)S(1)} %get-tuple-element.58, f32[8,24,136]{2,1,0:T(8,128)S(1)} %get-tuple-element.78, ...), kind=kLoop, calls=%fused_computation.232 | loop fusion | flops 528000 | bytes 2315776 | tf_op jit(solution)/shard_map/jit(_where)/select_n | solution.py:149
  43.2 0.1 slice.1041
  43.3 0.1 slice.1042
  43.4 0.1 slice.1046
  43.6 0.1 slice.1047
  43.7 0.1 slice.1044
  43.8 1.7 %fusion.34 = f32[4,8,18,130]{3,2,1,0:T(8,128)S(1)} fusion(f32[4,8,20,132]{3,2,1,0:T(8,128)S(1)} %get-tuple-element.59, f32[4,8,20,132]{3,2,1,0:T(8,128)S(1)} %get-tuple-element.55, f32[4,8,20,132]{3,2,1,0:T(8,128)S(1)} %get-tuple-element.54, f32[8,18,130]{2,1,0:T(8,128)S(1)} %slice.1047, f32[8,18,130]{2,1,0:T(8,128)S(1)} %slice.1046, ...), kind=kLoop, calls=%fused_computation.59 | loop fusion | flops 1722240 | bytes 7585792 | tf_op jit(solution)/shard_map/jit(_where)/select_n | solution.py:149
  45.6 0.2 multiply_reduce_fusion.9
  45.8 0.4 broadcast_select_fusion.2
  46.2 0.1 slice_bitcast_fusion.4
  46.3 0.2 fusion.161
  46.5 0.6 %fusion.93 = f32[4,8,16,128]{3,2,1,0:T(8,128)S(1)} fusion(f32[4,8,18,130]{3,2,1,0:T(8,128)S(1)} %fusion.34, f32[4,8,38,150]{3,2,1,0:T(8,128)S(1)} %get-tuple-element.65, f32[8,128]{1,0:T(8,128)S(1)} %broadcast_add_fusion.11, f32[128]{0:T(128)S(1)} %get-tuple-element.107, f32[128]{0:T(128)S(1)} %get-tuple-element.105, f32[128]{0:T(128)S(1)} %get-tuple-element.104, ...), kind=kLoop, calls=%fused_computation.169 | loop fusion | flops 1638400 | bytes 2955264 | tf_op jit(solution)/shard_map/jit(_where)/select_n | solution.py:149
  47.1 2.0 %collective-permute-start.7 = (f32[6,4,16,128]{3,2,1,0:T(8,128)S(1)}, f32[6,4,16,128]{3,2,1,0:T(8,128)S(1)}, u32[]{:S(2)}, u32[]{:S(2)}) collective-permute-start(f32[6,4,16,128]{3,2,1,0:T(8,128)S(1)} %constant_dynamic-slice_fusion), channel_id=1, source_target_pairs={{0,1},{1,0},{2,3},{3,2},{4,5},{5,4},{6,7},{7,6},{8,9},{9,8},{10,11... | collective-permute-start | bytes 589832 | tf_op jit(solution)/shard_map/ppermute | solution.py:116
  49.2 1.1 %collective-permute-done.7 = f32[6,4,16,128]{3,2,1,0:T(8,128)S(1)} collective-permute-done((f32[6,4,16,128]{3,2,1,0:T(8,128)S(1)}, f32[6,4,16,128]{3,2,1,0:T(8,128)S(1)}, u32[]{:S(2)}, u32[]{:S(2)}) %collective-permute-start.7) | collective-permute-done | bytes 196640 | tf_op jit(solution)/shard_map/ppermute | solution.py:116
  50.3 0.7 %maximum_select_fusion.2 = f32[4,4,16,256]{3,2,1,0:T(8,128)} fusion(f32[4,4,16,128]{3,2,1,0:T(8,128)S(1)} %slice.1065, f32[4,4,16,128]{3,2,1,0:T(8,128)S(1)} %constant_dynamic-slice_fusion.1, pred[]{:T(512)S(6)} %eq.46), kind=kLoop, calls=%fused_computation.211 | loop fusion | flops 196608 | bytes 524289 | tf_op jit(solution)/shard_map/jit(_where)/select_n | solution.py:120
  51.0 0.6 %maximum_select_fusion.4 = f32[4,16,256]{2,1,0:T(8,128)} fusion(f32[4,16,128]{2,1,0:T(8,128)S(1)} %get-tuple-element.84, f32[4,16,128]{2,1,0:T(8,128)S(1)} %get-tuple-element.62, pred[]{:T(512)S(6)} %eq.46), kind=kLoop, calls=%fused_computation.323 | loop fusion | flops 49152 | bytes 131073 | tf_op jit(solution)/shard_map/jit(_where)/select_n | solution.py:120
  51.6 0.6 %maximum_select_fusion.3 = f32[4,16,256]{2,1,0:T(8,128)} fusion(f32[4,16,128]{2,1,0:T(8,128)S(1)} %get-tuple-element.85, f32[4,16,128]{2,1,0:T(8,128)S(1)} %get-tuple-element.63, pred[]{:T(512)S(6)} %eq.46), kind=kLoop, calls=%fused_computation.322 | loop fusion | flops 49152 | bytes 131073 | tf_op jit(solution)/shard_map/jit(_where)/select_n | solution.py:120
  (93 shorter events, 2.2 us)
Async XLA Ops:
  3.3 10.3 %collective-permute-start.2 = (f32[4,4,16,256]{3,2,1,0:T(8,128)S(1)}, f32[4,4,16,256]{3,2,1,0:T(8,128)S(1)}, u32[]{:S(2)}, u32[]{:S(2)}) collective-permute-start(f32[4,4,16,256]{3,2,1,0:T(8,128)S(1)} %select_select_fusion), channel_id=1, source_target_pairs={{0,1},{1,0},{2,3},{3,2},{4,5},{5,4},{6,7},{7,6},{8,9},{9,8},{10,11... | collective-permute-start | bytes 786440 | tf_op jit(solution)/shard_map/ppermute | solution.py:55
  4.2 9.0 %collective-permute-start = (f32[4,4,16,12]{3,2,1,0:T(8,128)S(1)}, f32[4,4,16,12]{3,2,1,0:T(8,128)S(1)}, u32[]{:S(2)}, u32[]{:S(2)}) collective-permute-start(f32[4,4,16,12]{3,2,1,0:T(8,128)S(1)} %get-tuple-element.82), channel_id=1, source_target_pairs={{0,2},{3,1},{2,4},{5,3},{4,6},{7,5},{8,10},{11,9},{10,12},{13,11},... | collective-permute-start | bytes 36872 | tf_op jit(solution)/shard_map/ppermute | solution.py:94
  6.1 7.5 %collective-permute-start.1 = (f32[4,4,16,12]{3,2,1,0:T(8,128)S(1)}, f32[4,4,16,12]{3,2,1,0:T(8,128)S(1)}, u32[]{:S(2)}, u32[]{:S(2)}) collective-permute-start(f32[4,4,16,12]{3,2,1,0:T(8,128)S(1)} %get-tuple-element.83), channel_id=1, source_target_pairs={{1,2},{2,1},{3,4},{4,3},{5,6},{6,5},{9,10},{10,9},{11,12},{12,11},... | collective-permute-start | bytes 36872 | tf_op jit(solution)/shard_map/ppermute | solution.py:93
  14.1 2.6 %copy-start = (f32[4,8,16,152]{3,2,1,0:T(8,128)}, f32[4,8,16,152]{3,2,1,0:T(8,128)S(1)}, u32[]{:S(2)}) copy-start(f32[4,8,16,152]{3,2,1,0:T(8,128)S(1)} %fusion.44) | copy-start | bytes 933892
  14.2 7.0 %collective-permute-start.3 = (f32[8,23,152]{2,1,0:T(8,128)S(1)}, f32[8,23,152]{2,1,0:T(8,128)S(1)}, u32[]{:S(2)}, u32[]{:S(2)}) collective-permute-start(f32[8,23,152]{2,1,0:T(8,128)S(1)} %pad_maximum_fusion.8), channel_id=1, source_target_pairs={{0,8},{8,16},{16,24},{24,0},{1,9},{9,17},{17,25},{25,1},{2,10},{10... | collective-permute-start | bytes 335624 | tf_op jit(solution)/shard_map/ppermute | solution.py:39
  15.5 10.0 %collective-permute-start.4 = (f32[8,23,152]{2,1,0:T(8,128)S(1)}, f32[8,23,152]{2,1,0:T(8,128)S(1)}, u32[]{:S(2)}, u32[]{:S(2)}) collective-permute-start(f32[8,23,152]{2,1,0:T(8,128)S(1)} %pad_maximum_fusion.9), channel_id=1, source_target_pairs={{8,0},{16,8},{24,16},{0,24},{9,1},{17,9},{25,17},{1,25},{10,2},{18... | collective-permute-start | bytes 335624 | tf_op jit(solution)/shard_map/ppermute | solution.py:40
  31.9 1.0 %slice-start = ((f32[4,8,16,152]{3,2,1,0:T(8,128)}), f32[2,8,16,152]{3,2,1,0:T(8,128)S(1)}, s32[]{:S(2)}) async-start(f32[4,8,16,152]{3,2,1,0:T(8,128)} %copy-done), calls=%async_computation | async-start | bytes 524288 | tf_op jit(solution)/shard_map/slice | solution.py:259
  32.9 6.2 %collective-permute-start.5 = (f32[8,12,152]{2,1,0:T(8,128)S(1)}, f32[8,12,152]{2,1,0:T(8,128)S(1)}, u32[]{:S(2)}, u32[]{:S(2)}) collective-permute-start(f32[8,12,152]{2,1,0:T(8,128)S(1)} %pad_maximum_fusion.10), channel_id=1, source_target_pairs={{0,8},{8,16},{16,24},{24,0},{1,9},{9,17},{17,25},{25,1},{2,10},{10... | collective-permute-start | bytes 175112 | tf_op jit(solution)/shard_map/ppermute | solution.py:39
  34.2 5.6 %collective-permute-start.6 = (f32[8,12,152]{2,1,0:T(8,128)S(1)}, f32[8,12,152]{2,1,0:T(8,128)S(1)}, u32[]{:S(2)}, u32[]{:S(2)}) collective-permute-start(f32[8,12,152]{2,1,0:T(8,128)S(1)} %pad_maximum_fusion.11), channel_id=1, source_target_pairs={{8,0},{16,8},{24,16},{0,24},{9,1},{17,9},{25,17},{1,25},{10,2},{18... | collective-permute-start | bytes 175112 | tf_op jit(solution)/shard_map/ppermute | solution.py:40
  47.1 3.1 %collective-permute-start.7 = (f32[6,4,16,128]{3,2,1,0:T(8,128)S(1)}, f32[6,4,16,128]{3,2,1,0:T(8,128)S(1)}, u32[]{:S(2)}, u32[]{:S(2)}) collective-permute-start(f32[6,4,16,128]{3,2,1,0:T(8,128)S(1)} %constant_dynamic-slice_fusion), channel_id=1, source_target_pairs={{0,1},{1,0},{2,3},{3,2},{4,5},{5,4},{6,7},{7,6},{8,9},{9,8},{10,11... | collective-permute-start | bytes 589832 | tf_op jit(solution)/shard_map/ppermute | solution.py:116

commit v12 on v7

--- a/solution.py
+++ b/solution.py
@@ -271,7 +271,7 @@
             new_grains = crop(grains, e_width, next_e) - allen_step * (
                 crop(grain_drive, both, next_e) - allen_gradient * grain_spread
             )
-            grains = in_domain(new_grains, next_e, geometry)
+            grains = lax.optimization_barrier(in_domain(new_grains, next_e, geometry))
         density = in_domain(new_density, need_d[moment + 1], geometry)
     d_width = need_d[STEPS]
 

time: 51.1 us -> 54.6 us (1.068)
  waiting for transfers between devices: 10.8 us -> 14 us
    select_n x11 -> x13, other arithmetic: 6.49 us -> 11.4 us  [in_domain(): return jnp.where(radial_mask(width, geometry), x, 0.0)]
    reduce_sum x2, other arithmetic: 3.17 us -> 0.66 us  [chemical(): cube_sum = jnp.sum(grains * grains * grains, axis=0)]
    reduce_sum x1, other arithmetic: 2.25 us -> 0.21 us  [chemical(): square_sum = jnp.sum(grains * grains, axis=0)]
    ppermute x2, waiting for transfers between devices: 4.85 us -> 6.78 us  [azim_exchange(): after = lax.ppermute(leading, 'azim', down)]
    ppermute x2, waiting for transfers between devices: 4.52 us -> 5.78 us  [azim_exchange(): before = lax.ppermute(last, 'azim', up)]
    reduce_sum x1 -> x2, other arithmetic: 0.24 us -> 0.88 us  [chemical_pullback(): jnp.sum(codrive * drive_slope, axis=0)]
    slice x1 -> x0, other arithmetic: 0.6 us -> none  [crop(): return x[..., cut:x.shape[-2] - cut, cut:x.shape[-1] - cut]]
  transfers between devices with their start and end apart: 8 -> 8, of which waited for: 5 -> 6; matrix products, arithmetic and copies ran while one was open for 11% -> 6% of each run, Pallas kernels for 0% -> 0%
where the time goes in v12:
time: 54.6 us; the launch traced here: 54.3 us
  other arithmetic  19.9 us (36%)
  starting transfers between devices  14.2 us (26%)
  waiting for transfers between devices  14 us (26%)
  local copies, waits for them, and re-layouts  4.75 us (9%)
  between operations  1.47 us (3%)
    select_n x13, other arithmetic, in_domain(): return jnp.where(radial_mask(width, geometry), x, 0.0)  11.4 us
    ppermute x2, waiting for transfers between devices, azim_exchange(): after = lax.ppermute(leading, 'azim', down)  6.78 us
    ppermute x2, waiting for transfers between devices, azim_exchange(): before = lax.ppermute(last, 'azim', up)  5.78 us
    ppermute x1, starting transfers between devices, edge_columns(): lax.ppermute(jnp.where(own == 0, first, last), ('rad', 'hgt'), cross)  4.68 us
    ppermute x2, starting transfers between devices, azim_exchange(): before = lax.ppermute(last, 'azim', up)  2.71 us
    slice x15, local copies, waits for them, and re-layouts, crop(): return x[..., cut:x.shape[-2] - cut, cut:x.shape[-1] - cut]  2.63 us
    ppermute x2, starting transfers between devices, azim_exchange(): after = lax.ppermute(leading, 'azim', down)  2.41 us
    ppermute x1, starting transfers between devices, edge_columns(): lax.ppermute(jnp.where(own == 0, last, first), ('rad', 'hgt'), same)  1.92 us
  transfers between devices with their start and end apart: 8, of which 6 were waited for; matrix products, arithmetic and copies ran while one was open for 6% of the time, Pallas kernels for 0%

profile of v12, /device:TPU:9, one launch (start us, length us, event | category | flops | bytes accessed | tf_op | source)
XLA Modules:
  0.0 54.3 jit_solution(5909192563185261757)
XLA Ops:
  0.7 0.9 %convert_bitcast_fusion = (f32[1,4,16,256]{3,2,1,0:T(8,128)S(1)}, f32[1,4,16,256]{3,2,1,0:T(8,128)S(1)}) fusion(s32[4,16,256]{2,1,0:T(8,128)} %param.7, s32[4,16,256]{2,1,0:T(8,128)} %param.5), kind=kLoop, calls=%fused_computation.325 | loop fusion | flops 32768 | bytes 262144 | tf_op jit(solution)/shard_map/stack | solution.py:234
  1.6 0.9 %pad_maximum_fusion.8 = f32[4,4,16,256]{3,2,1,0:T(8,128)S(1)} fusion(f32[1,4,16,256]{3,2,1,0:T(8,128)S(1)} %get-tuple-element.143, f32[1,4,16,256]{3,2,1,0:T(8,128)} %bitcast.22, f32[1,4,16,256]{3,2,1,0:T(8,128)S(1)} %get-tuple-element.144, f32[1,4,16,256]{3,2,1,0:T(8,128)} %bitcast.24), kind=kLoop, calls=%fused_computation.211 | loop fusion | flops 196608 | bytes 524288 | tf_op jit(solution)/shard_map/stack | solution.py:234
  2.5 0.7 %collective-permute-start.2 = (f32[4,4,16,256]{3,2,1,0:T(8,128)S(1)}, f32[4,4,16,256]{3,2,1,0:T(8,128)S(1)}, u32[]{:S(2)}, u32[]{:S(2)}) collective-permute-start(f32[4,4,16,256]{3,2,1,0:T(8,128)S(1)} %pad_maximum_fusion.8), channel_id=1, source_target_pairs={{0,1},{1,0},{2,3},{3,2},{4,5},{5,4},{6,7},{7,6},{8,9},{9,8},{10,11... | collective-permute-start | bytes 786440 | tf_op jit(solution)/shard_map/ppermute | solution.py:55
  3.2 0.1 slice_select_fusion.1
  3.3 1.9 %collective-permute-start = (f32[4,4,16,12]{3,2,1,0:T(8,128)S(1)}, f32[4,4,16,12]{3,2,1,0:T(8,128)S(1)}, u32[]{:S(2)}, u32[]{:S(2)}) collective-permute-start(f32[4,4,16,12]{3,2,1,0:T(8,128)S(1)} %get-tuple-element.79), channel_id=1, source_target_pairs={{0,2},{3,1},{2,4},{5,3},{4,6},{7,5},{8,10},{11,9},{10,12},{13,11},... | collective-permute-start | bytes 36872 | tf_op jit(solution)/shard_map/ppermute | solution.py:94
  5.2 4.7 %collective-permute-start.1 = (f32[4,4,16,12]{3,2,1,0:T(8,128)S(1)}, f32[4,4,16,12]{3,2,1,0:T(8,128)S(1)}, u32[]{:S(2)}, u32[]{:S(2)}) collective-permute-start(f32[4,4,16,12]{3,2,1,0:T(8,128)S(1)} %get-tuple-element.80), channel_id=1, source_target_pairs={{1,2},{2,1},{3,4},{4,3},{5,6},{6,5},{9,10},{10,9},{11,12},{12,11},... | collective-permute-start | bytes 36872 | tf_op jit(solution)/shard_map/ppermute | solution.py:93
  10.4 0.1 fusion.169
  10.6 0.1 fusion.173
  10.7 0.1 fusion.168
  10.9 0.1 fusion.177
  11.4 0.1 broadcast_add_fusion.4
  12.3 0.4 collective-permute-done.1
  12.8 0.4 fusion.44
  13.4 1.3 %collective-permute-start.3 = (f32[8,23,152]{2,1,0:T(8,128)S(1)}, f32[8,23,152]{2,1,0:T(8,128)S(1)}, u32[]{:S(2)}, u32[]{:S(2)}) collective-permute-start(f32[8,23,152]{2,1,0:T(8,128)S(1)} %pad_maximum_fusion.9), channel_id=1, source_target_pairs={{0,8},{8,16},{16,24},{24,0},{1,9},{9,17},{17,25},{25,1},{2,10},{10... | collective-permute-start | bytes 335624 | tf_op jit(solution)/shard_map/ppermute | solution.py:39
  14.7 1.2 %collective-permute-start.4 = (f32[8,23,152]{2,1,0:T(8,128)S(1)}, f32[8,23,152]{2,1,0:T(8,128)S(1)}, u32[]{:S(2)}, u32[]{:S(2)}) collective-permute-start(f32[8,23,152]{2,1,0:T(8,128)S(1)} %pad_maximum_fusion.10), channel_id=1, source_target_pairs={{8,0},{16,8},{24,16},{0,24},{9,1},{17,9},{25,17},{1,25},{10,2},{18... | collective-permute-start | bytes 335624 | tf_op jit(solution)/shard_map/ppermute | solution.py:40
  15.9 4.5 %collective-permute-done.3 = f32[8,23,152]{2,1,0:T(8,128)S(1)} collective-permute-done((f32[8,23,152]{2,1,0:T(8,128)S(1)}, f32[8,23,152]{2,1,0:T(8,128)S(1)}, u32[]{:S(2)}, u32[]{:S(2)}) %collective-permute-start.3) | collective-permute-done | bytes 111904 | tf_op jit(solution)/shard_map/ppermute | solution.py:39
  20.4 4.3 %collective-permute-done.4 = f32[8,23,152]{2,1,0:T(8,128)S(1)} collective-permute-done((f32[8,23,152]{2,1,0:T(8,128)S(1)}, f32[8,23,152]{2,1,0:T(8,128)S(1)}, u32[]{:S(2)}, u32[]{:S(2)}) %collective-permute-start.4) | collective-permute-done | bytes 111904 | tf_op jit(solution)/shard_map/ppermute | solution.py:40
  24.8 0.2 pad_maximum_fusion.1
  25.0 0.4 multiply_reduce_fusion.2
  25.4 0.2 slice.937
  25.6 0.6 %fusion.48 = (f32[8,38,150]{2,1,0:T(8,128)S(1)}, f32[8,38,150]{2,1,0:T(8,128)S(1)}, f32[8,38,150]{2,1,0:T(8,128)S(1)}) fusion(f32[8,40,152]{2,1,0:T(8,128)S(1)} %broadcast_select_fusion, f32[8,38,150]{2,1,0:T(8,128)S(1)} %get-tuple-element.17, f32[8,38,150]{2,1,0:T(8,128)S(1)} %get-tuple-element.18, f32[8,150]{1,0:T(8,128)S(1)} %broadcast_add_fusion.10, ...), kind=kLoop, calls=%fused_computation.104 | loop fusion | flops 1048800 | bytes 3179904 | tf_op jit(solution)/shard_map/sub | solution.py:264
  26.2 0.2 slice.934
  26.3 0.2 slice.936
  26.5 0.4 slice.942
  26.9 2.7 %fusion.6 = f32[4,8,34,146]{3,2,1,0:T(8,128)S(1)} fusion(f32[4,8,36,148]{3,2,1,0:T(8,128)S(1)} %slice.942, f32[4,8,38,150]{3,2,1,0:T(8,128)S(1)} %get-tuple-element.62, f32[4,8,38,150]{3,2,1,0:T(8,128)S(1)} %get-tuple-element.61, f32[8,34,146]{2,1,0:T(8,128)S(1)} %slice.937, f32[8,34,146]{2,1,0:T(8,128)S(1)} %slice.936, f32[8,34,146]{2,1,0:T(8,128)S(1)} %slice.934, ...), kind=kLoop, calls=%fused_computation.12 | loop fusion | flops 3176960 | bytes 5612842 | tf_op jit(solution)/shard_map/jit(_where)/select_n | solution.py:145
  29.7 0.3 multiply_reduce_fusion.1
  29.9 0.4 slice.964
  30.3 0.1 slice.959
  30.4 0.6 %fusion.54 = f32[8,36,148]{2,1,0:T(8,128)S(1)} fusion(f32[8,38,150]{2,1,0:T(8,128)S(1)} %get-tuple-element.72, f32[8,40,152]{2,1,0:T(8,128)S(1)} %broadcast_select_fusion, f32[8,148]{1,0:T(8,128)S(1)} %broadcast_add_fusion.9, f32[148]{0:T(256)S(1)} %get-tuple-element.134, f32[148]{0:T(256)S(1)} %get-tuple-element.132, f32[148]{0:T(256)S(1)} %get-tuple-element.131, ...), kind=kLoop, calls=%fused_computation.110 | loop fusion | flops 554112 | bytes 2476032 | tf_op jit(solution)/shard_map/jit(_where)/select_n | solution.py:145
  31.1 0.6 %slice_subtract_fusion.1 = (f32[8,34,146]{2,1,0:T(8,128)S(1)}, f32[8,34,146]{2,1,0:T(8,128)S(1)}, f32[8,34,146]{2,1,0:T(8,128)S(1)}) fusion(f32[8,36,148]{2,1,0:T(8,128)S(1)} %fusion.54, f32[8,146]{1,0:T(8,128)S(1)} %broadcast_add_fusion.8, f32[146]{0:T(256)S(1)} %get-tuple-element.142, f32[146]{0:T(256)S(1)} %get-tuple-element.140, ...), kind=kLoop, calls=%fused_computation.138 | loop fusion | flops 913376 | bytes 3109248 | tf_op jit(solution)/shard_map/sub | solution.py:182
  31.7 0.1 slice.956
  31.8 0.1 slice.958
  32.0 2.2 %fusion.19 = f32[4,8,30,142]{3,2,1,0:T(8,128)S(1)} fusion(f32[4,8,32,144]{3,2,1,0:T(8,128)S(1)} %slice.964, f32[4,8,34,146]{3,2,1,0:T(8,128)S(1)} %fusion.6, f32[4,8,34,146]{3,2,1,0:T(8,128)S(1)} %get-tuple-element.52, f32[8,30,142]{2,1,0:T(8,128)S(1)} %slice.959, f32[8,30,142]{2,1,0:T(8,128)S(1)} %slice.958, f32[8,30,142]{2,1,0:T(8,128)S(1)} %slice.956, ...), kind=kLoop, calls=%fused_computation.36 | loop fusion | flops 2726400 | bytes 4822134 | tf_op jit(solution)/shard_map/jit(_where)/select_n | solution.py:145
  34.2 0.2 multiply_reduce_fusion
  34.4 0.3 slice.1004
  34.7 0.4 slice-done
  35.2 1.4 %collective-permute-start.5 = (f32[8,12,152]{2,1,0:T(8,128)S(1)}, f32[8,12,152]{2,1,0:T(8,128)S(1)}, u32[]{:S(2)}, u32[]{:S(2)}) collective-permute-start(f32[8,12,152]{2,1,0:T(8,128)S(1)} %pad_maximum_fusion.11), channel_id=1, source_target_pairs={{0,8},{8,16},{16,24},{24,0},{1,9},{9,17},{17,25},{25,1},{2,10},{10... | collective-permute-start | bytes 175112 | tf_op jit(solution)/shard_map/ppermute | solution.py:39
  36.6 0.5 fusion.87
  37.2 0.5 fusion.71
  37.7 1.2 %collective-permute-start.6 = (f32[8,12,152]{2,1,0:T(8,128)S(1)}, f32[8,12,152]{2,1,0:T(8,128)S(1)}, u32[]{:S(2)}, u32[]{:S(2)}) collective-permute-start(f32[8,12,152]{2,1,0:T(8,128)S(1)} %pad_maximum_fusion.12), channel_id=1, source_target_pairs={{8,0},{16,8},{24,16},{0,24},{9,1},{17,9},{25,17},{1,25},{10,2},{18... | collective-permute-start | bytes 175112 | tf_op jit(solution)/shard_map/ppermute | solution.py:40
  38.9 1.3 %collective-permute-done.5 = f32[8,12,152]{2,1,0:T(8,128)S(1)} collective-permute-done((f32[8,12,152]{2,1,0:T(8,128)S(1)}, f32[8,12,152]{2,1,0:T(8,128)S(1)}, u32[]{:S(2)}, u32[]{:S(2)}) %collective-permute-start.5) | collective-permute-done | bytes 58400 | tf_op jit(solution)/shard_map/ppermute | solution.py:39
  40.2 2.5 %collective-permute-done.6 = f32[8,12,152]{2,1,0:T(8,128)S(1)} collective-permute-done((f32[8,12,152]{2,1,0:T(8,128)S(1)}, f32[8,12,152]{2,1,0:T(8,128)S(1)}, u32[]{:S(2)}, u32[]{:S(2)}) %collective-permute-start.6) | collective-permute-done | bytes 58400 | tf_op jit(solution)/shard_map/ppermute | solution.py:40
  42.7 0.8 %fusion.102 = (f32[8,28,140]{2,1,0:T(8,128)S(1)}, f32[8,28,140]{2,1,0:T(8,128)S(1)}) fusion(f32[8,6,152]{2,1,0:T(8,128)S(1)} %get-tuple-element.86, f32[8,16,152]{2,1,0:T(8,128)S(1)} %get-tuple-element.77, f32[8,6,152]{2,1,0:T(8,128)S(1)} %get-tuple-element.84, f32[8,6,152]{2,1,0:T(8,128)S(1)} %get-tuple-element.85, ...), kind=kLoop, calls=%fused_computation.187 | loop fusion | flops 627200 | bytes 2621952 | tf_op jit(solution)/shard_map/jit(_where)/select_n | solution.py:145
  43.5 0.5 broadcast_select_fusion.1
  43.9 0.5 fusion.131
  44.5 0.1 slice.1006
  44.6 0.6 %multiply_reduce_fusion.5 = (f32[8,20,132]{2,1,0:T(8,128)S(1)}, f32[8,20,132]{2,1,0:T(8,128)S(1)}, f32[8,20,132]{2,1,0:T(8,128)S(1)}, f32[4,8,20,132]{3,2,1,0:T(...) fusion(f32[4,8,34,146]{3,2,1,0:T(8,128)S(1)} %fusion.6, f32[8,20,132]{2,1,0:T(8,128)S(1)} %slice.1006, ...), kind=kLoop, calls=%fused_computation.76 | loop fusion | flops 1034880 | bytes 2027652 | tf_op jit(solution)/shard_map/reduce_sum | solution.py:213
  45.2 0.4 broadcast_select_fusion.3
  45.6 0.5 fusion.120
  46.1 0.1 slice.1023
  46.3 0.1 slice.1024
  46.4 0.1 slice.1028
  46.5 0.1 slice.1029
  46.7 0.1 slice.1026
  46.8 1.7 %fusion.34 = f32[4,8,18,130]{3,2,1,0:T(8,128)S(1)} fusion(f32[4,8,20,132]{3,2,1,0:T(8,128)S(1)} %get-tuple-element.35, f32[4,8,20,132]{3,2,1,0:T(8,128)S(1)} %get-tuple-element.54, f32[4,8,20,132]{3,2,1,0:T(8,128)S(1)} %get-tuple-element.53, f32[8,18,130]{2,1,0:T(8,128)S(1)} %slice.1029, f32[8,18,130]{2,1,0:T(8,128)S(1)} %slice.1028, ...), kind=kLoop, calls=%fused_computation.59 | loop fusion | flops 1722240 | bytes 7585792 | tf_op jit(solution)/shard_map/jit(_where)/select_n | solution.py:145
  48.5 0.2 multiply_reduce_fusion.9
  48.7 0.4 broadcast_select_fusion.2
  49.1 0.1 slice_bitcast_fusion.6
  49.2 0.2 fusion.161
  49.4 0.6 %fusion.93 = f32[4,8,16,128]{3,2,1,0:T(8,128)S(1)} fusion(f32[4,8,18,130]{3,2,1,0:T(8,128)S(1)} %fusion.34, f32[4,8,38,150]{3,2,1,0:T(8,128)S(1)} %get-tuple-element.62, f32[8,128]{1,0:T(8,128)S(1)} %broadcast_add_fusion.11, f32[128]{0:T(128)S(1)} %get-tuple-element.102, f32[128]{0:T(128)S(1)} %get-tuple-element.100, f32[128]{0:T(128)S(1)} %get-tuple-element.99, ...), kind=kLoop, calls=%fused_computation.170 | loop fusion | flops 1638400 | bytes 2955264 | tf_op jit(solution)/shard_map/jit(_where)/select_n | solution.py:145
  50.1 1.8 %collective-permute-start.7 = (f32[6,4,16,128]{3,2,1,0:T(8,128)S(1)}, f32[6,4,16,128]{3,2,1,0:T(8,128)S(1)}, u32[]{:S(2)}, u32[]{:S(2)}) collective-permute-start(f32[6,4,16,128]{3,2,1,0:T(8,128)S(1)} %get-tuple-element.60), channel_id=1, source_target_pairs={{0,1},{1,0},{2,3},{3,2},{4,5},{5,4},{6,7},{7,6},{8,9},{9,8},{10,11... | collective-permute-start | bytes 589832 | tf_op jit(solution)/shard_map/ppermute | solution.py:116
  51.9 1.1 %collective-permute-done.7 = f32[6,4,16,128]{3,2,1,0:T(8,128)S(1)} collective-permute-done((f32[6,4,16,128]{3,2,1,0:T(8,128)S(1)}, f32[6,4,16,128]{3,2,1,0:T(8,128)S(1)}, u32[]{:S(2)}, u32[]{:S(2)}) %collective-permute-start.7) | collective-permute-done | bytes 196640 | tf_op jit(solution)/shard_map/ppermute | solution.py:116
  53.0 0.7 %slice.1047 = f32[4,4,16,256]{3,2,1,0:T(8,128)} slice(f32[6,4,16,256]{3,2,1,0:T(8,128)S(1)} %maximum_select_fusion.1), slice={[2:6], [0:4], [0:16], [0:256]} | slice | bytes 524288 | tf_op jit(solution)/shard_map/slice | solution.py:322
  53.7 0.7 %slice_bitcast_fusion.4 = (f32[4,16,256]{2,1,0:T(8,128)}, f32[4,16,256]{2,1,0:T(8,128)}) fusion(f32[6,4,16,256]{3,2,1,0:T(8,128)S(1)} %maximum_select_fusion.1), kind=kLoop, calls=%fused_computation.314 | loop fusion | bytes 262144 | tf_op jit(solution)/shard_map/squeeze | solution.py:322
  (91 shorter events, 2.2 us)
Async XLA Ops:
  0.6 12.1 %copy-start.2 = (f32[4,16,256]{2,1,0:T(8,128)S(1)}, f32[4,16,256]{2,1,0:T(8,128)}, u32[]{:S(2)}) copy-start(f32[4,16,256]{2,1,0:T(8,128)} %param.4) | copy-start | bytes 196612
  0.6 12.1 %copy-start.1 = (f32[4,16,256]{2,1,0:T(8,128)S(1)}, f32[4,16,256]{2,1,0:T(8,128)}, u32[]{:S(2)}) copy-start(f32[4,16,256]{2,1,0:T(8,128)} %param.6) | copy-start | bytes 196612
  2.5 10.3 %collective-permute-start.2 = (f32[4,4,16,256]{3,2,1,0:T(8,128)S(1)}, f32[4,4,16,256]{3,2,1,0:T(8,128)S(1)}, u32[]{:S(2)}, u32[]{:S(2)}) collective-permute-start(f32[4,4,16,256]{3,2,1,0:T(8,128)S(1)} %pad_maximum_fusion.8), channel_id=1, source_target_pairs={{0,1},{1,0},{2,3},{3,2},{4,5},{5,4},{6,7},{7,6},{8,9},{9,8},{10,11... | collective-permute-start | bytes 786440 | tf_op jit(solution)/shard_map/ppermute | solution.py:55
  3.3 9.0 %collective-permute-start = (f32[4,4,16,12]{3,2,1,0:T(8,128)S(1)}, f32[4,4,16,12]{3,2,1,0:T(8,128)S(1)}, u32[]{:S(2)}, u32[]{:S(2)}) collective-permute-start(f32[4,4,16,12]{3,2,1,0:T(8,128)S(1)} %get-tuple-element.79), channel_id=1, source_target_pairs={{0,2},{3,1},{2,4},{5,3},{4,6},{7,5},{8,10},{11,9},{10,12},{13,11},... | collective-permute-start | bytes 36872 | tf_op jit(solution)/shard_map/ppermute | solution.py:94
  5.2 7.5 %collective-permute-start.1 = (f32[4,4,16,12]{3,2,1,0:T(8,128)S(1)}, f32[4,4,16,12]{3,2,1,0:T(8,128)S(1)}, u32[]{:S(2)}, u32[]{:S(2)}) collective-permute-start(f32[4,4,16,12]{3,2,1,0:T(8,128)S(1)} %get-tuple-element.80), channel_id=1, source_target_pairs={{1,2},{2,1},{3,4},{4,3},{5,6},{6,5},{9,10},{10,9},{11,12},{12,11},... | collective-permute-start | bytes 36872 | tf_op jit(solution)/shard_map/ppermute | solution.py:93
  13.3 2.6 %copy-start = (f32[4,8,16,152]{3,2,1,0:T(8,128)}, f32[4,8,16,152]{3,2,1,0:T(8,128)S(1)}, u32[]{:S(2)}) copy-start(f32[4,8,16,152]{3,2,1,0:T(8,128)S(1)} %fusion.44) | copy-start | bytes 933892
  13.4 7.0 %collective-permute-start.3 = (f32[8,23,152]{2,1,0:T(8,128)S(1)}, f32[8,23,152]{2,1,0:T(8,128)S(1)}, u32[]{:S(2)}, u32[]{:S(2)}) collective-permute-start(f32[8,23,152]{2,1,0:T(8,128)S(1)} %pad_maximum_fusion.9), channel_id=1, source_target_pairs={{0,8},{8,16},{16,24},{24,0},{1,9},{9,17},{17,25},{25,1},{2,10},{10... | collective-permute-start | bytes 335624 | tf_op jit(solution)/shard_map/ppermute | solution.py:39
  14.7 10.0 %collective-permute-start.4 = (f32[8,23,152]{2,1,0:T(8,128)S(1)}, f32[8,23,152]{2,1,0:T(8,128)S(1)}, u32[]{:S(2)}, u32[]{:S(2)}) collective-permute-start(f32[8,23,152]{2,1,0:T(8,128)S(1)} %pad_maximum_fusion.10), channel_id=1, source_target_pairs={{8,0},{16,8},{24,16},{0,24},{9,1},{17,9},{25,17},{1,25},{10,2},{18... | collective-permute-start | bytes 335624 | tf_op jit(solution)/shard_map/ppermute | solution.py:40
  34.2 1.0 %slice-start = ((f32[4,8,16,152]{3,2,1,0:T(8,128)}), f32[2,8,16,152]{3,2,1,0:T(8,128)S(1)}, s32[]{:S(2)}) async-start(f32[4,8,16,152]{3,2,1,0:T(8,128)} %copy-done), calls=%async_computation | async-start | bytes 524288 | tf_op jit(solution)/shard_map/slice | solution.py:246
  35.2 5.0 %collective-permute-start.5 = (f32[8,12,152]{2,1,0:T(8,128)S(1)}, f32[8,12,152]{2,1,0:T(8,128)S(1)}, u32[]{:S(2)}, u32[]{:S(2)}) collective-permute-start(f32[8,12,152]{2,1,0:T(8,128)S(1)} %pad_maximum_fusion.11), channel_id=1, source_target_pairs={{0,8},{8,16},{16,24},{24,0},{1,9},{9,17},{17,25},{25,1},{2,10},{10... | collective-permute-start | bytes 175112 | tf_op jit(solution)/shard_map/ppermute | solution.py:39
  37.7 5.0 %collective-permute-start.6 = (f32[8,12,152]{2,1,0:T(8,128)S(1)}, f32[8,12,152]{2,1,0:T(8,128)S(1)}, u32[]{:S(2)}, u32[]{:S(2)}) collective-permute-start(f32[8,12,152]{2,1,0:T(8,128)S(1)} %pad_maximum_fusion.12), channel_id=1, source_target_pairs={{8,0},{16,8},{24,16},{0,24},{9,1},{17,9},{25,17},{1,25},{10,2},{18... | collective-permute-start | bytes 175112 | tf_op jit(solution)/shard_map/ppermute | solution.py:40
  50.1 2.8 %collective-permute-start.7 = (f32[6,4,16,128]{3,2,1,0:T(8,128)S(1)}, f32[6,4,16,128]{3,2,1,0:T(8,128)S(1)}, u32[]{:S(2)}, u32[]{:S(2)}) collective-permute-start(f32[6,4,16,128]{3,2,1,0:T(8,128)S(1)} %get-tuple-element.60), channel_id=1, source_target_pairs={{0,1},{1,0},{2,3},{3,2},{4,5},{5,4},{6,7},{7,6},{8,9},{9,8},{10,11... | collective-permute-start | bytes 589832 | tf_op jit(solution)/shard_map/ppermute | solution.py:116

commit v13 on v10

--- a/solution.py
+++ b/solution.py
@@ -244,9 +244,6 @@
         trim(f, w) for f, w in zip(azim_exchange([packed[0], packed[1]], widths[:2]), widths[:2])
     ]
     misfit_terms = packed[2:]
-    observed, measured = [
-        trim(f, w) for f, w in zip(azim_exchange([misfit_terms[0], misfit_terms[1]], widths[2:]), widths[2:])
-    ]
     grains = (
         grain_label[None] == jnp.arange(GRAINS, dtype=jnp.float32)[:, None, None, None]
     ).astype(jnp.float32)
@@ -273,6 +270,12 @@
             )
             grains = in_domain(new_grains, next_e, geometry)
         density = in_domain(new_density, need_d[moment + 1], geometry)
+        if moment == 0:
+            misfit_terms, marker = lax.optimization_barrier((misfit_terms, density[0, 0, 0]))
+            observed, measured = [
+                trim(f, w)
+                for f, w in zip(azim_exchange([misfit_terms[0], misfit_terms[1]], widths[2:]), widths[2:])
+            ]
     d_width = need_d[STEPS]
 
     observed = crop(observed, widths[2], d_width)

time: 52.7 us -> 53.3 us (1.011)
  the two profiles are of different devices: /device:TPU:9 before, /device:TPU:0 now
where the time goes in v13:
time: 53.3 us; the launch traced here: 53 us
  other arithmetic  19.7 us (37%)
  waiting for transfers between devices  14.3 us (27%)
  starting transfers between devices  13.1 us (25%)
  local copies, waits for them, and re-layouts  4.51 us (8%)
  between operations  1.5 us (3%)
    ppermute x2, waiting for transfers between devices, azim_exchange(): after = lax.ppermute(leading, 'azim', down)  9.07 us
    select_n x11, other arithmetic, in_domain(): return jnp.where(radial_mask(width, geometry), x, 0.0)  6.54 us
    ppermute x2, starting transfers between devices, azim_exchange(): after = lax.ppermute(leading, 'azim', down)  5.99 us
    ppermute x1, starting transfers between devices, edge_columns(): lax.ppermute(jnp.where(own == 0, last, first), ('rad', 'hgt'), same)  5.76 us
    ppermute x2, waiting for transfers between devices, azim_exchange(): before = lax.ppermute(last, 'azim', up)  3.68 us
    reduce_sum x2, other arithmetic, chemical(): cube_sum = jnp.sum(grains * grains * grains, axis=0)  3.17 us
    slice x15, local copies, waits for them, and re-layouts, crop(): return x[..., cut:x.shape[-2] - cut, cut:x.shape[-1] - cut]  2.81 us
    reduce_sum x1, other arithmetic, chemical(): square_sum = jnp.sum(grains * grains, axis=0)  2.25 us
  transfers between devices with their start and end apart: 8, of which 4 were waited for; matrix products, arithmetic and copies ran while one was open for 4% of the time, Pallas kernels for 0%

profile of v13, /device:TPU:0, one launch (start us, length us, event | category | flops | bytes accessed | tf_op | source)
XLA Modules:
  0.0 53.0 jit_solution(9846593343724994773)
XLA Ops:
  0.7 0.9 %convert_bitcast_fusion = (f32[1,4,16,256]{3,2,1,0:T(8,128)S(1)}, f32[1,4,16,256]{3,2,1,0:T(8,128)S(1)}) fusion(s32[4,16,256]{2,1,0:T(8,128)} %param.7, s32[4,16,256]{2,1,0:T(8,128)} %param.5), kind=kLoop, calls=%fused_computation.324 | loop fusion | flops 32768 | bytes 262144 | tf_op jit(solution)/shard_map/stack | solution.py:234
  1.6 0.9 %pad_maximum_fusion.7 = f32[4,4,16,256]{3,2,1,0:T(8,128)S(1)} fusion(f32[1,4,16,256]{3,2,1,0:T(8,128)S(1)} %get-tuple-element.144, f32[1,4,16,256]{3,2,1,0:T(8,128)} %bitcast.22, f32[1,4,16,256]{3,2,1,0:T(8,128)S(1)} %get-tuple-element.145, f32[1,4,16,256]{3,2,1,0:T(8,128)} %bitcast.24), kind=kLoop, calls=%fused_computation.211 | loop fusion | flops 196608 | bytes 524288 | tf_op jit(solution)/shard_map/stack | solution.py:234
  2.5 0.5 collective-permute-start.2
  3.0 0.1 slice_select_fusion.1
  3.1 0.7 %collective-permute-start.1 = (f32[4,4,16,12]{3,2,1,0:T(8,128)S(1)}, f32[4,4,16,12]{3,2,1,0:T(8,128)S(1)}, u32[]{:S(2)}, u32[]{:S(2)}) collective-permute-start(f32[4,4,16,12]{3,2,1,0:T(8,128)S(1)} %get-tuple-element.81), channel_id=1, source_target_pairs={{1,2},{2,1},{3,4},{4,3},{5,6},{6,5},{9,10},{10,9},{11,12},{12,11},... | collective-permute-start | bytes 36872 | tf_op jit(solution)/shard_map/ppermute | solution.py:93
  3.8 5.8 %collective-permute-start = (f32[4,4,16,12]{3,2,1,0:T(8,128)S(1)}, f32[4,4,16,12]{3,2,1,0:T(8,128)S(1)}, u32[]{:S(2)}, u32[]{:S(2)}) collective-permute-start(f32[4,4,16,12]{3,2,1,0:T(8,128)S(1)} %get-tuple-element.80), channel_id=1, source_target_pairs={{0,2},{3,1},{2,4},{5,3},{4,6},{7,5},{8,10},{11,9},{10,12},{13,11},... | collective-permute-start | bytes 36872 | tf_op jit(solution)/shard_map/ppermute | solution.py:94
  10.0 0.1 fusion.173
  10.2 0.1 fusion.169
  10.3 0.1 fusion.168
  10.5 0.1 fusion.172
  10.6 0.1 fusion.177
  10.8 0.1 fusion.176
  11.0 0.1 slice_divide_fusion.9
  11.0 0.1 broadcast_add_fusion.4
  11.2 0.1 broadcast_add_fusion.3
  11.4 0.1 broadcast_add_fusion.2
  11.5 0.1 broadcast_add_fusion.1
  11.7 0.1 broadcast_add_fusion
  11.8 0.1 broadcast_add_fusion.11
  12.1 0.4 fusion.44
  12.7 3.0 %collective-permute-start.4 = (f32[8,23,152]{2,1,0:T(8,128)S(1)}, f32[8,23,152]{2,1,0:T(8,128)S(1)}, u32[]{:S(2)}, u32[]{:S(2)}) collective-permute-start(f32[8,23,152]{2,1,0:T(8,128)S(1)} %pad_maximum_fusion.9), channel_id=1, source_target_pairs={{8,0},{16,8},{24,16},{0,24},{9,1},{17,9},{25,17},{1,25},{10,2},{18... | collective-permute-start | bytes 335624 | tf_op jit(solution)/shard_map/ppermute | solution.py:40
  15.9 3.0 %collective-permute-start.6 = (f32[8,12,152]{2,1,0:T(8,128)S(1)}, f32[8,12,152]{2,1,0:T(8,128)S(1)}, u32[]{:S(2)}, u32[]{:S(2)}) collective-permute-start(f32[8,12,152]{2,1,0:T(8,128)S(1)} %pad_maximum_fusion.11), channel_id=1, source_target_pairs={{8,0},{16,8},{24,16},{0,24},{9,1},{17,9},{25,17},{1,25},{10,2},{18... | collective-permute-start | bytes 175112 | tf_op jit(solution)/shard_map/ppermute | solution.py:40
  19.0 9.1 %collective-permute-done.6 = f32[8,12,152]{2,1,0:T(8,128)S(1)} collective-permute-done((f32[8,12,152]{2,1,0:T(8,128)S(1)}, f32[8,12,152]{2,1,0:T(8,128)S(1)}, u32[]{:S(2)}, u32[]{:S(2)}) %collective-permute-start.6) | collective-permute-done | bytes 58400 | tf_op jit(solution)/shard_map/ppermute | solution.py:40
  28.1 3.7 %collective-permute-done.5 = f32[8,12,152]{2,1,0:T(8,128)S(1)} collective-permute-done((f32[8,12,152]{2,1,0:T(8,128)S(1)}, f32[8,12,152]{2,1,0:T(8,128)S(1)}, u32[]{:S(2)}, u32[]{:S(2)}) %collective-permute-start.5) | collective-permute-done | bytes 58400 | tf_op jit(solution)/shard_map/ppermute | solution.py:39
  31.8 0.2 pad_maximum_fusion.1
  32.0 0.4 multiply_reduce_fusion.2
  32.4 0.4 slice.942
  32.9 0.2 slice.937
  33.1 0.6 %fusion.48 = (f32[8,38,150]{2,1,0:T(8,128)S(1)}, f32[8,38,150]{2,1,0:T(8,128)S(1)}, f32[8,38,150]{2,1,0:T(8,128)S(1)}) fusion(f32[8,40,152]{2,1,0:T(8,128)S(1)} %maximum_select_fusion.2, f32[8,38,150]{2,1,0:T(8,128)S(1)} %get-tuple-element.13, f32[8,38,150]{2,1,0:T(8,128)S(1)} %get-tuple-element.14, f32[8,150]{1,0:T(8,128)S(1)} %broadcast_add_fusion.10, ...), kind=kLoop, calls=%fused_computation.104 | loop fusion | flops 1048800 | bytes 3179904 | tf_op jit(solution)/shard_map/sub | solution.py:261
  33.7 0.2 slice.936
  33.9 0.2 slice.934
  34.0 2.8 %multiply_reduce_fusion.1 = (f32[8,34,146]{2,1,0:T(8,128)S(1)}, f32[8,34,146]{2,1,0:T(8,128)S(1)}, f32[4,8,34,146]{3,2,1,0:T(8,128)S(1)}) fusion(f32[8,146]{1,0:T(8,128)S(1)} %broadcast_add_fusion.8, f32[4,8,36,148]{3,2,1,0:T(8,128)S(1)} %slice.942, f32[4,8,38,150]{3,2,1,0:T(8,128)S(1)} %get-tuple-element.63, f32[146]{0:T(256)S(1)} %get-tuple-element.143, ...), kind=kLoop, calls=%fused_computation.23 | loop fusion | flops 3732928 | bytes 5930538 | tf_op jit(solution)/shard_map/reduce_sum | solution.py:181
  36.8 0.4 slice.964
  37.2 0.2 mul.1273
  37.4 0.1 slice.959
  37.5 0.6 %fusion.54 = f32[8,36,148]{2,1,0:T(8,128)S(1)} fusion(f32[8,38,150]{2,1,0:T(8,128)S(1)} %get-tuple-element.73, f32[8,40,152]{2,1,0:T(8,128)S(1)} %maximum_select_fusion.2, f32[8,148]{1,0:T(8,128)S(1)} %broadcast_add_fusion.9, f32[148]{0:T(256)S(1)} %get-tuple-element.135, f32[148]{0:T(256)S(1)} %get-tuple-element.133, f32[148]{0:T(256)S(1)} %get-tuple-element.132, ...), kind=kLoop, calls=%fused_computation.110 | loop fusion | flops 554112 | bytes 2476032 | tf_op jit(solution)/shard_map/jit(_where)/select_n | solution.py:145
  38.2 0.6 %slice_subtract_fusion.1 = (f32[8,34,146]{2,1,0:T(8,128)S(1)}, f32[8,34,146]{2,1,0:T(8,128)S(1)}, f32[8,34,146]{2,1,0:T(8,128)S(1)}) fusion(f32[8,36,148]{2,1,0:T(8,128)S(1)} %fusion.54, f32[8,146]{1,0:T(8,128)S(1)} %broadcast_add_fusion.8, f32[146]{0:T(256)S(1)} %get-tuple-element.143, f32[146]{0:T(256)S(1)} %get-tuple-element.141, ...), kind=kLoop, calls=%fused_computation.138 | loop fusion | flops 913376 | bytes 3109248 | tf_op jit(solution)/shard_map/sub | solution.py:182
  38.7 0.1 slice.958
  38.9 0.1 slice.956
  39.0 0.5 %fusion.87 = f32[8,32,144]{2,1,0:T(8,128)S(1)} fusion(f32[8,34,146]{2,1,0:T(8,128)S(1)} %get-tuple-element.72, f32[8,36,148]{2,1,0:T(8,128)S(1)} %fusion.54, f32[8,144]{1,0:T(8,128)S(1)} %broadcast_add_fusion.7, f32[144]{0:T(256)S(1)} %get-tuple-element.131, f32[144]{0:T(256)S(1)} %get-tuple-element.129, f32[144]{0:T(256)S(1)} %get-tuple-element.128, ...), kind=kLoop, calls=%fused_computation.164 | loop fusion | flops 479232 | bytes 2059776 | tf_op jit(solution)/shard_map/jit(_where)/select_n | solution.py:145
  39.5 2.3 %multiply_reduce_fusion = (f32[8,30,142]{2,1,0:T(8,128)S(1)}, f32[8,30,142]{2,1,0:T(8,128)S(1)}, f32[4,8,30,142]{3,2,1,0:T(8,128)S(1)}) fusion(f32[8,142]{1,0:T(8,128)S(1)} %broadcast_add_fusion.6, f32[4,8,32,144]{3,2,1,0:T(8,128)S(1)} %slice.964, f32[4,8,34,146]{3,2,1,0:T(8,128)S(1)} %get-tuple-element.47, f32[142]{0:T(256)S(1)} %get-tuple-element.127, ...), kind=kLoop, calls=%fused_computation.3 | loop fusion | flops 3203520 | bytes 5094774 | tf_op jit(solution)/shard_map/reduce_sum | solution.py:180
  41.8 0.5 fusion.71
  42.3 0.8 %fusion.102 = (f32[8,28,140]{2,1,0:T(8,128)S(1)}, f32[8,28,140]{2,1,0:T(8,128)S(1)}) fusion(f32[8,6,152]{2,1,0:T(8,128)S(1)} %get-tuple-element.87, f32[8,16,152]{2,1,0:T(8,128)S(1)} %get-tuple-element.78, f32[8,6,152]{2,1,0:T(8,128)S(1)} %get-tuple-element.85, f32[8,6,152]{2,1,0:T(8,128)S(1)} %get-tuple-element.86, ...), kind=kLoop, calls=%fused_computation.187 | loop fusion | flops 627200 | bytes 2621952 | tf_op jit(solution)/shard_map/jit(_where)/select_n | solution.py:145
  43.0 0.5 broadcast_select_fusion
  43.5 0.5 %fusion.131 = (f32[8,24,136]{2,1,0:T(8,128)S(1)}, f32[8,24,136]{2,1,0:T(8,128)S(1)}) fusion(f32[8,26,138]{2,1,0:T(8,128)S(1)} %get-tuple-element.29, f32[8,32,144]{2,1,0:T(8,128)S(1)} %fusion.87, f32[8,28,140]{2,1,0:T(8,128)S(1)} %get-tuple-element.34, f32[8,26,138]{2,1,0:T(8,128)S(1)} %get-tuple-element.30, f32[8,136]{1,0:T(8,128)S(1)} %broadcast_add_fusion.3, ...), kind=kLoop, calls=%fused_computation.243 | loop fusion | flops 548352 | bytes 2055680 | tf_op jit(solution)/shard_map/jit(_where)/select_n | solution.py:145
  44.0 0.3 slice.1009
  44.3 0.3 slice.1007
  44.6 0.6 %fusion.188 = (f32[4,8,20,132]{3,2,1,0:T(8,128)S(1)}, f32[4,8,20,132]{3,2,1,0:T(8,128)S(1)}, f32[8,20,132]{2,1,0:T(8,128)S(1)}, f32[8,20,132]{2,1,0:T(8,128)S(1)...) fusion(f32[4,8,34,146]{3,2,1,0:T(8,128)S(1)} %get-tuple-element.47, f32[8,20,132]{2,1,0:T(8,128)S(1)} %slice.1009, ...), kind=kLoop, calls=%fused_computation.455 | loop fusion | flops 1034880 | bytes 2027652 | tf_op jit(solution)/shard_map/slice | solution.py:135
  45.3 0.1 slice.1032
  45.4 0.4 broadcast_select_fusion.2
  45.8 0.5 fusion.120
  46.3 0.1 slice.1031
  46.4 0.1 slice.1029
  46.5 0.1 slice.1027
  46.7 0.1 slice.1026
  46.8 1.7 %fusion.34 = f32[4,8,18,130]{3,2,1,0:T(8,128)S(1)} fusion(f32[4,8,20,132]{3,2,1,0:T(8,128)S(1)} %get-tuple-element.55, f32[4,8,20,132]{3,2,1,0:T(8,128)S(1)} %get-tuple-element.51, f32[4,8,20,132]{3,2,1,0:T(8,128)S(1)} %get-tuple-element.50, f32[8,18,130]{2,1,0:T(8,128)S(1)} %slice.1032, f32[8,18,130]{2,1,0:T(8,128)S(1)} %slice.1031, ...), kind=kLoop, calls=%fused_computation.59 | loop fusion | flops 1722240 | bytes 7585792 | tf_op jit(solution)/shard_map/jit(_where)/select_n | solution.py:145
  48.5 0.2 multiply_reduce_fusion.9
  48.8 0.4 broadcast_select_fusion.1
  49.1 0.1 slice_bitcast_fusion.6
  49.2 0.2 fusion.161
  49.5 0.6 %fusion.93 = f32[4,8,16,128]{3,2,1,0:T(8,128)S(1)} fusion(f32[4,8,18,130]{3,2,1,0:T(8,128)S(1)} %fusion.34, f32[4,8,38,150]{3,2,1,0:T(8,128)S(1)} %get-tuple-element.63, f32[8,128]{1,0:T(8,128)S(1)} %broadcast_add_fusion.11, f32[128]{0:T(128)S(1)} %get-tuple-element.103, f32[128]{0:T(128)S(1)} %get-tuple-element.101, f32[128]{0:T(128)S(1)} %get-tuple-element.100, ...), kind=kLoop, calls=%fused_computation.170 | loop fusion | flops 1638400 | bytes 2955264 | tf_op jit(solution)/shard_map/jit(_where)/select_n | solution.py:145
  50.2 1.4 %collective-permute-done.7 = f32[6,4,16,128]{3,2,1,0:T(8,128)S(1)} collective-permute-done((f32[6,4,16,128]{3,2,1,0:T(8,128)S(1)}, f32[6,4,16,128]{3,2,1,0:T(8,128)S(1)}, u32[]{:S(2)}, u32[]{:S(2)}) %collective-permute-start.7) | collective-permute-done | bytes 196640 | tf_op jit(solution)/shard_map/ppermute | solution.py:116
  51.7 0.7 %slice_bitcast_fusion.4 = (f32[4,16,256]{2,1,0:T(8,128)}, f32[4,16,256]{2,1,0:T(8,128)}) fusion(f32[6,4,16,256]{3,2,1,0:T(8,128)S(1)} %maximum_select_fusion.1), kind=kLoop, calls=%fused_computation.313 | loop fusion | bytes 262144 | tf_op jit(solution)/shard_map/squeeze | solution.py:325
  52.3 0.7 %slice.1050 = f32[4,4,16,256]{3,2,1,0:T(8,128)} slice(f32[6,4,16,256]{3,2,1,0:T(8,128)S(1)} %maximum_select_fusion.1), slice={[2:6], [0:4], [0:16], [0:256]} | slice | bytes 524288 | tf_op jit(solution)/shard_map/slice | solution.py:325
  (86 shorter events, 1.9 us)
Async XLA Ops:
  0.6 11.4 %copy-start = (f32[4,16,256]{2,1,0:T(8,128)S(1)}, f32[4,16,256]{2,1,0:T(8,128)}, u32[]{:S(2)}) copy-start(f32[4,16,256]{2,1,0:T(8,128)} %param.6) | copy-start | bytes 196612
  0.6 11.4 %copy-start.1 = (f32[4,16,256]{2,1,0:T(8,128)S(1)}, f32[4,16,256]{2,1,0:T(8,128)}, u32[]{:S(2)}) copy-start(f32[4,16,256]{2,1,0:T(8,128)} %param.4) | copy-start | bytes 196612
  2.5 9.6 %collective-permute-start.2 = (f32[4,4,16,256]{3,2,1,0:T(8,128)S(1)}, f32[4,4,16,256]{3,2,1,0:T(8,128)S(1)}, u32[]{:S(2)}, u32[]{:S(2)}) collective-permute-start(f32[4,4,16,256]{3,2,1,0:T(8,128)S(1)} %pad_maximum_fusion.7), channel_id=1, source_target_pairs={{0,1},{1,0},{2,3},{3,2},{4,5},{5,4},{6,7},{7,6},{8,9},{9,8},{10,11... | collective-permute-start | bytes 786440 | tf_op jit(solution)/shard_map/ppermute | solution.py:55
  3.1 8.9 %collective-permute-start.1 = (f32[4,4,16,12]{3,2,1,0:T(8,128)S(1)}, f32[4,4,16,12]{3,2,1,0:T(8,128)S(1)}, u32[]{:S(2)}, u32[]{:S(2)}) collective-permute-start(f32[4,4,16,12]{3,2,1,0:T(8,128)S(1)} %get-tuple-element.81), channel_id=1, source_target_pairs={{1,2},{2,1},{3,4},{4,3},{5,6},{6,5},{9,10},{10,9},{11,12},{12,11},... | collective-permute-start | bytes 36872 | tf_op jit(solution)/shard_map/ppermute | solution.py:93
  3.8 8.3 %collective-permute-start = (f32[4,4,16,12]{3,2,1,0:T(8,128)S(1)}, f32[4,4,16,12]{3,2,1,0:T(8,128)S(1)}, u32[]{:S(2)}, u32[]{:S(2)}) collective-permute-start(f32[4,4,16,12]{3,2,1,0:T(8,128)S(1)} %get-tuple-element.80), channel_id=1, source_target_pairs={{0,2},{3,1},{2,4},{5,3},{4,6},{7,5},{8,10},{11,9},{10,12},{13,11},... | collective-permute-start | bytes 36872 | tf_op jit(solution)/shard_map/ppermute | solution.py:94
  12.7 19.1 %collective-permute-start.4 = (f32[8,23,152]{2,1,0:T(8,128)S(1)}, f32[8,23,152]{2,1,0:T(8,128)S(1)}, u32[]{:S(2)}, u32[]{:S(2)}) collective-permute-start(f32[8,23,152]{2,1,0:T(8,128)S(1)} %pad_maximum_fusion.9), channel_id=1, source_target_pairs={{8,0},{16,8},{24,16},{0,24},{9,1},{17,9},{25,17},{1,25},{10,2},{18... | collective-permute-start | bytes 335624 | tf_op jit(solution)/shard_map/ppermute | solution.py:40
  15.8 16.0 %collective-permute-start.3 = (f32[8,23,152]{2,1,0:T(8,128)S(1)}, f32[8,23,152]{2,1,0:T(8,128)S(1)}, u32[]{:S(2)}, u32[]{:S(2)}) collective-permute-start(f32[8,23,152]{2,1,0:T(8,128)S(1)} %pad_maximum_fusion.8), channel_id=1, source_target_pairs={{0,8},{8,16},{16,24},{24,0},{1,9},{9,17},{17,25},{25,1},{2,10},{10... | collective-permute-start | bytes 335624 | tf_op jit(solution)/shard_map/ppermute | solution.py:39
  15.9 12.1 %collective-permute-start.6 = (f32[8,12,152]{2,1,0:T(8,128)S(1)}, f32[8,12,152]{2,1,0:T(8,128)S(1)}, u32[]{:S(2)}, u32[]{:S(2)}) collective-permute-start(f32[8,12,152]{2,1,0:T(8,128)S(1)} %pad_maximum_fusion.11), channel_id=1, source_target_pairs={{8,0},{16,8},{24,16},{0,24},{9,1},{17,9},{25,17},{1,25},{10,2},{18... | collective-permute-start | bytes 175112 | tf_op jit(solution)/shard_map/ppermute | solution.py:40
  18.9 12.8 %collective-permute-start.5 = (f32[8,12,152]{2,1,0:T(8,128)S(1)}, f32[8,12,152]{2,1,0:T(8,128)S(1)}, u32[]{:S(2)}, u32[]{:S(2)}) collective-permute-start(f32[8,12,152]{2,1,0:T(8,128)S(1)} %pad_maximum_fusion.10), channel_id=1, source_target_pairs={{0,8},{8,16},{16,24},{24,0},{1,9},{9,17},{17,25},{25,1},{2,10},{10... | collective-permute-start | bytes 175112 | tf_op jit(solution)/shard_map/ppermute | solution.py:39
  50.1 1.5 %collective-permute-start.7 = (f32[6,4,16,128]{3,2,1,0:T(8,128)S(1)}, f32[6,4,16,128]{3,2,1,0:T(8,128)S(1)}, u32[]{:S(2)}, u32[]{:S(2)}) collective-permute-start(f32[6,4,16,128]{3,2,1,0:T(8,128)S(1)} %get-tuple-element.61), channel_id=1, source_target_pairs={{0,1},{1,0},{2,3},{3,2},{4,5},{5,4},{6,7},{7,6},{8,9},{9,8},{10,11... | collective-permute-start | bytes 589832 | tf_op jit(solution)/shard_map/ppermute | solution.py:116

commit v14 on v10

--- a/solution.py
+++ b/solution.py
@@ -231,22 +231,26 @@
         radius_rows * lax.axis_size("rad"),
         part,
     )
-    packed = jnp.stack([density, labels.astype(jnp.float32), observed, measured.astype(jnp.float32)])
-    if lax.axis_size("hgt") == 2:
-        received = edge_columns(packed, HALO)
-        packed = two_core_window(gather_axis(packed, "hgt", 1), received, HALO)
-    else:
-        packed = chip_window(gather_axis(packed, "hgt", 1), HALO)
     need_d, need_e, need_lc, need_lg = reach()
     widths = (need_d[0], need_e[0], need_lc[STEPS], need_lc[STEPS])
     trim = lambda f, w: f[..., HALO - w : f.shape[-1] - (HALO - w)]
-    density, grain_label = [
-        trim(f, w) for f, w in zip(azim_exchange([packed[0], packed[1]], widths[:2]), widths[:2])
-    ]
-    misfit_terms = packed[2:]
-    observed, measured = [
-        trim(f, w) for f, w in zip(azim_exchange([misfit_terms[0], misfit_terms[1]], widths[2:]), widths[2:])
-    ]
+    inputs = [density, labels.astype(jnp.float32), observed, measured.astype(jnp.float32)]
+    if lax.axis_size("hgt") == 2:
+        extended = azim_exchange(inputs, widths)
+        stacked = jnp.concatenate(extended, axis=-2)[None]
+        received = edge_columns(stacked, HALO)
+        stacked = two_core_window(gather_axis(stacked, "hgt", 1), received, HALO)[0]
+        fields, at = [], 0
+        for f, w in zip(extended, widths):
+            rows = f.shape[-2]
+            fields.append(trim(stacked[..., at : at + rows, :], w))
+            at += rows
+        density, grain_label, observed, measured = fields
+    else:
+        packed = chip_window(gather_axis(jnp.stack(inputs), "hgt", 1), HALO)
+        density, grain_label, observed, measured = [
+            trim(f, w) for f, w in zip(azim_exchange(list(packed), widths), widths)
+        ]
     grains = (
         grain_label[None] == jnp.arange(GRAINS, dtype=jnp.float32)[:, None, None, None]
     ).astype(jnp.float32)

time: 52.7 us -> 51 us (0.968)
  the two profiles are of different devices: /device:TPU:9 before, /device:TPU:0 now
where the time goes in v14:
time: 51 us; the launch traced here: 50.6 us
  other arithmetic  20.7 us (41%)
  starting transfers between devices  11.4 us (22%)
  waiting for transfers between devices  9.53 us (19%)
  local copies, waits for them, and re-layouts  7.54 us (15%)
  between operations  1.46 us (3%)
    select_n x11, other arithmetic, in_domain(): return jnp.where(radial_mask(width, geometry), x, 0.0)  6.59 us
    ppermute x1, starting transfers between devices, edge_columns(): lax.ppermute(jnp.where(own == 0, last, first), ('rad', 'hgt'), same)  5.27 us
    ppermute x1, waiting for transfers between devices, edge_columns(): lax.ppermute(jnp.where(own == 0, last, first), ('rad', 'hgt'), same)  3.94 us
    reduce_sum x2, other arithmetic, chemical(): cube_sum = jnp.sum(grains * grains * grains, axis=0)  3.17 us
    ppermute x1, starting transfers between devices, azim_exchange(): before = lax.ppermute(last, 'azim', up)  2.99 us
    slice x15, local copies, waits for them, and re-layouts, crop(): return x[..., cut:x.shape[-2] - cut, cut:x.shape[-1] - cut]  2.63 us
    ppermute x1, waiting for transfers between devices, azim_exchange(): after = lax.ppermute(leading, 'azim', down)  2.43 us
    reduce_sum x1, other arithmetic, chemical(): square_sum = jnp.sum(grains * grains, axis=0)  2.25 us
  transfers between devices with their start and end apart: 6, of which 4 were waited for; matrix products, arithmetic and copies ran while one was open for 5% of the time, Pallas kernels for 0%

profile of v14, /device:TPU:0, one launch (start us, length us, event | category | flops | bytes accessed | tf_op | source)
XLA Modules:
  0.0 50.6 jit_solution(4798047250209431823)
XLA Ops:
  0.7 0.9 %copy_convert_fusion = f32[4,16,256]{2,0,1:T(4,128)S(1)} fusion(s32[4,16,256]{2,1,0:T(8,128)} %param.7), kind=kLoop, calls=%fused_computation.311 | loop fusion | flops 16384 | bytes 131072 | tf_op jit(solution)/shard_map/convert_element_type | solution.py:237
  1.6 0.8 %fusion.192 = (f32[4,6,256]{2,1,0:T(8,128)S(1)}, f32[4,6,256]{2,1,0:T(8,128)S(1)}) fusion(f32[4,16,256]{2,1,0:T(8,128)} %param.6), kind=kLoop, calls=%fused_computation.459 | loop fusion | bytes 98304 | tf_op jit(solution)/shard_map/slice | solution.py:38
  2.5 0.9 %copy_convert_fusion.1 = f32[4,16,256]{2,0,1:T(4,128)S(1)} fusion(s32[4,16,256]{2,1,0:T(8,128)} %param.5), kind=kLoop, calls=%fused_computation.312 | loop fusion | flops 16384 | bytes 131072 | tf_op jit(solution)/shard_map/convert_element_type | solution.py:237
  3.4 0.9 %fusion.190 = (f32[4,12,256]{2,1,0:T(8,128)S(1)}, f32[4,12,256]{2,1,0:T(8,128)S(1)}) fusion(f32[4,16,256]{2,1,0:T(8,128)} %param.4), kind=kLoop, calls=%fused_computation.457 | loop fusion | bytes 196608 | tf_op jit(solution)/shard_map/slice | solution.py:38
  4.4 3.0 %collective-permute-start = (f32[4,35,256]{2,0,1:T(4,128)S(1)}, f32[4,35,256]{2,0,1:T(4,128)S(1)}, u32[]{:S(2)}, u32[]{:S(2)}) collective-permute-start(f32[4,35,256]{2,0,1:T(4,128)S(1)} %pad_maximum_fusion.1), channel_id=1, source_target_pairs={{0,8},{8,16},{16,24},{24,0},{1,9},{9,17},{17,25},{25,1},{2,10},{10... | collective-permute-start | bytes 430088 | tf_op jit(solution)/shard_map/ppermute | solution.py:39
  7.5 1.0 %collective-permute-start.1 = (f32[4,35,256]{2,0,1:T(4,128)S(1)}, f32[4,35,256]{2,0,1:T(4,128)S(1)}, u32[]{:S(2)}, u32[]{:S(2)}) collective-permute-start(f32[4,35,256]{2,0,1:T(4,128)S(1)} %pad_maximum_fusion.2), channel_id=1, source_target_pairs={{8,0},{16,8},{24,16},{0,24},{9,1},{17,9},{25,17},{1,25},{10,2},{18... | collective-permute-start | bytes 430088 | tf_op jit(solution)/shard_map/ppermute | solution.py:40
  9.0 0.1 fusion.173
  9.1 0.1 fusion.169
  10.0 0.1 broadcast_add_fusion.4
  10.8 2.1 %collective-permute-done = f32[4,35,256]{2,0,1:T(4,128)S(1)} collective-permute-done((f32[4,35,256]{2,0,1:T(4,128)S(1)}, f32[4,35,256]{2,0,1:T(4,128)S(1)}, u32[]{:S(2)}, u32[]{:S(2)}) %collective-permute-start) | collective-permute-done | bytes 143392 | tf_op jit(solution)/shard_map/ppermute | solution.py:39
  13.0 2.4 %collective-permute-done.1 = f32[4,35,256]{2,0,1:T(4,128)S(1)} collective-permute-done((f32[4,35,256]{2,0,1:T(4,128)S(1)}, f32[4,35,256]{2,0,1:T(4,128)S(1)}, u32[]{:S(2)}, u32[]{:S(2)}) %collective-permute-start.1) | collective-permute-done | bytes 143392 | tf_op jit(solution)/shard_map/ppermute | solution.py:40
  15.8 0.2 slice_select_fusion.1
  16.0 0.7 %collective-permute-start.3 = (f32[1,4,134,12]{3,1,2,0:T(4,128)S(1)}, f32[1,4,134,12]{3,1,2,0:T(4,128)S(1)}, u32[]{:S(2)}, u32[]{:S(2)}) collective-permute-start(f32[1,4,134,12]{3,1,2,0:T(4,128)S(1)} %get-tuple-element.59), channel_id=1, source_target_pairs={{1,2},{2,1},{3,4},{4,3},{5,6},{6,5},{9,10},{10,9},{11,12},{12,11},... | collective-permute-start | bytes 77192 | tf_op jit(solution)/shard_map/ppermute | solution.py:93
  16.7 5.3 %collective-permute-start.2 = (f32[1,4,134,12]{3,1,2,0:T(4,128)S(1)}, f32[1,4,134,12]{3,1,2,0:T(4,128)S(1)}, u32[]{:S(2)}, u32[]{:S(2)}) collective-permute-start(f32[1,4,134,12]{3,1,2,0:T(4,128)S(1)} %get-tuple-element.58), channel_id=1, source_target_pairs={{0,2},{3,1},{2,4},{5,3},{4,6},{7,5},{8,10},{11,9},{10,12},{13,11},... | collective-permute-start | bytes 77192 | tf_op jit(solution)/shard_map/ppermute | solution.py:94
  22.1 3.9 %collective-permute-done.2 = f32[1,4,134,12]{3,1,2,0:T(4,128)S(1)} collective-permute-done((f32[1,4,134,12]{3,1,2,0:T(4,128)S(1)}, f32[1,4,134,12]{3,1,2,0:T(4,128)S(1)}, u32[]{:S(2)}, u32[]{:S(2)}) %collective-permute-start.2) | collective-permute-done | bytes 25760 | tf_op jit(solution)/shard_map/ppermute | solution.py:94
  26.0 0.3 maximum_select_fusion.1
  26.3 0.4 maximum_select_fusion
  26.7 0.8 %fusion.15 = f32[8,134,152]{2,0,1:T(8,128)S(1)} fusion(s32[]{:T(128)S(6)} %select_n.147, f32[1,8,134,12]{3,1,2,0:T(8,128)S(1)} %maximum_select_fusion.1, f32[1,8,134,256]{3,1,2,0:T(8,128)S(1)} %maximum_select_fusion), kind=kLoop, calls=%fused_computation.35 | loop fusion | flops 325888 | bytes 1800964 | tf_op jit(solution)/shard_map/squeeze | solution.py:242
  27.5 0.1 slice.917
  27.6 0.2 fusion.189
  27.8 0.1 copy.78
  27.9 0.5 %copy-done = f32[8,134,152]{2,0,1:T(8,128)} copy-done((f32[8,134,152]{2,0,1:T(8,128)}, f32[8,134,152]{2,0,1:T(8,128)S(1)}, u32[]{:S(2)}) %copy-start) | copy-done | bytes 651800
  28.5 0.4 multiply_reduce_fusion.2
  28.9 0.4 slice.939
  29.3 0.2 slice.934
  29.5 0.4 slice-done
  29.9 0.1 copy_select_fusion
  30.0 0.6 %fusion.49 = (f32[8,38,150]{2,1,0:T(8,128)S(1)}, f32[8,38,150]{2,1,0:T(8,128)S(1)}, f32[8,38,150]{2,1,0:T(8,128)S(1)}) fusion(f32[8,40,152]{2,1,0:T(8,128)S(1)} %copy_select_fusion, f32[8,38,150]{2,1,0:T(8,128)S(1)} %get-tuple-element.13, f32[8,38,150]{2,1,0:T(8,128)S(1)} %get-tuple-element.14, f32[8,150]{1,0:T(8,128)S(1)} %broadcast_add_fusion.10, ...), kind=kLoop, calls=%fused_computation.106 | loop fusion | flops 1048800 | bytes 3179904 | tf_op jit(solution)/shard_map/sub | solution.py:268
  30.6 0.2 slice.933
  30.7 0.2 slice.931
  30.9 2.8 %multiply_reduce_fusion.1 = (f32[8,34,146]{2,1,0:T(8,128)S(1)}, f32[8,34,146]{2,1,0:T(8,128)S(1)}, f32[4,8,34,146]{3,2,1,0:T(8,128)S(1)}) fusion(f32[8,146]{1,0:T(8,128)S(1)} %broadcast_add_fusion.8, f32[4,8,36,148]{3,2,1,0:T(8,128)S(1)} %slice.939, f32[4,8,38,150]{3,2,1,0:T(8,128)S(1)} %get-tuple-element.65, f32[146]{0:T(256)S(1)} %get-tuple-element.137, ...), kind=kLoop, calls=%fused_computation.26 | loop fusion | flops 3732928 | bytes 5930538 | tf_op jit(solution)/shard_map/reduce_sum | solution.py:181
  33.7 0.4 slice.961
  34.0 0.2 mul.1273
  34.2 0.1 slice.956
  34.3 0.6 %fusion.55 = f32[8,36,148]{2,1,0:T(8,128)S(1)} fusion(f32[8,38,150]{2,1,0:T(8,128)S(1)} %get-tuple-element.75, f32[8,40,152]{2,1,0:T(8,128)S(1)} %copy_select_fusion, f32[8,148]{1,0:T(8,128)S(1)} %broadcast_add_fusion.9, f32[148]{0:T(256)S(1)} %get-tuple-element.129, f32[148]{0:T(256)S(1)} %get-tuple-element.127, f32[148]{0:T(256)S(1)} %get-tuple-element.126, ...), kind=kLoop, calls=%fused_computation.112 | loop fusion | flops 554112 | bytes 2476032 | tf_op jit(solution)/shard_map/jit(_where)/select_n | solution.py:145
  35.0 0.6 %slice_subtract_fusion.1 = (f32[8,34,146]{2,1,0:T(8,128)S(1)}, f32[8,34,146]{2,1,0:T(8,128)S(1)}, f32[8,34,146]{2,1,0:T(8,128)S(1)}) fusion(f32[8,36,148]{2,1,0:T(8,128)S(1)} %fusion.55, f32[8,146]{1,0:T(8,128)S(1)} %broadcast_add_fusion.8, f32[146]{0:T(256)S(1)} %get-tuple-element.137, f32[146]{0:T(256)S(1)} %get-tuple-element.135, ...), kind=kLoop, calls=%fused_computation.138 | loop fusion | flops 913376 | bytes 3109248 | tf_op jit(solution)/shard_map/sub | solution.py:182
  35.6 0.1 slice.955
  35.7 0.1 slice.953
  35.9 0.5 %fusion.88 = f32[8,32,144]{2,1,0:T(8,128)S(1)} fusion(f32[8,34,146]{2,1,0:T(8,128)S(1)} %get-tuple-element.74, f32[8,36,148]{2,1,0:T(8,128)S(1)} %fusion.55, f32[8,144]{1,0:T(8,128)S(1)} %broadcast_add_fusion.7, f32[144]{0:T(256)S(1)} %get-tuple-element.125, f32[144]{0:T(256)S(1)} %get-tuple-element.123, f32[144]{0:T(256)S(1)} %get-tuple-element.122, ...), kind=kLoop, calls=%fused_computation.164 | loop fusion | flops 479232 | bytes 2059776 | tf_op jit(solution)/shard_map/jit(_where)/select_n | solution.py:145
  36.4 2.3 %multiply_reduce_fusion = (f32[8,30,142]{2,1,0:T(8,128)S(1)}, f32[8,30,142]{2,1,0:T(8,128)S(1)}, f32[4,8,30,142]{3,2,1,0:T(8,128)S(1)}) fusion(f32[8,142]{1,0:T(8,128)S(1)} %broadcast_add_fusion.6, f32[4,8,32,144]{3,2,1,0:T(8,128)S(1)} %slice.961, f32[4,8,34,146]{3,2,1,0:T(8,128)S(1)} %get-tuple-element.47, f32[142]{0:T(256)S(1)} %get-tuple-element.121, ...), kind=kLoop, calls=%fused_computation.6 | loop fusion | flops 3203520 | bytes 5094774 | tf_op jit(solution)/shard_map/reduce_sum | solution.py:180
  38.7 0.5 fusion.72
  39.1 0.7 %fusion.111 = (f32[8,28,140]{2,1,0:T(8,128)S(1)}, f32[8,28,140]{2,1,0:T(8,128)S(1)}) fusion(f32[8,28,140]{2,0,1:T(8,128)S(1)} %get-tuple-element.57, f32[8,28,140]{2,0,1:T(8,128)S(1)} %get-tuple-element.56, pred[140]{0:T(512)(128)(4,1)S(1)} %compare_and_fusion.12, f32[8,30,142]{2,1,0:T(8,128)S(1)} %fusion.72, f32[8,140]{1,0:T(8,128)S(1)} %broadcast_add_fusion.5, ...), kind=kLoop, calls=%fused_computation.206 | loop fusion | flops 501760 | bytes 2556416 | tf_op jit(solution)/shard_map/jit(_where)/select_n | solution.py:145
  39.9 0.5 broadcast_select_fusion
  40.3 0.5 %fusion.131 = (f32[8,24,136]{2,1,0:T(8,128)S(1)}, f32[8,24,136]{2,1,0:T(8,128)S(1)}) fusion(f32[8,26,138]{2,1,0:T(8,128)S(1)} %get-tuple-element.29, f32[8,32,144]{2,1,0:T(8,128)S(1)} %fusion.88, f32[8,28,140]{2,1,0:T(8,128)S(1)} %get-tuple-element.34, f32[8,26,138]{2,1,0:T(8,128)S(1)} %get-tuple-element.30, f32[8,136]{1,0:T(8,128)S(1)} %broadcast_add_fusion.3, ...), kind=kLoop, calls=%fused_computation.239 | loop fusion | flops 548352 | bytes 2055680 | tf_op jit(solution)/shard_map/jit(_where)/select_n | solution.py:145
  40.9 0.1 slice.997
  41.0 0.3 slice.995
  41.3 0.6 %fusion.188 = (f32[4,8,20,132]{3,2,1,0:T(8,128)S(1)}, f32[4,8,20,132]{3,2,1,0:T(8,128)S(1)}, f32[8,20,132]{2,1,0:T(8,128)S(1)}, f32[8,20,132]{2,1,0:T(8,128)S(1)...) fusion(f32[4,8,34,146]{3,2,1,0:T(8,128)S(1)} %get-tuple-element.47, f32[8,20,132]{2,1,0:T(8,128)S(1)} %slice.997, ...), kind=kLoop, calls=%fused_computation.455 | loop fusion | flops 1034880 | bytes 2027652 | tf_op jit(solution)/shard_map/slice | solution.py:135
  41.9 0.4 broadcast_select_fusion.2
  42.3 0.5 %fusion.120 = (f32[8,20,132]{2,1,0:T(8,128)S(1)}, f32[8,20,132]{2,1,0:T(8,128)S(1)}, f32[8,20,132]{2,1,0:T(8,128)S(1)}, f32[8,20,132]{2,1,0:T(8,128)S(1)}, f32[8,20,132]{2,1,0:T(8,128)S(1)}) fusion(f32[8,22,134]{2,1,0:T(8,128)S(1)} %get-tuple-element.19, f32[8,20,132]{2,1,0:T(8,128)S(1)} %get-tuple-element.54, f32[8,24,136]{2,1,0:T(8,128)S(1)} %get-tuple-element.78, ...), kind=kLoop, calls=%fused_computation.228 | loop fusion | flops 549120 | bytes 2596864 | tf_op jit(solution)/shard_map/jit(_where)/select_n | solution.py:145
  42.8 0.1 slice.1020
  42.9 0.1 slice.1019
  43.0 0.1 slice.1017
  43.2 0.1 slice.1015
  43.3 0.1 slice.1014
  43.4 1.7 %fusion.37 = f32[4,8,18,130]{3,2,1,0:T(8,128)S(1)} fusion(f32[4,8,20,132]{3,2,1,0:T(8,128)S(1)} %get-tuple-element.55, f32[4,8,20,132]{3,2,1,0:T(8,128)S(1)} %get-tuple-element.51, f32[4,8,20,132]{3,2,1,0:T(8,128)S(1)} %get-tuple-element.50, f32[8,18,130]{2,1,0:T(8,128)S(1)} %slice.1020, f32[8,18,130]{2,1,0:T(8,128)S(1)} %slice.1019, ...), kind=kLoop, calls=%fused_computation.66 | loop fusion | flops 1722240 | bytes 7585792 | tf_op jit(solution)/shard_map/jit(_where)/select_n | solution.py:145
  45.1 0.2 multiply_reduce_fusion.9
  45.4 0.4 broadcast_select_fusion.1
  45.8 0.1 slice_bitcast_fusion.2
  45.9 0.2 fusion.161
  46.1 0.6 %fusion.94 = f32[4,8,16,128]{3,2,1,0:T(8,128)S(1)} fusion(f32[4,8,18,130]{3,2,1,0:T(8,128)S(1)} %fusion.37, f32[4,8,38,150]{3,2,1,0:T(8,128)S(1)} %get-tuple-element.65, f32[8,128]{1,0:T(8,128)S(1)} %broadcast_add_fusion.11, f32[128]{0:T(128)S(1)} %get-tuple-element.97, f32[128]{0:T(128)S(1)} %get-tuple-element.95, f32[128]{0:T(128)S(1)} %get-tuple-element.94, ...), kind=kLoop, calls=%fused_computation.170 | loop fusion | flops 1638400 | bytes 2955264 | tf_op jit(solution)/shard_map/jit(_where)/select_n | solution.py:145
  46.7 1.4 %collective-permute-start.5 = (f32[6,4,16,128]{3,2,1,0:T(8,128)S(1)}, f32[6,4,16,128]{3,2,1,0:T(8,128)S(1)}, u32[]{:S(2)}, u32[]{:S(2)}) collective-permute-start(f32[6,4,16,128]{3,2,1,0:T(8,128)S(1)} %get-tuple-element.63), channel_id=1, source_target_pairs={{0,1},{1,0},{2,3},{3,2},{4,5},{5,4},{6,7},{7,6},{8,9},{9,8},{10,11... | collective-permute-start | bytes 589832 | tf_op jit(solution)/shard_map/ppermute | solution.py:116
  48.1 1.1 %collective-permute-done.5 = f32[6,4,16,128]{3,2,1,0:T(8,128)S(1)} collective-permute-done((f32[6,4,16,128]{3,2,1,0:T(8,128)S(1)}, f32[6,4,16,128]{3,2,1,0:T(8,128)S(1)}, u32[]{:S(2)}, u32[]{:S(2)}) %collective-permute-start.5) | collective-permute-done | bytes 196640 | tf_op jit(solution)/shard_map/ppermute | solution.py:116
  49.2 0.7 %slice_bitcast_fusion = (f32[4,16,256]{2,1,0:T(8,128)}, f32[4,16,256]{2,1,0:T(8,128)}) fusion(f32[6,4,16,256]{3,2,1,0:T(8,128)S(1)} %maximum_select_fusion.2), kind=kLoop, calls=%fused_computation.301 | loop fusion | bytes 262144 | tf_op jit(solution)/shard_map/squeeze | solution.py:326
  49.9 0.7 %slice.1038 = f32[4,4,16,256]{3,2,1,0:T(8,128)} slice(f32[6,4,16,256]{3,2,1,0:T(8,128)S(1)} %maximum_select_fusion.2), slice={[2:6], [0:4], [0:16], [0:256]} | slice | bytes 524288 | tf_op jit(solution)/shard_map/slice | solution.py:326
  (96 shorter events, 2.5 us)
Async XLA Ops:
  0.6 14.8 %copy-start.2 = (s32[4,16,256]{2,1,0:T(8,128)S(1)}, s32[4,16,256]{2,1,0:T(8,128)}, u32[]{:S(2)}) copy-start(s32[4,16,256]{2,1,0:T(8,128)} %param.5) | copy-start | bytes 196612
  0.6 12.3 %copy-start.1 = (f32[4,16,256]{2,1,0:T(8,128)S(1)}, f32[4,16,256]{2,1,0:T(8,128)}, u32[]{:S(2)}) copy-start(f32[4,16,256]{2,1,0:T(8,128)} %param.4) | copy-start | bytes 196612
  1.6 14.0 %copy-start.3 = (f32[4,16,256]{2,1,0:T(8,128)S(1)}, f32[4,16,256]{2,1,0:T(8,128)}, u32[]{:S(2)}) copy-start(f32[4,16,256]{2,1,0:T(8,128)} %param.6) | copy-start | bytes 196612
  3.4 12.3 %copy-start.4 = (s32[4,16,256]{2,1,0:T(8,128)S(1)}, s32[4,16,256]{2,1,0:T(8,128)}, u32[]{:S(2)}) copy-start(s32[4,16,256]{2,1,0:T(8,128)} %param.7) | copy-start | bytes 196612
  4.4 8.5 %collective-permute-start = (f32[4,35,256]{2,0,1:T(4,128)S(1)}, f32[4,35,256]{2,0,1:T(4,128)S(1)}, u32[]{:S(2)}, u32[]{:S(2)}) collective-permute-start(f32[4,35,256]{2,0,1:T(4,128)S(1)} %pad_maximum_fusion.1), channel_id=1, source_target_pairs={{0,8},{8,16},{16,24},{24,0},{1,9},{9,17},{17,25},{25,1},{2,10},{10... | collective-permute-start | bytes 430088 | tf_op jit(solution)/shard_map/ppermute | solution.py:39
  7.5 7.9 %collective-permute-start.1 = (f32[4,35,256]{2,0,1:T(4,128)S(1)}, f32[4,35,256]{2,0,1:T(4,128)S(1)}, u32[]{:S(2)}, u32[]{:S(2)}) collective-permute-start(f32[4,35,256]{2,0,1:T(4,128)S(1)} %pad_maximum_fusion.2), channel_id=1, source_target_pairs={{8,0},{16,8},{24,16},{0,24},{9,1},{17,9},{25,17},{1,25},{10,2},{18... | collective-permute-start | bytes 430088 | tf_op jit(solution)/shard_map/ppermute | solution.py:40
  15.7 10.5 %collective-permute-start.4 = (f32[1,4,134,256]{3,1,2,0:T(4,128)S(1)}, f32[1,4,134,256]{3,1,2,0:T(4,128)S(1)}, u32[]{:S(2)}, u32[]{:S(2)}) collective-permute-start(f32[1,4,134,256]{3,1,2,0:T(4,128)S(1)} %bitcast.11), channel_id=1, source_target_pairs={{0,1},{1,0},{2,3},{3,2},{4,5},{5,4},{6,7},{7,6},{8,9},{9,8},{10,11... | collective-permute-start | bytes 1646600 | tf_op jit(solution)/shard_map/ppermute | solution.py:55
  16.0 6.0 %collective-permute-start.3 = (f32[1,4,134,12]{3,1,2,0:T(4,128)S(1)}, f32[1,4,134,12]{3,1,2,0:T(4,128)S(1)}, u32[]{:S(2)}, u32[]{:S(2)}) collective-permute-start(f32[1,4,134,12]{3,1,2,0:T(4,128)S(1)} %get-tuple-element.59), channel_id=1, source_target_pairs={{1,2},{2,1},{3,4},{4,3},{5,6},{6,5},{9,10},{10,9},{11,12},{12,11},... | collective-permute-start | bytes 77192 | tf_op jit(solution)/shard_map/ppermute | solution.py:93
  16.7 9.3 %collective-permute-start.2 = (f32[1,4,134,12]{3,1,2,0:T(4,128)S(1)}, f32[1,4,134,12]{3,1,2,0:T(4,128)S(1)}, u32[]{:S(2)}, u32[]{:S(2)}) collective-permute-start(f32[1,4,134,12]{3,1,2,0:T(4,128)S(1)} %get-tuple-element.58), channel_id=1, source_target_pairs={{0,2},{3,1},{2,4},{5,3},{4,6},{7,5},{8,10},{11,9},{10,12},{13,11},... | collective-permute-start | bytes 77192 | tf_op jit(solution)/shard_map/ppermute | solution.py:94
  27.5 1.0 %copy-start = (f32[8,134,152]{2,0,1:T(8,128)}, f32[8,134,152]{2,0,1:T(8,128)S(1)}, u32[]{:S(2)}) copy-start(f32[8,134,152]{2,0,1:T(8,128)S(1)} %fusion.15) | copy-start | bytes 1955332
  28.9 1.0 %slice-start = ((f32[8,134,152]{2,0,1:T(8,128)}), f32[8,40,152]{2,0,1:T(8,128)S(1)}, s32[]{:S(2)}) async-start(f32[8,134,152]{2,0,1:T(8,128)} %copy-done), calls=%async_computation | async-start | bytes 655360 | tf_op jit(solution)/shard_map/slice | solution.py:246
  46.7 2.4 %collective-permute-start.5 = (f32[6,4,16,128]{3,2,1,0:T(8,128)S(1)}, f32[6,4,16,128]{3,2,1,0:T(8,128)S(1)}, u32[]{:S(2)}, u32[]{:S(2)}) collective-permute-start(f32[6,4,16,128]{3,2,1,0:T(8,128)S(1)} %get-tuple-element.63), channel_id=1, source_target_pairs={{0,1},{1,0},{2,3},{3,2},{4,5},{5,4},{6,7},{7,6},{8,9},{9,8},{10,11... | collective-permute-start | bytes 589832 | tf_op jit(solution)/shard_map/ppermute | solution.py:116

commit v15 on v14

--- a/solution.py
+++ b/solution.py
@@ -104,6 +104,32 @@
     part = block.shape[-1] // 2
     padded = jnp.concatenate([received, block, received], axis=-1)
     return lax.dynamic_slice_in_dim(padded, own * part, part + 2 * width, axis=padded.ndim - 1)
+
+
+def two_core_join(block, received, width):
+    own = lax.axis_index("hgt")
+    cols = block.shape[-1]
+    part = cols // 2
+    span = part + width
+    piece = jnp.where(own == 0, block[..., cols - span :], block[..., :span])
+    partner = lax.ppermute(piece, "hgt", [(0, 1), (1, 0)])
+    halves = block.shape[1]
+    low, high = received[:, :halves], received[:, halves:]
+    first = jnp.concatenate(
+        [
+            jnp.concatenate([low, block[..., :span]], axis=-1),
+            jnp.concatenate([high, partner], axis=-1),
+        ],
+        axis=1,
+    )
+    second = jnp.concatenate(
+        [
+            jnp.concatenate([partner, low], axis=-1),
+            jnp.concatenate([block[..., cols - span :], high], axis=-1),
+        ],
+        axis=1,
+    )
+    return jnp.where(own == 0, first, second)
 
 
 def scatter_heights(x, height_rows):
@@ -239,7 +265,7 @@
         extended = azim_exchange(inputs, widths)
         stacked = jnp.concatenate(extended, axis=-2)[None]
         received = edge_columns(stacked, HALO)
-        stacked = two_core_window(gather_axis(stacked, "hgt", 1), received, HALO)[0]
+        stacked = two_core_join(stacked, received, HALO)[0]
         fields, at = [], 0
         for f, w in zip(extended, widths):
             rows = f.shape[-2]

time: 51 us -> 50 us (0.980)
  waiting for transfers between devices: 9.53 us -> 10.5 us
  starting transfers between devices: 11.4 us -> 10.5 us
  other arithmetic: 20.7 us -> 19.8 us
    concatenate x1, local copies, waits for them, and re-layouts: 0.01 us -> 0.92 us  [shards(): stacked = jnp.concatenate(extended, axis=-2)[None]]
    unnamed x23 -> x4, local copies, waits for them, and re-layouts: 0.84 us -> 0.01 us
    squeeze x1 -> x0, other arithmetic: 0.79 us -> none  [shards(): stacked = two_core_window(gather_axis(stacked, 'hgt', 1), received, HALO)[0]]
    ppermute x1, starting transfers between devices: 5.27 us -> 4.74 us  [edge_columns(): lax.ppermute(jnp.where(own == 0, last, first), ('rad', 'hgt'), same)]
    slice x4 -> x3, local copies, waits for them, and re-layouts: 1.78 us -> 1.77 us  [azim_exchange(): f[..., :w, :]]
where the time goes in v15:
time: 50 us; the launch traced here: 49.6 us
  other arithmetic  19.8 us (40%)
  starting transfers between devices  10.5 us (21%)
  waiting for transfers between devices  10.5 us (21%)
  local copies, waits for them, and re-layouts  7.37 us (15%)
  between operations  1.37 us (3%)
    select_n x11, other arithmetic, in_domain(): return jnp.where(radial_mask(width, geometry), x, 0.0)  6.61 us
    ppermute x1, starting transfers between devices, edge_columns(): lax.ppermute(jnp.where(own == 0, last, first), ('rad', 'hgt'), same)  4.74 us
    ppermute x1, waiting for transfers between devices, edge_columns(): lax.ppermute(jnp.where(own == 0, last, first), ('rad', 'hgt'), same)  3.98 us
    reduce_sum x2, other arithmetic, chemical(): cube_sum = jnp.sum(grains * grains * grains, axis=0)  3.17 us
    ppermute x1, starting transfers between devices, azim_exchange(): before = lax.ppermute(last, 'azim', up)  2.99 us
    ppermute x1, waiting for transfers between devices, azim_exchange(): after = lax.ppermute(leading, 'azim', down)  2.91 us
    slice x15, local copies, waits for them, and re-layouts, crop(): return x[..., cut:x.shape[-2] - cut, cut:x.shape[-1] - cut]  2.63 us
    ppermute x1, waiting for transfers between devices, azim_exchange(): before = lax.ppermute(last, 'azim', up)  2.57 us
  transfers between devices with their start and end apart: 6, of which 4 were waited for; matrix products, arithmetic and copies ran while one was open for 5% of the time, Pallas kernels for 0%

profile of v15, /device:TPU:0, one launch (start us, length us, event | category | flops | bytes accessed | tf_op | source)
XLA Modules:
  0.0 49.6 jit_solution(1411606478571787317)
XLA Ops:
  0.6 0.8 %convert_element_type.202 = f32[4,16,256]{2,1,0:T(8,128)S(1)} convert(s32[4,16,256]{2,1,0:T(8,128)} %param.7) | non-fusion elementwise | flops 16384 | bytes 131072 | tf_op jit(solution)/shard_map/convert_element_type | solution.py:263
  1.5 0.8 %convert_element_type.201 = f32[4,16,256]{2,1,0:T(8,128)S(1)} convert(s32[4,16,256]{2,1,0:T(8,128)} %param.5) | non-fusion elementwise | flops 16384 | bytes 131072 | tf_op jit(solution)/shard_map/convert_element_type | solution.py:263
  2.4 1.0 %fusion.190 = (f32[4,12,256]{2,1,0:T(8,128)S(1)}, f32[4,12,256]{2,1,0:T(8,128)S(1)}) fusion(f32[4,16,256]{2,1,0:T(8,128)} %param.4), kind=kLoop, calls=%fused_computation.445 | loop fusion | bytes 196608 | tf_op jit(solution)/shard_map/slice | solution.py:38
  3.3 0.8 %fusion.192 = (f32[4,6,256]{2,1,0:T(8,128)S(1)}, f32[4,6,256]{2,1,0:T(8,128)S(1)}, f32[4,6,256]{2,1,0:T(8,128)S(1)}, f32[4,6,256]{2,1,0:T(8,128)S(1)}) fusion(f32[4,16,256]{2,1,0:T(8,128)} %param.6, f32[4,16,256]{2,1,0:T(8,128)S(1)} %convert_element_type.202), kind=kLoop, calls=%fused_computation.447 | loop fusion | bytes 196608 | tf_op jit(solution)/shard_map/slice | solution.py:38
  4.2 3.0 %collective-permute-start = (f32[4,35,256]{2,1,0:T(8,128)S(1)}, f32[4,35,256]{2,1,0:T(8,128)S(1)}, u32[]{:S(2)}, u32[]{:S(2)}) collective-permute-start(f32[4,35,256]{2,1,0:T(8,128)S(1)} %pad_maximum_fusion.1), channel_id=1, source_target_pairs={{0,8},{8,16},{16,24},{24,0},{1,9},{9,17},{17,25},{25,1},{2,10},{10... | collective-permute-start | bytes 430088 | tf_op jit(solution)/shard_map/ppermute | solution.py:39
  7.2 1.0 %collective-permute-start.1 = (f32[4,35,256]{2,1,0:T(8,128)S(1)}, f32[4,35,256]{2,1,0:T(8,128)S(1)}, u32[]{:S(2)}, u32[]{:S(2)}) collective-permute-start(f32[4,35,256]{2,1,0:T(8,128)S(1)} %pad_maximum_fusion.2), channel_id=1, source_target_pairs={{8,0},{16,8},{24,16},{0,24},{9,1},{17,9},{25,17},{1,25},{10,2},{18... | collective-permute-start | bytes 430088 | tf_op jit(solution)/shard_map/ppermute | solution.py:40
  8.7 0.1 fusion.170
  8.8 0.1 fusion.166
  9.4 0.1 fusion.173
  9.7 0.1 broadcast_add_fusion.4
  10.5 0.1 broadcast_add_fusion.11
  10.6 2.6 %collective-permute-done = f32[4,35,256]{2,1,0:T(8,128)S(1)} collective-permute-done((f32[4,35,256]{2,1,0:T(8,128)S(1)}, f32[4,35,256]{2,1,0:T(8,128)S(1)}, u32[]{:S(2)}, u32[]{:S(2)}) %collective-permute-start) | collective-permute-done | bytes 143392 | tf_op jit(solution)/shard_map/ppermute | solution.py:39
  13.1 2.9 %collective-permute-done.1 = f32[4,35,256]{2,1,0:T(8,128)S(1)} collective-permute-done((f32[4,35,256]{2,1,0:T(8,128)S(1)}, f32[4,35,256]{2,1,0:T(8,128)S(1)}, u32[]{:S(2)}, u32[]{:S(2)}) %collective-permute-start.1) | collective-permute-done | bytes 143392 | tf_op jit(solution)/shard_map/ppermute | solution.py:40
  16.1 0.9 %concatenate.74 = f32[4,134,256]{2,1,0:T(8,128)S(1)} concatenate(f32[4,12,256]{2,1,0:T(8,128)S(1)} %slice.916, f32[4,16,256]{2,1,0:T(8,128)S(1)} %copy-done, f32[4,12,256]{2,1,0:T(8,128)S(1)} %slice.919, f32[4,11,256]{2,1,0:T(8,128)S(1)} %slice.920, f32[4,16,256]{2,1,0:T(8,128)S(1)} %convert_element_type.201, f32[4,11,256]{2,1,0:T(8,128)S(1)} %slice.921, ...), dimensions={1} | concatenate | bytes 1097728 | tf_op jit(solution)/shard_map/concatenate | solution.py:266
  17.1 0.1 slice_select_fusion.2
  17.2 0.7 %collective-permute-start.3 = (f32[1,4,134,12]{3,2,1,0:T(8,128)S(1)}, f32[1,4,134,12]{3,2,1,0:T(8,128)S(1)}, u32[]{:S(2)}, u32[]{:S(2)}) collective-permute-start(f32[1,4,134,12]{3,2,1,0:T(8,128)S(1)} %get-tuple-element.64), channel_id=1, source_target_pairs={{1,2},{2,1},{3,4},{4,3},{5,6},{6,5},{9,10},{10,9},{11,12},{12,11},... | collective-permute-start | bytes 77192 | tf_op jit(solution)/shard_map/ppermute | solution.py:93
  17.9 4.7 %collective-permute-start.2 = (f32[1,4,134,12]{3,2,1,0:T(8,128)S(1)}, f32[1,4,134,12]{3,2,1,0:T(8,128)S(1)}, u32[]{:S(2)}, u32[]{:S(2)}) collective-permute-start(f32[1,4,134,12]{3,2,1,0:T(8,128)S(1)} %get-tuple-element.63), channel_id=1, source_target_pairs={{0,2},{3,1},{2,4},{5,3},{4,6},{7,5},{8,10},{11,9},{10,12},{13,11},... | collective-permute-start | bytes 77192 | tf_op jit(solution)/shard_map/ppermute | solution.py:94
  22.6 0.2 fusion.186
  22.9 0.2 copy.46
  23.2 4.0 %collective-permute-done.2 = f32[1,4,134,12]{3,2,1,0:T(8,128)S(1)} collective-permute-done((f32[1,4,134,12]{3,2,1,0:T(8,128)S(1)}, f32[1,4,134,12]{3,2,1,0:T(8,128)S(1)}, u32[]{:S(2)}, u32[]{:S(2)}) %collective-permute-start.2) | collective-permute-done | bytes 25760 | tf_op jit(solution)/shard_map/ppermute | solution.py:94
  27.3 0.1 copy.47
  27.4 0.5 %maximum_bitcast_fusion.2 = (f32[4,134,152]{2,1,0:T(8,128)S(1)}, f32[4,134,152]{2,1,0:T(8,128)S(1)}, f32[4,134,152]{2,1,0:T(8,128)S(1)}, f32[4,134,152]{2,1,0:T(8,128)S(1)}) fusion(f32[1,4,134,12]{3,2,1,0:T(8,128)S(1)} %get-tuple-element.61, f32[1,4,134,140]{3,2,1,0:T(8,128)S(1)} %copy.47, f32[1,4,134,12]{3,2,1,0:T(8,128)S(1)} %get-tuple-element.62, ...), kind=kLoop, calls=%fused_computation.78 | loop fusion | flops 325888 | bytes 2255488 | tf_op jit(solution)/shard_map/concatenate | solution.py:125
  27.9 0.1 maximum_select_fusion
  28.0 0.1 slice.935
  28.2 0.4 multiply_reduce_fusion.2
  28.6 0.4 slice.957
  29.0 0.2 slice.952
  29.2 0.6 %fusion.46 = (f32[8,38,150]{2,1,0:T(8,128)S(1)}, f32[8,38,150]{2,1,0:T(8,128)S(1)}, f32[8,38,150]{2,1,0:T(8,128)S(1)}) fusion(f32[8,40,152]{2,1,0:T(8,128)S(1)} %slice_select_fusion, f32[8,38,150]{2,1,0:T(8,128)S(1)} %get-tuple-element.13, f32[8,38,150]{2,1,0:T(8,128)S(1)} %get-tuple-element.14, f32[8,150]{1,0:T(8,128)S(1)} %broadcast_add_fusion.10, ...), kind=kLoop, calls=%fused_computation.104 | loop fusion | flops 1048800 | bytes 3179904 | tf_op jit(solution)/shard_map/sub | solution.py:294
  29.8 0.2 slice.951
  30.0 0.2 slice.949
  30.1 2.8 %multiply_reduce_fusion.1 = (f32[8,34,146]{2,1,0:T(8,128)S(1)}, f32[8,34,146]{2,1,0:T(8,128)S(1)}, f32[4,8,34,146]{3,2,1,0:T(8,128)S(1)}) fusion(f32[8,146]{1,0:T(8,128)S(1)} %broadcast_add_fusion.8, f32[4,8,36,148]{3,2,1,0:T(8,128)S(1)} %slice.957, f32[4,8,38,150]{3,2,1,0:T(8,128)S(1)} %get-tuple-element.70, f32[146]{0:T(256)S(1)} %get-tuple-element.148, ...), kind=kLoop, calls=%fused_computation.23 | loop fusion | flops 3732928 | bytes 5930538 | tf_op jit(solution)/shard_map/reduce_sum | solution.py:207
  32.9 0.4 slice.979
  33.3 0.2 mul.1272
  33.4 0.1 slice.974
  33.6 0.6 %fusion.52 = f32[8,36,148]{2,1,0:T(8,128)S(1)} fusion(f32[8,38,150]{2,1,0:T(8,128)S(1)} %get-tuple-element.80, f32[8,40,152]{2,1,0:T(8,128)S(1)} %slice_select_fusion, f32[8,148]{1,0:T(8,128)S(1)} %broadcast_add_fusion.9, f32[148]{0:T(256)S(1)} %get-tuple-element.140, f32[148]{0:T(256)S(1)} %get-tuple-element.138, f32[148]{0:T(256)S(1)} %get-tuple-element.137, ...), kind=kLoop, calls=%fused_computation.110 | loop fusion | flops 554112 | bytes 2476032 | tf_op jit(solution)/shard_map/jit(_where)/select_n | solution.py:171
  34.2 0.6 %slice_subtract_fusion.1 = (f32[8,34,146]{2,1,0:T(8,128)S(1)}, f32[8,34,146]{2,1,0:T(8,128)S(1)}, f32[8,34,146]{2,1,0:T(8,128)S(1)}) fusion(f32[8,36,148]{2,1,0:T(8,128)S(1)} %fusion.52, f32[8,146]{1,0:T(8,128)S(1)} %broadcast_add_fusion.8, f32[146]{0:T(256)S(1)} %get-tuple-element.148, f32[146]{0:T(256)S(1)} %get-tuple-element.146, ...), kind=kLoop, calls=%fused_computation.136 | loop fusion | flops 913376 | bytes 3109248 | tf_op jit(solution)/shard_map/sub | solution.py:208
  34.8 0.1 slice.973
  35.0 0.1 slice.971
  35.1 0.5 %fusion.85 = f32[8,32,144]{2,1,0:T(8,128)S(1)} fusion(f32[8,34,146]{2,1,0:T(8,128)S(1)} %get-tuple-element.79, f32[8,36,148]{2,1,0:T(8,128)S(1)} %fusion.52, f32[8,144]{1,0:T(8,128)S(1)} %broadcast_add_fusion.7, f32[144]{0:T(256)S(1)} %get-tuple-element.136, f32[144]{0:T(256)S(1)} %get-tuple-element.134, f32[144]{0:T(256)S(1)} %get-tuple-element.133, ...), kind=kLoop, calls=%fused_computation.163 | loop fusion | flops 479232 | bytes 2059776 | tf_op jit(solution)/shard_map/jit(_where)/select_n | solution.py:171
  35.6 2.3 %multiply_reduce_fusion = (f32[8,30,142]{2,1,0:T(8,128)S(1)}, f32[8,30,142]{2,1,0:T(8,128)S(1)}, f32[4,8,30,142]{3,2,1,0:T(8,128)S(1)}) fusion(f32[8,142]{1,0:T(8,128)S(1)} %broadcast_add_fusion.6, f32[4,8,32,144]{3,2,1,0:T(8,128)S(1)} %slice.979, f32[4,8,34,146]{3,2,1,0:T(8,128)S(1)} %get-tuple-element.47, f32[142]{0:T(256)S(1)} %get-tuple-element.132, ...), kind=kLoop, calls=%fused_computation.3 | loop fusion | flops 3203520 | bytes 5094774 | tf_op jit(solution)/shard_map/reduce_sum | solution.py:206
  37.9 0.5 fusion.69
  38.4 0.9 %fusion.99 = (f32[8,28,140]{2,1,0:T(8,128)S(1)}, f32[8,28,140]{2,1,0:T(8,128)S(1)}) fusion(f32[8,134,152]{2,1,0:T(8,128)S(1)} %maximum_select_fusion, pred[140]{0:T(512)(128)(4,1)S(1)} %compare_and_fusion.12, f32[8,30,142]{2,1,0:T(8,128)S(1)} %fusion.69, f32[8,140]{1,0:T(8,128)S(1)} %broadcast_add_fusion.5, f32[140]{0:T(256)S(1)} %get-tuple-element.128, ...), kind=kLoop, calls=%fused_computation.185 | loop fusion | flops 501760 | bytes 2621952 | tf_op jit(solution)/shard_map/jit(_where)/select_n | solution.py:171
  39.2 0.5 broadcast_select_fusion.1
  39.7 0.5 %fusion.128 = (f32[8,24,136]{2,1,0:T(8,128)S(1)}, f32[8,24,136]{2,1,0:T(8,128)S(1)}) fusion(f32[8,26,138]{2,1,0:T(8,128)S(1)} %get-tuple-element.29, f32[8,32,144]{2,1,0:T(8,128)S(1)} %fusion.85, f32[8,28,140]{2,1,0:T(8,128)S(1)} %get-tuple-element.34, f32[8,26,138]{2,1,0:T(8,128)S(1)} %get-tuple-element.30, f32[8,136]{1,0:T(8,128)S(1)} %broadcast_add_fusion.3, ...), kind=kLoop, calls=%fused_computation.238 | loop fusion | flops 548352 | bytes 2055680 | tf_op jit(solution)/shard_map/jit(_where)/select_n | solution.py:171
  40.2 0.1 slice.1015
  40.4 0.3 slice.1013
  40.7 0.6 %fusion.185 = (f32[4,8,20,132]{3,2,1,0:T(8,128)S(1)}, f32[4,8,20,132]{3,2,1,0:T(8,128)S(1)}, f32[8,20,132]{2,1,0:T(8,128)S(1)}, f32[8,20,132]{2,1,0:T(8,128)S(1)...) fusion(f32[4,8,34,146]{3,2,1,0:T(8,128)S(1)} %get-tuple-element.47, f32[8,20,132]{2,1,0:T(8,128)S(1)} %slice.1015, ...), kind=kLoop, calls=%fused_computation.440 | loop fusion | flops 1034880 | bytes 2027652 | tf_op jit(solution)/shard_map/slice | solution.py:161
  41.3 0.1 slice.1038
  41.4 0.4 broadcast_select_fusion.3
  41.8 0.5 %fusion.117 = (f32[8,20,132]{2,1,0:T(8,128)S(1)}, f32[8,20,132]{2,1,0:T(8,128)S(1)}, f32[8,20,132]{2,1,0:T(8,128)S(1)}, f32[8,20,132]{2,1,0:T(8,128)S(1)}) fusion(f32[8,22,134]{2,1,0:T(8,128)S(1)} %get-tuple-element.19, f32[8,20,132]{2,1,0:T(8,128)S(1)} %get-tuple-element.54, f32[8,24,136]{2,1,0:T(8,128)S(1)} %get-tuple-element.85, ...), kind=kLoop, calls=%fused_computation.227 | loop fusion | flops 528000 | bytes 2315776 | tf_op jit(solution)/shard_map/jit(_where)/select_n | solution.py:171
  42.3 0.1 slice.1037
  42.4 0.1 slice.1035
  42.6 0.1 slice.1033
  42.7 0.1 slice.1032
  42.8 1.7 %fusion.34 = f32[4,8,18,130]{3,2,1,0:T(8,128)S(1)} fusion(f32[4,8,20,132]{3,2,1,0:T(8,128)S(1)} %get-tuple-element.55, f32[4,8,20,132]{3,2,1,0:T(8,128)S(1)} %get-tuple-element.51, f32[4,8,20,132]{3,2,1,0:T(8,128)S(1)} %get-tuple-element.50, f32[8,18,130]{2,1,0:T(8,128)S(1)} %slice.1038, f32[8,18,130]{2,1,0:T(8,128)S(1)} %slice.1037, ...), kind=kLoop, calls=%fused_computation.60 | loop fusion | flops 1722240 | bytes 7585792 | tf_op jit(solution)/shard_map/jit(_where)/select_n | solution.py:171
  44.5 0.2 multiply_reduce_fusion.9
  44.8 0.4 broadcast_select_fusion.2
  45.1 0.1 slice_bitcast_fusion.2
  45.2 0.2 fusion.158
  45.5 0.6 %fusion.91 = f32[4,8,16,128]{3,2,1,0:T(8,128)S(1)} fusion(f32[4,8,18,130]{3,2,1,0:T(8,128)S(1)} %fusion.34, f32[4,8,38,150]{3,2,1,0:T(8,128)S(1)} %get-tuple-element.70, f32[8,128]{1,0:T(8,128)S(1)} %broadcast_add_fusion.11, f32[128]{0:T(128)S(1)} %get-tuple-element.108, f32[128]{0:T(128)S(1)} %get-tuple-element.106, f32[128]{0:T(128)S(1)} %get-tuple-element.105, ...), kind=kLoop, calls=%fused_computation.169 | loop fusion | flops 1638400 | bytes 2955264 | tf_op jit(solution)/shard_map/jit(_where)/select_n | solution.py:171
  46.1 1.0 %collective-permute-start.5 = (f32[6,4,16,128]{3,2,1,0:T(8,128)S(1)}, f32[6,4,16,128]{3,2,1,0:T(8,128)S(1)}, u32[]{:S(2)}, u32[]{:S(2)}) collective-permute-start(f32[6,4,16,128]{3,2,1,0:T(8,128)S(1)} %get-tuple-element.68), channel_id=1, source_target_pairs={{0,1},{1,0},{2,3},{3,2},{4,5},{5,4},{6,7},{7,6},{8,9},{9,8},{10,11... | collective-permute-start | bytes 589832 | tf_op jit(solution)/shard_map/ppermute | solution.py:142
  47.1 1.1 %collective-permute-done.5 = f32[6,4,16,128]{3,2,1,0:T(8,128)S(1)} collective-permute-done((f32[6,4,16,128]{3,2,1,0:T(8,128)S(1)}, f32[6,4,16,128]{3,2,1,0:T(8,128)S(1)}, u32[]{:S(2)}, u32[]{:S(2)}) %collective-permute-start.5) | collective-permute-done | bytes 196640 | tf_op jit(solution)/shard_map/ppermute | solution.py:142
  48.2 0.7 %slice_bitcast_fusion = (f32[4,16,256]{2,1,0:T(8,128)}, f32[4,16,256]{2,1,0:T(8,128)}) fusion(f32[6,4,16,256]{3,2,1,0:T(8,128)S(1)} %maximum_select_fusion.2), kind=kLoop, calls=%fused_computation.300 | loop fusion | bytes 262144 | tf_op jit(solution)/shard_map/squeeze | solution.py:352
  48.9 0.7 %slice.1056 = f32[4,4,16,256]{3,2,1,0:T(8,128)} slice(f32[6,4,16,256]{3,2,1,0:T(8,128)S(1)} %maximum_select_fusion.2), slice={[2:6], [0:4], [0:16], [0:256]} | slice | bytes 524288 | tf_op jit(solution)/shard_map/slice | solution.py:352
  (81 shorter events, 2.1 us)
Async XLA Ops:
  2.3 13.8 %copy-start = (f32[4,16,256]{2,1,0:T(8,128)S(1)}, f32[4,16,256]{2,1,0:T(8,128)}, u32[]{:S(2)}) copy-start(f32[4,16,256]{2,1,0:T(8,128)} %param.4) | copy-start | bytes 196612
  2.3 13.8 %copy-start.1 = (f32[4,16,256]{2,1,0:T(8,128)S(1)}, f32[4,16,256]{2,1,0:T(8,128)}, u32[]{:S(2)}) copy-start(f32[4,16,256]{2,1,0:T(8,128)} %param.6) | copy-start | bytes 196612
  4.2 9.0 %collective-permute-start = (f32[4,35,256]{2,1,0:T(8,128)S(1)}, f32[4,35,256]{2,1,0:T(8,128)S(1)}, u32[]{:S(2)}, u32[]{:S(2)}) collective-permute-start(f32[4,35,256]{2,1,0:T(8,128)S(1)} %pad_maximum_fusion.1), channel_id=1, source_target_pairs={{0,8},{8,16},{16,24},{24,0},{1,9},{9,17},{17,25},{25,1},{2,10},{10... | collective-permute-start | bytes 430088 | tf_op jit(solution)/shard_map/ppermute | solution.py:39
  7.2 8.9 %collective-permute-start.1 = (f32[4,35,256]{2,1,0:T(8,128)S(1)}, f32[4,35,256]{2,1,0:T(8,128)S(1)}, u32[]{:S(2)}, u32[]{:S(2)}) collective-permute-start(f32[4,35,256]{2,1,0:T(8,128)S(1)} %pad_maximum_fusion.2), channel_id=1, source_target_pairs={{8,0},{16,8},{24,16},{0,24},{9,1},{17,9},{25,17},{1,25},{10,2},{18... | collective-permute-start | bytes 430088 | tf_op jit(solution)/shard_map/ppermute | solution.py:40
  17.2 6.0 %collective-permute-start.3 = (f32[1,4,134,12]{3,2,1,0:T(8,128)S(1)}, f32[1,4,134,12]{3,2,1,0:T(8,128)S(1)}, u32[]{:S(2)}, u32[]{:S(2)}) collective-permute-start(f32[1,4,134,12]{3,2,1,0:T(8,128)S(1)} %get-tuple-element.64), channel_id=1, source_target_pairs={{1,2},{2,1},{3,4},{4,3},{5,6},{6,5},{9,10},{10,9},{11,12},{12,11},... | collective-permute-start | bytes 77192 | tf_op jit(solution)/shard_map/ppermute | solution.py:93
  17.9 9.3 %collective-permute-start.2 = (f32[1,4,134,12]{3,2,1,0:T(8,128)S(1)}, f32[1,4,134,12]{3,2,1,0:T(8,128)S(1)}, u32[]{:S(2)}, u32[]{:S(2)}) collective-permute-start(f32[1,4,134,12]{3,2,1,0:T(8,128)S(1)} %get-tuple-element.63), channel_id=1, source_target_pairs={{0,2},{3,1},{2,4},{5,3},{4,6},{7,5},{8,10},{11,9},{10,12},{13,11},... | collective-permute-start | bytes 77192 | tf_op jit(solution)/shard_map/ppermute | solution.py:94
  23.1 4.2 %collective-permute-start.4 = (f32[1,4,134,140]{3,1,2,0:T(4,128)S(1)}, f32[1,4,134,140]{3,1,2,0:T(4,128)S(1)}, u32[]{:S(2)}, u32[]{:S(2)}) collective-permute-start(f32[1,4,134,140]{3,1,2,0:T(4,128)S(1)} %copy.46), channel_id=1, source_target_pairs={{0,1},{1,0},{2,3},{3,2},{4,5},{5,4},{6,7},{7,6},{8,9},{9,8},{10,11... | collective-permute-start | bytes 900488 | tf_op jit(solution)/shard_map/ppermute | solution.py:115
  46.1 2.1 %collective-permute-start.5 = (f32[6,4,16,128]{3,2,1,0:T(8,128)S(1)}, f32[6,4,16,128]{3,2,1,0:T(8,128)S(1)}, u32[]{:S(2)}, u32[]{:S(2)}) collective-permute-start(f32[6,4,16,128]{3,2,1,0:T(8,128)S(1)} %get-tuple-element.68), channel_id=1, source_target_pairs={{0,1},{1,0},{2,3},{3,2},{4,5},{5,4},{6,7},{7,6},{8,9},{9,8},{10,11... | collective-permute-start | bytes 589832 | tf_op jit(solution)/shard_map/ppermute | solution.py:142

commit v16 on v15

--- a/solution.py
+++ b/solution.py
@@ -168,6 +168,8 @@
 
 
 def in_domain(x, width, geometry):
+    if width <= 0:
+        return x
     return jnp.where(radial_mask(width, geometry), x, 0.0)
 
 

time: 50 us -> 50 us (level)
    select_n x11 -> x10, other arithmetic: 6.61 us -> 6.04 us  [in_domain(): return jnp.where(radial_mask(width, geometry), x, 0.0)]
    add x0 -> x1, other arithmetic: none -> 0.56 us  [shards(): crop(cograins, cg_width, new_cg_width)]
where the time goes in v16:
time: 50 us; the launch traced here: 49.6 us
  other arithmetic  19.8 us (40%)
  starting transfers between devices  10.5 us (21%)
  waiting for transfers between devices  10.5 us (21%)
  local copies, waits for them, and re-layouts  7.37 us (15%)
  between operations  1.36 us (3%)
    select_n x10, other arithmetic, in_domain(): return jnp.where(radial_mask(width, geometry), x, 0.0)  6.04 us
    ppermute x1, starting transfers between devices, edge_columns(): lax.ppermute(jnp.where(own == 0, last, first), ('rad', 'hgt'), same)  4.74 us
    ppermute x1, waiting for transfers between devices, edge_columns(): lax.ppermute(jnp.where(own == 0, last, first), ('rad', 'hgt'), same)  3.98 us
    reduce_sum x2, other arithmetic, chemical(): cube_sum = jnp.sum(grains * grains * grains, axis=0)  3.17 us
    ppermute x1, starting transfers between devices, azim_exchange(): before = lax.ppermute(last, 'azim', up)  2.99 us
    ppermute x1, waiting for transfers between devices, azim_exchange(): after = lax.ppermute(leading, 'azim', down)  2.91 us
    slice x15, local copies, waits for them, and re-layouts, crop(): return x[..., cut:x.shape[-2] - cut, cut:x.shape[-1] - cut]  2.63 us
    ppermute x1, waiting for transfers between devices, azim_exchange(): before = lax.ppermute(last, 'azim', up)  2.58 us
  transfers between devices with their start and end apart: 6, of which 4 were waited for; matrix products, arithmetic and copies ran while one was open for 5% of the time, Pallas kernels for 0%

profile of v16, /device:TPU:0, one launch (start us, length us, event | category | flops | bytes accessed | tf_op | source)
XLA Modules:
  0.0 49.6 jit_solution(16997337147470426882)
XLA Ops:
  0.6 0.8 %convert_element_type.202 = f32[4,16,256]{2,1,0:T(8,128)S(1)} convert(s32[4,16,256]{2,1,0:T(8,128)} %param.7) | non-fusion elementwise | flops 16384 | bytes 131072 | tf_op jit(solution)/shard_map/convert_element_type | solution.py:265
  1.5 0.8 %convert_element_type.201 = f32[4,16,256]{2,1,0:T(8,128)S(1)} convert(s32[4,16,256]{2,1,0:T(8,128)} %param.5) | non-fusion elementwise | flops 16384 | bytes 131072 | tf_op jit(solution)/shard_map/convert_element_type | solution.py:265
  2.4 1.0 %fusion.188 = (f32[4,12,256]{2,1,0:T(8,128)S(1)}, f32[4,12,256]{2,1,0:T(8,128)S(1)}) fusion(f32[4,16,256]{2,1,0:T(8,128)} %param.4), kind=kLoop, calls=%fused_computation.442 | loop fusion | bytes 196608 | tf_op jit(solution)/shard_map/slice | solution.py:38
  3.3 0.8 %fusion.190 = (f32[4,6,256]{2,1,0:T(8,128)S(1)}, f32[4,6,256]{2,1,0:T(8,128)S(1)}, f32[4,6,256]{2,1,0:T(8,128)S(1)}, f32[4,6,256]{2,1,0:T(8,128)S(1)}) fusion(f32[4,16,256]{2,1,0:T(8,128)} %param.6, f32[4,16,256]{2,1,0:T(8,128)S(1)} %convert_element_type.202), kind=kLoop, calls=%fused_computation.444 | loop fusion | bytes 196608 | tf_op jit(solution)/shard_map/slice | solution.py:38
  4.2 3.0 %collective-permute-start = (f32[4,35,256]{2,1,0:T(8,128)S(1)}, f32[4,35,256]{2,1,0:T(8,128)S(1)}, u32[]{:S(2)}, u32[]{:S(2)}) collective-permute-start(f32[4,35,256]{2,1,0:T(8,128)S(1)} %pad_maximum_fusion.1), channel_id=1, source_target_pairs={{0,8},{8,16},{16,24},{24,0},{1,9},{9,17},{17,25},{25,1},{2,10},{10... | collective-permute-start | bytes 430088 | tf_op jit(solution)/shard_map/ppermute | solution.py:39
  7.2 1.0 %collective-permute-start.1 = (f32[4,35,256]{2,1,0:T(8,128)S(1)}, f32[4,35,256]{2,1,0:T(8,128)S(1)}, u32[]{:S(2)}, u32[]{:S(2)}) collective-permute-start(f32[4,35,256]{2,1,0:T(8,128)S(1)} %pad_maximum_fusion.2), channel_id=1, source_target_pairs={{8,0},{16,8},{24,16},{0,24},{9,1},{17,9},{25,17},{1,25},{10,2},{18... | collective-permute-start | bytes 430088 | tf_op jit(solution)/shard_map/ppermute | solution.py:40
  8.7 0.1 fusion.168
  8.8 0.1 fusion.164
  9.1 0.1 fusion.167
  9.7 0.1 broadcast_add_fusion.4
  10.3 0.1 broadcast_add_fusion
  10.5 2.6 %collective-permute-done = f32[4,35,256]{2,1,0:T(8,128)S(1)} collective-permute-done((f32[4,35,256]{2,1,0:T(8,128)S(1)}, f32[4,35,256]{2,1,0:T(8,128)S(1)}, u32[]{:S(2)}, u32[]{:S(2)}) %collective-permute-start) | collective-permute-done | bytes 143392 | tf_op jit(solution)/shard_map/ppermute | solution.py:39
  13.1 2.9 %collective-permute-done.1 = f32[4,35,256]{2,1,0:T(8,128)S(1)} collective-permute-done((f32[4,35,256]{2,1,0:T(8,128)S(1)}, f32[4,35,256]{2,1,0:T(8,128)S(1)}, u32[]{:S(2)}, u32[]{:S(2)}) %collective-permute-start.1) | collective-permute-done | bytes 143392 | tf_op jit(solution)/shard_map/ppermute | solution.py:40
  16.1 0.9 %concatenate.74 = f32[4,134,256]{2,1,0:T(8,128)S(1)} concatenate(f32[4,12,256]{2,1,0:T(8,128)S(1)} %slice.916, f32[4,16,256]{2,1,0:T(8,128)S(1)} %copy-done, f32[4,12,256]{2,1,0:T(8,128)S(1)} %slice.919, f32[4,11,256]{2,1,0:T(8,128)S(1)} %slice.920, f32[4,16,256]{2,1,0:T(8,128)S(1)} %convert_element_type.201, f32[4,11,256]{2,1,0:T(8,128)S(1)} %slice.921, ...), dimensions={1} | concatenate | bytes 1097728 | tf_op jit(solution)/shard_map/concatenate | solution.py:268
  17.1 0.1 slice_select_fusion.2
  17.2 0.7 %collective-permute-start.3 = (f32[1,4,134,12]{3,2,1,0:T(8,128)S(1)}, f32[1,4,134,12]{3,2,1,0:T(8,128)S(1)}, u32[]{:S(2)}, u32[]{:S(2)}) collective-permute-start(f32[1,4,134,12]{3,2,1,0:T(8,128)S(1)} %get-tuple-element.64), channel_id=1, source_target_pairs={{1,2},{2,1},{3,4},{4,3},{5,6},{6,5},{9,10},{10,9},{11,12},{12,11},... | collective-permute-start | bytes 77192 | tf_op jit(solution)/shard_map/ppermute | solution.py:93
  17.9 4.7 %collective-permute-start.2 = (f32[1,4,134,12]{3,2,1,0:T(8,128)S(1)}, f32[1,4,134,12]{3,2,1,0:T(8,128)S(1)}, u32[]{:S(2)}, u32[]{:S(2)}) collective-permute-start(f32[1,4,134,12]{3,2,1,0:T(8,128)S(1)} %get-tuple-element.63), channel_id=1, source_target_pairs={{0,2},{3,1},{2,4},{5,3},{4,6},{7,5},{8,10},{11,9},{10,12},{13,11},... | collective-permute-start | bytes 77192 | tf_op jit(solution)/shard_map/ppermute | solution.py:94
  22.6 0.2 fusion.184
  22.9 0.2 copy.46
  23.2 4.0 %collective-permute-done.2 = f32[1,4,134,12]{3,2,1,0:T(8,128)S(1)} collective-permute-done((f32[1,4,134,12]{3,2,1,0:T(8,128)S(1)}, f32[1,4,134,12]{3,2,1,0:T(8,128)S(1)}, u32[]{:S(2)}, u32[]{:S(2)}) %collective-permute-start.2) | collective-permute-done | bytes 25760 | tf_op jit(solution)/shard_map/ppermute | solution.py:94
  27.3 0.1 copy.47
  27.4 0.5 %maximum_bitcast_fusion.2 = (f32[4,134,152]{2,1,0:T(8,128)S(1)}, f32[4,134,152]{2,1,0:T(8,128)S(1)}, f32[4,134,152]{2,1,0:T(8,128)S(1)}, f32[4,134,152]{2,1,0:T(8,128)S(1)}) fusion(f32[1,4,134,12]{3,2,1,0:T(8,128)S(1)} %get-tuple-element.61, f32[1,4,134,140]{3,2,1,0:T(8,128)S(1)} %copy.47, f32[1,4,134,12]{3,2,1,0:T(8,128)S(1)} %get-tuple-element.62, ...), kind=kLoop, calls=%fused_computation.78 | loop fusion | flops 325888 | bytes 2255488 | tf_op jit(solution)/shard_map/concatenate | solution.py:125
  27.9 0.1 maximum_select_fusion
  28.0 0.1 slice.935
  28.2 0.4 multiply_reduce_fusion.2
  28.6 0.4 slice.957
  29.0 0.2 slice.952
  29.2 0.6 %fusion.46 = (f32[8,38,150]{2,1,0:T(8,128)S(1)}, f32[8,38,150]{2,1,0:T(8,128)S(1)}, f32[8,38,150]{2,1,0:T(8,128)S(1)}) fusion(f32[8,40,152]{2,1,0:T(8,128)S(1)} %slice_select_fusion, f32[8,38,150]{2,1,0:T(8,128)S(1)} %get-tuple-element.13, f32[8,38,150]{2,1,0:T(8,128)S(1)} %get-tuple-element.14, f32[8,150]{1,0:T(8,128)S(1)} %broadcast_add_fusion.10, ...), kind=kLoop, calls=%fused_computation.104 | loop fusion | flops 1048800 | bytes 3179904 | tf_op jit(solution)/shard_map/sub | solution.py:296
  29.8 0.2 slice.951
  30.0 0.2 slice.949
  30.1 2.8 %multiply_reduce_fusion.1 = (f32[8,34,146]{2,1,0:T(8,128)S(1)}, f32[8,34,146]{2,1,0:T(8,128)S(1)}, f32[4,8,34,146]{3,2,1,0:T(8,128)S(1)}) fusion(f32[8,146]{1,0:T(8,128)S(1)} %broadcast_add_fusion.8, f32[4,8,36,148]{3,2,1,0:T(8,128)S(1)} %slice.957, f32[4,8,38,150]{3,2,1,0:T(8,128)S(1)} %get-tuple-element.70, f32[146]{0:T(256)S(1)} %get-tuple-element.148, ...), kind=kLoop, calls=%fused_computation.23 | loop fusion | flops 3732928 | bytes 5930538 | tf_op jit(solution)/shard_map/reduce_sum | solution.py:209
  32.9 0.4 slice.979
  33.3 0.2 mul.1272
  33.4 0.1 slice.974
  33.6 0.6 %fusion.52 = f32[8,36,148]{2,1,0:T(8,128)S(1)} fusion(f32[8,38,150]{2,1,0:T(8,128)S(1)} %get-tuple-element.80, f32[8,40,152]{2,1,0:T(8,128)S(1)} %slice_select_fusion, f32[8,148]{1,0:T(8,128)S(1)} %broadcast_add_fusion.9, f32[148]{0:T(256)S(1)} %get-tuple-element.140, f32[148]{0:T(256)S(1)} %get-tuple-element.138, f32[148]{0:T(256)S(1)} %get-tuple-element.137, ...), kind=kLoop, calls=%fused_computation.110 | loop fusion | flops 554112 | bytes 2476032 | tf_op jit(solution)/shard_map/jit(_where)/select_n | solution.py:173
  34.2 0.6 %slice_subtract_fusion.1 = (f32[8,34,146]{2,1,0:T(8,128)S(1)}, f32[8,34,146]{2,1,0:T(8,128)S(1)}, f32[8,34,146]{2,1,0:T(8,128)S(1)}) fusion(f32[8,36,148]{2,1,0:T(8,128)S(1)} %fusion.52, f32[8,146]{1,0:T(8,128)S(1)} %broadcast_add_fusion.8, f32[146]{0:T(256)S(1)} %get-tuple-element.148, f32[146]{0:T(256)S(1)} %get-tuple-element.146, ...), kind=kLoop, calls=%fused_computation.136 | loop fusion | flops 913376 | bytes 3109248 | tf_op jit(solution)/shard_map/sub | solution.py:210
  34.8 0.1 slice.973
  35.0 0.1 slice.971
  35.1 0.5 %fusion.85 = f32[8,32,144]{2,1,0:T(8,128)S(1)} fusion(f32[8,34,146]{2,1,0:T(8,128)S(1)} %get-tuple-element.79, f32[8,36,148]{2,1,0:T(8,128)S(1)} %fusion.52, f32[8,144]{1,0:T(8,128)S(1)} %broadcast_add_fusion.7, f32[144]{0:T(256)S(1)} %get-tuple-element.136, f32[144]{0:T(256)S(1)} %get-tuple-element.134, f32[144]{0:T(256)S(1)} %get-tuple-element.133, ...), kind=kLoop, calls=%fused_computation.163 | loop fusion | flops 479232 | bytes 2059776 | tf_op jit(solution)/shard_map/jit(_where)/select_n | solution.py:173
  35.6 2.3 %multiply_reduce_fusion = (f32[8,30,142]{2,1,0:T(8,128)S(1)}, f32[8,30,142]{2,1,0:T(8,128)S(1)}, f32[4,8,30,142]{3,2,1,0:T(8,128)S(1)}) fusion(f32[8,142]{1,0:T(8,128)S(1)} %broadcast_add_fusion.6, f32[4,8,32,144]{3,2,1,0:T(8,128)S(1)} %slice.979, f32[4,8,34,146]{3,2,1,0:T(8,128)S(1)} %get-tuple-element.47, f32[142]{0:T(256)S(1)} %get-tuple-element.132, ...), kind=kLoop, calls=%fused_computation.3 | loop fusion | flops 3203520 | bytes 5094774 | tf_op jit(solution)/shard_map/reduce_sum | solution.py:208
  37.9 0.5 fusion.69
  38.4 0.9 %fusion.98 = (f32[8,28,140]{2,1,0:T(8,128)S(1)}, f32[8,28,140]{2,1,0:T(8,128)S(1)}) fusion(f32[8,134,152]{2,1,0:T(8,128)S(1)} %maximum_select_fusion, pred[140]{0:T(512)(128)(4,1)S(1)} %compare_and_fusion.11, f32[8,30,142]{2,1,0:T(8,128)S(1)} %fusion.69, f32[8,140]{1,0:T(8,128)S(1)} %broadcast_add_fusion.5, f32[140]{0:T(256)S(1)} %get-tuple-element.128, ...), kind=kLoop, calls=%fused_computation.184 | loop fusion | flops 501760 | bytes 2621952 | tf_op jit(solution)/shard_map/jit(_where)/select_n | solution.py:173
  39.2 0.5 broadcast_select_fusion.1
  39.7 0.5 %fusion.127 = (f32[8,24,136]{2,1,0:T(8,128)S(1)}, f32[8,24,136]{2,1,0:T(8,128)S(1)}) fusion(f32[8,26,138]{2,1,0:T(8,128)S(1)} %get-tuple-element.29, f32[8,32,144]{2,1,0:T(8,128)S(1)} %fusion.85, f32[8,28,140]{2,1,0:T(8,128)S(1)} %get-tuple-element.34, f32[8,26,138]{2,1,0:T(8,128)S(1)} %get-tuple-element.30, f32[8,136]{1,0:T(8,128)S(1)} %broadcast_add_fusion.3, ...), kind=kLoop, calls=%fused_computation.237 | loop fusion | flops 548352 | bytes 2055680 | tf_op jit(solution)/shard_map/jit(_where)/select_n | solution.py:173
  40.2 0.1 slice.1015
  40.4 0.3 slice.1013
  40.7 0.6 %fusion.183 = (f32[4,8,20,132]{3,2,1,0:T(8,128)S(1)}, f32[4,8,20,132]{3,2,1,0:T(8,128)S(1)}, f32[8,20,132]{2,1,0:T(8,128)S(1)}, f32[8,20,132]{2,1,0:T(8,128)S(1)...) fusion(f32[4,8,34,146]{3,2,1,0:T(8,128)S(1)} %get-tuple-element.47, f32[8,20,132]{2,1,0:T(8,128)S(1)} %slice.1015, ...), kind=kLoop, calls=%fused_computation.437 | loop fusion | flops 1034880 | bytes 2027652 | tf_op jit(solution)/shard_map/slice | solution.py:161
  41.3 0.1 slice.1038
  41.4 0.4 broadcast_select_fusion.3
  41.8 0.5 %fusion.116 = (f32[8,20,132]{2,1,0:T(8,128)S(1)}, f32[8,20,132]{2,1,0:T(8,128)S(1)}, f32[8,20,132]{2,1,0:T(8,128)S(1)}, f32[8,20,132]{2,1,0:T(8,128)S(1)}) fusion(f32[8,22,134]{2,1,0:T(8,128)S(1)} %get-tuple-element.19, f32[8,20,132]{2,1,0:T(8,128)S(1)} %get-tuple-element.54, f32[8,24,136]{2,1,0:T(8,128)S(1)} %get-tuple-element.85, ...), kind=kLoop, calls=%fused_computation.226 | loop fusion | flops 528000 | bytes 2315776 | tf_op jit(solution)/shard_map/jit(_where)/select_n | solution.py:173
  42.3 0.1 slice.1037
  42.4 0.1 slice.1035
  42.6 0.1 slice.1033
  42.7 0.1 slice.1032
  42.8 1.7 %fusion.34 = f32[4,8,18,130]{3,2,1,0:T(8,128)S(1)} fusion(f32[4,8,20,132]{3,2,1,0:T(8,128)S(1)} %get-tuple-element.55, f32[4,8,20,132]{3,2,1,0:T(8,128)S(1)} %get-tuple-element.51, f32[4,8,20,132]{3,2,1,0:T(8,128)S(1)} %get-tuple-element.50, f32[8,18,130]{2,1,0:T(8,128)S(1)} %slice.1038, f32[8,18,130]{2,1,0:T(8,128)S(1)} %slice.1037, ...), kind=kLoop, calls=%fused_computation.60 | loop fusion | flops 1722240 | bytes 7585792 | tf_op jit(solution)/shard_map/jit(_where)/select_n | solution.py:173
  44.5 0.2 multiply_reduce_fusion.9
  44.8 0.4 broadcast_select_fusion.2
  45.1 0.1 slice_bitcast_fusion.2
  45.2 0.2 fusion.156
  45.5 0.6 %fusion.90 = f32[4,8,16,128]{3,2,1,0:T(8,128)S(1)} fusion(f32[4,8,18,130]{3,2,1,0:T(8,128)S(1)} %fusion.34, f32[4,8,38,150]{3,2,1,0:T(8,128)S(1)} %get-tuple-element.70, f32[8,128]{1,0:T(8,128)S(1)} %broadcast_add_fusion.11, f32[128]{0:T(128)S(1)} %get-tuple-element.108, f32[128]{0:T(128)S(1)} %get-tuple-element.106, f32[128]{0:T(128)S(1)} %get-tuple-element.105, ...), kind=kLoop, calls=%fused_computation.168 | loop fusion | flops 1572864 | bytes 2954752 | tf_op jit(solution)/shard_map/add | solution.py:342
  46.1 1.0 %collective-permute-start.5 = (f32[6,4,16,128]{3,2,1,0:T(8,128)S(1)}, f32[6,4,16,128]{3,2,1,0:T(8,128)S(1)}, u32[]{:S(2)}, u32[]{:S(2)}) collective-permute-start(f32[6,4,16,128]{3,2,1,0:T(8,128)S(1)} %get-tuple-element.68), channel_id=1, source_target_pairs={{0,1},{1,0},{2,3},{3,2},{4,5},{5,4},{6,7},{7,6},{8,9},{9,8},{10,11... | collective-permute-start | bytes 589832 | tf_op jit(solution)/shard_map/ppermute | solution.py:142
  47.1 1.1 %collective-permute-done.5 = f32[6,4,16,128]{3,2,1,0:T(8,128)S(1)} collective-permute-done((f32[6,4,16,128]{3,2,1,0:T(8,128)S(1)}, f32[6,4,16,128]{3,2,1,0:T(8,128)S(1)}, u32[]{:S(2)}, u32[]{:S(2)}) %collective-permute-start.5) | collective-permute-done | bytes 196640 | tf_op jit(solution)/shard_map/ppermute | solution.py:142
  48.2 0.7 %slice_bitcast_fusion = (f32[4,16,256]{2,1,0:T(8,128)}, f32[4,16,256]{2,1,0:T(8,128)}) fusion(f32[6,4,16,256]{3,2,1,0:T(8,128)S(1)} %maximum_select_fusion.2), kind=kLoop, calls=%fused_computation.298 | loop fusion | bytes 262144 | tf_op jit(solution)/shard_map/squeeze | solution.py:354
  48.9 0.7 %slice.1056 = f32[4,4,16,256]{3,2,1,0:T(8,128)} slice(f32[6,4,16,256]{3,2,1,0:T(8,128)S(1)} %maximum_select_fusion.2), slice={[2:6], [0:4], [0:16], [0:256]} | slice | bytes 524288 | tf_op jit(solution)/shard_map/slice | solution.py:354
  (80 shorter events, 2.1 us)
Async XLA Ops:
  2.3 13.8 %copy-start = (f32[4,16,256]{2,1,0:T(8,128)S(1)}, f32[4,16,256]{2,1,0:T(8,128)}, u32[]{:S(2)}) copy-start(f32[4,16,256]{2,1,0:T(8,128)} %param.4) | copy-start | bytes 196612
  2.3 13.8 %copy-start.1 = (f32[4,16,256]{2,1,0:T(8,128)S(1)}, f32[4,16,256]{2,1,0:T(8,128)}, u32[]{:S(2)}) copy-start(f32[4,16,256]{2,1,0:T(8,128)} %param.6) | copy-start | bytes 196612
  4.2 9.0 %collective-permute-start = (f32[4,35,256]{2,1,0:T(8,128)S(1)}, f32[4,35,256]{2,1,0:T(8,128)S(1)}, u32[]{:S(2)}, u32[]{:S(2)}) collective-permute-start(f32[4,35,256]{2,1,0:T(8,128)S(1)} %pad_maximum_fusion.1), channel_id=1, source_target_pairs={{0,8},{8,16},{16,24},{24,0},{1,9},{9,17},{17,25},{25,1},{2,10},{10... | collective-permute-start | bytes 430088 | tf_op jit(solution)/shard_map/ppermute | solution.py:39
  7.2 8.9 %collective-permute-start.1 = (f32[4,35,256]{2,1,0:T(8,128)S(1)}, f32[4,35,256]{2,1,0:T(8,128)S(1)}, u32[]{:S(2)}, u32[]{:S(2)}) collective-permute-start(f32[4,35,256]{2,1,0:T(8,128)S(1)} %pad_maximum_fusion.2), channel_id=1, source_target_pairs={{8,0},{16,8},{24,16},{0,24},{9,1},{17,9},{25,17},{1,25},{10,2},{18... | collective-permute-start | bytes 430088 | tf_op jit(solution)/shard_map/ppermute | solution.py:40
  17.2 6.0 %collective-permute-start.3 = (f32[1,4,134,12]{3,2,1,0:T(8,128)S(1)}, f32[1,4,134,12]{3,2,1,0:T(8,128)S(1)}, u32[]{:S(2)}, u32[]{:S(2)}) collective-permute-start(f32[1,4,134,12]{3,2,1,0:T(8,128)S(1)} %get-tuple-element.64), channel_id=1, source_target_pairs={{1,2},{2,1},{3,4},{4,3},{5,6},{6,5},{9,10},{10,9},{11,12},{12,11},... | collective-permute-start | bytes 77192 | tf_op jit(solution)/shard_map/ppermute | solution.py:93
  17.9 9.3 %collective-permute-start.2 = (f32[1,4,134,12]{3,2,1,0:T(8,128)S(1)}, f32[1,4,134,12]{3,2,1,0:T(8,128)S(1)}, u32[]{:S(2)}, u32[]{:S(2)}) collective-permute-start(f32[1,4,134,12]{3,2,1,0:T(8,128)S(1)} %get-tuple-element.63), channel_id=1, source_target_pairs={{0,2},{3,1},{2,4},{5,3},{4,6},{7,5},{8,10},{11,9},{10,12},{13,11},... | collective-permute-start | bytes 77192 | tf_op jit(solution)/shard_map/ppermute | solution.py:94
  23.1 4.2 %collective-permute-start.4 = (f32[1,4,134,140]{3,1,2,0:T(4,128)S(1)}, f32[1,4,134,140]{3,1,2,0:T(4,128)S(1)}, u32[]{:S(2)}, u32[]{:S(2)}) collective-permute-start(f32[1,4,134,140]{3,1,2,0:T(4,128)S(1)} %copy.46), channel_id=1, source_target_pairs={{0,1},{1,0},{2,3},{3,2},{4,5},{5,4},{6,7},{7,6},{8,9},{9,8},{10,11... | collective-permute-start | bytes 900488 | tf_op jit(solution)/shard_map/ppermute | solution.py:115
  46.1 2.1 %collective-permute-start.5 = (f32[6,4,16,128]{3,2,1,0:T(8,128)S(1)}, f32[6,4,16,128]{3,2,1,0:T(8,128)S(1)}, u32[]{:S(2)}, u32[]{:S(2)}) collective-permute-start(f32[6,4,16,128]{3,2,1,0:T(8,128)S(1)} %get-tuple-element.68), channel_id=1, source_target_pairs={{0,1},{1,0},{2,3},{3,2},{4,5},{5,4},{6,7},{7,6},{8,9},{9,8},{10,11... | collective-permute-start | bytes 589832 | tf_op jit(solution)/shard_map/ppermute | solution.py:142
